TPU v7x, 512 devices: a whole 4x4x16 slice. The times are simulated.
512 devices in a mesh: ctx: 32 (over y_hi, z), ch: 16 (over x, y_lo, core).
Axes of the slice: x: 4, y: 4 (y_hi: 2, y_lo: 2; y = y_hi * 2 + y_lo), z: 16, core: 2. Of those that a mesh axis runs over, the one named last changes fastest.
Arguments:
- tokens: bfloat16 [16384, 4096], P('ctx', 'ch'), may hold values from -6 to 6
- in_weight: bfloat16 [3, 4096, 4096], P(None, 'ctx', 'ch'), may hold values from -0.09375 to 0.09375
- short_taps: float32 [3, 3, 4096], P(None, None, 'ch'), may hold values from -3 to 3
- rates: float32 [4096, 16], P('ch'), may hold values from 3.0517578e-05 to 0.0333333333
- residues: float32 [4096, 16], P('ch'), may hold values from -0.4 to 0.4
- skip: float32 [4096], P('ch'), may hold values from -4 to 4
- out_weight: bfloat16 [4096, 4096], P('ch', 'ctx'), may hold values from -0.09375 to 0.09375
Outputs:
- mixed: bfloat16 [16384, 4096], P('ctx', 'ch')
All inputs are finite; a program needn't handle non-finite values.
Results may differ from a plain program's by a relative error of at most 0.023.
Values may be sent and summed in bfloat16 or wider, within the bound.
No kernel may reach another device: no remote copies, remote signals or barrier semaphores. Data moves between devices by JAX's collectives and lax.ppermute only.
A program may use at most 64 MiB of HBM per device.

v0:
```python
import jax
import jax.numpy as jnp
import numpy as np
from jax import lax
from jax.sharding import PartitionSpec as P

SHORT = 3
BLOCK = 64


def passed_along(block, axis, distance):
    devices = range(lax.axis_size(axis))
    route = [(i - distance, i) for i in devices if i - distance in devices]
    return lax.ppermute(block, axis, route)


def carried_in(array, axis, combine, identity):
    devices, position = (lax.axis_size(axis), lax.axis_index(axis))
    everything = jax.tree.map(lambda part: lax.all_gather(part, axis), array)
    start = jax.tree.map(
        lambda part, zero: jnp.broadcast_to(jnp.asarray(zero, part.dtype), part.shape),
        array,
        identity,
    )

    def hop(k, before):
        reached = k < position
        new = combine(before, jax.tree.map(lambda part: part[k], everything))
        return jax.tree.map(lambda a, b: jnp.where(reached, a, b), new, before)

    return lax.fori_loop(0, devices, hop, start)


def link_states(earlier, later):
    return (later[0] + later[1] * earlier[0], earlier[1] * later[1])


def block_terms(values, rates, residues):
    length, width = values.shape
    blocks = length // BLOCK
    where_in = jnp.arange(BLOCK, dtype=jnp.float32)
    decay_in = jnp.exp(-where_in[:, None, None] * rates[None])
    impulse = jnp.sum(residues[None] * decay_in, axis=2)
    lags = np.arange(BLOCK)[:, None] - np.arange(BLOCK)[None, :]
    toeplitz = jnp.where(jnp.asarray(lags >= 0)[:, :, None], impulse[np.maximum(lags, 0)], 0.0)
    tails = decay_in[::-1]
    heads = residues[None] * decay_in * jnp.exp(-rates)[None]
    shaped = values.reshape(blocks, BLOCK, width)
    inner = jnp.einsum("ijc,bjc->bic", toeplitz, shaped, precision=lax.Precision.HIGHEST)
    ends = jnp.einsum("jcm,bjc->bcm", tails, shaped, precision=lax.Precision.HIGHEST)
    factor = jnp.broadcast_to(jnp.exp(-BLOCK * rates)[None], ends.shape)
    states, _ = lax.associative_scan(link_states, (ends, factor))
    starts = jnp.concatenate([jnp.zeros_like(states[:1]), states[:-1]], axis=0)
    offsets = jnp.exp(-(BLOCK * jnp.arange(blocks, dtype=jnp.float32))[:, None, None] * rates[None])
    return (inner, starts, states[-1], heads, offsets)


def finish(inner, starts, heads, values, skip):
    carried = jnp.einsum("icm,bcm->bic", heads, starts, precision=lax.Precision.HIGHEST)
    return (inner + carried).reshape(values.shape) + skip[None] * values


def shards(tokens, in_weight, short_taps, rates, residues, skip, out_weight):
    rows = tokens.shape[0]
    width = in_weight.shape[2]
    whole = lax.all_gather(tokens, "ch", axis=1, tiled=True)
    proj = jnp.einsum(
        "td,jdc->jtc",
        whole,
        lax.all_gather(in_weight, "ctx", axis=1, tiled=True),
        preferred_element_type=jnp.float32,
    )
    proj = proj.astype(jnp.bfloat16)
    earlier = passed_along(proj[:, rows - (SHORT - 1) :, :], "ctx", 1)
    widened = jnp.concatenate([earlier, proj], axis=1).astype(jnp.float32)
    feats = jnp.zeros((3, rows, width), jnp.float32)
    for i in range(SHORT):
        feats = (
            feats + short_taps[i][:, None, :] * widened[:, SHORT - 1 - i : SHORT - 1 - i + rows, :]
        )
    query = feats[0]
    gated = (feats[1] * feats[2]).astype(jnp.bfloat16)
    values = gated.astype(jnp.float32)
    inner, starts, final, heads, offsets = block_terms(values, rates, residues)
    identity = (jnp.zeros_like(final), jnp.ones_like(final))
    incoming, _ = carried_in((final, jnp.exp(-rows * rates)), "ctx", link_states, identity)
    starts = starts + offsets * incoming[None]
    conv = finish(inner, starts, heads, values, skip)
    hidden = (query * conv).astype(jnp.bfloat16)
    terms = jnp.dot(
        hidden,
        lax.all_gather(out_weight, "ctx", axis=1, tiled=True),
        preferred_element_type=jnp.float32,
    )
    return lax.psum_scatter(terms.astype(jnp.bfloat16), "ch", scatter_dimension=1, tiled=True)


def solution(mesh):
    placed = (
        P("ctx", "ch"),
        P(None, "ctx", "ch"),
        P(None, None, "ch"),
        P("ch", None),
        P("ch", None),
        P("ch"),
        P("ch", "ctx"),
    )
    return jax.shard_map(
        shards, mesh=mesh, in_specs=placed, out_specs=P("ctx", "ch"), check_vma=False
    )
```

profile of v0, /device:TPU:1, one launch (start us, length us, event | category | flops | bytes accessed | tf_op | source)
XLA Modules:
  0.0 510.0 jit_solution(1679714973987235788)
XLA Ops:
  7.3 1.7 copy.90
  10.7 1.4 negate_exponential_fusion
  12.0 1.3 slice_bitcast_fusion.3
  14.2 72.7 %all-gather = f32[8192,16]{0,1:T(8,128)S(1)} all-gather(f32[256,16]{0,1:T(8,128)S(1)} %get-tuple-element.162), channel_id=2, replica_groups=mesh['ctx'=32,'ch'=16] {'ctx'}, dimensions={0}, use_global_device_ids=true | all-gather | bytes 540672 | tf_op jit(solution)/shard_map/all_gather | solution.py:19
  86.9 1.3 broadcast_clamp_fusion
  88.2 3.4 multiply_reduce_fusion
  91.6 158.9 %all-gather.5.cloned.1.call-done = bf16[3,4096,256]{1,2,0:T(8,128)(2,1)} async-done(((bf16[3,128,256]{1,2,0:T(8,128)(2,1)}), bf16[3,4096,256]{1,2,0:T(8,128)(2,1)}) %all-gather.5.cloned.1.call-update) | async-done | bytes 6291472 | tf_op jit(solution)/shard_map/all_gather | solution.py:70
  250.5 7.4 %fusion.23 = bf16[3,512,256]{1,2,0:T(8,128)(2,1)S(1)} fusion(bf16[3,4096,256]{1,2,0:T(8,128)(2,1)} %all-gather.5.cloned.1.call-done, bf16[512,4096]{1,0:T(8,128)(2,1)} %all-gather.7.cloned.1.call-done), kind=kOutput, calls=%fused_computation.26 | convolution fusion | flops 3221618688 | bytes 11272192 | tf_op jit(solution)/shard_map/td,jdc->jtc/dot_general | solution.py:67
  258.7 2.5 collective-permute-start
  261.9 2.7 rev.3
  264.6 1.0 copy.105
  265.6 1.5 copy.100
  267.1 1.0 copy.94
  268.1 17.3 %gather_fusion = f32[4096,256]{1,0:T(8,128)} fusion(f32[64,256]{1,0:T(8,128)S(1)} %copy.94, s32[4096]{0:T(1024)} %broadcast_clamp_fusion), kind=kCustom, calls=%fused_computation | custom fusion | bytes 8404992 | tf_op jit(solution)/shard_map/gather | solution.py:45
  285.4 9.2 %copy.95 = f32[64,64,256]{1,0,2:T(8,128)} copy(f32[64,64,256]{2,1,0:T(8,128)} %bitcast.65) | data formatting | bytes 8388608 | tf_op jit(solution)/shard_map/gather | solution.py:45
  294.6 1.3 maximum_convert_fusion
  296.0 1.4 fusion.12
  297.4 1.2 copy-done
  299.2 2.7 fusion.45
  301.9 1.5 copy.98
  303.7 61.0 %all_gather.20 = f32[32,256,16]{1,2,0:T(8,128)S(1)} all-gather(f32[1,256,16]{1,2,0:T(8,128)S(1)} %slice.192), channel_id=1, replica_groups=mesh['ctx'=32,'ch'=16] {'ctx'}, dimensions={0}, use_global_device_ids=true | all-gather | bytes 540672 | tf_op jit(solution)/shard_map/all_gather | solution.py:19
  364.7 30.9 %while.14 = (s32[]{:T(128)}, f32[256,16]{0,1:T(8,128)S(1)}, s32[]{:T(128)}, f32[32,256,16]{1,2,0:T(8,128)S(1)}, f32[32,256,16]{1,0,2:T(8,128)}, /*index=5*/s32[]{:T(128)}, s32[]{:T(128)}) while((s32[]{:T(128)}, f32[256,16]{0,1:T(8,128)S(1)}, s32[]{:T(128)}, f32[32,256,16]{1,2,0:T(8,128)S(1)}, f32[32,256,16]{1,0,2:T(8,128)}, ...), condition=%wide.region_2.3_spmd.clone, body=%wide.region_1.2_spmd.clone.sunk | while | flops 16388 | bytes 98409 | solution.py:31
  365.7 0.9 constant_dynamic-slice_fusion.2
  367.6 0.9 constant_dynamic-slice_fusion.2
  385.9 0.9 constant_dynamic-slice_fusion.2
  386.9 0.9 constant_dynamic-slice_fusion.2
  389.8 0.9 constant_dynamic-slice_fusion.2
  391.7 0.9 constant_dynamic-slice_fusion.2
  396.3 4.1 fusion.9
  400.4 8.9 %fusion.20 = f32[8,64,256]{1,0,2:T(8,128)S(1)} fusion(f32[256,8,64]{2,1,0:T(8,128)S(1)} %fusion.9, bf16[8,64,256]{1,0,2:T(8,128)(2,1)S(1)} %copy.96, f32[64,64,256]{1,0,2:T(8,128)} %copy.95, pred[64,64]{1,0:T(8,128)(4,1)S(1)} %bitcast.73), kind=kOutput, calls=%fused_computation.25 | convolution fusion | flops 101842944 | bytes 5509120 | tf_op jit(solution)/shard_map/ijc,bjc->bic/dot_general | solution.py:49
  410.0 5.2 %convolution_convert_fusion = bf16[512,4096]{1,0:T(8,128)(2,1)} fusion(bf16[256,4096]{1,0:T(8,128)(2,1)} %all-gather.9.cloned.1.call-done, f32[3,512,256]{1,2,0:T(8,128)} %copy-done, f32[512,256]{0,1:T(8,128)S(1)} %copy.103, bf16[1,512,256]{1,2,0:T(8,128)(2,1)S(1)} %fusion.30, f32[256]{0:T(256)S(1)} %copy-done.10), kind=kOutput, calls=%fused_computation.8 | convolution fusion | flops 1076494336 | bytes 7603200 | tf_op jit(solution)/shard_map/dot_general | solution.py:90
  415.2 88.2 %reduce-scatter.2.cloned.1.call-done = bf16[512,256]{1,0:T(8,128)(2,1)} async-done(((bf16[512,4096]{1,0:T(8,128)(2,1)}), bf16[512,256]{1,0:T(8,128)(2,1)}) %reduce-scatter.2.cloned.1.call-update) | async-done | bytes 262160 | tf_op jit(solution)/shard_map/reduce_scatter | solution.py:95
  (124 shorter events, 30.9 us)
Async XLA Ops:
  6.5 85.1 %all-gather.7.cloned.1.call-start = ((), (), s32[]{:S(2)}) async-start(), calls=%async_computation.2 | async-start | bytes 4456448 | tf_op jit(solution)/shard_map/all_gather | solution.py:66
  7.3 243.2 %all-gather.5.cloned.1.call-start = ((), (), s32[]{:S(2)}) async-start(), calls=%async_computation.1 | async-start | bytes 6488064 | tf_op jit(solution)/shard_map/all_gather | solution.py:70
  9.1 400.9 %all-gather.9.cloned.1.call-start = ((), (), s32[]{:S(2)}) async-start(), calls=%async_computation.3 | async-start | bytes 2162688 | tf_op jit(solution)/shard_map/all_gather | solution.py:92
  9.8 493.7 %reduce-scatter.2.cloned.1.call-start = ((), (), s32[]{:S(2)}) async-start(), calls=%async_computation.4 | async-start | bytes 4456448 | tf_op jit(solution)/shard_map/reduce_scatter | solution.py:95
  9.9 248.1 %copy-start.12 = (f32[64]{0:T(128)}, f32[64]{0:T(128)S(1)}, u32[]{:S(2)}) copy-start(f32[64]{0:T(128)S(1)} %iota_negate_fusion) | copy-start | bytes 772
  14.2 243.7 %copy-start.1 = (f32[256,16]{1,0:T(8,128)}, f32[256,16]{1,0:T(8,128)S(1)}, u32[]{:S(2)}) copy-start(f32[256,16]{1,0:T(8,128)S(1)} %copy.92) | copy-start | bytes 49156
  258.7 35.9 %collective-permute-start = (bf16[3,2,256]{1,2,0:T(8,128)(2,1)}, bf16[3,2,256]{1,2,0:T(8,128)(2,1)}, u32[]{:S(2)}, u32[]{:S(2)}) collective-permute-start(bf16[3,2,256]{1,2,0:T(8,128)(2,1)} %slice.124), channel_id=1, source_target_pairs={{0,16},{16,32},{32,48},{48,64},{64,80},{80,96},{96,112},{112,128},... | collective-permute-start | bytes 9224 | tf_op jit(solution)/shard_map/ppermute | solution.py:14
  294.6 1.4 copy-start.6
  294.6 1.4 copy-start.7
  294.6 1.4 copy-start.8
  297.4 1.2 copy-start
  299.1 4.3 copy-start.4
  299.1 4.3 copy-start.5
  299.2 4.3 copy-start.3
  301.9 93.9 %copy-start.11 = (f32[8]{0:T(128)S(1)}, f32[8]{0:T(128)}, u32[]{:S(2)}) copy-start(f32[8]{0:T(128)} %multiply_negate_fusion) | copy-start | bytes 100
  303.6 92.7 %copy-start.2 = (f32[256,16]{1,0:T(8,128)S(1)}, f32[256,16]{1,0:T(8,128)}, u32[]{:S(2)}) copy-start(f32[256,16]{1,0:T(8,128)} %copy-done.1) | copy-start | bytes 49156
  396.3 4.1 copy-start.9
  409.3 0.7 copy-start.10
Sparse Core Ops, SparseCore 0:
  9.4 60.8 all-gather.6
  73.2 177.2 all-gather.4
  253.4 139.8 all-gather.8
  415.4 88.0 reduce-scatter.1
where the time goes:
time: 513 us; the launch traced here: 510 us
  waiting for transfers between devices  249 us (49%)
  blocking collectives  134 us (26%)
  local copies, waits for them, and re-layouts  72.2 us (14%)
  matrix products  28.4 us (6%)
  between operations  13.5 us (3%)
  other arithmetic  10 us (2%)
    all_gather x1, waiting for transfers between devices, shards(): lax.all_gather(in_weight, 'ctx', axis=1, tiled=True)  159 us
    all_gather x2, blocking collectives, carried_in(): everything = jax.tree.map(lambda part: lax.all_gather(part, axis), array)  134 us
    reduce_scatter x1, waiting for transfers between devices, shards(): lax.psum_scatter(terms.astype(jnp.bfloat16), 'ch', scatter_dimension=1, t...  88.2 us
    dynamic_slice x32, local copies, waits for them, and re-layouts, hop(): new = combine(before, jax.tree.map(lambda part: part[k], everything))  29.5 us
    gather x2, local copies, waits for them, and re-layouts, block_terms(): impulse[np.maximum(lags, 0)]  26.5 us
  transfers between devices with their start and end apart: 5, of which 2 were waited for; matrix products, arithmetic and copies ran while one was open for 20% of the time, Pallas kernels for 0%

commit v1 on v0

v1 whole, which is shorter than its diff:
```python
import jax
import jax.numpy as jnp
import numpy as np
from jax import lax
from jax.sharding import Mesh
from jax.sharding import PartitionSpec as P

SHORT = 3
BLOCK = 64
CTX = ("yh", "z")
CH = ("x", "ylo", "core")


def passed_along(block, axis, count, distance):
    route = [(i - distance, i) for i in range(count) if i - distance >= 0]
    return lax.ppermute(block, axis, route)


def carried_in(final, rates, rows, count):
    incoming = passed_along(final, CTX, count, 1)
    shift = 1
    while shift < count:
        incoming = incoming + jnp.exp(-(shift * rows) * rates) * passed_along(incoming, CTX, count, shift)
        shift *= 2
    return incoming


def block_terms(values, rates, residues):
    length, width = values.shape
    blocks = length // BLOCK
    where_in = jnp.arange(BLOCK, dtype=jnp.float32)
    decay_in = jnp.exp(-where_in[:, None, None] * rates[None])
    impulse = jnp.sum(residues[None] * decay_in, axis=2)
    ii = lax.broadcasted_iota(jnp.int32, (BLOCK, BLOCK, BLOCK), 0)
    jj = lax.broadcasted_iota(jnp.int32, (BLOCK, BLOCK, BLOCK), 1)
    ll = lax.broadcasted_iota(jnp.int32, (BLOCK, BLOCK, BLOCK), 2)
    pick = (ii - jj == ll).astype(jnp.float32).reshape(BLOCK * BLOCK, BLOCK)
    toeplitz = jnp.dot(pick, impulse, precision=lax.Precision.HIGHEST).reshape(BLOCK, BLOCK, width)
    tails = decay_in[::-1]
    heads = residues[None] * decay_in * jnp.exp(-rates)[None]
    shaped = values.reshape(blocks, BLOCK, width)
    inner = jnp.einsum("ijc,bjc->bic", toeplitz, shaped, precision=lax.Precision.HIGHEST)
    ends = jnp.einsum("jcm,bjc->bcm", tails, shaped, precision=lax.Precision.HIGHEST)
    factor = jnp.broadcast_to(jnp.exp(-BLOCK * rates)[None], ends.shape)
    states, _ = lax.associative_scan(link_states, (ends, factor))
    starts = jnp.concatenate([jnp.zeros_like(states[:1]), states[:-1]], axis=0)
    offsets = jnp.exp(-(BLOCK * jnp.arange(blocks, dtype=jnp.float32))[:, None, None] * rates[None])
    return (inner, starts, states[-1], heads, offsets)


def link_states(earlier, later):
    return (later[0] + later[1] * earlier[0], earlier[1] * later[1])


def finish(inner, starts, heads, values, skip):
    carried = jnp.einsum("icm,bcm->bic", heads, starts, precision=lax.Precision.HIGHEST)
    return (inner + carried).reshape(values.shape) + skip[None] * values


def gathered_tokens(tokens):
    rows, width = tokens.shape
    parts = lax.all_gather(tokens, "x")
    parts = lax.all_gather(parts, "ylo")
    parts = lax.all_gather(parts, "core")
    return jnp.transpose(parts, (3, 2, 1, 0, 4)).reshape(rows, -1)


def scattered_terms(terms, sizes):
    rows, total = terms.shape
    x, ylo, core = sizes
    split = terms.reshape(rows, x, ylo, core, total // (x * ylo * core))
    split = lax.psum_scatter(split, "core", scatter_dimension=3, tiled=False)
    split = lax.psum_scatter(split, "ylo", scatter_dimension=2, tiled=False)
    split = lax.psum_scatter(split, "x", scatter_dimension=1, tiled=False)
    return split


def make_shards(count, sizes):
    def shards(tokens, in_weight, short_taps, rates, residues, skip, out_weight):
        rows = tokens.shape[0]
        width = in_weight.shape[2]
        whole = gathered_tokens(tokens)
        weight = lax.all_gather(in_weight, "z", axis=1, tiled=True)
        weight = lax.all_gather(weight, "yh", axis=1, tiled=True)
        proj = jnp.einsum("td,jdc->jtc", whole, weight, preferred_element_type=jnp.float32)
        proj = proj.astype(jnp.bfloat16)
        earlier = passed_along(proj[:, rows - (SHORT - 1) :, :], CTX, count, 1)
        widened = jnp.concatenate([earlier, proj], axis=1).astype(jnp.float32)
        feats = jnp.zeros((3, rows, width), jnp.float32)
        for i in range(SHORT):
            feats = (
                feats + short_taps[i][:, None, :] * widened[:, SHORT - 1 - i : SHORT - 1 - i + rows, :]
            )
        query = feats[0]
        gated = (feats[1] * feats[2]).astype(jnp.bfloat16)
        values = gated.astype(jnp.float32)
        inner, starts, final, heads, offsets = block_terms(values, rates, residues)
        incoming = carried_in(final, rates, rows, count)
        starts = starts + offsets * incoming[None]
        conv = finish(inner, starts, heads, values, skip)
        hidden = (query * conv).astype(jnp.bfloat16)
        out_w = lax.all_gather(out_weight, "z", axis=1, tiled=True)
        out_w = lax.all_gather(out_w, "yh", axis=1, tiled=True)
        terms = jnp.dot(hidden, out_w, preferred_element_type=jnp.float32)
        mixed = scattered_terms(terms.astype(jnp.bfloat16), sizes)
        return mixed.reshape(rows, -1)

    return shards


def solution(mesh):
    count = mesh.shape["ctx"]
    lanes = mesh.shape["ch"]
    sizes = (lanes // 4, 2, 2)
    fine = Mesh(mesh.devices.reshape(2, count // 2, *sizes), CTX + CH)
    placed = (
        P(CTX, CH),
        P(None, CTX, CH),
        P(None, None, CH),
        P(CH, None),
        P(CH, None),
        P(CH),
        P(CH, CTX),
    )
    return jax.shard_map(
        make_shards(count, sizes), mesh=fine, in_specs=placed, out_specs=P(CTX, CH), check_vma=False
    )
```

time: 513 us -> 546 us (1.064)
  waiting for transfers between devices: 249 us -> 398 us
  blocking collectives: 134 us -> 0 us
  starting transfers between devices: 2.67 us -> 46.7 us
  local copies, waits for them, and re-layouts: 72.2 us -> 48.9 us
    all_gather x2 -> x0, blocking collectives: 134 us -> none  [carried_in(): everything = jax.tree.map(lambda part: lax.all_gather(part, axis), array)]
    all_gather x3 -> x7, waiting for transfers between devices: 159 us -> 289 us  [the longest x1 81 us: shards(): weight = lax.all_gather(in_weight, 'z', axis=1, tiled=True)]
    ppermute x1 -> x7, starting transfers between devices: 2.55 us -> 46.4 us  [passed_along(): return lax.ppermute(block, axis, route)]
    dynamic_slice x32 -> x0, local copies, waits for them, and re-layouts: 29.5 us -> none  [hop(): new = combine(before, jax.tree.map(lambda part: part[k], everything))]
    gather x2 -> x0, local copies, waits for them, and re-layouts: 26.5 us -> none  [block_terms(): impulse[np.maximum(lags, 0)]]
    reshape x0 -> x3, local copies, waits for them, and re-layouts: none -> 21.3 us  [the longest x2 13.5 us: scattered_terms(): split = terms.reshape(rows, x, ylo, core, total // (x * ylo * core))]
    reduce_scatter x1 -> x3, waiting for transfers between devices: 88.2 us -> 103 us  [the longest x1 45.1 us: scattered_terms(): split = lax.psum_scatter(split, 'ylo', scatter_dimension=2, tiled=False)]
    dot_general x0 -> x1, local copies, waits for them, and re-layouts: none -> 9.18 us  [block_terms(): jnp.dot(pick, impulse, precision=lax.Precision.HIGHEST)]
  transfers between devices with their start and end apart: 5 -> 17, of which waited for: 2 -> 15; matrix products, arithmetic and copies ran while one was open for 20% -> 12% of each run, Pallas kernels for 0% -> 0%
where the time goes in v1:
time: 546 us; the launch traced here: 545 us
  waiting for transfers between devices  398 us (73%)
  local copies, waits for them, and re-layouts  48.9 us (9%)
  starting transfers between devices  46.7 us (9%)
  matrix products  31.8 us (6%)
  between operations  14 us (3%)
  other arithmetic  5.54 us (1%)
    all_gather x1, waiting for transfers between devices, shards(): weight = lax.all_gather(in_weight, 'z', axis=1, tiled=True)  81 us
    all_gather x1, waiting for transfers between devices, shards(): weight = lax.all_gather(weight, 'yh', axis=1, tiled=True)  77.6 us
    ppermute x7, starting transfers between devices, passed_along(): return lax.ppermute(block, axis, route)  46.4 us
    reduce_scatter x1, waiting for transfers between devices, scattered_terms(): split = lax.psum_scatter(split, 'ylo', scatter_dimension=2, tiled=False)  45.1 us
    all_gather x1, waiting for transfers between devices, gathered_tokens(): parts = lax.all_gather(parts, 'ylo')  44.9 us
    all_gather x1, waiting for transfers between devices, gathered_tokens(): parts = lax.all_gather(tokens, 'x')  38.2 us
    reduce_scatter x1, waiting for transfers between devices, scattered_terms(): split = lax.psum_scatter(split, 'x', scatter_dimension=1, tiled=False)  33.6 us
    all_gather x1, waiting for transfers between devices, gathered_tokens(): parts = lax.all_gather(parts, 'core')  27.7 us
  transfers between devices with their start and end apart: 17, of which 15 were waited for; matrix products, arithmetic and copies ran while one was open for 12% of the time, Pallas kernels for 0%

profile of v1, /device:TPU:1, one launch (start us, length us, event | category | flops | bytes accessed | tf_op | source)
XLA Modules:
  0.0 544.6 jit_solution(18363408098054498531)
XLA Ops:
  7.3 38.2 %all-gather.19.cloned.1.call-done = bf16[2048,256]{1,0:T(8,128)(2,1)} async-done(((bf16[512,256]{1,0:T(8,128)(2,1)}), bf16[2048,256]{1,0:T(8,128)(2,1)}) %all-gather.19.cloned.1.call-update) | async-done | bytes 1048592 | tf_op jit(solution)/shard_map/all_gather | solution.py:62
  45.6 1.7 copy.121
  47.4 44.9 %all-gather.21.cloned.1.call-done = bf16[8,512,256]{2,1,0:T(8,128)(2,1)} async-done(((bf16[4,512,256]{2,1,0:T(8,128)(2,1)}), bf16[8,512,256]{2,1,0:T(8,128)(2,1)}) %all-gather.21.cloned.1.call-update) | async-done | bytes 2097168 | tf_op jit(solution)/shard_map/all_gather | solution.py:63
  92.4 81.0 %all-gather.11.cloned.1.call-done = bf16[3,2048,256]{1,2,0:T(8,128)(2,1)} async-done(((bf16[3,128,256]{1,2,0:T(8,128)(2,1)}), bf16[3,2048,256]{1,2,0:T(8,128)(2,1)}) %all-gather.11.cloned.1.call-update) | async-done | bytes 3145744 | tf_op jit(solution)/shard_map/all_gather | solution.py:83
  174.8 2.8 multiply_reduce_fusion
  177.6 27.7 %all-gather.23.cloned.1.call-done = bf16[4,4,512,256]{3,2,1,0:T(8,128)(2,1)} async-done(((bf16[2,4,512,256]{3,2,1,0:T(8,128)(2,1)}), bf16[4,4,512,256]{3,2,1,0:T(8,128)(2,1)}) %all-gather.23.cloned.1.call-update) | async-done | bytes 4194320 | tf_op jit(solution)/shard_map/all_gather | solution.py:64
  205.3 8.6 %copy.122 = bf16[512,4,2,2,256]{4,3,2,1,0:T(2,128)(2,1)} copy(bf16[512,4,2,2,256]{4,0,1,2,3:T(8,128)(2,1)} %bitcast.53) | data formatting | bytes 8388608 | tf_op jit(solution)/shard_map/transpose | solution.py:65
  213.9 7.8 %reshape.63 = bf16[512,4096,1]{1,0,2:T(8,128)(2,1)} reshape(bf16[512,4,2,2,256]{4,3,2,1,0:T(2,128)(2,1)} %copy.122) | data formatting | bytes 8388608 | tf_op jit(solution)/shard_map/reshape | solution.py:65
  221.7 77.6 %all-gather.13.cloned.1.call-done = bf16[3,4096,256]{1,2,0:T(8,128)(2,1)} async-done(((bf16[3,2048,256]{1,2,0:T(8,128)(2,1)}), bf16[3,4096,256]{1,2,0:T(8,128)(2,1)}) %all-gather.13.cloned.1.call-update) | async-done | bytes 6291472 | tf_op jit(solution)/shard_map/all_gather | solution.py:84
  299.3 7.4 %fusion.7 = bf16[3,512,256]{1,2,0:T(8,128)(2,1)S(1)} fusion(bf16[3,4096,256]{1,2,0:T(8,128)(2,1)} %all-gather.13.cloned.1.call-done, bf16[512,4096,1]{1,0,2:T(8,128)(2,1)} %reshape.63), kind=kOutput, calls=%fused_computation.16 | convolution fusion | flops 3221618688 | bytes 11272192 | tf_op jit(solution)/shard_map/td,jdc->jtc/dot_general | solution.py:85
  307.5 3.4 collective-permute-start
  310.9 2.7 rev.3
  318.1 2.7 fusion.28
  320.8 1.5 copy.130
  322.6 4.0 collective-permute-start.1
  327.4 3.6 collective-permute-start.2
  331.1 3.8 fusion.2
  334.9 6.2 %collective-permute-start.3 = (f32[256,16]{0,1:T(8,128)S(1)}, f32[256,16]{0,1:T(8,128)S(1)}, u32[]{:S(2)}, u32[]{:S(2)}) collective-permute-start(f32[256,16]{0,1:T(8,128)S(1)} %multiply_add_fusion.7), channel_id=1, source_target_pairs={{0,32},{16,48},{32,64},{48,80},{64,96},{80,112},{96,128},{112,144}... | collective-permute-start | bytes 49160 | tf_op jit(solution)/shard_map/ppermute | solution.py:16
  341.2 9.2 %copy.128 = f32[64,64,256]{1,0,2:T(8,128)} copy(f32[64,64,256]{2,1,0:T(8,128)} %fusion.2) | data formatting | bytes 8388608 | tf_op jit(solution)/shard_map/dot_general | solution.py:38
  350.4 12.2 %all-gather.15.cloned.1.call-done = bf16[256,2048]{1,0:T(8,128)(2,1)} async-done(((bf16[256,128]{1,0:T(8,128)(2,1)}), bf16[256,2048]{1,0:T(8,128)(2,1)}) %all-gather.15.cloned.1.call-update) | async-done | bytes 1048592 | tf_op jit(solution)/shard_map/all_gather | solution.py:102
  362.7 3.8 collective-permute-start.4
  367.3 10.6 %collective-permute-start.5 = (f32[256,16]{0,1:T(8,128)S(1)}, f32[256,16]{0,1:T(8,128)S(1)}, u32[]{:S(2)}, u32[]{:S(2)}) collective-permute-start(f32[256,16]{0,1:T(8,128)S(1)} %multiply_add_fusion.5), channel_id=1, source_target_pairs={{0,128},{16,144},{32,160},{48,176},{64,192},{80,208},{96,224},{112... | collective-permute-start | bytes 49160 | tf_op jit(solution)/shard_map/ppermute | solution.py:16
  378.8 14.9 %collective-permute-start.6 = (f32[256,16]{0,1:T(8,128)S(1)}, f32[256,16]{0,1:T(8,128)S(1)}, u32[]{:S(2)}, u32[]{:S(2)}) collective-permute-start(f32[256,16]{0,1:T(8,128)S(1)} %multiply_add_fusion.4), channel_id=1, source_target_pairs={{0,256},{16,272},{32,288},{48,304},{64,320},{80,336},{96,352},{112... | collective-permute-start | bytes 49160 | tf_op jit(solution)/shard_map/ppermute | solution.py:16
  395.0 3.7 fusion
  398.7 8.9 %fusion.6 = f32[8,64,256]{1,0,2:T(8,128)S(1)} fusion(f32[256,8,64]{2,1,0:T(8,128)S(1)} %fusion, bf16[8,64,256]{1,0,2:T(8,128)(2,1)S(1)} %copy.127, f32[64,64,256]{1,0,2:T(8,128)} %copy.128), kind=kOutput, calls=%fused_computation.15 | convolution fusion | flops 100794368 | bytes 5505024 | tf_op jit(solution)/shard_map/ijc,bjc->bic/dot_general | solution.py:42
  408.2 7.5 %all-gather.17.cloned.1.call-done = bf16[256,4096]{1,0:T(8,128)(2,1)} async-done(((bf16[256,2048]{1,0:T(8,128)(2,1)}), bf16[256,4096]{1,0:T(8,128)(2,1)}) %all-gather.17.cloned.1.call-update) | async-done | bytes 2097168 | tf_op jit(solution)/shard_map/all_gather | solution.py:103
  415.8 5.2 convolution_convert_fusion
  420.9 7.8 %reshape.58 = bf16[512,4,2,2,256]{4,3,2,1,0:T(2,128)(2,1)} reshape(bf16[512,4096]{1,0:T(8,128)(2,1)} %convolution_convert_fusion) | data formatting | bytes 8388608 | tf_op jit(solution)/shard_map/reshape | solution.py:71
  428.8 5.6 %copy.135 = bf16[512,4,2,2,256]{4,0,1,2,3:T(8,128)(2,1)} copy(bf16[512,4,2,2,256]{4,3,2,1,0:T(2,128)(2,1)} %reshape.58) | data formatting | bytes 8388608 | tf_op jit(solution)/shard_map/reshape | solution.py:71
  434.5 24.4 %reduce-scatter.4.cloned.1.call-done = bf16[512,4,2,1,256]{4,0,1,2,3:T(8,128)(2,1)} async-done(((bf16[512,4,2,2,256]{4,0,1,2,3:T(8,128)(2,1)}), bf16[512,4,2,1,256]{4,0,1,2,3:T(8,128)(2,1)}) %reduce-scatter.4.cloned.1.call-update) | async-done | bytes 2097168 | tf_op jit(solution)/shard_map/reduce_scatter | solution.py:72
  459.0 45.1 %reduce-scatter.6.cloned.1.call-done = bf16[512,4,1,256]{3,0,1,2:T(8,128)(2,1)} async-done(((bf16[512,4,2,256]{3,0,1,2:T(8,128)(2,1)}), bf16[512,4,1,256]{3,0,1,2:T(8,128)(2,1)}) %reduce-scatter.6.cloned.1.call-update) | async-done | bytes 1048592 | tf_op jit(solution)/shard_map/reduce_scatter | solution.py:73
  504.2 33.6 %reduce-scatter.8.cloned.1.call-done = bf16[512,1,256]{2,0,1:T(8,128)(2,1)} async-done(((bf16[512,4,256]{2,0,1:T(8,128)(2,1)}), bf16[512,1,256]{2,0,1:T(8,128)(2,1)}) %reduce-scatter.8.cloned.1.call-update) | async-done | bytes 262160 | tf_op jit(solution)/shard_map/reduce_scatter | solution.py:74
  (85 shorter events, 12.4 us)
Async XLA Ops:
  6.5 39.0 %all-gather.19.cloned.1.call-start = ((), (), s32[]{:S(2)}) async-start(), calls=%async_computation.10 | async-start | bytes 1310720 | tf_op jit(solution)/shard_map/all_gather | solution.py:62
  7.3 85.0 %all-gather.21.cloned.1.call-start = ((), (), s32[]{:S(2)}) async-start(), calls=%async_computation.11 | async-start | bytes 3145728 | tf_op jit(solution)/shard_map/all_gather | solution.py:63
  45.5 127.8 %all-gather.11.cloned.1.call-start = ((), (), s32[]{:S(2)}) async-start(), calls=%async_computation.3 | async-start | bytes 3342336 | tf_op jit(solution)/shard_map/all_gather | solution.py:83
  47.3 158.0 %all-gather.23.cloned.1.call-start = ((), (), s32[]{:S(2)}) async-start(), calls=%async_computation.12 | async-start | bytes 6291456 | tf_op jit(solution)/shard_map/all_gather | solution.py:64
  92.3 81.7 %copy-start.1 = (f32[256,16]{0,1:T(8,128)S(1)}, f32[256,16]{0,1:T(8,128)}, u32[]{:S(2)}) copy-start(f32[256,16]{0,1:T(8,128)} %param.10) | copy-start | bytes 49156
  92.3 82.4 %copy-start.5 = (f32[256,16]{0,1:T(8,128)S(1)}, f32[256,16]{0,1:T(8,128)}, u32[]{:S(2)}) copy-start(f32[256,16]{0,1:T(8,128)} %param.11) | copy-start | bytes 49156
  92.3 207.0 %all-gather.13.cloned.1.call-start = ((), (), s32[]{:S(2)}) async-start(), calls=%async_computation.4 | async-start | bytes 9437184 | tf_op jit(solution)/shard_map/all_gather | solution.py:84
  173.4 189.2 %all-gather.15.cloned.1.call-start = ((), (), s32[]{:S(2)}) async-start(), calls=%async_computation.5 | async-start | bytes 1114112 | tf_op jit(solution)/shard_map/all_gather | solution.py:102
  173.9 241.8 %all-gather.17.cloned.1.call-start = ((), (), s32[]{:S(2)}) async-start(), calls=%async_computation.6 | async-start | bytes 3145728 | tf_op jit(solution)/shard_map/all_gather | solution.py:103
  174.0 39.9 %copy-start.8 = (f32[64]{0:T(128)}, f32[64]{0:T(128)S(1)}, u32[]{:S(2)}) copy-start(f32[64]{0:T(128)S(1)} %iota_negate_fusion) | copy-start | bytes 772
  221.7 89.2 %copy-start.6 = (f32[3,3,256]{2,1,0:T(4,128)S(1)}, f32[3,3,256]{2,1,0:T(4,128)}, u32[]{:S(2)}) copy-start(f32[3,3,256]{2,1,0:T(4,128)} %param.9) | copy-start | bytes 27652
  307.5 7.0 %collective-permute-start = (bf16[3,2,256]{1,2,0:T(8,128)(2,1)}, bf16[3,2,256]{1,2,0:T(8,128)(2,1)S(1)}, u32[]{:S(2)}, u32[]{:S(2)}) collective-permute-start(bf16[3,2,256]{1,2,0:T(8,128)(2,1)} %slice.122), channel_id=1, source_target_pairs={{0,16},{16,32},{32,48},{48,64},{64,80},{80,96},{96,112},{112,128},... | collective-permute-start | bytes 9224 | tf_op jit(solution)/shard_map/ppermute | solution.py:16
  316.4 1.1 copy-start
  318.0 4.3 copy-start.2
  318.0 4.3 copy-start.4
  322.6 4.9 collective-permute-start.1
  327.4 7.5 %collective-permute-start.2 = (f32[256,16]{0,1:T(8,128)S(1)}, f32[256,16]{0,1:T(8,128)S(1)}, u32[]{:S(2)}, u32[]{:S(2)}) collective-permute-start(f32[256,16]{0,1:T(8,128)S(1)} %collective-permute-done.1), channel_id=1, source_target_pairs={{0,16},{16,32},{32,48},{48,64},{64,80},{80,96},{96,112},{112,128},... | collective-permute-start | bytes 49160 | tf_op jit(solution)/shard_map/ppermute | solution.py:16
  331.1 10.0 %copy-start.3 = (f32[256,16]{0,1:T(8,128)S(1)}, f32[256,16]{0,1:T(8,128)}, u32[]{:S(2)}) copy-start(f32[256,16]{0,1:T(8,128)} %get-tuple-element.11) | copy-start | bytes 49156
  334.9 27.7 %collective-permute-start.3 = (f32[256,16]{0,1:T(8,128)S(1)}, f32[256,16]{0,1:T(8,128)S(1)}, u32[]{:S(2)}, u32[]{:S(2)}) collective-permute-start(f32[256,16]{0,1:T(8,128)S(1)} %multiply_add_fusion.7), channel_id=1, source_target_pairs={{0,32},{16,48},{32,64},{48,80},{64,96},{80,112},{96,128},{112,144}... | collective-permute-start | bytes 49160 | tf_op jit(solution)/shard_map/ppermute | solution.py:16
  362.6 96.3 %reduce-scatter.4.cloned.1.call-start = ((), (), s32[]{:S(2)}) async-start(), calls=%async_computation.7 | async-start | bytes 6291456 | tf_op jit(solution)/shard_map/reduce_scatter | solution.py:72
  362.7 4.6 collective-permute-start.4
  367.3 11.5 %collective-permute-start.5 = (f32[256,16]{0,1:T(8,128)S(1)}, f32[256,16]{0,1:T(8,128)S(1)}, u32[]{:S(2)}, u32[]{:S(2)}) collective-permute-start(f32[256,16]{0,1:T(8,128)S(1)} %multiply_add_fusion.5), channel_id=1, source_target_pairs={{0,128},{16,144},{32,160},{48,176},{64,192},{80,208},{96,224},{112... | collective-permute-start | bytes 49160 | tf_op jit(solution)/shard_map/ppermute | solution.py:16
  378.8 15.7 %collective-permute-start.6 = (f32[256,16]{0,1:T(8,128)S(1)}, f32[256,16]{0,1:T(8,128)S(1)}, u32[]{:S(2)}, u32[]{:S(2)}) collective-permute-start(f32[256,16]{0,1:T(8,128)S(1)} %multiply_add_fusion.4), channel_id=1, source_target_pairs={{0,256},{16,272},{32,288},{48,304},{64,320},{80,336},{96,352},{112... | collective-permute-start | bytes 49160 | tf_op jit(solution)/shard_map/ppermute | solution.py:16
  407.6 8.1 %copy-start.7 = (f32[256]{0:T(256)S(1)}, f32[256]{0:T(256)}, u32[]{:S(2)}) copy-start(f32[256]{0:T(256)} %param.12) | copy-start | bytes 3076
  434.4 69.7 %reduce-scatter.6.cloned.1.call-start = ((), (), s32[]{:S(2)}) async-start(), calls=%async_computation.8 | async-start | bytes 3145728 | tf_op jit(solution)/shard_map/reduce_scatter | solution.py:73
  459.0 78.8 %reduce-scatter.8.cloned.1.call-start = ((), (), s32[]{:S(2)}) async-start(), calls=%async_computation.9 | async-start | bytes 1310720 | tf_op jit(solution)/shard_map/reduce_scatter | solution.py:74
Sparse Core Ops, SparseCore 0:
  9.5 36.0 all-gather.18
  47.6 44.6 all-gather.20
  94.3 79.0 all-gather.10
  175.3 29.9 all-gather.22
  207.3 91.9 all-gather.12
  301.1 61.3 all-gather.14
  364.7 51.0 all-gather.16
  434.6 24.3 reduce-scatter.3
  462.0 42.1 reduce-scatter.5
  506.8 30.8 reduce-scatter.7

commit v2 on v1

--- a/solution.py
+++ b/solution.py
@@ -8,7 +8,7 @@
 SHORT = 3
 BLOCK = 64
 CTX = ("yh", "z")
-CH = ("x", "ylo", "core")
+CH = "ch"
 
 
 def passed_along(block, axis, count, distance):
@@ -57,31 +57,28 @@
     return (inner + carried).reshape(values.shape) + skip[None] * values
 
 
-def gathered_tokens(tokens):
+def gathered_tokens(tokens, lanes):
     rows, width = tokens.shape
-    parts = lax.all_gather(tokens, "x")
-    parts = lax.all_gather(parts, "ylo")
-    parts = lax.all_gather(parts, "core")
-    return jnp.transpose(parts, (3, 2, 1, 0, 4)).reshape(rows, -1)
+    copies = jnp.broadcast_to(tokens[None], (lanes, rows, width))
+    parts = lax.all_to_all(copies, CH, 0, 0)
+    return jnp.transpose(parts, (1, 0, 2)).reshape(rows, lanes * width)
 
 
-def scattered_terms(terms, sizes):
+def scattered_terms(terms, lanes):
     rows, total = terms.shape
-    x, ylo, core = sizes
-    split = terms.reshape(rows, x, ylo, core, total // (x * ylo * core))
-    split = lax.psum_scatter(split, "core", scatter_dimension=3, tiled=False)
-    split = lax.psum_scatter(split, "ylo", scatter_dimension=2, tiled=False)
-    split = lax.psum_scatter(split, "x", scatter_dimension=1, tiled=False)
-    return split
+    split = terms.reshape(rows, lanes, total // lanes)
+    parts = lax.all_to_all(split, CH, 1, 1)
+    return jnp.sum(parts.astype(jnp.float32), axis=1).astype(jnp.bfloat16)
 
 
-def make_shards(count, sizes):
+def make_shards(count, lanes):
     def shards(tokens, in_weight, short_taps, rates, residues, skip, out_weight):
         rows = tokens.shape[0]
         width = in_weight.shape[2]
-        whole = gathered_tokens(tokens)
-        weight = lax.all_gather(in_weight, "z", axis=1, tiled=True)
-        weight = lax.all_gather(weight, "yh", axis=1, tiled=True)
+        whole = gathered_tokens(tokens, lanes)
+        weight = lax.all_gather(in_weight, "yh", axis=1)
+        weight = lax.all_gather(weight, "z", axis=2)
+        weight = weight.reshape(3, -1, width)
         proj = jnp.einsum("td,jdc->jtc", whole, weight, preferred_element_type=jnp.float32)
         proj = proj.astype(jnp.bfloat16)
         earlier = passed_along(proj[:, rows - (SHORT - 1) :, :], CTX, count, 1)
@@ -99,11 +96,11 @@
         starts = starts + offsets * incoming[None]
         conv = finish(inner, starts, heads, values, skip)
         hidden = (query * conv).astype(jnp.bfloat16)
-        out_w = lax.all_gather(out_weight, "z", axis=1, tiled=True)
-        out_w = lax.all_gather(out_w, "yh", axis=1, tiled=True)
+        out_w = lax.all_gather(out_weight, "yh", axis=1)
+        out_w = lax.all_gather(out_w, "z", axis=2)
+        out_w = out_w.reshape(out_weight.shape[0], -1)
         terms = jnp.dot(hidden, out_w, preferred_element_type=jnp.float32)
-        mixed = scattered_terms(terms.astype(jnp.bfloat16), sizes)
-        return mixed.reshape(rows, -1)
+        return scattered_terms(terms.astype(jnp.bfloat16), lanes)
 
     return shards
 
@@ -111,8 +108,7 @@
 def solution(mesh):
     count = mesh.shape["ctx"]
     lanes = mesh.shape["ch"]
-    sizes = (lanes // 4, 2, 2)
-    fine = Mesh(mesh.devices.reshape(2, count // 2, *sizes), CTX + CH)
+    fine = Mesh(mesh.devices.reshape(2, count // 2, lanes), CTX + (CH,))
     placed = (
         P(CTX, CH),
         P(None, CTX, CH),
@@ -123,5 +119,5 @@
         P(CH, CTX),
     )
     return jax.shard_map(
-        make_shards(count, sizes), mesh=fine, in_specs=placed, out_specs=P(CTX, CH), check_vma=False
+        make_shards(count, lanes), mesh=fine, in_specs=placed, out_specs=P(CTX, CH), check_vma=False
     )

time: 546 us -> 411 us (0.75)
  waiting for transfers between devices: 398 us -> 147 us
  blocking collectives: 0 us -> 95.4 us
  starting transfers between devices: 46.7 us -> 58.2 us
    all_gather x7 -> x2, waiting for transfers between devices: 289 us -> 113 us  [the longest x1 84.5 us: shards(): weight = lax.all_gather(weight, 'z', axis=2)]
    reduce_scatter x3 -> x0, waiting for transfers between devices: 103 us -> none  [the longest x1 45.1 us: scattered_terms(): split = lax.psum_scatter(split, 'ylo', scatter_dimension=2, tiled=False)]
    all_to_all x0 -> x1, blocking collectives: none -> 68.3 us  [scattered_terms(): parts = lax.all_to_all(split, CH, 1, 1)]
    all_to_all x0 -> x1, waiting for transfers between devices: none -> 29 us  [gathered_tokens(): parts = lax.all_to_all(copies, CH, 0, 0)]
    all_gather x0 -> x2, blocking collectives: none -> 27.1 us  [the longest x1 19.3 us: shards(): out_w = lax.all_gather(out_weight, 'yh', axis=1)]
    all_to_all x0 -> x1, starting transfers between devices: none -> 11.6 us  [gathered_tokens(): parts = lax.all_to_all(copies, CH, 0, 0)]
  transfers between devices with their start and end apart: 17 -> 10, of which waited for: 15 -> 8; matrix products, arithmetic and copies ran while one was open for 12% -> 16% of each run, Pallas kernels for 0% -> 0%
where the time goes in v2:
time: 411 us; the launch traced here: 409 us
  waiting for transfers between devices  147 us (36%)
  blocking collectives  95.4 us (23%)
  starting transfers between devices  58.2 us (14%)
  local copies, waits for them, and re-layouts  53.1 us (13%)
  matrix products  31 us (8%)
  between operations  13.8 us (3%)
  other arithmetic  10.9 us (3%)
    all_gather x1, waiting for transfers between devices, shards(): weight = lax.all_gather(weight, 'z', axis=2)  84.5 us
    all_to_all x1, blocking collectives, scattered_terms(): parts = lax.all_to_all(split, CH, 1, 1)  68.3 us
    ppermute x7, starting transfers between devices, passed_along(): return lax.ppermute(block, axis, route)  46.6 us
    all_to_all x1, waiting for transfers between devices, gathered_tokens(): parts = lax.all_to_all(copies, CH, 0, 0)  29 us
    all_gather x1, waiting for transfers between devices, shards(): out_w = lax.all_gather(out_w, 'z', axis=2)  28.5 us
    all_gather x1, blocking collectives, shards(): out_w = lax.all_gather(out_weight, 'yh', axis=1)  19.3 us
    all_to_all x1, starting transfers between devices, gathered_tokens(): parts = lax.all_to_all(copies, CH, 0, 0)  11.6 us
    reshape x1, local copies, waits for them, and re-layouts, shards(): weight = weight.reshape(3, -1, width)  11.1 us
  transfers between devices with their start and end apart: 10, of which 8 were waited for; matrix products, arithmetic and copies ran while one was open for 16% of the time, Pallas kernels for 0%

profile of v2, /device:TPU:1, one launch (start us, length us, event | category | flops | bytes accessed | tf_op | source)
XLA Modules:
  0.0 409.0 jit_solution(14946608970753237143)
XLA Ops:
  6.5 7.7 %all-gather = bf16[3,256,256]{2,1,0:T(8,128)(2,1)S(1)} all-gather(bf16[3,128,256]{2,1,0:T(8,128)(2,1)} %param.8), channel_id=2, replica_groups=mesh['yh'=2,'z'=16,'ch'=16] {'yh'}, dimensions={1}, use_global_device_ids=true | all-gather | bytes 589824 | tf_op jit(solution)/shard_map/all_gather | solution.py:79
  15.4 3.3 broadcast_in_dim.2
  18.7 11.6 %all-to-all-start = ((bf16[16,512,256]{2,1,0:T(8,128)(2,1)}), bf16[16,512,256]{2,1,0:T(8,128)(2,1)}, u32[]{:S(2)}, u32[]{:S(2)}) async-start(bf16[16,512,256]{2,1,0:T(8,128)(2,1)} %broadcast_in_dim.2), calls=%async_computation | async-start | bytes 8388608 | tf_op jit(solution)/shard_map/all_to_all | solution.py:63
  30.4 19.3 %all-gather.2 = bf16[256,256]{1,0:T(8,128)(2,1)S(1)} all-gather(bf16[256,128]{1,0:T(8,128)(2,1)S(1)} %copy-done.6), channel_id=4, replica_groups=mesh['yh'=2,'z'=16,'ch'=16] {'yh'}, dimensions={1}, use_global_device_ids=true | all-gather | bytes 196608 | tf_op jit(solution)/shard_map/all_gather | solution.py:99
  51.3 2.8 multiply_reduce_fusion
  54.1 29.0 %all-to-all-done = bf16[16,512,256]{2,1,0:T(8,128)(2,1)} async-done(((bf16[16,512,256]{2,1,0:T(8,128)(2,1)}), bf16[16,512,256]{2,1,0:T(8,128)(2,1)}, u32[]{:S(2)}, u32[]{:S(2)}) %all-to-all-start) | async-done | bytes 4194336 | tf_op jit(solution)/shard_map/all_to_all | solution.py:63
  83.1 6.5 %copy.119 = bf16[512,16,256]{2,1,0:T(8,128)(2,1)} copy(bf16[512,16,256]{2,0,1:T(8,128)(2,1)} %bitcast.2) | data formatting | bytes 8388608 | tf_op jit(solution)/shard_map/transpose | solution.py:64
  89.6 7.4 %reshape.78 = bf16[512,4096,1]{1,0,2:T(8,128)(2,1)} reshape(bf16[512,16,256]{2,1,0:T(8,128)(2,1)} %copy.119) | data formatting | bytes 8388608 | tf_op jit(solution)/shard_map/reshape | solution.py:64
  97.0 84.5 %all-gather.7.cloned.1.call-done = bf16[3,2,2048,256]{2,1,3,0:T(2,128)(2,1)} async-done(((bf16[3,2,128,256]{2,1,3,0:T(2,128)(2,1)}), bf16[3,2,2048,256]{2,1,3,0:T(2,128)(2,1)}) %all-gather.7.cloned.1.call-update) | async-done | bytes 6291472 | tf_op jit(solution)/shard_map/all_gather | solution.py:80
  181.5 11.1 %reshape.67 = bf16[3,4096,256]{1,2,0:T(8,128)(2,1)} reshape(bf16[3,2,2048,256]{2,1,3,0:T(2,128)(2,1)} %all-gather.7.cloned.1.call-done) | data formatting | bytes 12582912 | tf_op jit(solution)/shard_map/reshape | solution.py:81
  192.6 7.5 %fusion.7 = bf16[3,512,256]{1,2,0:T(8,128)(2,1)S(1)} fusion(bf16[3,4096,256]{1,2,0:T(8,128)(2,1)} %reshape.67, bf16[512,4096,1]{1,0,2:T(8,128)(2,1)} %reshape.78), kind=kOutput, calls=%fused_computation.17 | convolution fusion | flops 3221618688 | bytes 11272192 | tf_op jit(solution)/shard_map/td,jdc->jtc/dot_general | solution.py:82
  200.9 4.5 %collective-permute-start = (bf16[3,2,256]{1,2,0:T(8,128)(2,1)}, bf16[3,2,256]{1,2,0:T(8,128)(2,1)S(1)}, u32[]{:S(2)}, u32[]{:S(2)}) collective-permute-start(bf16[3,2,256]{1,2,0:T(8,128)(2,1)} %slice.122), channel_id=1, source_target_pairs={{0,16},{16,32},{32,48},{48,64},{64,80},{80,96},{96,112},{112,128},... | collective-permute-start | bytes 9224 | tf_op jit(solution)/shard_map/ppermute | solution.py:16
  205.4 2.7 rev.3
  208.1 2.2 collective-permute-done
  213.8 2.7 fusion.26
  216.5 1.5 copy.127
  218.3 4.1 collective-permute-start.1
  223.3 3.6 collective-permute-start.2
  226.9 3.8 fusion.2
  230.7 4.8 %collective-permute-start.3 = (f32[256,16]{0,1:T(8,128)S(1)}, f32[256,16]{0,1:T(8,128)S(1)}, u32[]{:S(2)}, u32[]{:S(2)}) collective-permute-start(f32[256,16]{0,1:T(8,128)S(1)} %multiply_add_fusion.7), channel_id=1, source_target_pairs={{0,32},{16,48},{32,64},{48,80},{64,96},{80,112},{96,128},{112,144}... | collective-permute-start | bytes 49160 | tf_op jit(solution)/shard_map/ppermute | solution.py:16
  236.8 9.2 %copy.125 = f32[64,64,256]{1,0,2:T(8,128)} copy(f32[64,64,256]{2,1,0:T(8,128)} %fusion.2) | data formatting | bytes 8388608 | tf_op jit(solution)/shard_map/dot_general | solution.py:38
  245.9 28.5 %all-gather.9.cloned.1.call-done = bf16[256,2,2048]{2,1,0:T(2,128)(2,1)} async-done(((bf16[256,2,128]{2,1,0:T(2,128)(2,1)}), bf16[256,2,2048]{2,1,0:T(2,128)(2,1)}) %all-gather.9.cloned.1.call-update) | async-done | bytes 2097168 | tf_op jit(solution)/shard_map/all_gather | solution.py:100
  274.4 2.5 copy.136
  277.0 6.7 %collective-permute-start.4 = (f32[256,16]{0,1:T(8,128)S(1)}, f32[256,16]{0,1:T(8,128)S(1)}, u32[]{:S(2)}, u32[]{:S(2)}) collective-permute-start(f32[256,16]{0,1:T(8,128)S(1)} %multiply_add_fusion.6), channel_id=1, source_target_pairs={{0,64},{16,80},{32,96},{48,112},{64,128},{80,144},{96,160},{112,17... | collective-permute-start | bytes 49160 | tf_op jit(solution)/shard_map/ppermute | solution.py:16
  284.6 8.7 %collective-permute-start.5 = (f32[256,16]{0,1:T(8,128)S(1)}, f32[256,16]{0,1:T(8,128)}, u32[]{:S(2)}, u32[]{:S(2)}) collective-permute-start(f32[256,16]{0,1:T(8,128)S(1)} %multiply_add_fusion.5), channel_id=1, source_target_pairs={{0,128},{16,144},{32,160},{48,176},{64,192},{80,208},{96,224},{112... | collective-permute-start | bytes 49160 | tf_op jit(solution)/shard_map/ppermute | solution.py:16
  294.3 14.1 %collective-permute-start.6 = (f32[256,16]{0,1:T(8,128)S(1)}, f32[256,16]{0,1:T(8,128)S(1)}, u32[]{:S(2)}, u32[]{:S(2)}) collective-permute-start(f32[256,16]{0,1:T(8,128)S(1)} %multiply_add_fusion.4), channel_id=1, source_target_pairs={{0,256},{16,272},{32,288},{48,304},{64,320},{80,336},{96,352},{112... | collective-permute-start | bytes 49160 | tf_op jit(solution)/shard_map/ppermute | solution.py:16
  311.1 4.8 %fusion = f32[256,8,64]{2,1,0:T(8,128)S(1)} fusion(f32[8,256,16]{2,0,1:T(8,128)} %copy.129, f32[256,16]{1,0:T(8,128)} %copy.128, f32[256,16]{1,0:T(8,128)S(1)} %copy.122, f32[64]{0:T(128)} %copy-done.12, f32[256,16]{1,0:T(8,128)S(1)} %copy.121), kind=kOutput, calls=%fused_computation.2 | convolution fusion | flops 25952256 | bytes 704768 | tf_op jit(solution)/shard_map/icm,bcm->bic/dot_general | solution.py:56
  315.9 9.7 %fusion.6 = f32[8,64,256]{1,0,2:T(8,128)} fusion(f32[256,8,64]{2,1,0:T(8,128)S(1)} %fusion, bf16[8,64,256]{1,0,2:T(8,128)(2,1)S(1)} %copy.124, f32[64,64,256]{1,0,2:T(8,128)} %copy.125), kind=kOutput, calls=%fused_computation.16 | convolution fusion | flops 100794368 | bytes 5505024 | tf_op jit(solution)/shard_map/ijc,bjc->bic/dot_general | solution.py:42
  325.7 1.6 copy.130
  327.5 2.5 convolution_convert_fusion
  330.3 68.3 %all_to_all.10 = bf16[512,16,256]{2,0,1:T(8,128)(2,1)} all-to-all(bf16[512,16,256]{2,0,1:T(8,128)(2,1)S(1)} %bitcast.46), channel_id=1, replica_groups=mesh['yh'=2,'z'=16,'ch'=16] {'ch'}, dimensions={1} | all-to-all | bytes 8388608 | tf_op jit(solution)/shard_map/all_to_all | solution.py:70
  398.7 3.5 reduce_sum.22
  (78 shorter events, 14.3 us)
Async XLA Ops:
  6.5 175.0 %all-gather.7.cloned.1.call-start = ((), (), s32[]{:S(2)}) async-start(), calls=%async_computation.2 | async-start | bytes 6684672 | tf_op jit(solution)/shard_map/all_gather | solution.py:80
  18.7 11.7 %copy-start.6 = (bf16[256,128]{1,0:T(8,128)(2,1)S(1)}, bf16[256,128]{1,0:T(8,128)(2,1)}, u32[]{:S(2)}) copy-start(bf16[256,128]{1,0:T(8,128)(2,1)} %param.13) | copy-start | bytes 196612
  18.7 31.7 %copy-start.9 = (f32[256,16]{0,1:T(8,128)S(1)}, f32[256,16]{0,1:T(8,128)}, u32[]{:S(2)}) copy-start(f32[256,16]{0,1:T(8,128)} %param.11) | copy-start | bytes 49156
  18.7 31.8 %copy-start.1 = (f32[256,16]{0,1:T(8,128)S(1)}, f32[256,16]{0,1:T(8,128)}, u32[]{:S(2)}) copy-start(f32[256,16]{0,1:T(8,128)} %param.10) | copy-start | bytes 49156
  18.7 64.4 %all-to-all-start = ((bf16[16,512,256]{2,1,0:T(8,128)(2,1)}), bf16[16,512,256]{2,1,0:T(8,128)(2,1)}, u32[]{:S(2)}, u32[]{:S(2)}) async-start(bf16[16,512,256]{2,1,0:T(8,128)(2,1)} %broadcast_in_dim.2), calls=%async_computation | async-start | bytes 8388608 | tf_op jit(solution)/shard_map/all_to_all | solution.py:63
  30.3 244.1 %all-gather.9.cloned.1.call-start = ((), (), s32[]{:S(2)}) async-start(), calls=%async_computation.3 | async-start | bytes 2228224 | tf_op jit(solution)/shard_map/all_gather | solution.py:100
  50.6 39.0 %copy-start.12 = (f32[64]{0:T(128)}, f32[64]{0:T(128)S(1)}, u32[]{:S(2)}) copy-start(f32[64]{0:T(128)S(1)} %iota_negate_fusion) | copy-start | bytes 772
  192.6 12.7 %copy-start.10 = (f32[3,3,256]{2,1,0:T(4,128)S(1)}, f32[3,3,256]{2,1,0:T(4,128)}, u32[]{:S(2)}) copy-start(f32[3,3,256]{2,1,0:T(4,128)} %param.9) | copy-start | bytes 27652
  200.9 9.5 %collective-permute-start = (bf16[3,2,256]{1,2,0:T(8,128)(2,1)}, bf16[3,2,256]{1,2,0:T(8,128)(2,1)S(1)}, u32[]{:S(2)}, u32[]{:S(2)}) collective-permute-start(bf16[3,2,256]{1,2,0:T(8,128)(2,1)} %slice.122), channel_id=1, source_target_pairs={{0,16},{16,32},{32,48},{48,64},{64,80},{80,96},{96,112},{112,128},... | collective-permute-start | bytes 9224 | tf_op jit(solution)/shard_map/ppermute | solution.py:16
  212.1 1.1 copy-start
  213.8 4.3 %copy-start.4 = (f32[256,16]{0,1:T(8,128)S(1)}, f32[256,16]{0,1:T(8,128)}, u32[]{:S(2)}) copy-start(f32[256,16]{0,1:T(8,128)} %get-tuple-element.13) | copy-start | bytes 49156
  213.8 4.3 %copy-start.8 = (f32[256,16]{0,1:T(8,128)S(1)}, f32[256,16]{0,1:T(8,128)}, u32[]{:S(2)}) copy-start(f32[256,16]{0,1:T(8,128)} %get-tuple-element.12) | copy-start | bytes 49156
  218.2 12.5 %copy-start.2 = (f32[4,256,16]{1,2,0:T(8,128)}, f32[4,256,16]{1,2,0:T(8,128)S(1)}, u32[]{:S(2)}) copy-start(f32[4,256,16]{1,2,0:T(8,128)S(1)} %pad.23) | copy-start | bytes 196612
  218.3 4.9 %collective-permute-start.1 = (f32[256,16]{0,1:T(8,128)S(1)}, f32[256,16]{0,1:T(8,128)S(1)}, u32[]{:S(2)}, u32[]{:S(2)}) collective-permute-start(f32[256,16]{0,1:T(8,128)S(1)} %add_bitcast_fusion), channel_id=1, source_target_pairs={{0,16},{16,32},{32,48},{48,64},{64,80},{80,96},{96,112},{112,128},... | collective-permute-start | bytes 49160 | tf_op jit(solution)/shard_map/ppermute | solution.py:16
  223.3 7.4 %collective-permute-start.2 = (f32[256,16]{0,1:T(8,128)S(1)}, f32[256,16]{0,1:T(8,128)S(1)}, u32[]{:S(2)}, u32[]{:S(2)}) collective-permute-start(f32[256,16]{0,1:T(8,128)S(1)} %collective-permute-done.1), channel_id=1, source_target_pairs={{0,16},{16,32},{32,48},{48,64},{64,80},{80,96},{96,112},{112,128},... | collective-permute-start | bytes 49160 | tf_op jit(solution)/shard_map/ppermute | solution.py:16
  226.9 9.2 %copy-start.7 = (f32[256,16]{0,1:T(8,128)S(1)}, f32[256,16]{0,1:T(8,128)}, u32[]{:S(2)}) copy-start(f32[256,16]{0,1:T(8,128)} %get-tuple-element.11) | copy-start | bytes 49156
  230.7 46.2 %collective-permute-start.3 = (f32[256,16]{0,1:T(8,128)S(1)}, f32[256,16]{0,1:T(8,128)S(1)}, u32[]{:S(2)}, u32[]{:S(2)}) collective-permute-start(f32[256,16]{0,1:T(8,128)S(1)} %multiply_add_fusion.7), channel_id=1, source_target_pairs={{0,32},{16,48},{32,64},{48,80},{64,96},{80,112},{96,128},{112,144}... | collective-permute-start | bytes 49160 | tf_op jit(solution)/shard_map/ppermute | solution.py:16
  274.4 9.3 %copy-start.3 = (f32[4,256,16]{1,2,0:T(8,128)S(1)}, f32[4,256,16]{1,2,0:T(8,128)}, u32[]{:S(2)}) copy-start(f32[4,256,16]{1,2,0:T(8,128)} %copy-done.2) | copy-start | bytes 196612
  274.4 9.3 %copy-start.5 = (f32[256,16]{0,1:T(8,128)S(1)}, f32[256,16]{0,1:T(8,128)}, u32[]{:S(2)}) copy-start(f32[256,16]{0,1:T(8,128)} %get-tuple-element.13) | copy-start | bytes 49156
  277.0 7.6 %collective-permute-start.4 = (f32[256,16]{0,1:T(8,128)S(1)}, f32[256,16]{0,1:T(8,128)S(1)}, u32[]{:S(2)}, u32[]{:S(2)}) collective-permute-start(f32[256,16]{0,1:T(8,128)S(1)} %multiply_add_fusion.6), channel_id=1, source_target_pairs={{0,64},{16,80},{32,96},{48,112},{64,128},{80,144},{96,160},{112,17... | collective-permute-start | bytes 49160 | tf_op jit(solution)/shard_map/ppermute | solution.py:16
  284.6 9.0 %collective-permute-start.5 = (f32[256,16]{0,1:T(8,128)S(1)}, f32[256,16]{0,1:T(8,128)}, u32[]{:S(2)}, u32[]{:S(2)}) collective-permute-start(f32[256,16]{0,1:T(8,128)S(1)} %multiply_add_fusion.5), channel_id=1, source_target_pairs={{0,128},{16,144},{32,160},{48,176},{64,192},{80,208},{96,224},{112... | collective-permute-start | bytes 49160 | tf_op jit(solution)/shard_map/ppermute | solution.py:16
  294.3 14.8 %collective-permute-start.6 = (f32[256,16]{0,1:T(8,128)S(1)}, f32[256,16]{0,1:T(8,128)S(1)}, u32[]{:S(2)}, u32[]{:S(2)}) collective-permute-start(f32[256,16]{0,1:T(8,128)S(1)} %multiply_add_fusion.4), channel_id=1, source_target_pairs={{0,256},{16,272},{32,288},{48,304},{64,320},{80,336},{96,352},{112... | collective-permute-start | bytes 49160 | tf_op jit(solution)/shard_map/ppermute | solution.py:16
  325.7 1.8 copy-start.11
Sparse Core Ops, SparseCore 0:
  15.5 165.9 all-gather.6
  183.5 90.8 all-gather.8

commit v3 on v2

--- a/solution.py
+++ b/solution.py
@@ -75,10 +75,10 @@
     def shards(tokens, in_weight, short_taps, rates, residues, skip, out_weight):
         rows = tokens.shape[0]
         width = in_weight.shape[2]
-        whole = gathered_tokens(tokens, lanes)
-        weight = lax.all_gather(in_weight, "yh", axis=1)
-        weight = lax.all_gather(weight, "z", axis=2)
-        weight = weight.reshape(3, -1, width)
+        whole = lax.all_gather(tokens, CH, axis=1, tiled=True)
+        copies = jnp.broadcast_to(in_weight[None], (count,) + in_weight.shape)
+        weight = lax.all_to_all(copies, CTX, 0, 0)
+        weight = jnp.transpose(weight, (1, 0, 2, 3)).reshape(3, -1, width)
         proj = jnp.einsum("td,jdc->jtc", whole, weight, preferred_element_type=jnp.float32)
         proj = proj.astype(jnp.bfloat16)
         earlier = passed_along(proj[:, rows - (SHORT - 1) :, :], CTX, count, 1)

time: 411 us -> 522 us (1.27)
  waiting for transfers between devices: 147 us -> 294 us
  local copies, waits for them, and re-layouts: 53.1 us -> 29 us
  blocking collectives: 95.4 us -> 74.3 us
  starting transfers between devices: 58.2 us -> 67.6 us
    all_to_all x1, waiting for transfers between devices: 29 us -> 240 us  [shards(): weight = lax.all_to_all(copies, CTX, 0, 0)]
    all_gather x1, waiting for transfers between devices: 84.5 us -> 50.3 us  [shards(): whole = lax.all_gather(tokens, CH, axis=1, tiled=True)]
    all_gather x1, waiting for transfers between devices: 28.5 us -> 0.01 us  [shards(): out_w = lax.all_gather(out_w, 'z', axis=2)]
    reshape x2 -> x0, local copies, waits for them, and re-layouts: 18.5 us -> none  [the longest x1 11.1 us: shards(): weight = weight.reshape(3, -1, width)]
    all_gather x1, blocking collectives: 19.3 us -> 7.81 us  [shards(): out_w = lax.all_gather(out_weight, 'yh', axis=1)]
    all_gather x1 -> x0, blocking collectives: 7.72 us -> none  [shards(): weight = lax.all_gather(in_weight, 'yh', axis=1)]
    all_to_all x1, starting transfers between devices: 11.6 us -> 18.9 us  [shards(): weight = lax.all_to_all(copies, CTX, 0, 0)]
    transpose x1 -> x0, local copies, waits for them, and re-layouts: 6.54 us -> none  [gathered_tokens(): return jnp.transpose(parts, (1, 0, 2)).reshape(rows, lanes * width)]
  transfers between devices with their start and end apart: 10 -> 10, of which waited for: 8 -> 7; matrix products, arithmetic and copies ran while one was open for 16% -> 7% of each run, Pallas kernels for 0% -> 0%
where the time goes in v3:
time: 522 us; the launch traced here: 521 us
  waiting for transfers between devices  294 us (56%)
  blocking collectives  74.3 us (14%)
  starting transfers between devices  67.6 us (13%)
  matrix products  31 us (6%)
  local copies, waits for them, and re-layouts  29 us (6%)
  between operations  13.9 us (3%)
  other arithmetic  11 us (2%)
    all_to_all x1, waiting for transfers between devices, shards(): weight = lax.all_to_all(copies, CTX, 0, 0)  240 us
    all_to_all x1, blocking collectives, scattered_terms(): parts = lax.all_to_all(split, CH, 1, 1)  66.5 us
    all_gather x1, waiting for transfers between devices, shards(): whole = lax.all_gather(tokens, CH, axis=1, tiled=True)  50.3 us
    ppermute x7, starting transfers between devices, passed_along(): return lax.ppermute(block, axis, route)  48.6 us
    all_to_all x1, starting transfers between devices, shards(): weight = lax.all_to_all(copies, CTX, 0, 0)  18.9 us
  transfers between devices with their start and end apart: 10, of which 7 were waited for; matrix products, arithmetic and copies ran while one was open for 7% of the time, Pallas kernels for 0%

profile of v3, /device:TPU:1, one launch (start us, length us, event | category | flops | bytes accessed | tf_op | source)
XLA Modules:
  0.0 520.8 jit_solution(13243098144717582005)
XLA Ops:
  6.5 1.1 copy.118
  7.6 4.2 broadcast_in_dim.2
  11.8 18.9 %all-to-all-start = ((bf16[32,3,128,256]{2,3,1,0:T(8,128)(2,1)}), bf16[32,3,128,256]{2,3,1,0:T(8,128)(2,1)}, u32[]{:S(2)}, u32[]{:S(2)}) async-start(bf16[32,3,128,256]{2,3,1,0:T(8,128)(2,1)} %broadcast_in_dim.2), calls=%async_computation | async-start | bytes 12582912 | tf_op jit(solution)/shard_map/all_to_all | solution.py:80
  31.5 7.8 %all-gather = bf16[256,256]{1,0:T(8,128)(2,1)S(1)} all-gather(bf16[256,128]{1,0:T(8,128)(2,1)S(1)} %copy-done.6), channel_id=2, replica_groups=mesh['yh'=2,'z'=16,'ch'=16] {'yh'}, dimensions={1}, use_global_device_ids=true | all-gather | bytes 196608 | tf_op jit(solution)/shard_map/all_gather | solution.py:99
  40.9 2.8 multiply_reduce_fusion
  43.7 50.3 %all-gather.5.cloned.1.call-done = bf16[512,4096]{1,0:T(8,128)(2,1)} async-done(((bf16[512,256]{1,0:T(8,128)(2,1)}), bf16[512,4096]{1,0:T(8,128)(2,1)}) %all-gather.5.cloned.1.call-update) | async-done | bytes 4194320 | tf_op jit(solution)/shard_map/all_gather | solution.py:78
  93.9 239.6 %all-to-all-done = bf16[32,3,128,256]{2,3,1,0:T(8,128)(2,1)} async-done(((bf16[32,3,128,256]{2,3,1,0:T(8,128)(2,1)}), bf16[32,3,128,256]{2,3,1,0:T(8,128)(2,1)}, u32[]{:S(2)}, u32[]{:S(2)}) %all-to-all-start) | async-done | bytes 6291488 | tf_op jit(solution)/shard_map/all_to_all | solution.py:80
  333.6 7.4 %fusion.16 = bf16[3,512,256]{1,2,0:T(8,128)(2,1)S(1)} fusion(bf16[512,4096]{1,0:T(8,128)(2,1)} %all-gather.5.cloned.1.call-done, bf16[32,3,128,256]{2,3,1,0:T(8,128)(2,1)} %all-to-all-done), kind=kOutput, calls=%fused_computation.21 | convolution fusion | flops 3221618688 | bytes 11272192 | tf_op jit(solution)/shard_map/td,jdc->jtc/dot_general | solution.py:82
  341.8 1.3 collective-permute-start
  343.1 2.7 rev.3
  347.0 1.4 fusion.8
  348.4 1.2 copy-done
  350.1 2.7 fusion.39
  352.8 1.5 copy.127
  354.6 4.9 collective-permute-start.1
  359.5 0.8 collective-permute-done.1
  360.4 4.1 collective-permute-start.2
  364.5 3.8 fusion.6
  368.3 6.9 %collective-permute-start.3 = (f32[256,16]{0,1:T(8,128)S(1)}, f32[256,16]{0,1:T(8,128)S(1)}, u32[]{:S(2)}, u32[]{:S(2)}) collective-permute-start(f32[256,16]{0,1:T(8,128)S(1)} %multiply_add_fusion.7), channel_id=1, source_target_pairs={{0,32},{16,48},{32,64},{48,80},{64,96},{80,112},{96,128},{112,144}... | collective-permute-start | bytes 49160 | tf_op jit(solution)/shard_map/ppermute | solution.py:16
  376.6 9.2 %copy.125 = f32[64,64,256]{1,0,2:T(8,128)} copy(f32[64,64,256]{2,1,0:T(8,128)} %fusion.6) | data formatting | bytes 8388608 | tf_op jit(solution)/shard_map/dot_general | solution.py:38
  385.7 2.5 copy.137
  388.3 6.7 %collective-permute-start.4 = (f32[256,16]{0,1:T(8,128)S(1)}, f32[256,16]{0,1:T(8,128)S(1)}, u32[]{:S(2)}, u32[]{:S(2)}) collective-permute-start(f32[256,16]{0,1:T(8,128)S(1)} %multiply_add_fusion.6), channel_id=1, source_target_pairs={{0,64},{16,80},{32,96},{48,112},{64,128},{80,144},{96,160},{112,17... | collective-permute-start | bytes 49160 | tf_op jit(solution)/shard_map/ppermute | solution.py:16
  395.9 12.9 %collective-permute-start.5 = (f32[256,16]{0,1:T(8,128)S(1)}, f32[256,16]{0,1:T(8,128)}, u32[]{:S(2)}, u32[]{:S(2)}) collective-permute-start(f32[256,16]{0,1:T(8,128)S(1)} %multiply_add_fusion.5), channel_id=1, source_target_pairs={{0,128},{16,144},{32,160},{48,176},{64,192},{80,208},{96,224},{112... | collective-permute-start | bytes 49160 | tf_op jit(solution)/shard_map/ppermute | solution.py:16
  409.8 11.9 %collective-permute-start.6 = (f32[256,16]{0,1:T(8,128)S(1)}, f32[256,16]{0,1:T(8,128)S(1)}, u32[]{:S(2)}, u32[]{:S(2)}) collective-permute-start(f32[256,16]{0,1:T(8,128)S(1)} %multiply_add_fusion.4), channel_id=1, source_target_pairs={{0,256},{16,272},{32,288},{48,304},{64,320},{80,336},{96,352},{112... | collective-permute-start | bytes 49160 | tf_op jit(solution)/shard_map/ppermute | solution.py:16
  421.7 0.8 collective-permute-done.6
  423.3 1.4 copy.129
  424.7 4.8 fusion.4
  429.5 9.7 %fusion.15 = f32[8,64,256]{1,0,2:T(8,128)} fusion(f32[256,8,64]{2,1,0:T(8,128)S(1)} %fusion.4, bf16[8,64,256]{1,0,2:T(8,128)(2,1)S(1)} %copy.124, f32[64,64,256]{1,0,2:T(8,128)} %copy.125), kind=kOutput, calls=%fused_computation.20 | convolution fusion | flops 100794368 | bytes 5505024 | tf_op jit(solution)/shard_map/ijc,bjc->bic/dot_general | solution.py:42
  439.3 1.6 copy.130
  441.1 2.5 convolution_convert_fusion
  443.9 66.5 %all_to_all.10 = bf16[512,16,256]{2,0,1:T(8,128)(2,1)} all-to-all(bf16[512,16,256]{2,0,1:T(8,128)(2,1)S(1)} %bitcast.59), channel_id=1, replica_groups=mesh['yh'=2,'z'=16,'ch'=16] {'ch'}, dimensions={1} | all-to-all | bytes 8388608 | tf_op jit(solution)/shard_map/all_to_all | solution.py:70
  510.4 3.5 reduce_sum.22
  (74 shorter events, 9.5 us)
Async XLA Ops:
  11.8 19.7 %copy-start.6 = (bf16[256,128]{1,0:T(8,128)(2,1)S(1)}, bf16[256,128]{1,0:T(8,128)(2,1)}, u32[]{:S(2)}) copy-start(bf16[256,128]{1,0:T(8,128)(2,1)} %param.13) | copy-start | bytes 196612
  11.8 28.2 %copy-start.9 = (f32[256,16]{0,1:T(8,128)S(1)}, f32[256,16]{0,1:T(8,128)}, u32[]{:S(2)}) copy-start(f32[256,16]{0,1:T(8,128)} %param.11) | copy-start | bytes 49156
  11.8 28.3 %copy-start.1 = (f32[256,16]{0,1:T(8,128)S(1)}, f32[256,16]{0,1:T(8,128)}, u32[]{:S(2)}) copy-start(f32[256,16]{0,1:T(8,128)} %param.10) | copy-start | bytes 49156
  11.8 321.8 %all-to-all-start = ((bf16[32,3,128,256]{2,3,1,0:T(8,128)(2,1)}), bf16[32,3,128,256]{2,3,1,0:T(8,128)(2,1)}, u32[]{:S(2)}, u32[]{:S(2)}) async-start(bf16[32,3,128,256]{2,3,1,0:T(8,128)(2,1)} %broadcast_in_dim.2), calls=%async_computation | async-start | bytes 12582912 | tf_op jit(solution)/shard_map/all_to_all | solution.py:80
  30.7 63.2 %all-gather.5.cloned.1.call-start = ((), (), s32[]{:S(2)}) async-start(), calls=%async_computation.2 | async-start | bytes 4456448 | tf_op jit(solution)/shard_map/all_gather | solution.py:78
  31.4 354.3 %all-gather.7.cloned.1.call-start = ((), (), s32[]{:S(2)}) async-start(), calls=%async_computation.3 | async-start | bytes 2228224 | tf_op jit(solution)/shard_map/all_gather | solution.py:100
  40.2 300.8 %copy-start.12 = (f32[64]{0:T(128)}, f32[64]{0:T(128)S(1)}, u32[]{:S(2)}) copy-start(f32[64]{0:T(128)S(1)} %iota_negate_fusion) | copy-start | bytes 772
  43.7 299.5 %copy-start.10 = (f32[3,3,256]{2,1,0:T(4,128)S(1)}, f32[3,3,256]{2,1,0:T(4,128)}, u32[]{:S(2)}) copy-start(f32[3,3,256]{2,1,0:T(4,128)} %param.9) | copy-start | bytes 27652
  341.8 4.8 collective-permute-start
  348.4 1.2 copy-start
  350.1 4.3 copy-start.4
  350.1 4.3 copy-start.8
  354.5 13.8 %copy-start.2 = (f32[4,256,16]{1,2,0:T(8,128)}, f32[4,256,16]{1,2,0:T(8,128)S(1)}, u32[]{:S(2)}) copy-start(f32[4,256,16]{1,2,0:T(8,128)S(1)} %pad.23) | copy-start | bytes 196612
  354.6 5.7 %collective-permute-start.1 = (f32[256,16]{0,1:T(8,128)S(1)}, f32[256,16]{0,1:T(8,128)S(1)}, u32[]{:S(2)}, u32[]{:S(2)}) collective-permute-start(f32[256,16]{0,1:T(8,128)S(1)} %add_bitcast_fusion), channel_id=1, source_target_pairs={{0,16},{16,32},{32,48},{48,64},{64,80},{80,96},{96,112},{112,128},... | collective-permute-start | bytes 49160 | tf_op jit(solution)/shard_map/ppermute | solution.py:16
  360.4 8.0 %collective-permute-start.2 = (f32[256,16]{0,1:T(8,128)S(1)}, f32[256,16]{0,1:T(8,128)S(1)}, u32[]{:S(2)}, u32[]{:S(2)}) collective-permute-start(f32[256,16]{0,1:T(8,128)S(1)} %collective-permute-done.1), channel_id=1, source_target_pairs={{0,16},{16,32},{32,48},{48,64},{64,80},{80,96},{96,112},{112,128},... | collective-permute-start | bytes 49160 | tf_op jit(solution)/shard_map/ppermute | solution.py:16
  364.5 11.3 %copy-start.7 = (f32[256,16]{0,1:T(8,128)S(1)}, f32[256,16]{0,1:T(8,128)}, u32[]{:S(2)}) copy-start(f32[256,16]{0,1:T(8,128)} %get-tuple-element.11) | copy-start | bytes 49156
  368.3 19.9 %collective-permute-start.3 = (f32[256,16]{0,1:T(8,128)S(1)}, f32[256,16]{0,1:T(8,128)S(1)}, u32[]{:S(2)}, u32[]{:S(2)}) collective-permute-start(f32[256,16]{0,1:T(8,128)S(1)} %multiply_add_fusion.7), channel_id=1, source_target_pairs={{0,32},{16,48},{32,64},{48,80},{64,96},{80,112},{96,128},{112,144}... | collective-permute-start | bytes 49160 | tf_op jit(solution)/shard_map/ppermute | solution.py:16
  385.7 9.3 %copy-start.3 = (f32[4,256,16]{1,2,0:T(8,128)S(1)}, f32[4,256,16]{1,2,0:T(8,128)}, u32[]{:S(2)}) copy-start(f32[4,256,16]{1,2,0:T(8,128)} %copy-done.2) | copy-start | bytes 196612
  385.7 9.3 %copy-start.5 = (f32[256,16]{0,1:T(8,128)S(1)}, f32[256,16]{0,1:T(8,128)}, u32[]{:S(2)}) copy-start(f32[256,16]{0,1:T(8,128)} %get-tuple-element.13) | copy-start | bytes 49156
  388.3 7.6 %collective-permute-start.4 = (f32[256,16]{0,1:T(8,128)S(1)}, f32[256,16]{0,1:T(8,128)S(1)}, u32[]{:S(2)}, u32[]{:S(2)}) collective-permute-start(f32[256,16]{0,1:T(8,128)S(1)} %multiply_add_fusion.6), channel_id=1, source_target_pairs={{0,64},{16,80},{32,96},{48,112},{64,128},{80,144},{96,160},{112,17... | collective-permute-start | bytes 49160 | tf_op jit(solution)/shard_map/ppermute | solution.py:16
  395.9 13.2 %collective-permute-start.5 = (f32[256,16]{0,1:T(8,128)S(1)}, f32[256,16]{0,1:T(8,128)}, u32[]{:S(2)}, u32[]{:S(2)}) collective-permute-start(f32[256,16]{0,1:T(8,128)S(1)} %multiply_add_fusion.5), channel_id=1, source_target_pairs={{0,128},{16,144},{32,160},{48,176},{64,192},{80,208},{96,224},{112... | collective-permute-start | bytes 49160 | tf_op jit(solution)/shard_map/ppermute | solution.py:16
  409.8 12.7 %collective-permute-start.6 = (f32[256,16]{0,1:T(8,128)S(1)}, f32[256,16]{0,1:T(8,128)S(1)}, u32[]{:S(2)}, u32[]{:S(2)}) collective-permute-start(f32[256,16]{0,1:T(8,128)S(1)} %multiply_add_fusion.4), channel_id=1, source_target_pairs={{0,256},{16,272},{32,288},{48,304},{64,320},{80,336},{96,352},{112... | collective-permute-start | bytes 49160 | tf_op jit(solution)/shard_map/ppermute | solution.py:16
  439.3 1.8 copy-start.11
Sparse Core Ops, SparseCore 0:
  33.6 60.3 all-gather.4
  95.9 261.3 all-gather.6

commit v4 on v2

--- a/solution.py
+++ b/solution.py
@@ -76,27 +76,38 @@
         rows = tokens.shape[0]
         width = in_weight.shape[2]
         whole = gathered_tokens(tokens, lanes)
-        weight = lax.all_gather(in_weight, "yh", axis=1)
-        weight = lax.all_gather(weight, "z", axis=2)
-        weight = weight.reshape(3, -1, width)
-        proj = jnp.einsum("td,jdc->jtc", whole, weight, preferred_element_type=jnp.float32)
-        proj = proj.astype(jnp.bfloat16)
-        earlier = passed_along(proj[:, rows - (SHORT - 1) :, :], CTX, count, 1)
-        widened = jnp.concatenate([earlier, proj], axis=1).astype(jnp.float32)
-        feats = jnp.zeros((3, rows, width), jnp.float32)
-        for i in range(SHORT):
-            feats = (
-                feats + short_taps[i][:, None, :] * widened[:, SHORT - 1 - i : SHORT - 1 - i + rows, :]
-            )
-        query = feats[0]
-        gated = (feats[1] * feats[2]).astype(jnp.bfloat16)
+
+        def spread(part):
+            part = lax.all_gather(part, "yh", axis=1)
+            part = lax.all_gather(part, "z", axis=2)
+            return part.reshape(part.shape[0], -1, part.shape[-1])
+
+        def shortened(weight):
+            proj = jnp.einsum("td,jdc->jtc", whole, weight, preferred_element_type=jnp.float32)
+            proj = proj.astype(jnp.bfloat16)
+            earlier = passed_along(proj[:, rows - (SHORT - 1) :, :], CTX, count, 1)
+            return jnp.concatenate([earlier, proj], axis=1).astype(jnp.float32)
+
+        def filtered(widened, taps):
+            feats = jnp.zeros((widened.shape[0], rows, width), jnp.float32)
+            for i in range(SHORT):
+                feats = feats + taps[i][:, None, :] * widened[:, SHORT - 1 - i : SHORT - 1 - i + rows, :]
+            return feats
+
+        pair = spread(in_weight[1:])
+        first, pair = lax.optimization_barrier((in_weight[:1], pair))
+        feats = filtered(shortened(pair), short_taps[:, 1:])
+        alone = spread(first)
+        out_src, alone = lax.optimization_barrier((out_weight, alone))
+        query = filtered(shortened(alone), short_taps[:, :1])[0]
+        gated = (feats[0] * feats[1]).astype(jnp.bfloat16)
         values = gated.astype(jnp.float32)
         inner, starts, final, heads, offsets = block_terms(values, rates, residues)
         incoming = carried_in(final, rates, rows, count)
         starts = starts + offsets * incoming[None]
         conv = finish(inner, starts, heads, values, skip)
         hidden = (query * conv).astype(jnp.bfloat16)
-        out_w = lax.all_gather(out_weight, "yh", axis=1)
+        out_w = lax.all_gather(out_src, "yh", axis=1)
         out_w = lax.all_gather(out_w, "z", axis=2)
         out_w = out_w.reshape(out_weight.shape[0], -1)
         terms = jnp.dot(hidden, out_w, preferred_element_type=jnp.float32)

time: 411 us -> 352 us (0.86)
  waiting for transfers between devices: 147 us -> 108 us
  blocking collectives: 95.4 us -> 81.1 us
    all_to_all x1, waiting for transfers between devices: 29 us -> 0.01 us  [gathered_tokens(): parts = lax.all_to_all(copies, CH, 0, 0)]
    all_gather x1, waiting for transfers between devices: 28.5 us -> 11.7 us  [shards(): out_w = lax.all_gather(out_w, 'z', axis=2)]
    all_gather x2 -> x3, blocking collectives: 27.1 us -> 17.6 us  [the longest x2 12.3 us: spread(): part = lax.all_gather(part, 'yh', axis=1)]
    all_gather x1 -> x2, waiting for transfers between devices: 84.5 us -> 94 us  [spread(): part = lax.all_gather(part, 'z', axis=2)]
    all_to_all x1, blocking collectives: 68.3 us -> 63.4 us  [scattered_terms(): parts = lax.all_to_all(split, CH, 1, 1)]
    reshape x1 -> x2, local copies, waits for them, and re-layouts: 7.4 us -> 12.1 us  [gathered_tokens(): return jnp.transpose(parts, (1, 0, 2)).reshape(rows, lanes * width)]
    reshape x1, local copies, waits for them, and re-layouts: 11.1 us -> 6.44 us  [spread(): return part.reshape(part.shape[0], -1, part.shape[-1])]
    dot_general x1 -> x2, matrix products: 7.45 us -> 8.71 us  [shortened(): jnp.einsum('td,jdc->jtc', whole, weight, preferred_element_type=jnp.float32)]
  transfers between devices with their start and end apart: 10 -> 12, of which waited for: 8 -> 6; matrix products, arithmetic and copies ran while one was open for 16% -> 23% of each run, Pallas kernels for 0% -> 0%
where the time goes in v4:
time: 352 us; the launch traced here: 350 us
  waiting for transfers between devices  108 us (31%)
  blocking collectives  81.1 us (23%)
  starting transfers between devices  58 us (16%)
  local copies, waits for them, and re-layouts  49.8 us (14%)
  matrix products  30 us (9%)
  between operations  13.6 us (4%)
  other arithmetic  9.31 us (3%)
    all_gather x2, waiting for transfers between devices, spread(): part = lax.all_gather(part, 'z', axis=2)  94 us
    all_to_all x1, blocking collectives, scattered_terms(): parts = lax.all_to_all(split, CH, 1, 1)  63.4 us
    ppermute x8, starting transfers between devices, passed_along(): return lax.ppermute(block, axis, route)  46.3 us
    all_gather x2, blocking collectives, spread(): part = lax.all_gather(part, 'yh', axis=1)  12.3 us
    reshape x2, local copies, waits for them, and re-layouts, gathered_tokens(): return jnp.transpose(parts, (1, 0, 2)).reshape(rows, lanes * width)  12.1 us
    all_gather x1, waiting for transfers between devices, shards(): out_w = lax.all_gather(out_w, 'z', axis=2)  11.7 us
    all_to_all x1, starting transfers between devices, gathered_tokens(): parts = lax.all_to_all(copies, CH, 0, 0)  11.6 us
    dot_general x1, local copies, waits for them, and re-layouts, block_terms(): jnp.dot(pick, impulse, precision=lax.Precision.HIGHEST)  9.17 us
  transfers between devices with their start and end apart: 12, of which 6 were waited for; matrix products, arithmetic and copies ran while one was open for 23% of the time, Pallas kernels for 0%

profile of v4, /device:TPU:1, one launch (start us, length us, event | category | flops | bytes accessed | tf_op | source)
XLA Modules:
  0.0 349.9 jit_solution(5347401486737279758)
XLA Ops:
  7.5 6.9 %all-gather = bf16[2,256,256]{2,1,0:T(8,128)(2,1)} all-gather(bf16[2,128,256]{2,1,0:T(8,128)(2,1)S(1)} %slice.127), channel_id=2, replica_groups=mesh['yh'=2,'z'=16,'ch'=16] {'yh'}, dimensions={1}, use_global_device_ids=true | all-gather | bytes 393216 | tf_op jit(solution)/shard_map/all_gather | solution.py:81
  14.3 3.4 broadcast_in_dim.2
  17.7 11.6 %all-to-all-start = ((bf16[16,512,256]{2,1,0:T(8,128)(2,1)}), bf16[16,512,256]{2,1,0:T(8,128)(2,1)}, u32[]{:S(2)}, u32[]{:S(2)}) async-start(bf16[16,512,256]{2,1,0:T(8,128)(2,1)} %broadcast_in_dim.2), calls=%async_computation | async-start | bytes 8388608 | tf_op jit(solution)/shard_map/all_to_all | solution.py:63
  29.3 62.2 %all-gather.10.cloned.1.call-done = bf16[2,2,2048,256]{3,2,1,0:T(8,128)(2,1)} async-done(((bf16[2,2,128,256]{3,2,1,0:T(8,128)(2,1)}), bf16[2,2,2048,256]{3,2,1,0:T(8,128)(2,1)}) %all-gather.10.cloned.1.call-update) | async-done | bytes 4194320 | tf_op jit(solution)/shard_map/all_gather | solution.py:82
  91.6 6.4 %copy.134 = bf16[2,4096,256]{1,2,0:T(8,128)(2,1)} copy(bf16[2,4096,256]{2,1,0:T(8,128)(2,1)} %bitcast.66) | data formatting | bytes 8388608 | tf_op jit(solution)/shard_map/reshape | solution.py:83
  98.0 5.4 %all-gather.2 = bf16[2,128,256]{2,1,0:T(8,128)(2,1)} all-gather(bf16[1,128,256]{2,1,0:T(8,128)(2,1)S(1)} %slice-done), channel_id=4, replica_groups=mesh['yh'=2,'z'=16,'ch'=16] {'yh'}, dimensions={0}, use_global_device_ids=true | all-gather | bytes 196608 | tf_op jit(solution)/shard_map/all_gather | solution.py:81
  104.4 2.8 multiply_reduce_fusion
  107.2 6.5 %copy.119 = bf16[512,16,256]{2,1,0:T(8,128)(2,1)} copy(bf16[512,16,256]{2,0,1:T(8,128)(2,1)} %bitcast.5) | data formatting | bytes 8388608 | tf_op jit(solution)/shard_map/transpose | solution.py:64
  113.6 7.4 %reshape.125 = bf16[512,4096,1]{1,0,2:T(8,128)(2,1)} reshape(bf16[512,16,256]{2,1,0:T(8,128)(2,1)} %copy.119) | data formatting | bytes 8388608 | tf_op jit(solution)/shard_map/reshape | solution.py:64
  121.1 5.8 %fusion.7 = bf16[2,512,256]{1,2,0:T(8,128)(2,1)S(1)} fusion(bf16[2,4096,256]{1,2,0:T(8,128)(2,1)} %copy.134, bf16[512,4096,1]{1,0,2:T(8,128)(2,1)} %reshape.125), kind=kOutput, calls=%fused_computation.14 | convolution fusion | flops 2147745792 | bytes 8912896 | tf_op jit(solution)/shard_map/td,jdc->jtc/dot_general | solution.py:86
  127.0 1.9 collective-permute-start.1
  129.6 2.7 rev.3
  134.1 2.7 fusion.40
  138.7 3.8 %collective-permute-start.2 = (f32[256,16]{0,1:T(8,128)S(1)}, f32[256,16]{0,1:T(8,128)S(1)}, u32[]{:S(2)}, u32[]{:S(2)}) collective-permute-start(f32[256,16]{0,1:T(8,128)S(1)} %add_bitcast_fusion), channel_id=1, source_target_pairs={{0,16},{16,32},{32,48},{48,64},{64,80},{80,96},{96,112},{112,128},... | collective-permute-start | bytes 49160 | tf_op jit(solution)/shard_map/ppermute | solution.py:16
  142.5 31.7 %all-gather.12.cloned.1.call-done = bf16[2,2048,256]{2,1,0:T(8,128)(2,1)} async-done(((bf16[2,128,256]{2,1,0:T(8,128)(2,1)}), bf16[2,2048,256]{2,1,0:T(8,128)(2,1)}) %all-gather.12.cloned.1.call-update) | async-done | bytes 2097168 | tf_op jit(solution)/shard_map/all_gather | solution.py:82
  174.2 5.4 %all-gather.4 = bf16[256,256]{1,0:T(8,128)(2,1)S(1)} all-gather(bf16[256,128]{1,0:T(8,128)(2,1)S(1)} %copy-done.4), channel_id=6, replica_groups=mesh['yh'=2,'z'=16,'ch'=16] {'yh'}, dimensions={1}, use_global_device_ids=true | all-gather | bytes 196608 | tf_op jit(solution)/shard_map/all_gather | solution.py:110
  180.3 3.7 %fusion.4 = f32[64,64,256]{2,1,0:T(8,128)} fusion(s32[64,64]{1,0:T(8,128)S(1)} %copy-done.3, f32[64,256]{0,1:T(8,128)S(1)} %get-tuple-element.13), kind=kOutput, calls=%fused_computation.8 | convolution fusion | flops 805568512 | bytes 4276224 | tf_op jit(solution)/shard_map/dot_general | solution.py:38
  184.1 2.5 collective-permute-start.3
  187.9 4.1 %collective-permute-start.4 = (f32[256,16]{0,1:T(8,128)S(1)}, f32[256,16]{0,1:T(8,128)S(1)}, u32[]{:S(2)}, u32[]{:S(2)}) collective-permute-start(f32[256,16]{0,1:T(8,128)S(1)} %multiply_add_fusion.7), channel_id=1, source_target_pairs={{0,32},{16,48},{32,64},{48,80},{64,96},{80,112},{96,128},{112,144}... | collective-permute-start | bytes 49160 | tf_op jit(solution)/shard_map/ppermute | solution.py:16
  192.1 9.2 %copy.125 = f32[64,64,256]{1,0,2:T(8,128)} copy(f32[64,64,256]{2,1,0:T(8,128)} %fusion.4) | data formatting | bytes 8388608 | tf_op jit(solution)/shard_map/dot_general | solution.py:38
  201.3 4.7 %copy.137 = bf16[16,64,8,256]{3,2,0,1:T(8,128)(2,1)} copy(bf16[16,64,8,256]{3,2,1,0:T(8,128)(2,1)} %bitcast.26) | data formatting | bytes 8388608 | tf_op jit(solution)/shard_map/reshape | solution.py:64
  206.0 5.4 %collective-permute-start.5 = (f32[256,16]{0,1:T(8,128)S(1)}, f32[256,16]{0,1:T(8,128)S(1)}, u32[]{:S(2)}, u32[]{:S(2)}) collective-permute-start(f32[256,16]{0,1:T(8,128)S(1)} %multiply_add_fusion.6), channel_id=1, source_target_pairs={{0,64},{16,80},{32,96},{48,112},{64,128},{80,144},{96,160},{112,17... | collective-permute-start | bytes 49160 | tf_op jit(solution)/shard_map/ppermute | solution.py:16
  212.2 9.8 %collective-permute-start.6 = (f32[256,16]{0,1:T(8,128)S(1)}, f32[256,16]{0,1:T(8,128)S(1)}, u32[]{:S(2)}, u32[]{:S(2)}) collective-permute-start(f32[256,16]{0,1:T(8,128)S(1)} %multiply_add_fusion.5), channel_id=1, source_target_pairs={{0,128},{16,144},{32,160},{48,176},{64,192},{80,208},{96,224},{112... | collective-permute-start | bytes 49160 | tf_op jit(solution)/shard_map/ppermute | solution.py:16
  222.9 17.4 %collective-permute-start.7 = (f32[256,16]{0,1:T(8,128)S(1)}, f32[256,16]{0,1:T(8,128)S(1)}, u32[]{:S(2)}, u32[]{:S(2)}) collective-permute-start(f32[256,16]{0,1:T(8,128)S(1)} %multiply_add_fusion.4), channel_id=1, source_target_pairs={{0,256},{16,272},{32,288},{48,304},{64,320},{80,336},{96,352},{112... | collective-permute-start | bytes 49160 | tf_op jit(solution)/shard_map/ppermute | solution.py:16
  241.6 4.0 %fusion.2 = f32[256,8,64]{2,1,0:T(8,128)S(1)} fusion(f32[8,256,16]{2,0,1:T(8,128)S(1)} %copy.129, f32[256,16]{1,0:T(8,128)S(1)} %copy.128, f32[256,16]{1,0:T(8,128)S(1)} %copy.122, f32[64]{0:T(128)} %copy-done.13, f32[256,16]{1,0:T(8,128)S(1)} %copy.121), kind=kOutput, calls=%fused_computation.4 | convolution fusion | flops 25952256 | bytes 704768 | tf_op jit(solution)/shard_map/icm,bcm->bic/dot_general | solution.py:56
  245.6 2.9 fusion.11
  250.1 9.0 %fusion.6 = f32[8,64,256]{1,0,2:T(8,128)S(1)} fusion(f32[256,8,64]{2,1,0:T(8,128)S(1)} %fusion.2, bf16[8,64,256]{1,0,2:T(8,128)(2,1)S(1)} %copy.124, f32[64,64,256]{1,0,2:T(8,128)} %copy.125), kind=kOutput, calls=%fused_computation.12 | convolution fusion | flops 100794368 | bytes 5505024 | tf_op jit(solution)/shard_map/ijc,bjc->bic/dot_general | solution.py:42
  259.9 11.7 %all-gather.14.cloned.1.call-done = bf16[256,2,2048]{2,1,0:T(2,128)(2,1)} async-done(((bf16[256,2,128]{2,1,0:T(2,128)(2,1)}), bf16[256,2,2048]{2,1,0:T(2,128)(2,1)}) %all-gather.14.cloned.1.call-update) | async-done | bytes 2097168 | tf_op jit(solution)/shard_map/all_gather | solution.py:111
  271.6 2.5 copy.138
  274.1 1.8 convolution_convert_fusion
  276.4 63.4 %all_to_all.10 = bf16[512,16,256]{2,0,1:T(8,128)(2,1)} all-to-all(bf16[512,16,256]{2,0,1:T(8,128)(2,1)S(1)} %bitcast.63), channel_id=1, replica_groups=mesh['yh'=2,'z'=16,'ch'=16] {'ch'}, dimensions={1} | all-to-all | bytes 8388608 | tf_op jit(solution)/shard_map/all_to_all | solution.py:70
  339.8 3.5 %reduce_sum.22 = bf16[512,256]{1,0:T(8,128)(2,1)} reduce(bf16[512,16,256]{2,0,1:T(8,128)(2,1)} %all_to_all.10, bf16[]{:T(256)} %constant.18.clone.1), dimensions={1}, to_apply=%region_1.0 | reduce | flops 1966080 | bytes 4456450 | tf_op jit(solution)/shard_map/reduce_sum | solution.py:71
  (93 shorter events, 14.0 us)
Async XLA Ops:
  6.5 85.0 %all-gather.10.cloned.1.call-start = ((), (), s32[]{:S(2)}) async-start(), calls=%async_computation.2 | async-start | bytes 4456448 | tf_op jit(solution)/shard_map/all_gather | solution.py:82
  17.7 89.4 %all-to-all-start = ((bf16[16,512,256]{2,1,0:T(8,128)(2,1)}), bf16[16,512,256]{2,1,0:T(8,128)(2,1)}, u32[]{:S(2)}, u32[]{:S(2)}) async-start(bf16[16,512,256]{2,1,0:T(8,128)(2,1)} %broadcast_in_dim.2), calls=%async_computation | async-start | bytes 8388608 | tf_op jit(solution)/shard_map/all_to_all | solution.py:63
  29.3 144.9 %all-gather.12.cloned.1.call-start = ((), (), s32[]{:S(2)}) async-start(), calls=%async_computation.3 | async-start | bytes 2228224 | tf_op jit(solution)/shard_map/all_gather | solution.py:82
  91.5 6.5 %slice-start = ((bf16[3,128,256]{2,1,0:T(8,128)(2,1)}), bf16[1,128,256]{2,1,0:T(8,128)(2,1)S(1)}, s32[]{:S(2)}) async-start(bf16[3,128,256]{2,1,0:T(8,128)(2,1)} %param.8), calls=%async_computation.5 | async-start | bytes 131072 | tf_op jit(solution)/shard_map/slice | solution.py:98
  91.5 11.9 %copy-start.1 = (f32[256,16]{0,1:T(8,128)S(1)}, f32[256,16]{0,1:T(8,128)}, u32[]{:S(2)}) copy-start(f32[256,16]{0,1:T(8,128)} %param.10) | copy-start | bytes 49156
  91.5 12.1 %copy-start.7 = (f32[256,16]{0,1:T(8,128)S(1)}, f32[256,16]{0,1:T(8,128)}, u32[]{:S(2)}) copy-start(f32[256,16]{0,1:T(8,128)} %param.11) | copy-start | bytes 49156
  91.5 12.2 %copy-start.11 = (f32[3,3,256]{2,1,0:T(4,128)S(1)}, f32[3,3,256]{2,1,0:T(4,128)}, u32[]{:S(2)}) copy-start(f32[3,3,256]{2,1,0:T(4,128)} %param.9) | copy-start | bytes 27652
  103.4 168.1 %all-gather.14.cloned.1.call-start = ((), (), s32[]{:S(2)}) async-start(), calls=%async_computation.4 | async-start | bytes 2228224 | tf_op jit(solution)/shard_map/all_gather | solution.py:111
  103.5 10.2 %copy-start.13 = (f32[64]{0:T(128)}, f32[64]{0:T(128)S(1)}, u32[]{:S(2)}) copy-start(f32[64]{0:T(128)S(1)} %iota_negate_fusion) | copy-start | bytes 772
  127.0 5.3 %collective-permute-start.1 = (bf16[2,2,256]{1,2,0:T(8,128)(2,1)S(1)}, bf16[2,2,256]{1,2,0:T(8,128)(2,1)S(1)}, u32[]{:S(2)}, u32[]{:S(2)}) collective-permute-start(bf16[2,2,256]{1,2,0:T(8,128)(2,1)S(1)} %slice.166), channel_id=1, source_target_pairs={{0,16},{16,32},{32,48},{48,64},{64,80},{80,96},{96,112},{112,128},... | collective-permute-start | bytes 6152 | tf_op jit(solution)/shard_map/ppermute | solution.py:16
  134.1 4.3 %copy-start.2 = (f32[256,16]{0,1:T(8,128)S(1)}, f32[256,16]{0,1:T(8,128)}, u32[]{:S(2)}) copy-start(f32[256,16]{0,1:T(8,128)} %get-tuple-element.21) | copy-start | bytes 49156
  134.1 4.3 %copy-start.6 = (f32[256,16]{0,1:T(8,128)S(1)}, f32[256,16]{0,1:T(8,128)}, u32[]{:S(2)}) copy-start(f32[256,16]{0,1:T(8,128)} %get-tuple-element.20) | copy-start | bytes 49156
  136.9 37.4 %copy-start.4 = (bf16[256,128]{1,0:T(8,128)(2,1)S(1)}, bf16[256,128]{1,0:T(8,128)(2,1)}, u32[]{:S(2)}) copy-start(bf16[256,128]{1,0:T(8,128)(2,1)} %param.13) | copy-start | bytes 196612
  136.9 43.5 %copy-start.3 = (s32[64,64]{1,0:T(8,128)S(1)}, s32[64,64]{1,0:T(8,128)}, u32[]{:S(2)}) copy-start(s32[64,64]{1,0:T(8,128)} %iota_subtract_fusion) | copy-start | bytes 49156
  138.7 45.4 %collective-permute-start.2 = (f32[256,16]{0,1:T(8,128)S(1)}, f32[256,16]{0,1:T(8,128)S(1)}, u32[]{:S(2)}, u32[]{:S(2)}) collective-permute-start(f32[256,16]{0,1:T(8,128)S(1)} %add_bitcast_fusion), channel_id=1, source_target_pairs={{0,16},{16,32},{32,48},{48,64},{64,80},{80,96},{96,112},{112,128},... | collective-permute-start | bytes 49160 | tf_op jit(solution)/shard_map/ppermute | solution.py:16
  180.3 11.7 %copy-start.5 = (f32[256,16]{0,1:T(8,128)S(1)}, f32[256,16]{0,1:T(8,128)}, u32[]{:S(2)}) copy-start(f32[256,16]{0,1:T(8,128)} %get-tuple-element.19) | copy-start | bytes 49156
  184.1 3.8 %collective-permute-start.3 = (f32[256,16]{0,1:T(8,128)S(1)}, f32[256,16]{0,1:T(8,128)S(1)}, u32[]{:S(2)}, u32[]{:S(2)}) collective-permute-start(f32[256,16]{0,1:T(8,128)S(1)} %collective-permute-done.2), channel_id=1, source_target_pairs={{0,16},{16,32},{32,48},{48,64},{64,80},{80,96},{96,112},{112,128},... | collective-permute-start | bytes 49160 | tf_op jit(solution)/shard_map/ppermute | solution.py:16
  187.9 18.1 %collective-permute-start.4 = (f32[256,16]{0,1:T(8,128)S(1)}, f32[256,16]{0,1:T(8,128)S(1)}, u32[]{:S(2)}, u32[]{:S(2)}) collective-permute-start(f32[256,16]{0,1:T(8,128)S(1)} %multiply_add_fusion.7), channel_id=1, source_target_pairs={{0,32},{16,48},{32,64},{48,80},{64,96},{80,112},{96,128},{112,144}... | collective-permute-start | bytes 49160 | tf_op jit(solution)/shard_map/ppermute | solution.py:16
  206.0 6.2 %collective-permute-start.5 = (f32[256,16]{0,1:T(8,128)S(1)}, f32[256,16]{0,1:T(8,128)S(1)}, u32[]{:S(2)}, u32[]{:S(2)}) collective-permute-start(f32[256,16]{0,1:T(8,128)S(1)} %multiply_add_fusion.6), channel_id=1, source_target_pairs={{0,64},{16,80},{32,96},{48,112},{64,128},{80,144},{96,160},{112,17... | collective-permute-start | bytes 49160 | tf_op jit(solution)/shard_map/ppermute | solution.py:16
  212.2 10.6 %collective-permute-start.6 = (f32[256,16]{0,1:T(8,128)S(1)}, f32[256,16]{0,1:T(8,128)S(1)}, u32[]{:S(2)}, u32[]{:S(2)}) collective-permute-start(f32[256,16]{0,1:T(8,128)S(1)} %multiply_add_fusion.5), channel_id=1, source_target_pairs={{0,128},{16,144},{32,160},{48,176},{64,192},{80,208},{96,224},{112... | collective-permute-start | bytes 49160 | tf_op jit(solution)/shard_map/ppermute | solution.py:16
  222.9 18.2 %collective-permute-start.7 = (f32[256,16]{0,1:T(8,128)S(1)}, f32[256,16]{0,1:T(8,128)S(1)}, u32[]{:S(2)}, u32[]{:S(2)}) collective-permute-start(f32[256,16]{0,1:T(8,128)S(1)} %multiply_add_fusion.4), channel_id=1, source_target_pairs={{0,256},{16,272},{32,288},{48,304},{64,320},{80,336},{96,352},{112... | collective-permute-start | bytes 49160 | tf_op jit(solution)/shard_map/ppermute | solution.py:16
  241.6 4.0 %copy-start = (bf16[16,64,8,256]{3,2,0,1:T(8,128)(2,1)S(1)}, bf16[16,64,8,256]{3,2,0,1:T(8,128)(2,1)}, u32[]{:S(2)}) copy-start(bf16[16,64,8,256]{3,2,0,1:T(8,128)(2,1)} %copy.137) | copy-start | bytes 12582916
  248.6 11.1 %collective-permute-start = (bf16[1,2,256]{1,2,0:T(8,128)(2,1)S(1)}, bf16[1,2,256]{1,2,0:T(8,128)(2,1)S(1)}, u32[]{:S(2)}, u32[]{:S(2)}) collective-permute-start(bf16[1,2,256]{1,2,0:T(8,128)(2,1)S(1)} %slice.162), channel_id=1, source_target_pairs={{0,16},{16,32},{32,48},{48,64},{64,80},{80,96},{96,112},{112,128},... | collective-permute-start | bytes 3080 | tf_op jit(solution)/shard_map/ppermute | solution.py:16
  271.6 2.5 copy-start.8
  271.6 2.5 copy-start.9
  271.6 2.5 copy-start.10
  271.6 2.5 copy-start.12
Sparse Core Ops, SparseCore 0:
  14.5 77.0 all-gather.9
  103.5 70.6 all-gather.11
  180.4 91.0 all-gather.13

commit v5 on v4

--- a/solution.py
+++ b/solution.py
@@ -58,10 +58,8 @@
 
 
 def gathered_tokens(tokens, lanes):
-    rows, width = tokens.shape
-    copies = jnp.broadcast_to(tokens[None], (lanes, rows, width))
-    parts = lax.all_to_all(copies, CH, 0, 0)
-    return jnp.transpose(parts, (1, 0, 2)).reshape(rows, lanes * width)
+    copies = jnp.tile(tokens, (1, lanes))
+    return lax.all_to_all(copies, CH, 1, 1, tiled=True)
 
 
 def scattered_terms(terms, lanes):
@@ -95,11 +93,11 @@
             return feats
 
         pair = spread(in_weight[1:])
-        first, pair = lax.optimization_barrier((in_weight[:1], pair))
+        packed = jnp.concatenate([in_weight[0], out_weight.T], axis=1)[None]
+        packed, pair = lax.optimization_barrier((packed, pair))
         feats = filtered(shortened(pair), short_taps[:, 1:])
-        alone = spread(first)
-        out_src, alone = lax.optimization_barrier((out_weight, alone))
-        query = filtered(shortened(alone), short_taps[:, :1])[0]
+        packed = spread(packed)[0]
+        query = filtered(shortened(packed[None, :, :width]), short_taps[:, :1])[0]
         gated = (feats[0] * feats[1]).astype(jnp.bfloat16)
         values = gated.astype(jnp.float32)
         inner, starts, final, heads, offsets = block_terms(values, rates, residues)
@@ -107,10 +105,7 @@
         starts = starts + offsets * incoming[None]
         conv = finish(inner, starts, heads, values, skip)
         hidden = (query * conv).astype(jnp.bfloat16)
-        out_w = lax.all_gather(out_src, "yh", axis=1)
-        out_w = lax.all_gather(out_w, "z", axis=2)
-        out_w = out_w.reshape(out_weight.shape[0], -1)
-        terms = jnp.dot(hidden, out_w, preferred_element_type=jnp.float32)
+        terms = jnp.einsum("tc,ec->te", hidden, packed[:, width:], preferred_element_type=jnp.float32)
         return scattered_terms(terms.astype(jnp.bfloat16), lanes)
 
     return shards

time: 352 us -> 315 us (0.89)
  waiting for transfers between devices: 108 us -> 63.6 us
  starting transfers between devices: 58 us -> 62.8 us
    all_gather x2, waiting for transfers between devices: 94 us -> 61.1 us  [spread(): part = lax.all_gather(part, 'z', axis=2)]
    all_to_all x0 -> x3, local copies, waits for them, and re-layouts: none -> 18.7 us  [gathered_tokens(): return lax.all_to_all(copies, CH, 1, 1, tiled=True)]
    reshape x2 -> x0, local copies, waits for them, and re-layouts: 12.1 us -> none  [gathered_tokens(): return jnp.transpose(parts, (1, 0, 2)).reshape(rows, lanes * width)]
    all_gather x1 -> x0, waiting for transfers between devices: 11.7 us -> none  [shards(): out_w = lax.all_gather(out_w, 'z', axis=2)]
    transpose x1 -> x0, local copies, waits for them, and re-layouts: 6.49 us -> none  [gathered_tokens(): return jnp.transpose(parts, (1, 0, 2)).reshape(rows, lanes * width)]
    all_to_all x1, blocking collectives: 63.4 us -> 68.9 us  [scattered_terms(): parts = lax.all_to_all(split, CH, 1, 1)]
    all_gather x1 -> x0, blocking collectives: 5.38 us -> none  [shards(): out_w = lax.all_gather(out_src, 'yh', axis=1)]
    ppermute x8, starting transfers between devices: 46.3 us -> 51.1 us  [passed_along(): return lax.ppermute(block, axis, route)]
  transfers between devices with their start and end apart: 12 -> 11, of which waited for: 6 -> 4; matrix products, arithmetic and copies ran while one was open for 23% -> 25% of each run, Pallas kernels for 0% -> 0%
where the time goes in v5:
time: 315 us; the launch traced here: 313 us
  blocking collectives  81.8 us (26%)
  waiting for transfers between devices  63.6 us (20%)
  starting transfers between devices  62.8 us (20%)
  local copies, waits for them, and re-layouts  47.8 us (15%)
  matrix products  33.3 us (11%)
  between operations  13.9 us (4%)
  other arithmetic  9.33 us (3%)
    all_to_all x1, blocking collectives, scattered_terms(): parts = lax.all_to_all(split, CH, 1, 1)  68.9 us
    all_gather x2, waiting for transfers between devices, spread(): part = lax.all_gather(part, 'z', axis=2)  61.1 us
    ppermute x8, starting transfers between devices, passed_along(): return lax.ppermute(block, axis, route)  51.1 us
    all_to_all x3, local copies, waits for them, and re-layouts, gathered_tokens(): return lax.all_to_all(copies, CH, 1, 1, tiled=True)  18.7 us
    all_gather x2, blocking collectives, spread(): part = lax.all_gather(part, 'yh', axis=1)  13 us
    all_to_all x1, starting transfers between devices, gathered_tokens(): return lax.all_to_all(copies, CH, 1, 1, tiled=True)  11.7 us
    dot_general x2, matrix products, shortened(): jnp.einsum('td,jdc->jtc', whole, weight, preferred_element_type=jnp.float32)  9.94 us
    dot_general x1, local copies, waits for them, and re-layouts, block_terms(): jnp.dot(pick, impulse, precision=lax.Precision.HIGHEST)  9.24 us
  transfers between devices with their start and end apart: 11, of which 4 were waited for; matrix products, arithmetic and copies ran while one was open for 25% of the time, Pallas kernels for 0%

profile of v5, /device:TPU:1, one launch (start us, length us, event | category | flops | bytes accessed | tf_op | source)
XLA Modules:
  0.0 312.6 jit_solution(8823503929718640926)
XLA Ops:
  6.5 0.9 slice.133
  7.5 6.9 %all-gather = bf16[2,256,256]{2,1,0:T(8,128)(2,1)} all-gather(bf16[2,128,256]{2,1,0:T(8,128)(2,1)S(1)} %slice.133), channel_id=2, replica_groups=mesh['yh'=2,'z'=16,'ch'=16] {'yh'}, dimensions={1}, use_global_device_ids=true | all-gather | bytes 393216 | tf_op jit(solution)/shard_map/all_gather | solution.py:79
  14.3 3.4 %tile.2 = bf16[512,16,256]{2,0,1:T(8,128)(2,1)} broadcast(bf16[512,256]{1,0:T(8,128)(2,1)} %param.7), dimensions={0,2} | broadcast | bytes 4456448 | tf_op jit(solution)/shard_map/tile | solution.py:61
  17.7 11.7 %all-to-all-start = ((bf16[512,16,256]{2,0,1:T(8,128)(2,1)}), bf16[512,16,256]{2,0,1:T(8,128)(2,1)}, u32[]{:S(2)}, u32[]{:S(2)}) async-start(bf16[512,16,256]{2,0,1:T(8,128)(2,1)} %tile.2), calls=%async_computation | async-start | bytes 8388608 | tf_op jit(solution)/shard_map/all_to_all | solution.py:62
  30.4 61.1 %all-gather.7.cloned.1.call-done = bf16[2,2,2048,256]{3,2,1,0:T(8,128)(2,1)} async-done(((bf16[2,2,128,256]{3,2,1,0:T(8,128)(2,1)}), bf16[2,2,2048,256]{3,2,1,0:T(8,128)(2,1)}) %all-gather.7.cloned.1.call-update) | async-done | bytes 4194320 | tf_op jit(solution)/shard_map/all_gather | solution.py:80
  91.5 6.5 %copy.139 = bf16[2,4096,256]{1,2,0:T(8,128)(2,1)} copy(bf16[2,4096,256]{2,1,0:T(8,128)(2,1)} %bitcast.69) | data formatting | bytes 8388608 | tf_op jit(solution)/shard_map/reshape | solution.py:81
  98.0 6.1 %all-gather.2 = bf16[2,128,512]{2,1,0:T(8,128)(2,1)} all-gather(bf16[1,128,512]{2,1,0:T(8,128)(2,1)S(1)} %maximum_bitcast_fusion), channel_id=4, replica_groups=mesh['yh'=2,'z'=16,'ch'=16] {'yh'}, dimensions={0}, use_global_device_ids=true | all-gather | bytes 393216 | tf_op jit(solution)/shard_map/all_gather | solution.py:79
  105.0 2.8 multiply_reduce_fusion
  107.8 6.5 %copy.124 = bf16[512,16,256]{2,1,0:T(8,128)(2,1)} copy(bf16[512,16,256]{2,0,1:T(8,128)(2,1)} %all-to-all-done) | data formatting | bytes 8388608 | tf_op jit(solution)/shard_map/all_to_all | solution.py:62
  114.3 7.5 %reshape.111 = bf16[512,4096,1]{1,0,2:T(8,128)(2,1)} reshape(bf16[512,16,256]{2,1,0:T(8,128)(2,1)} %copy.124) | data formatting | bytes 8388608 | tf_op jit(solution)/shard_map/all_to_all | solution.py:62
  121.8 5.8 %fusion.8 = bf16[2,512,256]{1,2,0:T(8,128)(2,1)S(1)} fusion(bf16[2,4096,256]{1,2,0:T(8,128)(2,1)} %copy.139, bf16[512,4096,1]{1,0,2:T(8,128)(2,1)} %reshape.111), kind=kOutput, calls=%fused_computation.15 | convolution fusion | flops 2147745792 | bytes 8912896 | tf_op jit(solution)/shard_map/td,jdc->jtc/dot_general | solution.py:84
  127.7 1.9 collective-permute-start.1
  130.3 2.7 rev.3
  134.8 2.8 fusion.44
  137.6 1.5 copy.132
  139.4 4.0 %collective-permute-start.2 = (f32[256,16]{0,1:T(8,128)S(1)}, f32[256,16]{0,1:T(8,128)S(1)}, u32[]{:S(2)}, u32[]{:S(2)}) collective-permute-start(f32[256,16]{0,1:T(8,128)S(1)} %add_bitcast_fusion), channel_id=1, source_target_pairs={{0,16},{16,32},{32,48},{48,64},{64,80},{80,96},{96,112},{112,128},... | collective-permute-start | bytes 49160 | tf_op jit(solution)/shard_map/ppermute | solution.py:16
  143.4 4.5 %fusion.5 = f32[64,64,256]{2,1,0:T(8,128)} fusion(s32[64,64]{1,0:T(8,128)} %iota_subtract_fusion, f32[64,256]{0,1:T(8,128)S(1)} %get-tuple-element.9), kind=kOutput, calls=%fused_computation.9 | convolution fusion | flops 805568512 | bytes 4276224 | tf_op jit(solution)/shard_map/dot_general | solution.py:38
  147.9 4.1 %collective-permute-start.3 = (f32[256,16]{0,1:T(8,128)S(1)}, f32[256,16]{0,1:T(8,128)S(1)}, u32[]{:S(2)}, u32[]{:S(2)}) collective-permute-start(f32[256,16]{0,1:T(8,128)S(1)} %collective-permute-done.2), channel_id=1, source_target_pairs={{0,16},{16,32},{32,48},{48,64},{64,80},{80,96},{96,112},{112,128},... | collective-permute-start | bytes 49160 | tf_op jit(solution)/shard_map/ppermute | solution.py:16
  152.0 1.3 fusion.43
  153.3 4.7 %collective-permute-start.4 = (f32[256,16]{0,1:T(8,128)S(1)}, f32[256,16]{0,1:T(8,128)S(1)}, u32[]{:S(2)}, u32[]{:S(2)}) collective-permute-start(f32[256,16]{0,1:T(8,128)S(1)} %multiply_add_fusion.7), channel_id=1, source_target_pairs={{0,32},{16,48},{32,64},{48,80},{64,96},{80,112},{96,128},{112,144}... | collective-permute-start | bytes 49160 | tf_op jit(solution)/shard_map/ppermute | solution.py:16
  158.2 9.2 %copy.130 = f32[64,64,256]{1,0,2:T(8,128)} copy(f32[64,64,256]{2,1,0:T(8,128)} %fusion.5) | data formatting | bytes 8388608 | tf_op jit(solution)/shard_map/dot_general | solution.py:38
  167.4 4.8 %copy.142 = bf16[16,64,8,256]{3,2,0,1:T(8,128)(2,1)} copy(bf16[16,64,8,256]{3,2,1,0:T(8,128)(2,1)} %bitcast.29) | data formatting | bytes 8388608 | tf_op jit(solution)/shard_map/all_to_all | solution.py:62
  172.2 5.0 %collective-permute-start.5 = (f32[256,16]{0,1:T(8,128)S(1)}, f32[256,16]{0,1:T(8,128)S(1)}, u32[]{:S(2)}, u32[]{:S(2)}) collective-permute-start(f32[256,16]{0,1:T(8,128)S(1)} %multiply_add_fusion.6), channel_id=1, source_target_pairs={{0,64},{16,80},{32,96},{48,112},{64,128},{80,144},{96,160},{112,17... | collective-permute-start | bytes 49160 | tf_op jit(solution)/shard_map/ppermute | solution.py:16
  178.1 11.0 %collective-permute-start.6 = (f32[256,16]{0,1:T(8,128)S(1)}, f32[256,16]{0,1:T(8,128)S(1)}, u32[]{:S(2)}, u32[]{:S(2)}) collective-permute-start(f32[256,16]{0,1:T(8,128)S(1)} %multiply_add_fusion.5), channel_id=1, source_target_pairs={{0,128},{16,144},{32,160},{48,176},{64,192},{80,208},{96,224},{112... | collective-permute-start | bytes 49160 | tf_op jit(solution)/shard_map/ppermute | solution.py:16
  190.0 18.8 %collective-permute-start.7 = (f32[256,16]{0,1:T(8,128)S(1)}, f32[256,16]{0,1:T(8,128)S(1)}, u32[]{:S(2)}, u32[]{:S(2)}) collective-permute-start(f32[256,16]{0,1:T(8,128)S(1)} %multiply_add_fusion.4), channel_id=1, source_target_pairs={{0,256},{16,272},{32,288},{48,304},{64,320},{80,336},{96,352},{112... | collective-permute-start | bytes 49160 | tf_op jit(solution)/shard_map/ppermute | solution.py:16
  210.1 3.8 %fusion.3 = f32[256,8,64]{2,1,0:T(8,128)S(1)} fusion(f32[8,256,16]{2,0,1:T(8,128)S(1)} %copy.134, f32[256,16]{1,0:T(8,128)S(1)} %copy.133, f32[256,16]{1,0:T(8,128)S(1)} %copy.127, f32[64]{0:T(128)} %copy-done.11, f32[256,16]{1,0:T(8,128)S(1)} %copy.126), kind=kOutput, calls=%fused_computation.5 | convolution fusion | flops 25952256 | bytes 704768 | tf_op jit(solution)/shard_map/icm,bcm->bic/dot_general | solution.py:56
  214.0 4.1 %fusion.12 = bf16[1,512,256]{1,2,0:T(8,128)(2,1)S(1)} fusion(bf16[512,4096]{1,0:T(8,128)(2,1)} %bitcast.68, bf16[4096,512]{1,0:T(8,128)(2,1)} %bitcast.73), kind=kOutput, calls=%fused_computation.17 | convolution fusion | flops 1073872896 | bytes 6553600 | tf_op jit(solution)/shard_map/td,jdc->jtc/dot_general | solution.py:84
  218.2 1.5 collective-permute-start
  219.7 8.9 %fusion.7 = f32[8,64,256]{1,0,2:T(8,128)S(1)} fusion(f32[256,8,64]{2,1,0:T(8,128)S(1)} %fusion.3, bf16[8,64,256]{1,0,2:T(8,128)(2,1)S(1)} %copy.129, f32[64,64,256]{1,0,2:T(8,128)} %copy.130), kind=kOutput, calls=%fused_computation.13 | convolution fusion | flops 100794368 | bytes 5505024 | tf_op jit(solution)/shard_map/ijc,bjc->bic/dot_general | solution.py:42
  229.5 3.4 %convolution_convert_fusion = bf16[512,4096]{1,0:T(8,128)(2,1)S(1)} fusion(bf16[4096,512]{1,0:T(8,128)(2,1)} %bitcast.74, f32[1,514,256]{1,2,0:T(8,128)S(1)} %maximum_convert_fusion.1, f32[512,256]{0,1:T(8,128)S(1)} %copy.136, bf16[1,512,256]{1,2,0:T(8,128)(2,1)S(1)} %fusion.22, f32[256]{0:T(256)S(1)} %copy-done.10, f32[256]{0:T(256)S(1)} %bitcast.80, ...), kind=kOutput, calls=%fused_computation | convolution fusion | flops 1077149696 | bytes 8654848 | tf_op jit(solution)/shard_map/tc,ec->te/dot_general | solution.py:108
  233.3 68.9 %all_to_all.14 = bf16[512,16,256]{2,0,1:T(8,128)(2,1)} all-to-all(bf16[512,16,256]{2,0,1:T(8,128)(2,1)S(1)} %bitcast.67), channel_id=1, replica_groups=mesh['yh'=2,'z'=16,'ch'=16] {'ch'}, dimensions={1} | all-to-all | bytes 8388608 | tf_op jit(solution)/shard_map/all_to_all | solution.py:68
  302.2 3.5 %reduce_sum.22 = bf16[512,256]{1,0:T(8,128)(2,1)} reduce(bf16[512,16,256]{2,0,1:T(8,128)(2,1)} %all_to_all.14, bf16[]{:T(256)} %constant.18.clone.1), dimensions={1}, to_apply=%region_1.0 | reduce | flops 1966080 | bytes 4456450 | tf_op jit(solution)/shard_map/reduce_sum | solution.py:69
  (84 shorter events, 9.0 us)
Async XLA Ops:
  6.5 85.0 %all-gather.7.cloned.1.call-start = ((), (), s32[]{:S(2)}) async-start(), calls=%async_computation.2 | async-start | bytes 4456448 | tf_op jit(solution)/shard_map/all_gather | solution.py:80
  17.7 11.7 %copy-start.2 = (bf16[256,128]{1,0:T(8,128)(2,1)S(1)}, bf16[256,128]{1,0:T(8,128)(2,1)}, u32[]{:S(2)}) copy-start(bf16[256,128]{1,0:T(8,128)(2,1)} %param.13) | copy-start | bytes 196612
  17.7 90.1 %all-to-all-start = ((bf16[512,16,256]{2,0,1:T(8,128)(2,1)}), bf16[512,16,256]{2,0,1:T(8,128)(2,1)}, u32[]{:S(2)}, u32[]{:S(2)}) async-start(bf16[512,16,256]{2,0,1:T(8,128)(2,1)} %tile.2), calls=%async_computation | async-start | bytes 8388608 | tf_op jit(solution)/shard_map/all_to_all | solution.py:62
  29.4 184.5 %all-gather.9.cloned.1.call-start = ((), (), s32[]{:S(2)}) async-start(), calls=%async_computation.3 | async-start | bytes 4456448 | tf_op jit(solution)/shard_map/all_gather | solution.py:80
  91.5 12.6 %copy-start.5 = (f32[256,16]{0,1:T(8,128)S(1)}, f32[256,16]{0,1:T(8,128)}, u32[]{:S(2)}) copy-start(f32[256,16]{0,1:T(8,128)} %param.11) | copy-start | bytes 49156
  91.5 12.7 %copy-start = (f32[256,16]{0,1:T(8,128)S(1)}, f32[256,16]{0,1:T(8,128)}, u32[]{:S(2)}) copy-start(f32[256,16]{0,1:T(8,128)} %param.10) | copy-start | bytes 49156
  91.5 12.8 %copy-start.9 = (f32[3,3,256]{2,1,0:T(4,128)S(1)}, f32[3,3,256]{2,1,0:T(4,128)}, u32[]{:S(2)}) copy-start(f32[3,3,256]{2,1,0:T(4,128)} %param.9) | copy-start | bytes 27652
  104.4 10.0 %copy-start.11 = (f32[64]{0:T(128)}, f32[64]{0:T(128)S(1)}, u32[]{:S(2)}) copy-start(f32[64]{0:T(128)S(1)} %iota_negate_fusion) | copy-start | bytes 772
  127.7 5.3 %collective-permute-start.1 = (bf16[2,2,256]{1,2,0:T(8,128)(2,1)S(1)}, bf16[2,2,256]{1,2,0:T(8,128)(2,1)S(1)}, u32[]{:S(2)}, u32[]{:S(2)}) collective-permute-start(bf16[2,2,256]{1,2,0:T(8,128)(2,1)S(1)} %slice.175), channel_id=1, source_target_pairs={{0,16},{16,32},{32,48},{48,64},{64,80},{80,96},{96,112},{112,128},... | collective-permute-start | bytes 6152 | tf_op jit(solution)/shard_map/ppermute | solution.py:16
  134.8 4.3 %copy-start.1 = (f32[256,16]{0,1:T(8,128)S(1)}, f32[256,16]{0,1:T(8,128)}, u32[]{:S(2)}) copy-start(f32[256,16]{0,1:T(8,128)} %get-tuple-element.17) | copy-start | bytes 49156
  134.8 4.3 %copy-start.4 = (f32[256,16]{0,1:T(8,128)S(1)}, f32[256,16]{0,1:T(8,128)}, u32[]{:S(2)}) copy-start(f32[256,16]{0,1:T(8,128)} %get-tuple-element.16) | copy-start | bytes 49156
  137.6 20.5 %copy-start.3 = (f32[256,16]{0,1:T(8,128)S(1)}, f32[256,16]{0,1:T(8,128)}, u32[]{:S(2)}) copy-start(f32[256,16]{0,1:T(8,128)} %get-tuple-element.15) | copy-start | bytes 49156
  139.4 8.5 %collective-permute-start.2 = (f32[256,16]{0,1:T(8,128)S(1)}, f32[256,16]{0,1:T(8,128)S(1)}, u32[]{:S(2)}, u32[]{:S(2)}) collective-permute-start(f32[256,16]{0,1:T(8,128)S(1)} %add_bitcast_fusion), channel_id=1, source_target_pairs={{0,16},{16,32},{32,48},{48,64},{64,80},{80,96},{96,112},{112,128},... | collective-permute-start | bytes 49160 | tf_op jit(solution)/shard_map/ppermute | solution.py:16
  147.9 5.5 %collective-permute-start.3 = (f32[256,16]{0,1:T(8,128)S(1)}, f32[256,16]{0,1:T(8,128)S(1)}, u32[]{:S(2)}, u32[]{:S(2)}) collective-permute-start(f32[256,16]{0,1:T(8,128)S(1)} %collective-permute-done.2), channel_id=1, source_target_pairs={{0,16},{16,32},{32,48},{48,64},{64,80},{80,96},{96,112},{112,128},... | collective-permute-start | bytes 49160 | tf_op jit(solution)/shard_map/ppermute | solution.py:16
  153.3 18.9 %collective-permute-start.4 = (f32[256,16]{0,1:T(8,128)S(1)}, f32[256,16]{0,1:T(8,128)S(1)}, u32[]{:S(2)}, u32[]{:S(2)}) collective-permute-start(f32[256,16]{0,1:T(8,128)S(1)} %multiply_add_fusion.7), channel_id=1, source_target_pairs={{0,32},{16,48},{32,64},{48,80},{64,96},{80,112},{96,128},{112,144}... | collective-permute-start | bytes 49160 | tf_op jit(solution)/shard_map/ppermute | solution.py:16
  172.2 5.8 %collective-permute-start.5 = (f32[256,16]{0,1:T(8,128)S(1)}, f32[256,16]{0,1:T(8,128)S(1)}, u32[]{:S(2)}, u32[]{:S(2)}) collective-permute-start(f32[256,16]{0,1:T(8,128)S(1)} %multiply_add_fusion.6), channel_id=1, source_target_pairs={{0,64},{16,80},{32,96},{48,112},{64,128},{80,144},{96,160},{112,17... | collective-permute-start | bytes 49160 | tf_op jit(solution)/shard_map/ppermute | solution.py:16
  178.1 11.9 %collective-permute-start.6 = (f32[256,16]{0,1:T(8,128)S(1)}, f32[256,16]{0,1:T(8,128)S(1)}, u32[]{:S(2)}, u32[]{:S(2)}) collective-permute-start(f32[256,16]{0,1:T(8,128)S(1)} %multiply_add_fusion.5), channel_id=1, source_target_pairs={{0,128},{16,144},{32,160},{48,176},{64,192},{80,208},{96,224},{112... | collective-permute-start | bytes 49160 | tf_op jit(solution)/shard_map/ppermute | solution.py:16
  190.0 19.6 %collective-permute-start.7 = (f32[256,16]{0,1:T(8,128)S(1)}, f32[256,16]{0,1:T(8,128)S(1)}, u32[]{:S(2)}, u32[]{:S(2)}) collective-permute-start(f32[256,16]{0,1:T(8,128)S(1)} %multiply_add_fusion.4), channel_id=1, source_target_pairs={{0,256},{16,272},{32,288},{48,304},{64,320},{80,336},{96,352},{112... | collective-permute-start | bytes 49160 | tf_op jit(solution)/shard_map/ppermute | solution.py:16
  218.2 11.3 %copy-start.6 = (f32[1,1,256]{2,1,0:T(1,128)S(1)}, f32[1,1,256]{2,1,0:T(1,128)}, u32[]{:S(2)}) copy-start(f32[1,1,256]{2,1,0:T(1,128)} %get-tuple-element.18) | copy-start | bytes 3076
  218.2 11.3 %copy-start.7 = (f32[1,1,256]{2,1,0:T(1,128)S(1)}, f32[1,1,256]{2,1,0:T(1,128)}, u32[]{:S(2)}) copy-start(f32[1,1,256]{2,1,0:T(1,128)} %get-tuple-element.19) | copy-start | bytes 3076
  218.2 11.3 %copy-start.8 = (f32[1,1,256]{2,1,0:T(1,128)S(1)}, f32[1,1,256]{2,1,0:T(1,128)}, u32[]{:S(2)}) copy-start(f32[1,1,256]{2,1,0:T(1,128)} %get-tuple-element.20) | copy-start | bytes 3076
  218.2 11.3 %copy-start.10 = (f32[256]{0:T(256)S(1)}, f32[256]{0:T(256)}, u32[]{:S(2)}) copy-start(f32[256]{0:T(256)} %param.12) | copy-start | bytes 3076
  218.2 11.0 %collective-permute-start = (bf16[1,2,256]{1,2,0:T(8,128)(2,1)S(1)}, bf16[1,2,256]{1,2,0:T(8,128)(2,1)S(1)}, u32[]{:S(2)}, u32[]{:S(2)}) collective-permute-start(bf16[1,2,256]{1,2,0:T(8,128)(2,1)S(1)} %slice.171), channel_id=1, source_target_pairs={{0,16},{16,32},{32,48},{48,64},{64,80},{80,96},{96,112},{112,128},... | collective-permute-start | bytes 3080 | tf_op jit(solution)/shard_map/ppermute | solution.py:16
Sparse Core Ops, SparseCore 0:
  14.5 77.0 all-gather.6
  104.2 78.4 all-gather.8

commit v6 on v5

--- a/solution.py
+++ b/solution.py
@@ -17,12 +17,14 @@
 
 
 def carried_in(final, rates, rows, count):
-    incoming = passed_along(final, CTX, count, 1)
-    shift = 1
-    while shift < count:
-        incoming = incoming + jnp.exp(-(shift * rows) * rates) * passed_along(incoming, CTX, count, shift)
-        shift *= 2
-    return incoming
+    copies = jnp.broadcast_to(final[None], (count,) + final.shape)
+    every = lax.all_to_all(copies, CTX, 0, 0)
+    position = lax.axis_index(CTX)
+    earlier = jnp.arange(count)
+    gap = jnp.maximum(position - 1 - earlier, 0).astype(jnp.float32)
+    weight = jnp.exp(-(gap[:, None, None] * rows) * rates[None])
+    weight = jnp.where((earlier < position)[:, None, None], weight, 0.0)
+    return jnp.sum(weight * every, axis=0)
 
 
 def block_terms(values, rates, residues):
@@ -58,8 +60,8 @@
 
 
 def gathered_tokens(tokens, lanes):
-    copies = jnp.tile(tokens, (1, lanes))
-    return lax.all_to_all(copies, CH, 1, 1, tiled=True)
+    copies = jnp.broadcast_to(tokens[:, None], (tokens.shape[0], lanes, tokens.shape[1]))
+    return lax.all_to_all(copies, CH, 1, 1)
 
 
 def scattered_terms(terms, lanes):
@@ -81,7 +83,8 @@
             return part.reshape(part.shape[0], -1, part.shape[-1])
 
         def shortened(weight):
-            proj = jnp.einsum("td,jdc->jtc", whole, weight, preferred_element_type=jnp.float32)
+            weight = weight.reshape(weight.shape[0], lanes, -1, weight.shape[-1])
+            proj = jnp.einsum("tkd,jkdc->jtc", whole, weight, preferred_element_type=jnp.float32)
             proj = proj.astype(jnp.bfloat16)
             earlier = passed_along(proj[:, rows - (SHORT - 1) :, :], CTX, count, 1)
             return jnp.concatenate([earlier, proj], axis=1).astype(jnp.float32)

time: 315 us -> 290 us (0.921)
  waiting for transfers between devices: 63.6 us -> 105 us
  starting transfers between devices: 62.8 us -> 28 us
  local copies, waits for them, and re-layouts: 47.8 us -> 25.7 us
  blocking collectives: 81.8 us -> 75.6 us
    ppermute x8 -> x2, starting transfers between devices: 51.1 us -> 5.1 us  [passed_along(): return lax.ppermute(block, axis, route)]
    all_gather x2, waiting for transfers between devices: 61.1 us -> 89.2 us  [spread(): part = lax.all_gather(part, 'z', axis=2)]
    all_to_all x3 -> x0, local copies, waits for them, and re-layouts: 18.7 us -> none  [gathered_tokens(): return lax.all_to_all(copies, CH, 1, 1, tiled=True)]
    all_to_all x1 -> x2, waiting for transfers between devices: 0.01 us -> 15.3 us  [the longest x1 15.3 us: carried_in(): every = lax.all_to_all(copies, CTX, 0, 0)]
    all_to_all x1 -> x2, starting transfers between devices: 11.7 us -> 22.9 us  [the longest x1 11.7 us: gathered_tokens(): return lax.all_to_all(copies, CH, 1, 1)]
    all_to_all x1, blocking collectives: 68.9 us -> 62.3 us  [scattered_terms(): parts = lax.all_to_all(split, CH, 1, 1)]
    reshape x1 -> x0, local copies, waits for them, and re-layouts: 6.45 us -> none  [spread(): return part.reshape(part.shape[0], -1, part.shape[-1])]
    broadcast_in_dim x0 -> x2, local copies, waits for them, and re-layouts: none -> 4.21 us  [the longest x1 3.35 us: gathered_tokens(): jnp.broadcast_to(tokens[:, None], (tokens.shape[0], lanes, tokens.shape[1]))]
  transfers between devices with their start and end apart: 11 -> 6, of which waited for: 4 -> 3; matrix products, arithmetic and copies ran while one was open for 25% -> 18% of each run, Pallas kernels for 0% -> 0%
where the time goes in v6:
time: 290 us; the launch traced here: 289 us
  waiting for transfers between devices  105 us (36%)
  blocking collectives  75.6 us (26%)
  matrix products  32.2 us (11%)
  starting transfers between devices  28 us (10%)
  local copies, waits for them, and re-layouts  25.7 us (9%)
  between operations  13.9 us (5%)
  other arithmetic  8.87 us (3%)
    all_gather x2, waiting for transfers between devices, spread(): part = lax.all_gather(part, 'z', axis=2)  89.2 us
    all_to_all x1, blocking collectives, scattered_terms(): parts = lax.all_to_all(split, CH, 1, 1)  62.3 us
    all_to_all x1, waiting for transfers between devices, carried_in(): every = lax.all_to_all(copies, CTX, 0, 0)  15.3 us
    all_gather x2, blocking collectives, spread(): part = lax.all_gather(part, 'yh', axis=1)  13.3 us
    all_to_all x1, starting transfers between devices, gathered_tokens(): return lax.all_to_all(copies, CH, 1, 1)  11.7 us
    all_to_all x1, starting transfers between devices, carried_in(): every = lax.all_to_all(copies, CTX, 0, 0)  11.2 us
    dot_general x2, matrix products, shortened(): jnp.einsum('tkd,jkdc->jtc', whole, weight, preferred_element_type=jnp.flo...  9.34 us
    dot_general x1, local copies, waits for them, and re-layouts, block_terms(): jnp.dot(pick, impulse, precision=lax.Precision.HIGHEST)  9.17 us
  transfers between devices with their start and end apart: 6, of which 3 were waited for; matrix products, arithmetic and copies ran while one was open for 18% of the time, Pallas kernels for 0%

profile of v6, /device:TPU:1, one launch (start us, length us, event | category | flops | bytes accessed | tf_op | source)
XLA Modules:
  0.0 288.9 jit_solution(8172861564023488586)
XLA Ops:
  6.5 0.9 slice.133
  7.5 6.9 %all-gather = bf16[2,256,256]{2,1,0:T(8,128)(2,1)} all-gather(bf16[2,128,256]{2,1,0:T(8,128)(2,1)S(1)} %slice.133), channel_id=2, replica_groups=mesh['yh'=2,'z'=16,'ch'=16] {'yh'}, dimensions={1}, use_global_device_ids=true | all-gather | bytes 393216 | tf_op jit(solution)/shard_map/all_gather | solution.py:81
  14.3 3.3 %broadcast_in_dim.17 = bf16[512,16,256]{2,0,1:T(8,128)(2,1)} broadcast(bf16[512,256]{1,0:T(8,128)(2,1)} %param.7), dimensions={0,2} | broadcast | bytes 4456448 | tf_op jit(solution)/shard_map/broadcast_in_dim | solution.py:63
  17.7 11.7 %all-to-all-start = ((bf16[512,16,256]{2,0,1:T(8,128)(2,1)}), bf16[512,16,256]{2,0,1:T(8,128)(2,1)}, u32[]{:S(2)}, u32[]{:S(2)}) async-start(bf16[512,16,256]{2,0,1:T(8,128)(2,1)} %broadcast_in_dim.17), calls=%async_computation | async-start | bytes 8388608 | tf_op jit(solution)/shard_map/all_to_all | solution.py:64
  29.6 0.8 slice_bitcast_fusion
  30.4 60.5 %all-gather.7.cloned.1.call-done = bf16[2,2,2048,256]{3,2,1,0:T(8,128)(2,1)} async-done(((bf16[2,2,128,256]{3,2,1,0:T(8,128)(2,1)}), bf16[2,2,2048,256]{3,2,1,0:T(8,128)(2,1)}) %all-gather.7.cloned.1.call-update) | async-done | bytes 4194320 | tf_op jit(solution)/shard_map/all_gather | solution.py:82
  90.9 6.5 %all-gather.2 = bf16[2,128,512]{2,1,0:T(8,128)(2,1)} all-gather(bf16[1,128,512]{2,1,0:T(8,128)(2,1)S(1)} %maximum_bitcast_fusion), channel_id=4, replica_groups=mesh['yh'=2,'z'=16,'ch'=16] {'yh'}, dimensions={0}, use_global_device_ids=true | all-gather | bytes 393216 | tf_op jit(solution)/shard_map/all_gather | solution.py:81
  97.6 0.6 negate_exponential_fusion
  98.3 2.8 multiply_reduce_fusion
  101.1 5.9 %fusion.14 = bf16[2,512,256]{1,2,0:T(8,128)(2,1)S(1)} fusion(bf16[2,16,256,256]{3,2,1,0:T(8,128)(2,1)} %bitcast.103, bf16[512,16,256]{2,0,1:T(8,128)(2,1)} %all-to-all-done), kind=kOutput, calls=%fused_computation.16 | convolution fusion | flops 2147745792 | bytes 8912896 | tf_op jit(solution)/shard_map/tkd,jkdc->jtc/dot_general | solution.py:87
  107.1 2.2 collective-permute-start.1
  109.3 2.7 rev.3
  112.4 0.9 fusion.19
  113.8 2.7 fusion.48
  116.6 1.5 copy.126
  118.4 0.9 broadcast_in_dim.21
  119.2 11.2 %all-to-all-start.1 = ((f32[32,256,16]{1,2,0:T(8,128)}), f32[32,256,16]{1,2,0:T(8,128)S(1)}, u32[]{:S(2)}, u32[]{:S(2)}) async-start(f32[32,256,16]{1,2,0:T(8,128)} %broadcast_in_dim.21), calls=%async_computation.1 | async-start | bytes 1048576 | tf_op jit(solution)/shard_map/all_to_all | solution.py:21
  130.4 0.8 copy.127
  131.2 3.8 %fusion.5 = f32[64,64,256]{2,1,0:T(8,128)} fusion(s32[64,64]{1,0:T(8,128)S(1)} %iota_subtract_fusion, f32[64,256]{0,1:T(8,128)S(1)} %get-tuple-element.9), kind=kOutput, calls=%fused_computation.9 | convolution fusion | flops 805568512 | bytes 4276224 | tf_op jit(solution)/shard_map/dot_general | solution.py:40
  135.0 9.2 %copy.124 = f32[64,64,256]{1,0,2:T(8,128)} copy(f32[64,64,256]{2,1,0:T(8,128)} %fusion.5) | data formatting | bytes 8388608 | tf_op jit(solution)/shard_map/dot_general | solution.py:40
  144.2 1.3 fusion.47
  145.6 15.3 %all-to-all-done.1 = f32[32,256,16]{1,2,0:T(8,128)S(1)} async-done(((f32[32,256,16]{1,2,0:T(8,128)}), f32[32,256,16]{1,2,0:T(8,128)S(1)}, u32[]{:S(2)}, u32[]{:S(2)}) %all-to-all-start.1) | async-done | bytes 524320 | tf_op jit(solution)/shard_map/all_to_all | solution.py:21
  161.6 4.1 %fusion.3 = f32[256,8,64]{2,1,0:T(8,128)S(1)} fusion(f32[8,256,16]{2,0,1:T(8,128)S(1)} %copy.128, f32[256,16]{1,0:T(8,128)} %copy.127, f32[256,16]{1,0:T(8,128)S(1)} %copy.121, f32[64]{0:T(128)} %copy-done.11, f32[256,16]{1,0:T(8,128)S(1)} %copy.120), kind=kOutput, calls=%fused_computation.5 | convolution fusion | flops 25952256 | bytes 704768 | tf_op jit(solution)/shard_map/icm,bcm->bic/dot_general | solution.py:58
  165.7 28.7 %all-gather.9.cloned.1.call-done = bf16[2,2048,512]{2,1,0:T(8,128)(2,1)} async-done(((bf16[2,128,512]{2,1,0:T(8,128)(2,1)}), bf16[2,2048,512]{2,1,0:T(8,128)(2,1)}) %all-gather.9.cloned.1.call-update) | async-done | bytes 4194320 | tf_op jit(solution)/shard_map/all_gather | solution.py:82
  194.4 1.7 slice.170
  196.1 3.5 %fusion.18 = bf16[1,512,256]{1,2,0:T(8,128)(2,1)S(1)} fusion(bf16[16,256,256]{2,1,0:T(8,128)(2,1)S(1)} %bitcast.93, bf16[512,16,256]{2,0,1:T(8,128)(2,1)} %all-to-all-done), kind=kOutput, calls=%fused_computation.19 | convolution fusion | flops 1073872896 | bytes 6553600 | tf_op jit(solution)/shard_map/tkd,jkdc->jtc/dot_general | solution.py:87
  199.7 2.9 %collective-permute-start = (bf16[1,2,256]{1,2,0:T(8,128)(2,1)S(1)}, bf16[1,2,256]{1,2,0:T(8,128)(2,1)S(1)}, u32[]{:S(2)}, u32[]{:S(2)}) collective-permute-start(bf16[1,2,256]{1,2,0:T(8,128)(2,1)S(1)} %slice.171), channel_id=1, source_target_pairs={{0,16},{16,32},{32,48},{48,64},{64,80},{80,96},{96,112},{112,128},... | collective-permute-start | bytes 3080 | tf_op jit(solution)/shard_map/ppermute | solution.py:16
  202.6 8.9 %fusion.10 = f32[8,64,256]{1,0,2:T(8,128)S(1)} fusion(f32[256,8,64]{2,1,0:T(8,128)S(1)} %fusion.3, bf16[8,64,256]{1,0,2:T(8,128)(2,1)S(1)} %copy.123, f32[64,64,256]{1,0,2:T(8,128)} %copy.124), kind=kOutput, calls=%fused_computation.14 | convolution fusion | flops 100794368 | bytes 5505024 | tf_op jit(solution)/shard_map/ijc,bjc->bic/dot_general | solution.py:44
  212.4 3.4 %convolution_convert_fusion = bf16[512,4096]{1,0:T(8,128)(2,1)S(1)} fusion(bf16[4096,512]{1,0:T(8,128)(2,1)} %bitcast.91, f32[1,514,256]{1,2,0:T(8,128)S(1)} %maximum_convert_fusion.1, f32[512,256]{0,1:T(8,128)S(1)} %copy.130, bf16[1,512,256]{1,2,0:T(8,128)(2,1)S(1)} %fusion.26, f32[256]{0:T(256)S(1)} %copy-done.10, f32[256]{0:T(256)S(1)} %bitcast.101, ...), kind=kOutput, calls=%fused_computation | convolution fusion | flops 1077149696 | bytes 8654848 | tf_op jit(solution)/shard_map/tc,ec->te/dot_general | solution.py:111
  215.8 0.4 copy.139
  216.2 62.3 %all_to_all.15 = bf16[512,16,256]{2,0,1:T(8,128)(2,1)} all-to-all(bf16[512,16,256]{2,0,1:T(8,128)(2,1)S(1)} %bitcast.89), channel_id=1, replica_groups=mesh['yh'=2,'z'=16,'ch'=16] {'ch'}, dimensions={1} | all-to-all | bytes 8388608 | tf_op jit(solution)/shard_map/all_to_all | solution.py:70
  278.5 3.5 %reduce_sum.32 = bf16[512,256]{1,0:T(8,128)(2,1)} reduce(bf16[512,16,256]{2,0,1:T(8,128)(2,1)} %all_to_all.15, bf16[]{:T(256)} %constant.28.clone.1), dimensions={1}, to_apply=%region_2.3 | reduce | flops 1966080 | bytes 4456450 | tf_op jit(solution)/shard_map/reduce_sum | solution.py:71
  (70 shorter events, 3.2 us)
Async XLA Ops:
  6.5 84.4 %all-gather.7.cloned.1.call-start = ((), (), s32[]{:S(2)}) async-start(), calls=%async_computation.3 | async-start | bytes 4456448 | tf_op jit(solution)/shard_map/all_gather | solution.py:82
  17.7 11.8 %copy-start.2 = (bf16[256,128]{1,0:T(8,128)(2,1)S(1)}, bf16[256,128]{1,0:T(8,128)(2,1)}, u32[]{:S(2)}) copy-start(bf16[256,128]{1,0:T(8,128)(2,1)} %param.13) | copy-start | bytes 196612
  17.7 79.7 %copy-start.5 = (f32[256,16]{0,1:T(8,128)S(1)}, f32[256,16]{0,1:T(8,128)}, u32[]{:S(2)}) copy-start(f32[256,16]{0,1:T(8,128)} %param.11) | copy-start | bytes 49156
  17.7 79.8 %copy-start = (f32[256,16]{0,1:T(8,128)S(1)}, f32[256,16]{0,1:T(8,128)}, u32[]{:S(2)}) copy-start(f32[256,16]{0,1:T(8,128)} %param.10) | copy-start | bytes 49156
  17.7 83.4 %all-to-all-start = ((bf16[512,16,256]{2,0,1:T(8,128)(2,1)}), bf16[512,16,256]{2,0,1:T(8,128)(2,1)}, u32[]{:S(2)}, u32[]{:S(2)}) async-start(bf16[512,16,256]{2,0,1:T(8,128)(2,1)} %broadcast_in_dim.17), calls=%async_computation | async-start | bytes 8388608 | tf_op jit(solution)/shard_map/all_to_all | solution.py:64
  29.4 165.0 %all-gather.9.cloned.1.call-start = ((), (), s32[]{:S(2)}) async-start(), calls=%async_computation.4 | async-start | bytes 4456448 | tf_op jit(solution)/shard_map/all_gather | solution.py:82
  97.6 0.7 copy-start.11
  101.1 8.2 %copy-start.9 = (f32[3,3,256]{2,1,0:T(4,128)S(1)}, f32[3,3,256]{2,1,0:T(4,128)}, u32[]{:S(2)}) copy-start(f32[3,3,256]{2,1,0:T(4,128)} %param.9) | copy-start | bytes 27652
  107.1 5.0 %collective-permute-start.1 = (bf16[2,2,256]{1,2,0:T(8,128)(2,1)S(1)}, bf16[2,2,256]{1,2,0:T(8,128)(2,1)S(1)}, u32[]{:S(2)}, u32[]{:S(2)}) collective-permute-start(bf16[2,2,256]{1,2,0:T(8,128)(2,1)S(1)} %slice.175), channel_id=1, source_target_pairs={{0,16},{16,32},{32,48},{48,64},{64,80},{80,96},{96,112},{112,128},... | collective-permute-start | bytes 6152 | tf_op jit(solution)/shard_map/ppermute | solution.py:16
  113.8 4.3 %copy-start.1 = (f32[256,16]{0,1:T(8,128)S(1)}, f32[256,16]{0,1:T(8,128)}, u32[]{:S(2)}) copy-start(f32[256,16]{0,1:T(8,128)} %get-tuple-element.17) | copy-start | bytes 49156
  113.8 4.3 %copy-start.4 = (f32[256,16]{0,1:T(8,128)S(1)}, f32[256,16]{0,1:T(8,128)}, u32[]{:S(2)}) copy-start(f32[256,16]{0,1:T(8,128)} %get-tuple-element.16) | copy-start | bytes 49156
  116.6 13.9 %copy-start.3 = (f32[256,16]{0,1:T(8,128)S(1)}, f32[256,16]{0,1:T(8,128)}, u32[]{:S(2)}) copy-start(f32[256,16]{0,1:T(8,128)} %get-tuple-element.15) | copy-start | bytes 49156
  119.2 41.7 %all-to-all-start.1 = ((f32[32,256,16]{1,2,0:T(8,128)}), f32[32,256,16]{1,2,0:T(8,128)S(1)}, u32[]{:S(2)}, u32[]{:S(2)}) async-start(f32[32,256,16]{1,2,0:T(8,128)} %broadcast_in_dim.21), calls=%async_computation.1 | async-start | bytes 1048576 | tf_op jit(solution)/shard_map/all_to_all | solution.py:21
  199.7 12.5 %collective-permute-start = (bf16[1,2,256]{1,2,0:T(8,128)(2,1)S(1)}, bf16[1,2,256]{1,2,0:T(8,128)(2,1)S(1)}, u32[]{:S(2)}, u32[]{:S(2)}) collective-permute-start(bf16[1,2,256]{1,2,0:T(8,128)(2,1)S(1)} %slice.171), channel_id=1, source_target_pairs={{0,16},{16,32},{32,48},{48,64},{64,80},{80,96},{96,112},{112,128},... | collective-permute-start | bytes 3080 | tf_op jit(solution)/shard_map/ppermute | solution.py:16
  211.6 0.8 copy-start.6
  211.6 0.8 copy-start.7
  211.6 0.8 copy-start.8
  211.6 0.8 copy-start.10
Sparse Core Ops, SparseCore 0:
  14.5 76.4 all-gather.6
  97.5 96.8 all-gather.8

commit v7 on v6

--- a/solution.py
+++ b/solution.py
@@ -76,18 +76,21 @@
         rows = tokens.shape[0]
         width = in_weight.shape[2]
         whole = gathered_tokens(tokens, lanes)
+        halo = passed_along(whole[rows - (SHORT - 1) :], CTX, count, 1)
 
-        def spread(part):
-            part = lax.all_gather(part, "yh", axis=1)
+        def across_yh(part):
+            return lax.all_gather(part, "yh", axis=1)
+
+        def across_z(part):
             part = lax.all_gather(part, "z", axis=2)
             return part.reshape(part.shape[0], -1, part.shape[-1])
 
         def shortened(weight):
             weight = weight.reshape(weight.shape[0], lanes, -1, weight.shape[-1])
             proj = jnp.einsum("tkd,jkdc->jtc", whole, weight, preferred_element_type=jnp.float32)
-            proj = proj.astype(jnp.bfloat16)
-            earlier = passed_along(proj[:, rows - (SHORT - 1) :, :], CTX, count, 1)
-            return jnp.concatenate([earlier, proj], axis=1).astype(jnp.float32)
+            earlier = jnp.einsum("tkd,jkdc->jtc", halo, weight, preferred_element_type=jnp.float32)
+            proj = jnp.concatenate([earlier, proj], axis=1).astype(jnp.bfloat16)
+            return proj.astype(jnp.float32)
 
         def filtered(widened, taps):
             feats = jnp.zeros((widened.shape[0], rows, width), jnp.float32)
@@ -95,11 +98,11 @@
                 feats = feats + taps[i][:, None, :] * widened[:, SHORT - 1 - i : SHORT - 1 - i + rows, :]
             return feats
 
-        pair = spread(in_weight[1:])
-        packed = jnp.concatenate([in_weight[0], out_weight.T], axis=1)[None]
+        pair = across_z(across_yh(in_weight[1:]))
+        packed = across_yh(jnp.concatenate([in_weight[0], out_weight.T], axis=1)[None])
         packed, pair = lax.optimization_barrier((packed, pair))
         feats = filtered(shortened(pair), short_taps[:, 1:])
-        packed = spread(packed)[0]
+        packed = across_z(packed)[0]
         query = filtered(shortened(packed[None, :, :width]), short_taps[:, :1])[0]
         gated = (feats[0] * feats[1]).astype(jnp.bfloat16)
         values = gated.astype(jnp.float32)

time: 290 us -> 334 us (1.15)
  blocking collectives: 75.6 us -> 110 us
  local copies, waits for them, and re-layouts: 25.7 us -> 37.9 us
  starting transfers between devices: 28 us -> 23.9 us
    all_gather x2, blocking collectives: 13.3 us -> 44.2 us  [across_yh(): return lax.all_gather(part, 'yh', axis=1)]
    all_gather x0 -> x2, local copies, waits for them, and re-layouts: none -> 11.9 us  [the longest x1 11.1 us: across_z(): part = lax.all_gather(part, 'z', axis=2)]
    all_to_all x1, blocking collectives: 62.3 us -> 65.7 us  [scattered_terms(): parts = lax.all_to_all(split, CH, 1, 1)]
  transfers between devices with their start and end apart: 6 -> 5, of which waited for: 3 -> 3; matrix products, arithmetic and copies ran while one was open for 18% -> 17% of each run, Pallas kernels for 0% -> 0%
where the time goes in v7:
time: 334 us; the launch traced here: 333 us
  blocking collectives  110 us (33%)
  waiting for transfers between devices  105 us (31%)
  local copies, waits for them, and re-layouts  37.9 us (11%)
  matrix products  34 us (10%)
  starting transfers between devices  23.9 us (7%)
  between operations  13.9 us (4%)
  other arithmetic  8.82 us (3%)
    all_gather x2, waiting for transfers between devices, across_z(): part = lax.all_gather(part, 'z', axis=2)  90.5 us
    all_to_all x1, blocking collectives, scattered_terms(): parts = lax.all_to_all(split, CH, 1, 1)  65.7 us
    all_gather x2, blocking collectives, across_yh(): return lax.all_gather(part, 'yh', axis=1)  44.2 us
    all_to_all x1, waiting for transfers between devices, carried_in(): every = lax.all_to_all(copies, CTX, 0, 0)  14 us
    all_to_all x1, starting transfers between devices, gathered_tokens(): return lax.all_to_all(copies, CH, 1, 1)  11.7 us
    all_gather x1, local copies, waits for them, and re-layouts, across_z(): part = lax.all_gather(part, 'z', axis=2)  11.1 us
    all_to_all x1, starting transfers between devices, carried_in(): every = lax.all_to_all(copies, CTX, 0, 0)  9.78 us
    dot_general x2, matrix products, shortened(): jnp.einsum('tkd,jkdc->jtc', whole, weight, preferred_element_type=jnp.flo...  9.49 us
  transfers between devices with their start and end apart: 5, of which 3 were waited for; matrix products, arithmetic and copies ran while one was open for 17% of the time, Pallas kernels for 0%

profile of v7, /device:TPU:1, one launch (start us, length us, event | category | flops | bytes accessed | tf_op | source)
XLA Modules:
  0.0 333.0 jit_solution(8756740000981403255)
XLA Ops:
  6.5 0.9 slice.130
  7.5 6.9 %all-gather.1 = bf16[2,256,256]{2,1,0:T(8,128)(2,1)} all-gather(bf16[2,128,256]{2,1,0:T(8,128)(2,1)S(1)} %slice.130), channel_id=3, replica_groups=mesh['yh'=2,'z'=16,'ch'=16] {'yh'}, dimensions={1}, use_global_device_ids=true | all-gather | bytes 393216 | tf_op jit(solution)/shard_map/all_gather | solution.py:82
  14.3 3.4 %broadcast_in_dim.14 = bf16[512,16,256]{2,0,1:T(8,128)(2,1)} broadcast(bf16[512,256]{1,0:T(8,128)(2,1)} %param.7), dimensions={0,2} | broadcast | bytes 4456448 | tf_op jit(solution)/shard_map/broadcast_in_dim | solution.py:63
  17.7 11.7 %all-to-all-start = ((bf16[512,16,256]{2,0,1:T(8,128)(2,1)}), bf16[512,16,256]{2,0,1:T(8,128)(2,1)}, u32[]{:S(2)}, u32[]{:S(2)}) async-start(bf16[512,16,256]{2,0,1:T(8,128)(2,1)} %broadcast_in_dim.14), calls=%async_computation | async-start | bytes 8388608 | tf_op jit(solution)/shard_map/all_to_all | solution.py:64
  29.6 37.3 %all-gather = bf16[256,512]{0,1:T(8,128)(2,1)S(1)} all-gather(bf16[128,512]{0,1:T(8,128)(2,1)S(1)} %pad_maximum_fusion), channel_id=2, replica_groups=mesh['yh'=2,'z'=16,'ch'=16] {'yh'}, dimensions={0}, use_global_device_ids=true | all-gather | bytes 393216 | tf_op jit(solution)/shard_map/all_gather | solution.py:82
  67.0 0.8 reshape.128
  67.7 23.4 %all-gather.7.cloned.1.call-done = bf16[2,2,2048,256]{3,2,1,0:T(8,128)(2,1)} async-done(((bf16[2,2,128,256]{3,2,1,0:T(8,128)(2,1)}), bf16[2,2,2048,256]{3,2,1,0:T(8,128)(2,1)}) %all-gather.7.cloned.1.call-update) | async-done | bytes 4194320 | tf_op jit(solution)/shard_map/all_gather | solution.py:85
  92.0 2.8 multiply_reduce_fusion
  94.8 0.9 slice.167
  95.6 2.4 collective-permute-start
  98.1 2.7 rev.3
  100.8 2.8 fusion.20
  103.9 5.8 %fusion.14 = bf16[2,512,256]{1,2,0:T(8,128)(2,1)S(1)} fusion(bf16[2,16,256,256]{3,2,1,0:T(8,128)(2,1)} %bitcast.119, bf16[512,16,256]{2,0,1:T(8,128)(2,1)} %all-to-all-done), kind=kOutput, calls=%fused_computation.16 | convolution fusion | flops 2147745792 | bytes 8912896 | tf_op jit(solution)/shard_map/tkd,jkdc->jtc/dot_general | solution.py:90
  110.0 0.9 fusion.23
  111.5 2.8 fusion.53
  114.3 1.5 copy.146
  116.1 0.9 broadcast_in_dim.18
  116.9 9.8 %all-to-all-start.1 = ((f32[32,256,16]{1,2,0:T(8,128)}), f32[32,256,16]{1,2,0:T(8,128)S(1)}, u32[]{:S(2)}, u32[]{:S(2)}) async-start(f32[32,256,16]{1,2,0:T(8,128)} %broadcast_in_dim.18), calls=%async_computation.1 | async-start | bytes 1048576 | tf_op jit(solution)/shard_map/all_to_all | solution.py:21
  126.7 0.7 copy.147
  127.5 3.8 %fusion.5 = f32[64,64,256]{2,1,0:T(8,128)} fusion(s32[64,64]{1,0:T(8,128)S(1)} %iota_subtract_fusion, f32[64,256]{0,1:T(8,128)S(1)} %get-tuple-element.9), kind=kOutput, calls=%fused_computation.9 | convolution fusion | flops 805568512 | bytes 4276224 | tf_op jit(solution)/shard_map/dot_general | solution.py:40
  131.2 9.2 %copy.144 = f32[64,64,256]{1,0,2:T(8,128)} copy(f32[64,64,256]{2,1,0:T(8,128)} %fusion.5) | data formatting | bytes 8388608 | tf_op jit(solution)/shard_map/dot_general | solution.py:40
  140.4 1.3 fusion.52
  141.9 14.0 %all-to-all-done.1 = f32[32,256,16]{1,2,0:T(8,128)S(1)} async-done(((f32[32,256,16]{1,2,0:T(8,128)}), f32[32,256,16]{1,2,0:T(8,128)S(1)}, u32[]{:S(2)}, u32[]{:S(2)}) %all-to-all-start.1) | async-done | bytes 524320 | tf_op jit(solution)/shard_map/all_to_all | solution.py:21
  156.6 4.1 %fusion.3 = f32[256,8,64]{2,1,0:T(8,128)S(1)} fusion(f32[8,256,16]{2,0,1:T(8,128)S(1)} %copy.148, f32[256,16]{1,0:T(8,128)} %copy.147, f32[256,16]{1,0:T(8,128)S(1)} %copy.141, f32[64]{0:T(128)} %copy-done.14, f32[256,16]{1,0:T(8,128)S(1)} %copy.140), kind=kOutput, calls=%fused_computation.5 | convolution fusion | flops 25952256 | bytes 704768 | tf_op jit(solution)/shard_map/icm,bcm->bic/dot_general | solution.py:58
  160.7 8.9 %fusion.10 = f32[8,64,256]{1,0,2:T(8,128)S(1)} fusion(f32[256,8,64]{2,1,0:T(8,128)S(1)} %fusion.3, bf16[8,64,256]{1,0,2:T(8,128)(2,1)S(1)} %copy.143, f32[64,64,256]{1,0,2:T(8,128)} %copy.144), kind=kOutput, calls=%fused_computation.14 | convolution fusion | flops 100794368 | bytes 5505024 | tf_op jit(solution)/shard_map/ijc,bjc->bic/dot_general | solution.py:44
  170.2 67.1 %all-gather.9.cloned.1.call-done = bf16[1,2,2048,512]{2,1,3,0:T(2,128)(2,1)} async-done(((bf16[1,2,128,512]{2,1,3,0:T(2,128)(2,1)}), bf16[1,2,2048,512]{2,1,3,0:T(2,128)(2,1)}) %all-gather.9.cloned.1.call-update) | async-done | bytes 4194320 | tf_op jit(solution)/shard_map/all_gather | solution.py:85
  237.4 11.1 %copy.134 = bf16[1,2,2048,512]{3,2,1,0:T(8,128)(2,1)} copy(bf16[1,2,2048,512]{2,1,3,0:T(2,128)(2,1)} %all-gather.9.cloned.1.call-done) | data formatting | bytes 8388608 | tf_op jit(solution)/shard_map/all_gather | solution.py:85
  248.5 1.7 slice.166
  250.8 3.6 %fusion.18 = bf16[1,512,256]{1,2,0:T(8,128)(2,1)S(1)} fusion(bf16[16,256,256]{2,1,0:T(8,128)(2,1)S(1)} %bitcast.117, bf16[512,16,256]{2,0,1:T(8,128)(2,1)} %all-to-all-done), kind=kOutput, calls=%fused_computation.19 | convolution fusion | flops 1073872896 | bytes 6553600 | tf_op jit(solution)/shard_map/tkd,jkdc->jtc/dot_general | solution.py:90
  254.7 1.8 convolution_convert_fusion
  256.9 65.7 %all_to_all.15 = bf16[512,16,256]{2,0,1:T(8,128)(2,1)} all-to-all(bf16[512,16,256]{2,0,1:T(8,128)(2,1)S(1)} %bitcast.113), channel_id=1, replica_groups=mesh['yh'=2,'z'=16,'ch'=16] {'ch'}, dimensions={1} | all-to-all | bytes 8388608 | tf_op jit(solution)/shard_map/all_to_all | solution.py:70
  322.6 3.5 %reduce_sum.32 = bf16[512,256]{1,0:T(8,128)(2,1)} reduce(bf16[512,16,256]{2,0,1:T(8,128)(2,1)} %all_to_all.15, bf16[]{:T(256)} %constant.28.clone.1), dimensions={1}, to_apply=%region_2.3 | reduce | flops 1966080 | bytes 4456450 | tf_op jit(solution)/shard_map/reduce_sum | solution.py:71
  (80 shorter events, 4.8 us)
Async XLA Ops:
  6.5 84.6 %all-gather.7.cloned.1.call-start = ((), (), s32[]{:S(2)}) async-start(), calls=%async_computation.3 | async-start | bytes 4456448 | tf_op jit(solution)/shard_map/all_gather | solution.py:85
  17.7 11.8 %slice-start = ((bf16[3,128,256]{2,1,0:T(8,128)(2,1)}), bf16[1,128,256]{2,1,0:T(8,128)(2,1)S(1)}, s32[]{:S(2)}) async-start(bf16[3,128,256]{2,1,0:T(8,128)(2,1)} %param.8), calls=%async_computation.5 | async-start | bytes 131072 | tf_op jit(solution)/shard_map/slice | solution.py:102
  17.7 11.9 %copy-start.7 = (bf16[256,128]{1,0:T(8,128)(2,1)S(1)}, bf16[256,128]{1,0:T(8,128)(2,1)}, u32[]{:S(2)}) copy-start(bf16[256,128]{1,0:T(8,128)(2,1)} %param.13) | copy-start | bytes 196612
  17.7 73.4 %copy-start.8 = (f32[256,16]{0,1:T(8,128)S(1)}, f32[256,16]{0,1:T(8,128)}, u32[]{:S(2)}) copy-start(f32[256,16]{0,1:T(8,128)} %param.11) | copy-start | bytes 49156
  17.7 73.5 %copy-start.1 = (f32[256,16]{0,1:T(8,128)S(1)}, f32[256,16]{0,1:T(8,128)}, u32[]{:S(2)}) copy-start(f32[256,16]{0,1:T(8,128)} %param.10) | copy-start | bytes 49156
  17.7 77.1 %all-to-all-start = ((bf16[512,16,256]{2,0,1:T(8,128)(2,1)}), bf16[512,16,256]{2,0,1:T(8,128)(2,1)}, u32[]{:S(2)}, u32[]{:S(2)}) async-start(bf16[512,16,256]{2,0,1:T(8,128)(2,1)} %broadcast_in_dim.14), calls=%async_computation | async-start | bytes 8388608 | tf_op jit(solution)/shard_map/all_to_all | solution.py:64
  29.4 207.9 %all-gather.9.cloned.1.call-start = ((), (), s32[]{:S(2)}) async-start(), calls=%async_computation.4 | async-start | bytes 4456448 | tf_op jit(solution)/shard_map/all_gather | solution.py:85
  29.6 68.4 %copy-start.12 = (f32[3,3,256]{2,1,0:T(4,128)S(1)}, f32[3,3,256]{2,1,0:T(4,128)}, u32[]{:S(2)}) copy-start(f32[3,3,256]{2,1,0:T(4,128)} %param.9) | copy-start | bytes 27652
  91.4 9.4 %copy-start.14 = (f32[64]{0:T(128)}, f32[64]{0:T(128)S(1)}, u32[]{:S(2)}) copy-start(f32[64]{0:T(128)S(1)} %iota_negate_fusion) | copy-start | bytes 772
  95.6 5.2 %collective-permute-start = (bf16[2,16,256]{2,0,1:T(2,128)(2,1)S(1)}, bf16[2,16,256]{2,0,1:T(2,128)(2,1)S(1)}, u32[]{:S(2)}, u32[]{:S(2)}) collective-permute-start(bf16[2,16,256]{2,0,1:T(2,128)(2,1)S(1)} %slice.167), channel_id=1, source_target_pairs={{0,16},{16,32},{32,48},{48,64},{64,80},{80,96},{96,112},{112,128},... | collective-permute-start | bytes 49160 | tf_op jit(solution)/shard_map/ppermute | solution.py:16
  100.8 2.8 copy-start.3
  111.5 4.3 %copy-start.2 = (f32[256,16]{0,1:T(8,128)S(1)}, f32[256,16]{0,1:T(8,128)}, u32[]{:S(2)}) copy-start(f32[256,16]{0,1:T(8,128)} %get-tuple-element.17) | copy-start | bytes 49156
  111.5 4.3 %copy-start.6 = (f32[256,16]{0,1:T(8,128)S(1)}, f32[256,16]{0,1:T(8,128)}, u32[]{:S(2)}) copy-start(f32[256,16]{0,1:T(8,128)} %get-tuple-element.16) | copy-start | bytes 49156
  114.3 12.5 %copy-start.5 = (f32[256,16]{0,1:T(8,128)S(1)}, f32[256,16]{0,1:T(8,128)}, u32[]{:S(2)}) copy-start(f32[256,16]{0,1:T(8,128)} %get-tuple-element.15) | copy-start | bytes 49156
  116.9 39.0 %all-to-all-start.1 = ((f32[32,256,16]{1,2,0:T(8,128)}), f32[32,256,16]{1,2,0:T(8,128)S(1)}, u32[]{:S(2)}, u32[]{:S(2)}) async-start(f32[32,256,16]{1,2,0:T(8,128)} %broadcast_in_dim.18), calls=%async_computation.1 | async-start | bytes 1048576 | tf_op jit(solution)/shard_map/all_to_all | solution.py:21
  248.5 1.7 copy-start.4
  250.8 3.9 %copy-start = (bf16[1,2,2048,512]{3,2,1,0:T(8,128)(2,1)S(1)}, bf16[1,2,2048,512]{3,2,1,0:T(8,128)(2,1)}, u32[]{:S(2)}) copy-start(bf16[1,2,2048,512]{3,2,1,0:T(8,128)(2,1)} %copy.134) | copy-start | bytes 12582916
  250.8 3.9 %copy-start.9 = (f32[1,1,256]{2,1,0:T(1,128)S(1)}, f32[1,1,256]{2,1,0:T(1,128)}, u32[]{:S(2)}) copy-start(f32[1,1,256]{2,1,0:T(1,128)} %get-tuple-element.18) | copy-start | bytes 3076
  250.8 3.9 %copy-start.10 = (f32[1,1,256]{2,1,0:T(1,128)S(1)}, f32[1,1,256]{2,1,0:T(1,128)}, u32[]{:S(2)}) copy-start(f32[1,1,256]{2,1,0:T(1,128)} %get-tuple-element.19) | copy-start | bytes 3076
  250.8 3.9 %copy-start.11 = (f32[1,1,256]{2,1,0:T(1,128)S(1)}, f32[1,1,256]{2,1,0:T(1,128)}, u32[]{:S(2)}) copy-start(f32[1,1,256]{2,1,0:T(1,128)} %get-tuple-element.20) | copy-start | bytes 3076
  250.8 3.9 %copy-start.13 = (f32[256]{0:T(256)S(1)}, f32[256]{0:T(256)}, u32[]{:S(2)}) copy-start(f32[256]{0:T(256)} %param.12) | copy-start | bytes 3076
Sparse Core Ops, SparseCore 0:
  14.5 76.6 all-gather.6
  93.1 144.1 all-gather.8

commit v8 on v7

--- a/solution.py
+++ b/solution.py
@@ -99,10 +99,10 @@
             return feats
 
         pair = across_z(across_yh(in_weight[1:]))
-        packed = across_yh(jnp.concatenate([in_weight[0], out_weight.T], axis=1)[None])
+        packed = jnp.concatenate([in_weight[0], out_weight.T], axis=1)[None]
         packed, pair = lax.optimization_barrier((packed, pair))
         feats = filtered(shortened(pair), short_taps[:, 1:])
-        packed = across_z(packed)[0]
+        packed = across_z(across_yh(packed))[0]
         query = filtered(shortened(packed[None, :, :width]), short_taps[:, :1])[0]
         gated = (feats[0] * feats[1]).astype(jnp.bfloat16)
         values = gated.astype(jnp.float32)

time: 334 us -> 276 us (0.83)
  blocking collectives: 110 us -> 74.5 us
  waiting for transfers between devices: 105 us -> 92.6 us
  local copies, waits for them, and re-layouts: 37.9 us -> 26.8 us
    all_gather x2, blocking collectives: 44.2 us -> 13.3 us  [across_yh(): return lax.all_gather(part, 'yh', axis=1)]
    all_gather x2, waiting for transfers between devices: 90.5 us -> 78.2 us  [across_z(): part = lax.all_gather(part, 'z', axis=2)]
    all_gather x2 -> x0, local copies, waits for them, and re-layouts: 11.9 us -> none  [the longest x1 11.1 us: across_z(): part = lax.all_gather(part, 'z', axis=2)]
    all_to_all x1, blocking collectives: 65.7 us -> 61.2 us  [scattered_terms(): parts = lax.all_to_all(split, CH, 1, 1)]
  transfers between devices with their start and end apart: 5 -> 5, of which waited for: 3 -> 3; matrix products, arithmetic and copies ran while one was open for 17% -> 21% of each run, Pallas kernels for 0% -> 0%
where the time goes in v8:
time: 276 us; the launch traced here: 275 us
  waiting for transfers between devices  92.6 us (34%)
  blocking collectives  74.5 us (27%)
  matrix products  34.2 us (12%)
  local copies, waits for them, and re-layouts  26.8 us (10%)
  starting transfers between devices  23.9 us (9%)
  between operations  13.9 us (5%)
  other arithmetic  8.85 us (3%)
    all_gather x2, waiting for transfers between devices, across_z(): part = lax.all_gather(part, 'z', axis=2)  78.2 us
    all_to_all x1, blocking collectives, scattered_terms(): parts = lax.all_to_all(split, CH, 1, 1)  61.2 us
    all_to_all x1, waiting for transfers between devices, carried_in(): every = lax.all_to_all(copies, CTX, 0, 0)  14.4 us
    all_gather x2, blocking collectives, across_yh(): return lax.all_gather(part, 'yh', axis=1)  13.3 us
    all_to_all x1, starting transfers between devices, gathered_tokens(): return lax.all_to_all(copies, CH, 1, 1)  11.7 us
    all_to_all x1, starting transfers between devices, carried_in(): every = lax.all_to_all(copies, CTX, 0, 0)  9.95 us
    dot_general x2, matrix products, shortened(): jnp.einsum('tkd,jkdc->jtc', whole, weight, preferred_element_type=jnp.flo...  9.49 us
    dot_general x1, local copies, waits for them, and re-layouts, block_terms(): jnp.dot(pick, impulse, precision=lax.Precision.HIGHEST)  9.17 us
  transfers between devices with their start and end apart: 5, of which 3 were waited for; matrix products, arithmetic and copies ran while one was open for 21% of the time, Pallas kernels for 0%

profile of v8, /device:TPU:1, one launch (start us, length us, event | category | flops | bytes accessed | tf_op | source)
XLA Modules:
  0.0 274.8 jit_solution(14728171996644254077)
XLA Ops:
  6.5 0.9 slice.130
  7.5 6.9 %all-gather = bf16[2,256,256]{2,1,0:T(8,128)(2,1)} all-gather(bf16[2,128,256]{2,1,0:T(8,128)(2,1)S(1)} %slice.130), channel_id=2, replica_groups=mesh['yh'=2,'z'=16,'ch'=16] {'yh'}, dimensions={1}, use_global_device_ids=true | all-gather | bytes 393216 | tf_op jit(solution)/shard_map/all_gather | solution.py:82
  14.3 3.4 %broadcast_in_dim.17 = bf16[512,16,256]{2,0,1:T(8,128)(2,1)} broadcast(bf16[512,256]{1,0:T(8,128)(2,1)} %param.7), dimensions={0,2} | broadcast | bytes 4456448 | tf_op jit(solution)/shard_map/broadcast_in_dim | solution.py:63
  17.7 11.7 %all-to-all-start = ((bf16[512,16,256]{2,0,1:T(8,128)(2,1)}), bf16[512,16,256]{2,0,1:T(8,128)(2,1)}, u32[]{:S(2)}, u32[]{:S(2)}) async-start(bf16[512,16,256]{2,0,1:T(8,128)(2,1)} %broadcast_in_dim.17), calls=%async_computation | async-start | bytes 8388608 | tf_op jit(solution)/shard_map/all_to_all | solution.py:64
  29.6 0.8 slice_bitcast_fusion
  30.4 60.5 %all-gather.7.cloned.1.call-done = bf16[2,2,2048,256]{3,2,1,0:T(8,128)(2,1)} async-done(((bf16[2,2,128,256]{3,2,1,0:T(8,128)(2,1)}), bf16[2,2,2048,256]{3,2,1,0:T(8,128)(2,1)}) %all-gather.7.cloned.1.call-update) | async-done | bytes 4194320 | tf_op jit(solution)/shard_map/all_gather | solution.py:85
  90.9 6.5 %all-gather.2 = bf16[2,128,512]{2,1,0:T(8,128)(2,1)} all-gather(bf16[1,128,512]{2,1,0:T(8,128)(2,1)S(1)} %maximum_bitcast_fusion), channel_id=4, replica_groups=mesh['yh'=2,'z'=16,'ch'=16] {'yh'}, dimensions={0}, use_global_device_ids=true | all-gather | bytes 393216 | tf_op jit(solution)/shard_map/all_gather | solution.py:82
  97.6 0.6 negate_exponential_fusion
  98.3 2.8 %multiply_reduce_fusion = (f32[64,256]{0,1:T(8,128)S(1)}, f32[64,256,16]{0,2,1:T(8,128)}) fusion(f32[256,16]{1,0:T(8,128)S(1)} %copy.135, f32[64]{0:T(128)S(1)} %iota_negate_fusion, f32[256,16]{1,0:T(8,128)S(1)} %copy.134), kind=kLoop, calls=%fused_computation.11 | loop fusion | flops 770048 | bytes 1147136 | tf_op jit(solution)/shard_map/reduce_sum | solution.py:35
  101.1 0.9 slice.167
  101.9 2.2 collective-permute-start
  104.2 2.7 rev.3
  106.9 2.8 %fusion.20 = bf16[2,2,256]{2,1,0:T(2,128)(2,1)S(1)} fusion(bf16[2,16,256,256]{3,2,1,0:T(8,128)(2,1)} %bitcast.117, bf16[2,16,256]{2,0,1:T(2,128)(2,1)S(1)} %collective-permute-done), kind=kOutput, calls=%fused_computation.22 | convolution fusion | flops 8389632 | bytes 4212736 | tf_op jit(solution)/shard_map/tkd,jkdc->jtc/dot_general | solution.py:91
  110.0 5.9 %fusion.14 = bf16[2,512,256]{1,2,0:T(8,128)(2,1)S(1)} fusion(bf16[2,16,256,256]{3,2,1,0:T(8,128)(2,1)} %bitcast.118, bf16[512,16,256]{2,0,1:T(8,128)(2,1)} %all-to-all-done), kind=kOutput, calls=%fused_computation.16 | convolution fusion | flops 2147745792 | bytes 8912896 | tf_op jit(solution)/shard_map/tkd,jkdc->jtc/dot_general | solution.py:90
  116.1 0.9 fusion.23
  117.6 2.7 fusion.53
  120.4 1.5 copy.140
  122.2 0.9 broadcast_in_dim.21
  123.0 10.0 %all-to-all-start.1 = ((f32[32,256,16]{1,2,0:T(8,128)}), f32[32,256,16]{1,2,0:T(8,128)S(1)}, u32[]{:S(2)}, u32[]{:S(2)}) async-start(f32[32,256,16]{1,2,0:T(8,128)} %broadcast_in_dim.21), calls=%async_computation.1 | async-start | bytes 1048576 | tf_op jit(solution)/shard_map/all_to_all | solution.py:21
  133.0 0.8 copy.141
  133.8 3.7 %fusion.5 = f32[64,64,256]{2,1,0:T(8,128)} fusion(s32[64,64]{1,0:T(8,128)S(1)} %iota_subtract_fusion, f32[64,256]{0,1:T(8,128)S(1)} %get-tuple-element.9), kind=kOutput, calls=%fused_computation.9 | convolution fusion | flops 805568512 | bytes 4276224 | tf_op jit(solution)/shard_map/dot_general | solution.py:40
  137.5 9.2 %copy.138 = f32[64,64,256]{1,0,2:T(8,128)} copy(f32[64,64,256]{2,1,0:T(8,128)} %fusion.5) | data formatting | bytes 8388608 | tf_op jit(solution)/shard_map/dot_general | solution.py:40
  146.7 1.3 fusion.52
  148.2 14.4 %all-to-all-done.1 = f32[32,256,16]{1,2,0:T(8,128)S(1)} async-done(((f32[32,256,16]{1,2,0:T(8,128)}), f32[32,256,16]{1,2,0:T(8,128)S(1)}, u32[]{:S(2)}, u32[]{:S(2)}) %all-to-all-start.1) | async-done | bytes 524320 | tf_op jit(solution)/shard_map/all_to_all | solution.py:21
  163.2 4.1 %fusion.3 = f32[256,8,64]{2,1,0:T(8,128)S(1)} fusion(f32[8,256,16]{2,0,1:T(8,128)S(1)} %copy.142, f32[256,16]{1,0:T(8,128)} %copy.141, f32[256,16]{1,0:T(8,128)S(1)} %copy.135, f32[64]{0:T(128)} %copy-done.14, f32[256,16]{1,0:T(8,128)S(1)} %copy.134), kind=kOutput, calls=%fused_computation.5 | convolution fusion | flops 25952256 | bytes 704768 | tf_op jit(solution)/shard_map/icm,bcm->bic/dot_general | solution.py:58
  167.3 9.2 %fusion.10 = f32[8,64,256]{1,0,2:T(8,128)S(1)} fusion(f32[256,8,64]{2,1,0:T(8,128)S(1)} %fusion.3, bf16[8,64,256]{1,0,2:T(8,128)(2,1)S(1)} %copy.137, f32[64,64,256]{1,0,2:T(8,128)} %copy.138), kind=kOutput, calls=%fused_computation.14 | convolution fusion | flops 100794368 | bytes 5505024 | tf_op jit(solution)/shard_map/ijc,bjc->bic/dot_general | solution.py:44
  177.1 17.7 %all-gather.9.cloned.1.call-done = bf16[2,2048,512]{2,1,0:T(8,128)(2,1)} async-done(((bf16[2,128,512]{2,1,0:T(8,128)(2,1)}), bf16[2,2048,512]{2,1,0:T(8,128)(2,1)}) %all-gather.9.cloned.1.call-update) | async-done | bytes 4194320 | tf_op jit(solution)/shard_map/all_gather | solution.py:85
  194.7 1.7 slice.166
  197.1 3.6 %fusion.18 = bf16[1,512,256]{1,2,0:T(8,128)(2,1)S(1)} fusion(bf16[16,256,256]{2,1,0:T(8,128)(2,1)S(1)} %bitcast.116, bf16[512,16,256]{2,0,1:T(8,128)(2,1)} %all-to-all-done), kind=kOutput, calls=%fused_computation.19 | convolution fusion | flops 1073872896 | bytes 6553600 | tf_op jit(solution)/shard_map/tkd,jkdc->jtc/dot_general | solution.py:90
  200.9 1.8 convolution_convert_fusion
  203.2 61.2 %all_to_all.15 = bf16[512,16,256]{2,0,1:T(8,128)(2,1)} all-to-all(bf16[512,16,256]{2,0,1:T(8,128)(2,1)S(1)} %bitcast.114), channel_id=1, replica_groups=mesh['yh'=2,'z'=16,'ch'=16] {'ch'}, dimensions={1} | all-to-all | bytes 8388608 | tf_op jit(solution)/shard_map/all_to_all | solution.py:70
  264.4 3.5 %reduce_sum.32 = bf16[512,256]{1,0:T(8,128)(2,1)} reduce(bf16[512,16,256]{2,0,1:T(8,128)(2,1)} %all_to_all.15, bf16[]{:T(256)} %constant.28.clone.1), dimensions={1}, to_apply=%region_2.3 | reduce | flops 1966080 | bytes 4456450 | tf_op jit(solution)/shard_map/reduce_sum | solution.py:71
  (77 shorter events, 4.1 us)
Async XLA Ops:
  6.5 84.4 %all-gather.7.cloned.1.call-start = ((), (), s32[]{:S(2)}) async-start(), calls=%async_computation.3 | async-start | bytes 4456448 | tf_op jit(solution)/shard_map/all_gather | solution.py:85
  17.7 11.7 %copy-start.5 = (bf16[256,128]{1,0:T(8,128)(2,1)S(1)}, bf16[256,128]{1,0:T(8,128)(2,1)}, u32[]{:S(2)}) copy-start(bf16[256,128]{1,0:T(8,128)(2,1)} %param.13) | copy-start | bytes 196612
  17.7 79.7 %copy-start.8 = (f32[256,16]{0,1:T(8,128)S(1)}, f32[256,16]{0,1:T(8,128)}, u32[]{:S(2)}) copy-start(f32[256,16]{0,1:T(8,128)} %param.11) | copy-start | bytes 49156
  17.7 79.8 %copy-start.1 = (f32[256,16]{0,1:T(8,128)S(1)}, f32[256,16]{0,1:T(8,128)}, u32[]{:S(2)}) copy-start(f32[256,16]{0,1:T(8,128)} %param.10) | copy-start | bytes 49156
  17.7 83.4 %all-to-all-start = ((bf16[512,16,256]{2,0,1:T(8,128)(2,1)}), bf16[512,16,256]{2,0,1:T(8,128)(2,1)}, u32[]{:S(2)}, u32[]{:S(2)}) async-start(bf16[512,16,256]{2,0,1:T(8,128)(2,1)} %broadcast_in_dim.17), calls=%async_computation | async-start | bytes 8388608 | tf_op jit(solution)/shard_map/all_to_all | solution.py:64
  29.4 74.8 %copy-start.12 = (f32[3,3,256]{2,1,0:T(4,128)S(1)}, f32[3,3,256]{2,1,0:T(4,128)}, u32[]{:S(2)}) copy-start(f32[3,3,256]{2,1,0:T(4,128)} %param.9) | copy-start | bytes 27652
  29.4 165.3 %all-gather.9.cloned.1.call-start = ((), (), s32[]{:S(2)}) async-start(), calls=%async_computation.4 | async-start | bytes 4456448 | tf_op jit(solution)/shard_map/all_gather | solution.py:85
  97.6 9.3 %copy-start.14 = (f32[64]{0:T(128)}, f32[64]{0:T(128)S(1)}, u32[]{:S(2)}) copy-start(f32[64]{0:T(128)S(1)} %iota_negate_fusion) | copy-start | bytes 772
  101.9 5.0 %collective-permute-start = (bf16[2,16,256]{2,0,1:T(2,128)(2,1)S(1)}, bf16[2,16,256]{2,0,1:T(2,128)(2,1)S(1)}, u32[]{:S(2)}, u32[]{:S(2)}) collective-permute-start(bf16[2,16,256]{2,0,1:T(2,128)(2,1)S(1)} %slice.167), channel_id=1, source_target_pairs={{0,16},{16,32},{32,48},{48,64},{64,80},{80,96},{96,112},{112,128},... | collective-permute-start | bytes 49160 | tf_op jit(solution)/shard_map/ppermute | solution.py:16
  106.9 2.8 %copy-start.3 = (bf16[2,16,256]{2,0,1:T(2,128)(2,1)}, bf16[2,16,256]{2,0,1:T(2,128)(2,1)S(1)}, u32[]{:S(2)}) copy-start(bf16[2,16,256]{2,0,1:T(2,128)(2,1)S(1)} %collective-permute-done) | copy-start | bytes 49156
  117.6 4.3 %copy-start.2 = (f32[256,16]{0,1:T(8,128)S(1)}, f32[256,16]{0,1:T(8,128)}, u32[]{:S(2)}) copy-start(f32[256,16]{0,1:T(8,128)} %get-tuple-element.17) | copy-start | bytes 49156
  117.6 4.3 %copy-start.7 = (f32[256,16]{0,1:T(8,128)S(1)}, f32[256,16]{0,1:T(8,128)}, u32[]{:S(2)}) copy-start(f32[256,16]{0,1:T(8,128)} %get-tuple-element.16) | copy-start | bytes 49156
  120.4 12.6 %copy-start.6 = (f32[256,16]{0,1:T(8,128)S(1)}, f32[256,16]{0,1:T(8,128)}, u32[]{:S(2)}) copy-start(f32[256,16]{0,1:T(8,128)} %get-tuple-element.15) | copy-start | bytes 49156
  123.0 39.5 %all-to-all-start.1 = ((f32[32,256,16]{1,2,0:T(8,128)}), f32[32,256,16]{1,2,0:T(8,128)S(1)}, u32[]{:S(2)}, u32[]{:S(2)}) async-start(f32[32,256,16]{1,2,0:T(8,128)} %broadcast_in_dim.21), calls=%async_computation.1 | async-start | bytes 1048576 | tf_op jit(solution)/shard_map/all_to_all | solution.py:21
  194.7 1.7 copy-start.4
  197.0 3.9 %copy-start = (bf16[2,2048,512]{2,1,0:T(8,128)(2,1)S(1)}, bf16[2,2048,512]{2,1,0:T(8,128)(2,1)}, u32[]{:S(2)}) copy-start(bf16[2,2048,512]{2,1,0:T(8,128)(2,1)} %all-gather.9.cloned.1.call-done) | copy-start | bytes 12582916
  197.0 3.9 %copy-start.9 = (f32[1,1,256]{2,1,0:T(1,128)S(1)}, f32[1,1,256]{2,1,0:T(1,128)}, u32[]{:S(2)}) copy-start(f32[1,1,256]{2,1,0:T(1,128)} %get-tuple-element.18) | copy-start | bytes 3076
  197.0 3.9 %copy-start.10 = (f32[1,1,256]{2,1,0:T(1,128)S(1)}, f32[1,1,256]{2,1,0:T(1,128)}, u32[]{:S(2)}) copy-start(f32[1,1,256]{2,1,0:T(1,128)} %get-tuple-element.19) | copy-start | bytes 3076
  197.1 3.9 %copy-start.11 = (f32[1,1,256]{2,1,0:T(1,128)S(1)}, f32[1,1,256]{2,1,0:T(1,128)}, u32[]{:S(2)}) copy-start(f32[1,1,256]{2,1,0:T(1,128)} %get-tuple-element.20) | copy-start | bytes 3076
  197.1 3.9 %copy-start.13 = (f32[256]{0:T(256)S(1)}, f32[256]{0:T(256)}, u32[]{:S(2)}) copy-start(f32[256]{0:T(256)} %param.12) | copy-start | bytes 3076
Sparse Core Ops, SparseCore 0:
  14.5 76.4 all-gather.6
  97.5 97.1 all-gather.8

commit v9 on v8

--- a/solution.py
+++ b/solution.py
@@ -59,6 +59,24 @@
     return (inner + carried).reshape(values.shape) + skip[None] * values
 
 
+def ring_z(block, zcount):
+    ahead_route = [(i, (i + 1) % zcount) for i in range(zcount)]
+    behind_route = [((i + 1) % zcount, i) for i in range(zcount)]
+    ahead, behind = block, block
+    got_ahead, got_behind = [], []
+    for step in range(1, zcount // 2 + 1):
+        ahead = lax.ppermute(ahead, "z", ahead_route)
+        got_ahead.append(ahead)
+        if step < zcount - step:
+            behind = lax.ppermute(behind, "z", behind_route)
+            got_behind.append(behind)
+    by_offset = jnp.stack([block] + got_ahead + got_behind[::-1])
+    flipped = by_offset[::-1]
+    doubled = jnp.concatenate([flipped, flipped], axis=0)
+    start = zcount - 1 - lax.axis_index("z")
+    return lax.dynamic_slice_in_dim(doubled, start, zcount, axis=0)
+
+
 def gathered_tokens(tokens, lanes):
     copies = jnp.broadcast_to(tokens[:, None], (tokens.shape[0], lanes, tokens.shape[1]))
     return lax.all_to_all(copies, CH, 1, 1)
@@ -98,11 +116,12 @@
                 feats = feats + taps[i][:, None, :] * widened[:, SHORT - 1 - i : SHORT - 1 - i + rows, :]
             return feats
 
-        pair = across_z(across_yh(in_weight[1:]))
-        packed = jnp.concatenate([in_weight[0], out_weight.T], axis=1)[None]
-        packed, pair = lax.optimization_barrier((packed, pair))
+        packed = jnp.concatenate([in_weight[0], out_weight.T], axis=1)
+        packed = lax.all_gather(packed, "yh", axis=0)
+        packed = lax.all_gather(packed, "z", axis=1).reshape(-1, packed.shape[-1])
+        pair = ring_z(across_yh(in_weight[1:]), count // 2)
+        pair = jnp.transpose(pair, (1, 2, 0, 3, 4)).reshape(2, -1, width)
         feats = filtered(shortened(pair), short_taps[:, 1:])
-        packed = across_z(across_yh(packed))[0]
         query = filtered(shortened(packed[None, :, :width]), short_taps[:, :1])[0]
         gated = (feats[0] * feats[1]).astype(jnp.bfloat16)
         values = gated.astype(jnp.float32)

time: 276 us -> 360 us (1.30)
  waiting for transfers between devices: 92.6 us -> 40.3 us
  starting transfers between devices: 23.9 us -> 75.9 us
  blocking collectives: 74.5 us -> 124 us
  local copies, waits for them, and re-layouts: 26.8 us -> 59 us
  other arithmetic: 8.85 us -> 13.4 us
    all_gather x2 -> x1, waiting for transfers between devices: 78.2 us -> 0.19 us  [shards(): packed = lax.all_gather(packed, 'z', axis=1).reshape(-1, packed.shape[-1])]
    ppermute x0 -> x15, starting transfers between devices: none -> 53.5 us  [the longest x7 31.5 us: ring_z(): behind = lax.ppermute(behind, 'z', behind_route)]
    all_gather x0 -> x1, blocking collectives: none -> 38.3 us  [shards(): packed = lax.all_gather(packed, 'yh', axis=0)]
    ppermute x0 -> x15, waiting for transfers between devices: none -> 23.5 us  [the longest x8 23.5 us: ring_z(): ahead = lax.ppermute(ahead, 'z', ahead_route)]
    all_to_all x1, blocking collectives: 61.2 us -> 78.5 us  [scattered_terms(): parts = lax.all_to_all(split, CH, 1, 1)]
    unnamed x34 -> x61, local copies, waits for them, and re-layouts: 0.41 us -> 15.7 us
    all_gather x0 -> x2, local copies, waits for them, and re-layouts: none -> 11.9 us  [the longest x1 11.1 us: shards(): packed = lax.all_gather(packed, 'z', axis=1).reshape(-1, packed.shape[-1])]
    all_gather x2 -> x1, blocking collectives: 13.3 us -> 6.76 us  [across_yh(): return lax.all_gather(part, 'yh', axis=1)]
  transfers between devices with their start and end apart: 5 -> 19, of which waited for: 3 -> 8; matrix products, arithmetic and copies ran while one was open for 21% -> 22% of each run, Pallas kernels for 0% -> 0%
where the time goes in v9:
time: 360 us; the launch traced here: 358 us
  blocking collectives  124 us (34%)
  starting transfers between devices  75.9 us (21%)
  local copies, waits for them, and re-layouts  59 us (16%)
  waiting for transfers between devices  40.3 us (11%)
  matrix products  32 us (9%)
  between operations  14.2 us (4%)
  other arithmetic  13.4 us (4%)
    all_to_all x1, blocking collectives, scattered_terms(): parts = lax.all_to_all(split, CH, 1, 1)  78.5 us
    all_gather x1, blocking collectives, shards(): packed = lax.all_gather(packed, 'yh', axis=0)  38.3 us
    ppermute x7, starting transfers between devices, ring_z(): behind = lax.ppermute(behind, 'z', behind_route)  31.5 us
    ppermute x8, waiting for transfers between devices, ring_z(): ahead = lax.ppermute(ahead, 'z', ahead_route)  23.5 us
    ppermute x8, starting transfers between devices, ring_z(): ahead = lax.ppermute(ahead, 'z', ahead_route)  22 us
    all_to_all x1, waiting for transfers between devices, carried_in(): every = lax.all_to_all(copies, CTX, 0, 0)  16.6 us
    unnamed x61, local copies, waits for them, and re-layouts  15.7 us
    all_gather x1, local copies, waits for them, and re-layouts, shards(): packed = lax.all_gather(packed, 'z', axis=1).reshape(-1, packed.shape[-1])  11.1 us
  transfers between devices with their start and end apart: 19, of which 8 were waited for; matrix products, arithmetic and copies ran while one was open for 22% of the time, Pallas kernels for 0%

profile of v9, /device:TPU:1, one launch (start us, length us, event | category | flops | bytes accessed | tf_op | source)
XLA Modules:
  0.0 358.3 jit_solution(4168836751122623038)
XLA Ops:
  7.5 6.8 %all-gather.2 = bf16[2,256,256]{2,1,0:T(8,128)(2,1)S(1)} all-gather(bf16[2,128,256]{2,1,0:T(8,128)(2,1)S(1)} %slice.138), channel_id=4, replica_groups=mesh['yh'=2,'z'=16,'ch'=16] {'yh'}, dimensions={1}, use_global_device_ids=true | all-gather | bytes 393216 | tf_op jit(solution)/shard_map/all_gather | solution.py:100
  14.2 4.2 %collective-permute-start.1 = (bf16[2,2,128,256]{3,2,1,0:T(8,128)(2,1)S(1)}, bf16[2,2,128,256]{3,2,1,0:T(8,128)(2,1)S(1)}, u32[]{:S(2)}, u32[]{:S(2)}) collective-permute-start(bf16[2,2,128,256]{3,2,1,0:T(8,128)(2,1)S(1)} %bitcast.184), channel_id=1, source_target_pairs={{0,16},{16,32},{32,48},{48,64},{64,80},{80,96},{96,112},{112,128},... | collective-permute-start | bytes 786440 | tf_op jit(solution)/shard_map/ppermute | solution.py:68
  18.4 9.5 %collective-permute-start.9 = (bf16[2,2,128,256]{3,2,1,0:T(8,128)(2,1)S(1)}, bf16[2,2,128,256]{3,2,1,0:T(8,128)(2,1)S(1)}, u32[]{:S(2)}, u32[]{:S(2)}) collective-permute-start(bf16[2,2,128,256]{3,2,1,0:T(8,128)(2,1)S(1)} %bitcast.185), channel_id=1, source_target_pairs={{16,0},{32,16},{48,32},{64,48},{80,64},{96,80},{112,96},{128,112},... | collective-permute-start | bytes 786440 | tf_op jit(solution)/shard_map/ppermute | solution.py:71
  27.9 3.3 broadcast_in_dim.14
  31.2 7.3 %all-to-all-start = ((bf16[512,16,256]{2,0,1:T(8,128)(2,1)}), bf16[512,16,256]{2,0,1:T(8,128)(2,1)}, u32[]{:S(2)}, u32[]{:S(2)}) async-start(bf16[512,16,256]{2,0,1:T(8,128)(2,1)} %broadcast_in_dim.14), calls=%async_computation | async-start | bytes 8388608 | tf_op jit(solution)/shard_map/all_to_all | solution.py:82
  40.7 38.3 %all-gather = bf16[256,512]{0,1:T(8,128)(2,1)S(1)} all-gather(bf16[128,512]{0,1:T(8,128)(2,1)S(1)} %pad_maximum_fusion), channel_id=2, replica_groups=mesh['yh'=2,'z'=16,'ch'=16] {'yh'}, dimensions={0}, use_global_device_ids=true | all-gather | bytes 393216 | tf_op jit(solution)/shard_map/all_gather | solution.py:120
  80.0 3.6 %collective-permute-start.10 = (bf16[2,2,128,256]{3,2,1,0:T(8,128)(2,1)S(1)}, bf16[2,2,128,256]{3,2,1,0:T(8,128)(2,1)S(1)}, u32[]{:S(2)}, u32[]{:S(2)}) collective-permute-start(bf16[2,2,128,256]{3,2,1,0:T(8,128)(2,1)S(1)} %collective-permute-done.9), channel_id=1, source_target_pairs={{16,0},{32,16},{48,32},{64,48},{80,64},{96,80},{112,96},{128,112},... | collective-permute-start | bytes 786440 | tf_op jit(solution)/shard_map/ppermute | solution.py:71
  85.6 2.8 multiply_reduce_fusion
  88.4 5.3 %collective-permute-done.3 = bf16[2,2,128,256]{3,2,1,0:T(8,128)(2,1)S(1)} collective-permute-done((bf16[2,2,128,256]{3,2,1,0:T(8,128)(2,1)S(1)}, bf16[2,2,128,256]{3,2,1,0:T(8,128)(2,1)S(1)}, u32[]{:S(2)}, u32[]{:S(2)}) %collective-permute-start.3) | collective-permute-done | bytes 262176 | tf_op jit(solution)/shard_map/ppermute | solution.py:68
  96.3 4.6 %collective-permute-start.11 = (bf16[2,2,128,256]{3,2,1,0:T(8,128)(2,1)S(1)}, bf16[2,2,128,256]{3,2,1,0:T(8,128)(2,1)S(1)}, u32[]{:S(2)}, u32[]{:S(2)}) collective-permute-start(bf16[2,2,128,256]{3,2,1,0:T(8,128)(2,1)S(1)} %collective-permute-done.10), channel_id=1, source_target_pairs={{16,0},{32,16},{48,32},{64,48},{80,64},{96,80},{112,96},{128,112},... | collective-permute-start | bytes 786440 | tf_op jit(solution)/shard_map/ppermute | solution.py:71
  108.3 4.6 %collective-permute-start.12 = (bf16[2,2,128,256]{3,2,1,0:T(8,128)(2,1)S(1)}, bf16[2,2,128,256]{3,2,1,0:T(8,128)(2,1)S(1)}, u32[]{:S(2)}, u32[]{:S(2)}) collective-permute-start(bf16[2,2,128,256]{3,2,1,0:T(8,128)(2,1)S(1)} %collective-permute-done.11), channel_id=1, source_target_pairs={{16,0},{32,16},{48,32},{64,48},{80,64},{96,80},{112,96},{128,112},... | collective-permute-start | bytes 786440 | tf_op jit(solution)/shard_map/ppermute | solution.py:71
  113.7 5.0 %collective-permute-done.5 = bf16[2,2,128,256]{3,2,1,0:T(8,128)(2,1)} collective-permute-done((bf16[2,2,128,256]{3,2,1,0:T(8,128)(2,1)}, bf16[2,2,128,256]{3,2,1,0:T(8,128)(2,1)}, u32[]{:S(2)}, u32[]{:S(2)}) %collective-permute-start.5) | collective-permute-done | bytes 262176 | tf_op jit(solution)/shard_map/ppermute | solution.py:68
  122.2 4.6 %collective-permute-start.13 = (bf16[2,2,128,256]{3,2,1,0:T(8,128)(2,1)S(1)}, bf16[2,2,128,256]{3,2,1,0:T(8,128)(2,1)S(1)}, u32[]{:S(2)}, u32[]{:S(2)}) collective-permute-start(bf16[2,2,128,256]{3,2,1,0:T(8,128)(2,1)S(1)} %collective-permute-done.12), channel_id=1, source_target_pairs={{16,0},{32,16},{48,32},{64,48},{80,64},{96,80},{112,96},{128,112},... | collective-permute-start | bytes 786440 | tf_op jit(solution)/shard_map/ppermute | solution.py:71
  128.5 2.9 collective-permute-done.6
  131.4 4.1 %collective-permute-start.7 = (bf16[2,2,128,256]{3,2,1,0:T(8,128)(2,1)S(1)}, bf16[2,2,128,256]{3,2,1,0:T(8,128)(2,1)S(1)}, u32[]{:S(2)}, u32[]{:S(2)}) collective-permute-start(bf16[2,2,128,256]{3,2,1,0:T(8,128)(2,1)S(1)} %collective-permute-done.6), channel_id=1, source_target_pairs={{0,16},{16,32},{32,48},{48,64},{64,80},{80,96},{96,112},{112,128},... | collective-permute-start | bytes 786440 | tf_op jit(solution)/shard_map/ppermute | solution.py:68
  141.2 3.4 collective-permute-done.7
  144.6 4.2 %collective-permute-start.8 = (bf16[2,2,128,256]{3,2,1,0:T(8,128)(2,1)S(1)}, bf16[2,2,128,256]{3,2,1,0:T(8,128)(2,1)S(1)}, u32[]{:S(2)}, u32[]{:S(2)}) collective-permute-start(bf16[2,2,128,256]{3,2,1,0:T(8,128)(2,1)S(1)} %collective-permute-done.7), channel_id=1, source_target_pairs={{0,16},{16,32},{32,48},{48,64},{64,80},{80,96},{96,112},{112,128},... | collective-permute-start | bytes 786440 | tf_op jit(solution)/shard_map/ppermute | solution.py:68
  152.5 5.4 %collective-permute-done.8 = bf16[2,2,128,256]{3,2,1,0:T(8,128)(2,1)S(1)} collective-permute-done((bf16[2,2,128,256]{3,2,1,0:T(8,128)(2,1)S(1)}, bf16[2,2,128,256]{3,2,1,0:T(8,128)(2,1)S(1)}, u32[]{:S(2)}, u32[]{:S(2)}) %collective-permute-start.8) | collective-permute-done | bytes 262176 | tf_op jit(solution)/shard_map/ppermute | solution.py:68
  163.7 4.7 %rev.6 = bf16[16,2,2,128,256]{4,3,0,2,1:T(8,128)(2,1)} reverse(bf16[16,2,2,128,256]{4,3,0,2,1:T(8,128)(2,1)} %bitcast_dynamic-update-slice_fusion.14), dimensions={0} | reverse | bytes 8388608 | tf_op jit(solution)/shard_map/rev | solution.py:74
  168.3 4.6 %fusion = bf16[16,2,2,128,256]{4,3,0,2,1:T(8,128)(2,1)} fusion(s32[]{:T(128)S(6)} %select_n.7, bf16[16,2,2,128,256]{4,3,0,2,1:T(8,128)(2,1)} %rev.6), kind=kLoop, calls=%fused_computation.3 | loop fusion | flops 2097152 | bytes 8388612 | tf_op jit(solution)/shard_map/concatenate | solution.py:75
  173.8 4.2 %collective-permute-start = (bf16[2,16,256]{2,0,1:T(2,128)(2,1)S(1)}, bf16[2,16,256]{2,0,1:T(2,128)(2,1)S(1)}, u32[]{:S(2)}, u32[]{:S(2)}) collective-permute-start(bf16[2,16,256]{2,0,1:T(2,128)(2,1)S(1)} %slice.167), channel_id=1, source_target_pairs={{0,16},{16,32},{32,48},{48,64},{64,80},{80,96},{96,112},{112,128},... | collective-permute-start | bytes 49160 | tf_op jit(solution)/shard_map/ppermute | solution.py:16
  178.0 6.0 %fusion.15 = bf16[2,512,256]{1,2,0:T(8,128)(2,1)S(1)} fusion(bf16[2,16,256,256]{3,2,1,0:T(8,128)(2,1)} %bitcast.175, bf16[512,16,256]{2,0,1:T(8,128)(2,1)} %all-to-all-done), kind=kOutput, calls=%fused_computation.19 | convolution fusion | flops 2147745792 | bytes 8912896 | tf_op jit(solution)/shard_map/tkd,jkdc->jtc/dot_general | solution.py:108
  192.8 10.8 %all-to-all-start.1 = ((f32[32,256,16]{1,2,0:T(8,128)}), f32[32,256,16]{1,2,0:T(8,128)S(1)}, u32[]{:S(2)}, u32[]{:S(2)}) async-start(f32[32,256,16]{1,2,0:T(8,128)} %broadcast_in_dim.18), calls=%async_computation.1 | async-start | bytes 1048576 | tf_op jit(solution)/shard_map/all_to_all | solution.py:21
  204.3 3.8 %fusion.6 = f32[64,64,256]{2,1,0:T(8,128)} fusion(s32[64,64]{1,0:T(8,128)S(1)} %iota_subtract_fusion, f32[64,256]{0,1:T(8,128)S(1)} %get-tuple-element.5), kind=kOutput, calls=%fused_computation.12 | convolution fusion | flops 805568512 | bytes 4276224 | tf_op jit(solution)/shard_map/dot_general | solution.py:40
  208.1 9.2 %copy.234 = f32[64,64,256]{1,0,2:T(8,128)} copy(f32[64,64,256]{2,1,0:T(8,128)} %fusion.6) | data formatting | bytes 8388608 | tf_op jit(solution)/shard_map/dot_general | solution.py:40
  218.8 16.6 %all-to-all-done.1 = f32[32,256,16]{1,2,0:T(8,128)S(1)} async-done(((f32[32,256,16]{1,2,0:T(8,128)}), f32[32,256,16]{1,2,0:T(8,128)S(1)}, u32[]{:S(2)}, u32[]{:S(2)}) %all-to-all-start.1) | async-done | bytes 524320 | tf_op jit(solution)/shard_map/all_to_all | solution.py:21
  236.1 4.1 %fusion.4 = f32[256,8,64]{2,1,0:T(8,128)S(1)} fusion(f32[8,256,16]{2,0,1:T(8,128)S(1)} %copy.238, f32[256,16]{1,0:T(8,128)} %copy.237, f32[256,16]{1,0:T(8,128)S(1)} %copy.231, f32[64]{0:T(128)} %copy-done.20, f32[256,16]{1,0:T(8,128)S(1)} %copy.230), kind=kOutput, calls=%fused_computation.8 | convolution fusion | flops 25952256 | bytes 704768 | tf_op jit(solution)/shard_map/icm,bcm->bic/dot_general | solution.py:58
  240.2 8.9 %fusion.11 = f32[8,64,256]{1,0,2:T(8,128)S(1)} fusion(f32[256,8,64]{2,1,0:T(8,128)S(1)} %fusion.4, bf16[8,64,256]{1,0,2:T(8,128)(2,1)S(1)} %copy.233, f32[64,64,256]{1,0,2:T(8,128)} %copy.234), kind=kOutput, calls=%fused_computation.17 | convolution fusion | flops 100794368 | bytes 5505024 | tf_op jit(solution)/shard_map/ijc,bjc->bic/dot_general | solution.py:44
  249.9 11.1 %copy.209 = bf16[2,2048,512]{2,1,0:T(8,128)(2,1)} copy(bf16[2,2048,512]{1,0,2:T(2,128)(2,1)} %all-gather.5.cloned.1.call-done) | data formatting | bytes 8388608 | tf_op jit(solution)/shard_map/all_gather | solution.py:121
  263.3 3.6 %fusion.19 = bf16[1,512,256]{1,2,0:T(8,128)(2,1)S(1)} fusion(bf16[16,256,256]{2,1,0:T(8,128)(2,1)S(1)} %bitcast.181, bf16[512,16,256]{2,0,1:T(8,128)(2,1)} %all-to-all-done), kind=kOutput, calls=%fused_computation.22 | convolution fusion | flops 1073872896 | bytes 6553600 | tf_op jit(solution)/shard_map/tkd,jkdc->jtc/dot_general | solution.py:108
  269.4 78.5 %all_to_all.15 = bf16[512,16,256]{2,0,1:T(8,128)(2,1)} all-to-all(bf16[512,16,256]{2,0,1:T(8,128)(2,1)S(1)} %bitcast.177), channel_id=1, replica_groups=mesh['yh'=2,'z'=16,'ch'=16] {'ch'}, dimensions={1} | all-to-all | bytes 8388608 | tf_op jit(solution)/shard_map/all_to_all | solution.py:88
  348.0 3.5 reduce_sum.32
  (137 shorter events, 54.9 us)
Async XLA Ops:
  14.2 24.5 %collective-permute-start.1 = (bf16[2,2,128,256]{3,2,1,0:T(8,128)(2,1)S(1)}, bf16[2,2,128,256]{3,2,1,0:T(8,128)(2,1)S(1)}, u32[]{:S(2)}, u32[]{:S(2)}) collective-permute-start(bf16[2,2,128,256]{3,2,1,0:T(8,128)(2,1)S(1)} %bitcast.184), channel_id=1, source_target_pairs={{0,16},{16,32},{32,48},{48,64},{64,80},{80,96},{96,112},{112,128},... | collective-permute-start | bytes 786440 | tf_op jit(solution)/shard_map/ppermute | solution.py:68
  18.4 61.6 %collective-permute-start.9 = (bf16[2,2,128,256]{3,2,1,0:T(8,128)(2,1)S(1)}, bf16[2,2,128,256]{3,2,1,0:T(8,128)(2,1)S(1)}, u32[]{:S(2)}, u32[]{:S(2)}) collective-permute-start(bf16[2,2,128,256]{3,2,1,0:T(8,128)(2,1)S(1)} %bitcast.185), channel_id=1, source_target_pairs={{16,0},{32,16},{48,32},{64,48},{80,64},{96,80},{112,96},{128,112},... | collective-permute-start | bytes 786440 | tf_op jit(solution)/shard_map/ppermute | solution.py:71
  31.2 7.4 %slice-start = ((bf16[3,128,256]{2,1,0:T(8,128)(2,1)}), bf16[1,128,256]{2,1,0:T(8,128)(2,1)S(1)}, s32[]{:S(2)}) async-start(bf16[3,128,256]{2,1,0:T(8,128)(2,1)} %param.8), calls=%async_computation.4 | async-start | bytes 131072 | tf_op jit(solution)/shard_map/slice | solution.py:119
  31.2 9.4 %copy-start.10 = (bf16[256,128]{1,0:T(8,128)(2,1)S(1)}, bf16[256,128]{1,0:T(8,128)(2,1)}, u32[]{:S(2)}) copy-start(bf16[256,128]{1,0:T(8,128)(2,1)} %param.13) | copy-start | bytes 196612
  31.2 48.5 %copy-start.11 = (f32[256,16]{0,1:T(8,128)S(1)}, f32[256,16]{0,1:T(8,128)}, u32[]{:S(2)}) copy-start(f32[256,16]{0,1:T(8,128)} %param.11) | copy-start | bytes 49156
  31.2 48.6 %copy-start.2 = (f32[256,16]{0,1:T(8,128)S(1)}, f32[256,16]{0,1:T(8,128)}, u32[]{:S(2)}) copy-start(f32[256,16]{0,1:T(8,128)} %param.10) | copy-start | bytes 49156
  31.2 141.7 %all-to-all-start = ((bf16[512,16,256]{2,0,1:T(8,128)(2,1)}), bf16[512,16,256]{2,0,1:T(8,128)(2,1)}, u32[]{:S(2)}, u32[]{:S(2)}) async-start(bf16[512,16,256]{2,0,1:T(8,128)(2,1)} %broadcast_in_dim.14), calls=%async_computation | async-start | bytes 8388608 | tf_op jit(solution)/shard_map/all_to_all | solution.py:82
  38.5 62.3 %copy-start.18 = (f32[3,3,256]{2,1,0:T(4,128)S(1)}, f32[3,3,256]{2,1,0:T(4,128)}, u32[]{:S(2)}) copy-start(f32[3,3,256]{2,1,0:T(4,128)} %param.9) | copy-start | bytes 27652
  38.5 211.4 %all-gather.5.cloned.1.call-start = ((), (), s32[]{:S(2)}) async-start(), calls=%async_computation.3 | async-start | bytes 4456448 | tf_op jit(solution)/shard_map/all_gather | solution.py:121
  38.7 44.9 %collective-permute-start.2 = (bf16[2,2,128,256]{3,2,1,0:T(8,128)(2,1)S(1)}, bf16[2,2,128,256]{3,2,1,0:T(8,128)(2,1)S(1)}, u32[]{:S(2)}, u32[]{:S(2)}) collective-permute-start(bf16[2,2,128,256]{3,2,1,0:T(8,128)(2,1)S(1)} %collective-permute-done.1), channel_id=1, source_target_pairs={{0,16},{16,32},{32,48},{48,64},{64,80},{80,96},{96,112},{112,128},... | collective-permute-start | bytes 786440 | tf_op jit(solution)/shard_map/ppermute | solution.py:68
  79.9 25.7 %copy-start.20 = (f32[64]{0:T(128)}, f32[64]{0:T(128)S(1)}, u32[]{:S(2)}) copy-start(f32[64]{0:T(128)S(1)} %iota_negate_fusion) | copy-start | bytes 772
  80.0 16.3 %collective-permute-start.10 = (bf16[2,2,128,256]{3,2,1,0:T(8,128)(2,1)S(1)}, bf16[2,2,128,256]{3,2,1,0:T(8,128)(2,1)S(1)}, u32[]{:S(2)}, u32[]{:S(2)}) collective-permute-start(bf16[2,2,128,256]{3,2,1,0:T(8,128)(2,1)S(1)} %collective-permute-done.9), channel_id=1, source_target_pairs={{16,0},{32,16},{48,32},{64,48},{80,64},{96,80},{112,96},{128,112},... | collective-permute-start | bytes 786440 | tf_op jit(solution)/shard_map/ppermute | solution.py:71
  83.6 12.6 %copy-start.3 = (bf16[2,2,128,256]{3,2,1,0:T(8,128)(2,1)}, bf16[2,2,128,256]{3,2,1,0:T(8,128)(2,1)S(1)}, u32[]{:S(2)}) copy-start(bf16[2,2,128,256]{3,2,1,0:T(8,128)(2,1)S(1)} %collective-permute-done.2) | copy-start | bytes 786436
  83.6 10.1 %collective-permute-start.3 = (bf16[2,2,128,256]{3,2,1,0:T(8,128)(2,1)S(1)}, bf16[2,2,128,256]{3,2,1,0:T(8,128)(2,1)S(1)}, u32[]{:S(2)}, u32[]{:S(2)}) collective-permute-start(bf16[2,2,128,256]{3,2,1,0:T(8,128)(2,1)S(1)} %collective-permute-done.2), channel_id=1, source_target_pairs={{0,16},{16,32},{32,48},{48,64},{64,80},{80,96},{96,112},{112,128},... | collective-permute-start | bytes 786440 | tf_op jit(solution)/shard_map/ppermute | solution.py:68
  93.7 11.9 %copy-start.4 = (bf16[2,2,128,256]{3,2,1,0:T(8,128)(2,1)}, bf16[2,2,128,256]{3,2,1,0:T(8,128)(2,1)S(1)}, u32[]{:S(2)}) copy-start(bf16[2,2,128,256]{3,2,1,0:T(8,128)(2,1)S(1)} %collective-permute-done.3) | copy-start | bytes 786436
  93.7 9.2 %collective-permute-start.4 = (bf16[2,2,128,256]{3,2,1,0:T(8,128)(2,1)S(1)}, bf16[2,2,128,256]{3,2,1,0:T(8,128)(2,1)}, u32[]{:S(2)}, u32[]{:S(2)}) collective-permute-start(bf16[2,2,128,256]{3,2,1,0:T(8,128)(2,1)S(1)} %collective-permute-done.3), channel_id=1, source_target_pairs={{0,16},{16,32},{32,48},{48,64},{64,80},{80,96},{96,112},{112,128},... | collective-permute-start | bytes 786440 | tf_op jit(solution)/shard_map/ppermute | solution.py:68
  96.3 12.1 %collective-permute-start.11 = (bf16[2,2,128,256]{3,2,1,0:T(8,128)(2,1)S(1)}, bf16[2,2,128,256]{3,2,1,0:T(8,128)(2,1)S(1)}, u32[]{:S(2)}, u32[]{:S(2)}) collective-permute-start(bf16[2,2,128,256]{3,2,1,0:T(8,128)(2,1)S(1)} %collective-permute-done.10), channel_id=1, source_target_pairs={{16,0},{32,16},{48,32},{64,48},{80,64},{96,80},{112,96},{128,112},... | collective-permute-start | bytes 786440 | tf_op jit(solution)/shard_map/ppermute | solution.py:71
  102.9 15.7 %collective-permute-start.5 = (bf16[2,2,128,256]{3,2,1,0:T(8,128)(2,1)}, bf16[2,2,128,256]{3,2,1,0:T(8,128)(2,1)}, u32[]{:S(2)}, u32[]{:S(2)}) collective-permute-start(bf16[2,2,128,256]{3,2,1,0:T(8,128)(2,1)} %collective-permute-done.4), channel_id=1, source_target_pairs={{0,16},{16,32},{32,48},{48,64},{64,80},{80,96},{96,112},{112,128},... | collective-permute-start | bytes 786440 | tf_op jit(solution)/shard_map/ppermute | solution.py:68
  108.3 13.9 %collective-permute-start.12 = (bf16[2,2,128,256]{3,2,1,0:T(8,128)(2,1)S(1)}, bf16[2,2,128,256]{3,2,1,0:T(8,128)(2,1)S(1)}, u32[]{:S(2)}, u32[]{:S(2)}) collective-permute-start(bf16[2,2,128,256]{3,2,1,0:T(8,128)(2,1)S(1)} %collective-permute-done.11), channel_id=1, source_target_pairs={{16,0},{32,16},{48,32},{64,48},{80,64},{96,80},{112,96},{128,112},... | collective-permute-start | bytes 786440 | tf_op jit(solution)/shard_map/ppermute | solution.py:71
  118.6 12.7 %collective-permute-start.6 = (bf16[2,2,128,256]{3,2,1,0:T(8,128)(2,1)}, bf16[2,2,128,256]{3,2,1,0:T(8,128)(2,1)S(1)}, u32[]{:S(2)}, u32[]{:S(2)}) collective-permute-start(bf16[2,2,128,256]{3,2,1,0:T(8,128)(2,1)} %collective-permute-done.5), channel_id=1, source_target_pairs={{0,16},{16,32},{32,48},{48,64},{64,80},{80,96},{96,112},{112,128},... | collective-permute-start | bytes 786440 | tf_op jit(solution)/shard_map/ppermute | solution.py:68
  122.2 14.9 %collective-permute-start.13 = (bf16[2,2,128,256]{3,2,1,0:T(8,128)(2,1)S(1)}, bf16[2,2,128,256]{3,2,1,0:T(8,128)(2,1)S(1)}, u32[]{:S(2)}, u32[]{:S(2)}) collective-permute-start(bf16[2,2,128,256]{3,2,1,0:T(8,128)(2,1)S(1)} %collective-permute-done.12), channel_id=1, source_target_pairs={{16,0},{32,16},{48,32},{64,48},{80,64},{96,80},{112,96},{128,112},... | collective-permute-start | bytes 786440 | tf_op jit(solution)/shard_map/ppermute | solution.py:71
  131.4 13.2 %collective-permute-start.7 = (bf16[2,2,128,256]{3,2,1,0:T(8,128)(2,1)S(1)}, bf16[2,2,128,256]{3,2,1,0:T(8,128)(2,1)S(1)}, u32[]{:S(2)}, u32[]{:S(2)}) collective-permute-start(bf16[2,2,128,256]{3,2,1,0:T(8,128)(2,1)S(1)} %collective-permute-done.6), channel_id=1, source_target_pairs={{0,16},{16,32},{32,48},{48,64},{64,80},{80,96},{96,112},{112,128},... | collective-permute-start | bytes 786440 | tf_op jit(solution)/shard_map/ppermute | solution.py:68
  137.1 12.4 %collective-permute-start.14 = (bf16[2,2,128,256]{3,2,1,0:T(8,128)(2,1)S(1)}, bf16[2,2,128,256]{3,2,1,0:T(8,128)(2,1)S(1)}, u32[]{:S(2)}, u32[]{:S(2)}) collective-permute-start(bf16[2,2,128,256]{3,2,1,0:T(8,128)(2,1)S(1)} %collective-permute-done.13), channel_id=1, source_target_pairs={{16,0},{32,16},{48,32},{64,48},{80,64},{96,80},{112,96},{128,112},... | collective-permute-start | bytes 786440 | tf_op jit(solution)/shard_map/ppermute | solution.py:71
  144.6 13.3 %collective-permute-start.8 = (bf16[2,2,128,256]{3,2,1,0:T(8,128)(2,1)S(1)}, bf16[2,2,128,256]{3,2,1,0:T(8,128)(2,1)S(1)}, u32[]{:S(2)}, u32[]{:S(2)}) collective-permute-start(bf16[2,2,128,256]{3,2,1,0:T(8,128)(2,1)S(1)} %collective-permute-done.7), channel_id=1, source_target_pairs={{0,16},{16,32},{32,48},{48,64},{64,80},{80,96},{96,112},{112,128},... | collective-permute-start | bytes 786440 | tf_op jit(solution)/shard_map/ppermute | solution.py:68
  149.5 9.1 %collective-permute-start.15 = (bf16[2,2,128,256]{3,2,1,0:T(8,128)(2,1)S(1)}, bf16[2,2,128,256]{3,2,1,0:T(8,128)(2,1)S(1)}, u32[]{:S(2)}, u32[]{:S(2)}) collective-permute-start(bf16[2,2,128,256]{3,2,1,0:T(8,128)(2,1)S(1)} %collective-permute-done.14), channel_id=1, source_target_pairs={{16,0},{32,16},{48,32},{64,48},{80,64},{96,80},{112,96},{128,112},... | collective-permute-start | bytes 786440 | tf_op jit(solution)/shard_map/ppermute | solution.py:71
  173.8 10.3 %collective-permute-start = (bf16[2,16,256]{2,0,1:T(2,128)(2,1)S(1)}, bf16[2,16,256]{2,0,1:T(2,128)(2,1)S(1)}, u32[]{:S(2)}, u32[]{:S(2)}) collective-permute-start(bf16[2,16,256]{2,0,1:T(2,128)(2,1)S(1)} %slice.167), channel_id=1, source_target_pairs={{0,16},{16,32},{32,48},{48,64},{64,80},{80,96},{96,112},{112,128},... | collective-permute-start | bytes 49160 | tf_op jit(solution)/shard_map/ppermute | solution.py:16
  178.0 6.7 %copy-start = (bf16[16,2,2,128,256]{4,3,0,2,1:T(8,128)(2,1)S(1)}, bf16[16,2,2,128,256]{4,3,0,2,1:T(8,128)(2,1)}, u32[]{:S(2)}) copy-start(bf16[16,2,2,128,256]{4,3,0,2,1:T(8,128)(2,1)} %fusion) | copy-start | bytes 12582916
  187.3 4.3 %copy-start.5 = (f32[256,16]{0,1:T(8,128)S(1)}, f32[256,16]{0,1:T(8,128)}, u32[]{:S(2)}) copy-start(f32[256,16]{0,1:T(8,128)} %get-tuple-element.13) | copy-start | bytes 49156
  187.3 4.3 %copy-start.9 = (f32[256,16]{0,1:T(8,128)S(1)}, f32[256,16]{0,1:T(8,128)}, u32[]{:S(2)}) copy-start(f32[256,16]{0,1:T(8,128)} %get-tuple-element.12) | copy-start | bytes 49156
  187.4 16.2 %copy-start.8 = (f32[256,16]{0,1:T(8,128)S(1)}, f32[256,16]{0,1:T(8,128)}, u32[]{:S(2)}) copy-start(f32[256,16]{0,1:T(8,128)} %get-tuple-element.11) | copy-start | bytes 49156
  192.8 42.6 %all-to-all-start.1 = ((f32[32,256,16]{1,2,0:T(8,128)}), f32[32,256,16]{1,2,0:T(8,128)S(1)}, u32[]{:S(2)}, u32[]{:S(2)}) async-start(f32[32,256,16]{1,2,0:T(8,128)} %broadcast_in_dim.18), calls=%async_computation.1 | async-start | bytes 1048576 | tf_op jit(solution)/shard_map/all_to_all | solution.py:21
  263.3 3.9 %copy-start.1 = (bf16[2,2048,512]{2,1,0:T(8,128)(2,1)S(1)}, bf16[2,2048,512]{2,1,0:T(8,128)(2,1)}, u32[]{:S(2)}) copy-start(bf16[2,2048,512]{2,1,0:T(8,128)(2,1)} %copy.209) | copy-start | bytes 12582916
  (9 other events, 23.2 us)
Sparse Core Ops, SparseCore 0:
  79.8 169.9 all-gather.4

commit v10 on v8

--- a/solution.py
+++ b/solution.py
@@ -99,11 +99,11 @@
             return feats
 
         pair = across_z(across_yh(in_weight[1:]))
-        packed = jnp.concatenate([in_weight[0], out_weight.T], axis=1)[None]
+        packed = jnp.stack([in_weight[0], out_weight.T])
         packed, pair = lax.optimization_barrier((packed, pair))
         feats = filtered(shortened(pair), short_taps[:, 1:])
-        packed = across_z(across_yh(packed))[0]
-        query = filtered(shortened(packed[None, :, :width]), short_taps[:, :1])[0]
+        packed = across_z(across_yh(packed))
+        query = filtered(shortened(packed[:1]), short_taps[:, :1])[0]
         gated = (feats[0] * feats[1]).astype(jnp.bfloat16)
         values = gated.astype(jnp.float32)
         inner, starts, final, heads, offsets = block_terms(values, rates, residues)
@@ -111,7 +111,7 @@
         starts = starts + offsets * incoming[None]
         conv = finish(inner, starts, heads, values, skip)
         hidden = (query * conv).astype(jnp.bfloat16)
-        terms = jnp.einsum("tc,ec->te", hidden, packed[:, width:], preferred_element_type=jnp.float32)
+        terms = jnp.einsum("tc,ec->te", hidden, packed[1], preferred_element_type=jnp.float32)
         return scattered_terms(terms.astype(jnp.bfloat16), lanes)
 
     return shards

time: 276 us -> 278 us (level)
  no operation moved by 1% of the time
where the time goes in v10:
time: 278 us
  waiting for transfers between devices  94 us (34%)
  blocking collectives  74 us (27%)
  matrix products  34.3 us (12%)
  local copies, waits for them, and re-layouts  28.9 us (10%)
  starting transfers between devices  23.7 us (9%)
  between operations  13.9 us (5%)
  other arithmetic  8.83 us (3%)
    all_gather x2, waiting for transfers between devices, across_z(): part = lax.all_gather(part, 'z', axis=2)  79.6 us
    all_to_all x1, blocking collectives, scattered_terms(): parts = lax.all_to_all(split, CH, 1, 1)  61.1 us
    all_to_all x1, waiting for transfers between devices, carried_in(): every = lax.all_to_all(copies, CTX, 0, 0)  14.3 us
    all_gather x2, blocking collectives, across_yh(): return lax.all_gather(part, 'yh', axis=1)  12.9 us
    all_to_all x1, starting transfers between devices, gathered_tokens(): return lax.all_to_all(copies, CH, 1, 1)  11.7 us
    all_to_all x1, starting transfers between devices, carried_in(): every = lax.all_to_all(copies, CTX, 0, 0)  10 us
    dot_general x2, matrix products, shortened(): jnp.einsum('tkd,jkdc->jtc', whole, weight, preferred_element_type=jnp.flo...  9.48 us
    dot_general x1, local copies, waits for them, and re-layouts, block_terms(): jnp.dot(pick, impulse, precision=lax.Precision.HIGHEST)  9.2 us
  transfers between devices with their start and end apart: 5, of which 3 were waited for; matrix products, arithmetic and copies ran while one was open for 21% of the time, Pallas kernels for 0%

profile of v10, /device:TPU:1, one launch (start us, length us, event | category | flops | bytes accessed | tf_op | source)
XLA Modules:
  0.0 277.6 jit_solution(9748539707480749384)
XLA Ops:
  6.5 0.9 slice.132
  7.5 6.9 %all-gather = bf16[2,256,256]{2,1,0:T(8,128)(2,1)} all-gather(bf16[2,128,256]{2,1,0:T(8,128)(2,1)S(1)} %slice.132), channel_id=2, replica_groups=mesh['yh'=2,'z'=16,'ch'=16] {'yh'}, dimensions={1}, use_global_device_ids=true | all-gather | bytes 393216 | tf_op jit(solution)/shard_map/all_gather | solution.py:82
  14.3 3.4 %broadcast_in_dim.14 = bf16[512,16,256]{2,0,1:T(8,128)(2,1)} broadcast(bf16[512,256]{1,0:T(8,128)(2,1)} %param.7), dimensions={0,2} | broadcast | bytes 4456448 | tf_op jit(solution)/shard_map/broadcast_in_dim | solution.py:63
  17.7 11.7 %all-to-all-start = ((bf16[512,16,256]{2,0,1:T(8,128)(2,1)}), bf16[512,16,256]{2,0,1:T(8,128)(2,1)}, u32[]{:S(2)}, u32[]{:S(2)}) async-start(bf16[512,16,256]{2,0,1:T(8,128)(2,1)} %broadcast_in_dim.14), calls=%async_computation | async-start | bytes 8388608 | tf_op jit(solution)/shard_map/all_to_all | solution.py:64
  29.6 61.9 %all-gather.7.cloned.1.call-done = bf16[2,2,2048,256]{3,2,1,0:T(8,128)(2,1)} async-done(((bf16[2,2,128,256]{3,2,1,0:T(8,128)(2,1)}), bf16[2,2,2048,256]{3,2,1,0:T(8,128)(2,1)}) %all-gather.7.cloned.1.call-update) | async-done | bytes 4194320 | tf_op jit(solution)/shard_map/all_gather | solution.py:85
  91.5 6.1 %all-gather.2 = bf16[2,256,256]{1,2,0:T(8,128)(2,1)S(1)} all-gather(bf16[2,128,256]{1,2,0:T(8,128)(2,1)S(1)} %pad_maximum_fusion), channel_id=4, replica_groups=mesh['yh'=2,'z'=16,'ch'=16] {'yh'}, dimensions={1}, use_global_device_ids=true | all-gather | bytes 393216 | tf_op jit(solution)/shard_map/all_gather | solution.py:82
  97.6 0.8 copy.157
  98.7 0.6 negate_exponential_fusion
  99.3 2.8 multiply_reduce_fusion
  102.1 0.9 slice.171
  103.0 1.9 collective-permute-start
  104.9 2.7 rev.3
  107.7 2.8 %fusion.19 = bf16[2,2,256]{2,1,0:T(2,128)(2,1)S(1)} fusion(bf16[2,16,256,256]{3,2,1,0:T(8,128)(2,1)} %bitcast.108, bf16[2,16,256]{2,0,1:T(2,128)(2,1)S(1)} %collective-permute-done), kind=kOutput, calls=%fused_computation.21 | convolution fusion | flops 8389632 | bytes 4212736 | tf_op jit(solution)/shard_map/tkd,jkdc->jtc/dot_general | solution.py:91
  110.7 5.9 %fusion.13 = bf16[2,512,256]{1,2,0:T(8,128)(2,1)S(1)} fusion(bf16[2,16,256,256]{3,2,1,0:T(8,128)(2,1)} %bitcast.109, bf16[512,16,256]{2,0,1:T(8,128)(2,1)} %all-to-all-done), kind=kOutput, calls=%fused_computation.15 | convolution fusion | flops 2147745792 | bytes 8912896 | tf_op jit(solution)/shard_map/tkd,jkdc->jtc/dot_general | solution.py:90
  116.9 0.9 fusion.22
  118.3 2.8 fusion.50
  121.1 1.5 copy.146
  122.9 0.9 broadcast_in_dim.18
  123.8 10.0 %all-to-all-start.1 = ((f32[32,256,16]{1,2,0:T(8,128)}), f32[32,256,16]{1,2,0:T(8,128)S(1)}, u32[]{:S(2)}, u32[]{:S(2)}) async-start(f32[32,256,16]{1,2,0:T(8,128)} %broadcast_in_dim.18), calls=%async_computation.1 | async-start | bytes 1048576 | tf_op jit(solution)/shard_map/all_to_all | solution.py:21
  133.8 0.8 copy.147
  134.6 3.7 %fusion.4 = f32[64,64,256]{2,1,0:T(8,128)} fusion(s32[64,64]{1,0:T(8,128)S(1)} %iota_subtract_fusion, f32[64,256]{0,1:T(8,128)S(1)} %get-tuple-element.11), kind=kOutput, calls=%fused_computation.8 | convolution fusion | flops 805568512 | bytes 4276224 | tf_op jit(solution)/shard_map/dot_general | solution.py:40
  138.3 9.2 %copy.144 = f32[64,64,256]{1,0,2:T(8,128)} copy(f32[64,64,256]{2,1,0:T(8,128)} %fusion.4) | data formatting | bytes 8388608 | tf_op jit(solution)/shard_map/dot_general | solution.py:40
  147.6 1.3 fusion.49
  149.1 14.3 %all-to-all-done.1 = f32[32,256,16]{1,2,0:T(8,128)S(1)} async-done(((f32[32,256,16]{1,2,0:T(8,128)}), f32[32,256,16]{1,2,0:T(8,128)S(1)}, u32[]{:S(2)}, u32[]{:S(2)}) %all-to-all-start.1) | async-done | bytes 524320 | tf_op jit(solution)/shard_map/all_to_all | solution.py:21
  164.1 4.1 %fusion.2 = f32[256,8,64]{2,1,0:T(8,128)S(1)} fusion(f32[8,256,16]{2,0,1:T(8,128)S(1)} %copy.148, f32[256,16]{1,0:T(8,128)} %copy.147, f32[256,16]{1,0:T(8,128)S(1)} %copy.141, f32[64]{0:T(128)} %copy-done.14, f32[256,16]{1,0:T(8,128)S(1)} %copy.140), kind=kOutput, calls=%fused_computation.4 | convolution fusion | flops 25952256 | bytes 704768 | tf_op jit(solution)/shard_map/icm,bcm->bic/dot_general | solution.py:58
  168.2 9.2 %fusion.9 = f32[8,64,256]{1,0,2:T(8,128)S(1)} fusion(f32[256,8,64]{2,1,0:T(8,128)S(1)} %fusion.2, bf16[8,64,256]{1,0,2:T(8,128)(2,1)S(1)} %copy.143, f32[64,64,256]{1,0,2:T(8,128)} %copy.144), kind=kOutput, calls=%fused_computation.13 | convolution fusion | flops 100794368 | bytes 5505024 | tf_op jit(solution)/shard_map/ijc,bjc->bic/dot_general | solution.py:44
  177.9 17.7 %all-gather.9.cloned.1.call-done = bf16[2,2,2048,256]{3,2,1,0:T(8,128)(2,1)} async-done(((bf16[2,2,128,256]{3,2,1,0:T(8,128)(2,1)}), bf16[2,2,2048,256]{3,2,1,0:T(8,128)(2,1)}) %all-gather.9.cloned.1.call-update) | async-done | bytes 4194320 | tf_op jit(solution)/shard_map/all_gather | solution.py:85
  195.6 3.8 %fusion.46 = (bf16[1,2,2048,256]{3,2,1,0:T(8,128)(2,1)S(1)}, bf16[1,2,2048,256]{3,2,1,0:T(8,128)(2,1)}) fusion(bf16[2,2,2048,256]{3,2,1,0:T(8,128)(2,1)} %all-gather.9.cloned.1.call-done), kind=kLoop, calls=%fused_computation.82 | loop fusion | bytes 8388608 | tf_op jit(solution)/shard_map/slice | solution.py:106
  200.0 3.6 %fusion.17 = bf16[1,512,256]{1,2,0:T(8,128)(2,1)S(1)} fusion(bf16[16,256,256]{2,1,0:T(8,128)(2,1)S(1)} %bitcast.106, bf16[512,16,256]{2,0,1:T(8,128)(2,1)} %all-to-all-done), kind=kOutput, calls=%fused_computation.18 | convolution fusion | flops 1073872896 | bytes 6553600 | tf_op jit(solution)/shard_map/tkd,jkdc->jtc/dot_general | solution.py:90
  203.9 1.8 convolution_convert_fusion
  206.2 61.1 %all_to_all.15 = bf16[512,16,256]{2,0,1:T(8,128)(2,1)} all-to-all(bf16[512,16,256]{2,0,1:T(8,128)(2,1)S(1)} %bitcast.104), channel_id=1, replica_groups=mesh['yh'=2,'z'=16,'ch'=16] {'ch'}, dimensions={1} | all-to-all | bytes 8388608 | tf_op jit(solution)/shard_map/all_to_all | solution.py:70
  267.2 3.5 %reduce_sum.32 = bf16[512,256]{1,0:T(8,128)(2,1)} reduce(bf16[512,16,256]{2,0,1:T(8,128)(2,1)} %all_to_all.15, bf16[]{:T(256)} %constant.28.clone.1), dimensions={1}, to_apply=%region_2.3 | reduce | flops 1966080 | bytes 4456450 | tf_op jit(solution)/shard_map/reduce_sum | solution.py:71
  (79 shorter events, 4.2 us)
Async XLA Ops:
  6.5 85.0 %all-gather.7.cloned.1.call-start = ((), (), s32[]{:S(2)}) async-start(), calls=%async_computation.3 | async-start | bytes 4456448 | tf_op jit(solution)/shard_map/all_gather | solution.py:85
  17.7 11.8 %slice-start = ((bf16[3,128,256]{2,1,0:T(8,128)(2,1)}), bf16[1,128,256]{2,1,0:T(8,128)(2,1)S(1)}, s32[]{:S(2)}) async-start(bf16[3,128,256]{2,1,0:T(8,128)(2,1)} %param.8), calls=%async_computation.5 | async-start | bytes 131072 | tf_op jit(solution)/shard_map/slice | solution.py:102
  17.7 11.9 %copy-start.7 = (bf16[256,128]{1,0:T(8,128)(2,1)S(1)}, bf16[256,128]{1,0:T(8,128)(2,1)}, u32[]{:S(2)}) copy-start(bf16[256,128]{1,0:T(8,128)(2,1)} %param.13) | copy-start | bytes 196612
  17.7 80.7 %copy-start.1 = (f32[256,16]{0,1:T(8,128)S(1)}, f32[256,16]{0,1:T(8,128)}, u32[]{:S(2)}) copy-start(f32[256,16]{0,1:T(8,128)} %param.10) | copy-start | bytes 49156
  17.7 80.8 %copy-start.8 = (f32[256,16]{0,1:T(8,128)S(1)}, f32[256,16]{0,1:T(8,128)}, u32[]{:S(2)}) copy-start(f32[256,16]{0,1:T(8,128)} %param.11) | copy-start | bytes 49156
  17.7 84.4 %all-to-all-start = ((bf16[512,16,256]{2,0,1:T(8,128)(2,1)}), bf16[512,16,256]{2,0,1:T(8,128)(2,1)}, u32[]{:S(2)}, u32[]{:S(2)}) async-start(bf16[512,16,256]{2,0,1:T(8,128)(2,1)} %broadcast_in_dim.14), calls=%async_computation | async-start | bytes 8388608 | tf_op jit(solution)/shard_map/all_to_all | solution.py:64
  29.4 166.2 %all-gather.9.cloned.1.call-start = ((), (), s32[]{:S(2)}) async-start(), calls=%async_computation.4 | async-start | bytes 4456448 | tf_op jit(solution)/shard_map/all_gather | solution.py:85
  29.6 75.2 %copy-start.12 = (f32[3,3,256]{2,1,0:T(4,128)S(1)}, f32[3,3,256]{2,1,0:T(4,128)}, u32[]{:S(2)}) copy-start(f32[3,3,256]{2,1,0:T(4,128)} %param.9) | copy-start | bytes 27652
  98.7 9.0 %copy-start.14 = (f32[64]{0:T(128)}, f32[64]{0:T(128)S(1)}, u32[]{:S(2)}) copy-start(f32[64]{0:T(128)S(1)} %iota_negate_fusion) | copy-start | bytes 772
  103.0 4.7 %collective-permute-start = (bf16[2,16,256]{2,0,1:T(2,128)(2,1)S(1)}, bf16[2,16,256]{2,0,1:T(2,128)(2,1)S(1)}, u32[]{:S(2)}, u32[]{:S(2)}) collective-permute-start(bf16[2,16,256]{2,0,1:T(2,128)(2,1)S(1)} %slice.171), channel_id=1, source_target_pairs={{0,16},{16,32},{32,48},{48,64},{64,80},{80,96},{96,112},{112,128},... | collective-permute-start | bytes 49160 | tf_op jit(solution)/shard_map/ppermute | solution.py:16
  107.7 2.8 %copy-start.3 = (bf16[2,16,256]{2,0,1:T(2,128)(2,1)}, bf16[2,16,256]{2,0,1:T(2,128)(2,1)S(1)}, u32[]{:S(2)}) copy-start(bf16[2,16,256]{2,0,1:T(2,128)(2,1)S(1)} %collective-permute-done) | copy-start | bytes 49156
  118.3 4.3 %copy-start.2 = (f32[256,16]{0,1:T(8,128)S(1)}, f32[256,16]{0,1:T(8,128)}, u32[]{:S(2)}) copy-start(f32[256,16]{0,1:T(8,128)} %get-tuple-element.19) | copy-start | bytes 49156
  118.3 4.3 %copy-start.6 = (f32[256,16]{0,1:T(8,128)S(1)}, f32[256,16]{0,1:T(8,128)}, u32[]{:S(2)}) copy-start(f32[256,16]{0,1:T(8,128)} %get-tuple-element.18) | copy-start | bytes 49156
  121.1 12.7 %copy-start.5 = (f32[256,16]{0,1:T(8,128)S(1)}, f32[256,16]{0,1:T(8,128)}, u32[]{:S(2)}) copy-start(f32[256,16]{0,1:T(8,128)} %get-tuple-element.17) | copy-start | bytes 49156
  123.8 39.6 %all-to-all-start.1 = ((f32[32,256,16]{1,2,0:T(8,128)}), f32[32,256,16]{1,2,0:T(8,128)S(1)}, u32[]{:S(2)}, u32[]{:S(2)}) async-start(f32[32,256,16]{1,2,0:T(8,128)} %broadcast_in_dim.18), calls=%async_computation.1 | async-start | bytes 1048576 | tf_op jit(solution)/shard_map/all_to_all | solution.py:21
  177.9 21.5 %copy-start.4 = (bf16[2,16,256]{2,0,1:T(2,128)(2,1)S(1)}, bf16[2,16,256]{2,0,1:T(2,128)(2,1)}, u32[]{:S(2)}) copy-start(bf16[2,16,256]{2,0,1:T(2,128)(2,1)} %copy-done.3) | copy-start | bytes 49156
  200.0 3.9 %copy-start = (bf16[1,2,2048,256]{3,2,1,0:T(8,128)(2,1)S(1)}, bf16[1,2,2048,256]{3,2,1,0:T(8,128)(2,1)}, u32[]{:S(2)}) copy-start(bf16[1,2,2048,256]{3,2,1,0:T(8,128)(2,1)} %get-tuple-element.10) | copy-start | bytes 6291460
  200.0 3.9 %copy-start.9 = (f32[1,1,256]{2,1,0:T(1,128)S(1)}, f32[1,1,256]{2,1,0:T(1,128)}, u32[]{:S(2)}) copy-start(f32[1,1,256]{2,1,0:T(1,128)} %get-tuple-element.20) | copy-start | bytes 3076
  200.0 3.9 %copy-start.10 = (f32[1,1,256]{2,1,0:T(1,128)S(1)}, f32[1,1,256]{2,1,0:T(1,128)}, u32[]{:S(2)}) copy-start(f32[1,1,256]{2,1,0:T(1,128)} %get-tuple-element.21) | copy-start | bytes 3076
  200.0 3.9 %copy-start.11 = (f32[1,1,256]{2,1,0:T(1,128)S(1)}, f32[1,1,256]{2,1,0:T(1,128)}, u32[]{:S(2)}) copy-start(f32[1,1,256]{2,1,0:T(1,128)} %get-tuple-element.22) | copy-start | bytes 3076
  200.0 3.9 %copy-start.13 = (f32[256]{0:T(256)S(1)}, f32[256]{0:T(256)}, u32[]{:S(2)}) copy-start(f32[256]{0:T(256)} %param.12) | copy-start | bytes 3076
Sparse Core Ops, SparseCore 0:
  14.5 77.0 all-gather.6
  98.6 96.9 all-gather.8

commit v11 on v8

--- a/solution.py
+++ b/solution.py
@@ -8,7 +8,7 @@
 SHORT = 3
 BLOCK = 64
 CTX = ("yh", "z")
-CH = "ch"
+CH = ("cx", "core")
 
 
 def passed_along(block, axis, count, distance):
@@ -66,8 +66,10 @@
 
 def scattered_terms(terms, lanes):
     rows, total = terms.shape
-    split = terms.reshape(rows, lanes, total // lanes)
-    parts = lax.all_to_all(split, CH, 1, 1)
+    split = terms.reshape(rows, lanes // 2, 2, total // lanes)
+    pairs = lax.all_to_all(split, "core", 2, 2)
+    pairs = jnp.sum(pairs.astype(jnp.float32), axis=2).astype(jnp.bfloat16)
+    parts = lax.all_to_all(pairs, "cx", 1, 1)
     return jnp.sum(parts.astype(jnp.float32), axis=1).astype(jnp.bfloat16)
 
 
@@ -120,7 +122,7 @@
 def solution(mesh):
     count = mesh.shape["ctx"]
     lanes = mesh.shape["ch"]
-    fine = Mesh(mesh.devices.reshape(2, count // 2, lanes), CTX + (CH,))
+    fine = Mesh(mesh.devices.reshape(2, count // 2, lanes // 2, 2), CTX + CH)
     placed = (
         P(CTX, CH),
         P(None, CTX, CH),

time: 276 us -> 275 us (level)
  blocking collectives: 74.5 us -> 57.7 us
  local copies, waits for them, and re-layouts: 26.8 us -> 37.4 us
    all_to_all x1 -> x2, blocking collectives: 61.2 us -> 44.4 us  [the longest x1 29.7 us: scattered_terms(): parts = lax.all_to_all(pairs, 'cx', 1, 1)]
    reshape x1 -> x2, local copies, waits for them, and re-layouts: 0.41 us -> 10.6 us  [scattered_terms(): split = terms.reshape(rows, lanes // 2, 2, total // lanes)]
    reduce_sum x0 -> x1, other arithmetic: none -> 4.42 us  [scattered_terms(): pairs = jnp.sum(pairs.astype(jnp.float32), axis=2).astype(jnp.bfloat16)]
where the time goes in v11:
time: 275 us; the launch traced here: 273 us
  waiting for transfers between devices  93.2 us (34%)
  blocking collectives  57.7 us (21%)
  local copies, waits for them, and re-layouts  37.4 us (14%)
  matrix products  36.2 us (13%)
  starting transfers between devices  23.9 us (9%)
  between operations  13.9 us (5%)
  other arithmetic  10.8 us (4%)
    all_gather x2, waiting for transfers between devices, across_z(): part = lax.all_gather(part, 'z', axis=2)  78.9 us
    all_to_all x1, blocking collectives, scattered_terms(): parts = lax.all_to_all(pairs, 'cx', 1, 1)  29.7 us
    all_to_all x1, blocking collectives, scattered_terms(): pairs = lax.all_to_all(split, 'core', 2, 2)  14.7 us
    all_to_all x1, waiting for transfers between devices, carried_in(): every = lax.all_to_all(copies, CTX, 0, 0)  14.3 us
    all_gather x2, blocking collectives, across_yh(): return lax.all_gather(part, 'yh', axis=1)  13.3 us
    all_to_all x1, starting transfers between devices, gathered_tokens(): return lax.all_to_all(copies, CH, 1, 1)  11.7 us
    reshape x2, local copies, waits for them, and re-layouts, scattered_terms(): split = terms.reshape(rows, lanes // 2, 2, total // lanes)  10.6 us
    all_to_all x1, starting transfers between devices, carried_in(): every = lax.all_to_all(copies, CTX, 0, 0)  9.95 us
  transfers between devices with their start and end apart: 5, of which 3 were waited for; matrix products, arithmetic and copies ran while one was open for 21% of the time, Pallas kernels for 0%

profile of v11, /device:TPU:1, one launch (start us, length us, event | category | flops | bytes accessed | tf_op | source)
XLA Modules:
  0.0 273.1 jit_solution(17933003883281289639)
XLA Ops:
  6.5 0.9 slice.130
  7.5 6.9 %all-gather = bf16[2,256,256]{2,1,0:T(8,128)(2,1)} all-gather(bf16[2,128,256]{2,1,0:T(8,128)(2,1)S(1)} %slice.130), channel_id=2, replica_groups=mesh['yh'=2,'z'=16,'cx'=8,'core'=2] {'yh'}, dimensions={1}, use_global_device_ids=true | all-gather | bytes 393216 | tf_op jit(solution)/shard_map/all_gather | solution.py:84
  14.3 3.3 %broadcast_in_dim.17 = bf16[512,16,256]{2,0,1:T(8,128)(2,1)} broadcast(bf16[512,256]{1,0:T(8,128)(2,1)} %param.7), dimensions={0,2} | broadcast | bytes 4456448 | tf_op jit(solution)/shard_map/broadcast_in_dim | solution.py:63
  17.7 11.7 %all-to-all-start = ((bf16[512,16,256]{2,0,1:T(8,128)(2,1)}), bf16[512,16,256]{2,0,1:T(8,128)(2,1)}, u32[]{:S(2)}, u32[]{:S(2)}) async-start(bf16[512,16,256]{2,0,1:T(8,128)(2,1)} %broadcast_in_dim.17), calls=%async_computation | async-start | bytes 8388608 | tf_op jit(solution)/shard_map/all_to_all | solution.py:64
  30.4 60.5 %all-gather.7.cloned.1.call-done = bf16[2,2,2048,256]{3,2,1,0:T(8,128)(2,1)} async-done(((bf16[2,2,128,256]{3,2,1,0:T(8,128)(2,1)}), bf16[2,2,2048,256]{3,2,1,0:T(8,128)(2,1)}) %all-gather.7.cloned.1.call-update) | async-done | bytes 4194320 | tf_op jit(solution)/shard_map/all_gather | solution.py:87
  90.9 6.5 %all-gather.2 = bf16[2,128,512]{2,1,0:T(8,128)(2,1)} all-gather(bf16[1,128,512]{2,1,0:T(8,128)(2,1)S(1)} %maximum_bitcast_fusion), channel_id=4, replica_groups=mesh['yh'=2,'z'=16,'cx'=8,'core'=2] {'yh'}, dimensions={0}, use_global_device_ids=true | all-gather | bytes 393216 | tf_op jit(solution)/shard_map/all_gather | solution.py:84
  98.3 2.8 %multiply_reduce_fusion = (f32[64,256]{0,1:T(8,128)S(1)}, f32[64,256,16]{0,2,1:T(8,128)}) fusion(f32[256,16]{1,0:T(8,128)S(1)} %copy.137, f32[64]{0:T(128)S(1)} %iota_negate_fusion, f32[256,16]{1,0:T(8,128)S(1)} %copy.136), kind=kLoop, calls=%fused_computation.10 | loop fusion | flops 770048 | bytes 1147136 | tf_op jit(solution)/shard_map/reduce_sum | solution.py:35
  102.0 2.2 collective-permute-start
  104.2 2.7 %rev.3 = f32[64,256,16]{0,2,1:T(8,128)S(1)} reverse(f32[64,256,16]{0,2,1:T(8,128)} %get-tuple-element.10), dimensions={0} | reverse | bytes 2097152 | tf_op jit(solution)/shard_map/rev | solution.py:41
  107.0 2.8 %fusion.20 = bf16[2,2,256]{2,1,0:T(2,128)(2,1)S(1)} fusion(bf16[2,16,256,256]{3,2,1,0:T(8,128)(2,1)} %bitcast.111, bf16[2,16,256]{2,0,1:T(2,128)(2,1)S(1)} %collective-permute-done), kind=kOutput, calls=%fused_computation.21 | convolution fusion | flops 8389632 | bytes 4212736 | tf_op jit(solution)/shard_map/tkd,jkdc->jtc/dot_general | solution.py:93
  110.0 5.9 %fusion.14 = bf16[2,512,256]{1,2,0:T(8,128)(2,1)S(1)} fusion(bf16[2,16,256,256]{3,2,1,0:T(8,128)(2,1)} %bitcast.112, bf16[512,16,256]{2,0,1:T(8,128)(2,1)} %all-to-all-done), kind=kOutput, calls=%fused_computation.15 | convolution fusion | flops 2147745792 | bytes 8912896 | tf_op jit(solution)/shard_map/tkd,jkdc->jtc/dot_general | solution.py:92
  116.2 0.9 fusion.23
  117.7 2.7 %fusion.53 = f32[256,8,16]{2,1,0:T(8,128)} fusion(bf16[8,64,256]{1,0,2:T(8,128)(2,1)S(1)} %copy.139, f32[64,256,16]{0,2,1:T(8,128)S(1)} %rev.3), kind=kOutput, calls=%fused_computation.90 | convolution fusion | flops 25165824 | bytes 1441792 | tf_op jit(solution)/shard_map/jcm,bjc->bcm/dot_general | solution.py:45
  120.4 1.5 copy.142
  122.2 0.9 broadcast_in_dim.21
  123.0 9.9 %all-to-all-start.1 = ((f32[32,256,16]{1,2,0:T(8,128)}), f32[32,256,16]{1,2,0:T(8,128)S(1)}, u32[]{:S(2)}, u32[]{:S(2)}) async-start(f32[32,256,16]{1,2,0:T(8,128)} %broadcast_in_dim.21), calls=%async_computation.1 | async-start | bytes 1048576 | tf_op jit(solution)/shard_map/all_to_all | solution.py:21
  133.8 3.8 %fusion.5 = f32[64,64,256]{2,1,0:T(8,128)} fusion(s32[64,64]{1,0:T(8,128)S(1)} %iota_subtract_fusion, f32[64,256]{0,1:T(8,128)S(1)} %get-tuple-element.9), kind=kOutput, calls=%fused_computation.8 | convolution fusion | flops 805568512 | bytes 4276224 | tf_op jit(solution)/shard_map/dot_general | solution.py:40
  137.5 9.2 %copy.140 = f32[64,64,256]{1,0,2:T(8,128)} copy(f32[64,64,256]{2,1,0:T(8,128)} %fusion.5) | data formatting | bytes 8388608 | tf_op jit(solution)/shard_map/dot_general | solution.py:40
  146.8 1.3 fusion.52
  148.2 14.3 %all-to-all-done.1 = f32[32,256,16]{1,2,0:T(8,128)S(1)} async-done(((f32[32,256,16]{1,2,0:T(8,128)}), f32[32,256,16]{1,2,0:T(8,128)S(1)}, u32[]{:S(2)}, u32[]{:S(2)}) %all-to-all-start.1) | async-done | bytes 524320 | tf_op jit(solution)/shard_map/all_to_all | solution.py:21
  163.2 4.1 %fusion.3 = f32[256,8,64]{2,1,0:T(8,128)S(1)} fusion(f32[8,256,16]{2,0,1:T(8,128)S(1)} %copy.144, f32[256,16]{1,0:T(8,128)} %copy.143, f32[256,16]{1,0:T(8,128)S(1)} %copy.137, f32[64]{0:T(128)} %copy-done.14, f32[256,16]{1,0:T(8,128)S(1)} %copy.136), kind=kOutput, calls=%fused_computation.4 | convolution fusion | flops 25952256 | bytes 704768 | tf_op jit(solution)/shard_map/icm,bcm->bic/dot_general | solution.py:58
  167.3 9.2 %fusion.10 = f32[8,64,256]{1,0,2:T(8,128)S(1)} fusion(f32[256,8,64]{2,1,0:T(8,128)S(1)} %fusion.3, bf16[8,64,256]{1,0,2:T(8,128)(2,1)S(1)} %copy.139, f32[64,64,256]{1,0,2:T(8,128)} %copy.140), kind=kOutput, calls=%fused_computation.13 | convolution fusion | flops 100794368 | bytes 5505024 | tf_op jit(solution)/shard_map/ijc,bjc->bic/dot_general | solution.py:44
  177.1 18.4 %all-gather.9.cloned.1.call-done = bf16[2,2048,512]{2,1,0:T(8,128)(2,1)} async-done(((bf16[2,128,512]{2,1,0:T(8,128)(2,1)}), bf16[2,2048,512]{2,1,0:T(8,128)(2,1)}) %all-gather.9.cloned.1.call-update) | async-done | bytes 4194320 | tf_op jit(solution)/shard_map/all_gather | solution.py:87
  195.5 1.7 slice.166
  197.8 3.6 %fusion.18 = bf16[1,512,256]{1,2,0:T(8,128)(2,1)S(1)} fusion(bf16[16,256,256]{2,1,0:T(8,128)(2,1)S(1)} %bitcast.110, bf16[512,16,256]{2,0,1:T(8,128)(2,1)} %all-to-all-done), kind=kOutput, calls=%fused_computation.18 | convolution fusion | flops 1073872896 | bytes 6553600 | tf_op jit(solution)/shard_map/tkd,jkdc->jtc/dot_general | solution.py:92
  201.6 3.8 %convolution_convert_fusion = bf16[512,4096]{1,0:T(8,128)(2,1)} fusion(bf16[4096,512]{1,0:T(8,128)(2,1)S(1)} %bitcast.114, f32[1,514,256]{1,2,0:T(8,128)S(1)} %maximum_convert_fusion.1, f32[512,256]{0,1:T(8,128)S(1)} %copy.146, bf16[1,512,256]{1,2,0:T(8,128)(2,1)S(1)} %fusion.30, f32[256]{0:T(256)S(1)} %copy-done.13, f32[256]{0:T(256)S(1)} %bitcast.123, ...), kind=kOutput, calls=%fused_computation | convolution fusion | flops 1077149696 | bytes 8654848 | tf_op jit(solution)/shard_map/tc,ec->te/dot_general | solution.py:116
  205.4 7.8 %reshape.126 = bf16[512,8,2,256]{3,2,1,0:T(2,128)(2,1)} reshape(bf16[512,4096]{1,0:T(8,128)(2,1)} %convolution_convert_fusion) | data formatting | bytes 8388608 | tf_op jit(solution)/shard_map/reshape | solution.py:69
  213.3 2.7 copy.147
  216.0 14.7 %all_to_all.20 = bf16[512,8,2,256]{3,1,0,2:T(8,128)(2,1)} all-to-all(bf16[512,8,2,256]{3,1,0,2:T(8,128)(2,1)S(1)} %copy.147), channel_id=1, replica_groups=mesh['yh'=2,'z'=16,'cx'=8,'core'=2] {'core'}, dimensions={2} | all-to-all | bytes 8388608 | tf_op jit(solution)/shard_map/all_to_all | solution.py:70
  230.7 4.4 %reduce_sum.44 = bf16[512,8,256]{2,1,0:T(8,128)(2,1)S(1)} reduce(bf16[512,8,2,256]{3,1,0,2:T(8,128)(2,1)} %all_to_all.20, bf16[]{:T(256)} %constant.29.clone.1), dimensions={2}, to_apply=%region_2.3 | reduce | flops 1048576 | bytes 6291458 | tf_op jit(solution)/shard_map/reduce_sum | solution.py:71
  235.5 29.7 %all_to_all.21 = bf16[512,8,256]{2,0,1:T(8,128)(2,1)S(1)} all-to-all(bf16[512,8,256]{2,0,1:T(8,128)(2,1)S(1)} %copy.148), channel_id=1, replica_groups=mesh['yh'=2,'z'=16,'cx'=8,'core'=2] {'cx'}, dimensions={1} | all-to-all | bytes 4194304 | tf_op jit(solution)/shard_map/all_to_all | solution.py:72
  265.2 1.0 reduce_sum.45
  (81 shorter events, 7.3 us)
Async XLA Ops:
  6.5 84.4 %all-gather.7.cloned.1.call-start = ((), (), s32[]{:S(2)}) async-start(), calls=%async_computation.4 | async-start | bytes 4456448 | tf_op jit(solution)/shard_map/all_gather | solution.py:87
  17.7 11.8 %copy-start.5 = (bf16[256,128]{1,0:T(8,128)(2,1)S(1)}, bf16[256,128]{1,0:T(8,128)(2,1)}, u32[]{:S(2)}) copy-start(bf16[256,128]{1,0:T(8,128)(2,1)} %param.13) | copy-start | bytes 196612
  17.7 79.7 %copy-start.8 = (f32[256,16]{0,1:T(8,128)S(1)}, f32[256,16]{0,1:T(8,128)}, u32[]{:S(2)}) copy-start(f32[256,16]{0,1:T(8,128)} %param.11) | copy-start | bytes 49156
  17.7 79.8 %copy-start.1 = (f32[256,16]{0,1:T(8,128)S(1)}, f32[256,16]{0,1:T(8,128)}, u32[]{:S(2)}) copy-start(f32[256,16]{0,1:T(8,128)} %param.10) | copy-start | bytes 49156
  17.7 83.4 %all-to-all-start = ((bf16[512,16,256]{2,0,1:T(8,128)(2,1)}), bf16[512,16,256]{2,0,1:T(8,128)(2,1)}, u32[]{:S(2)}, u32[]{:S(2)}) async-start(bf16[512,16,256]{2,0,1:T(8,128)(2,1)} %broadcast_in_dim.17), calls=%async_computation | async-start | bytes 8388608 | tf_op jit(solution)/shard_map/all_to_all | solution.py:64
  29.4 74.8 %copy-start.12 = (f32[3,3,256]{2,1,0:T(4,128)S(1)}, f32[3,3,256]{2,1,0:T(4,128)}, u32[]{:S(2)}) copy-start(f32[3,3,256]{2,1,0:T(4,128)} %param.9) | copy-start | bytes 27652
  29.4 166.1 %all-gather.9.cloned.1.call-start = ((), (), s32[]{:S(2)}) async-start(), calls=%async_computation.5 | async-start | bytes 4456448 | tf_op jit(solution)/shard_map/all_gather | solution.py:87
  97.6 9.3 %copy-start.14 = (f32[64]{0:T(128)}, f32[64]{0:T(128)S(1)}, u32[]{:S(2)}) copy-start(f32[64]{0:T(128)S(1)} %iota_negate_fusion) | copy-start | bytes 772
  102.0 5.0 %collective-permute-start = (bf16[2,16,256]{2,0,1:T(2,128)(2,1)S(1)}, bf16[2,16,256]{2,0,1:T(2,128)(2,1)S(1)}, u32[]{:S(2)}, u32[]{:S(2)}) collective-permute-start(bf16[2,16,256]{2,0,1:T(2,128)(2,1)S(1)} %slice.167), channel_id=1, source_target_pairs={{0,16},{16,32},{32,48},{48,64},{64,80},{80,96},{96,112},{112,128},... | collective-permute-start | bytes 49160 | tf_op jit(solution)/shard_map/ppermute | solution.py:16
  107.0 2.8 %copy-start.3 = (bf16[2,16,256]{2,0,1:T(2,128)(2,1)}, bf16[2,16,256]{2,0,1:T(2,128)(2,1)S(1)}, u32[]{:S(2)}) copy-start(bf16[2,16,256]{2,0,1:T(2,128)(2,1)S(1)} %collective-permute-done) | copy-start | bytes 49156
  117.6 4.3 %copy-start.2 = (f32[256,16]{0,1:T(8,128)S(1)}, f32[256,16]{0,1:T(8,128)}, u32[]{:S(2)}) copy-start(f32[256,16]{0,1:T(8,128)} %get-tuple-element.17) | copy-start | bytes 49156
  117.6 4.3 %copy-start.7 = (f32[256,16]{0,1:T(8,128)S(1)}, f32[256,16]{0,1:T(8,128)}, u32[]{:S(2)}) copy-start(f32[256,16]{0,1:T(8,128)} %get-tuple-element.16) | copy-start | bytes 49156
  120.4 12.6 %copy-start.6 = (f32[256,16]{0,1:T(8,128)S(1)}, f32[256,16]{0,1:T(8,128)}, u32[]{:S(2)}) copy-start(f32[256,16]{0,1:T(8,128)} %get-tuple-element.15) | copy-start | bytes 49156
  123.0 39.5 %all-to-all-start.1 = ((f32[32,256,16]{1,2,0:T(8,128)}), f32[32,256,16]{1,2,0:T(8,128)S(1)}, u32[]{:S(2)}, u32[]{:S(2)}) async-start(f32[32,256,16]{1,2,0:T(8,128)} %broadcast_in_dim.21), calls=%async_computation.1 | async-start | bytes 1048576 | tf_op jit(solution)/shard_map/all_to_all | solution.py:21
  195.4 1.7 copy-start.4
  197.7 3.9 %copy-start = (bf16[2,2048,512]{2,1,0:T(8,128)(2,1)S(1)}, bf16[2,2048,512]{2,1,0:T(8,128)(2,1)}, u32[]{:S(2)}) copy-start(bf16[2,2048,512]{2,1,0:T(8,128)(2,1)} %all-gather.9.cloned.1.call-done) | copy-start | bytes 12582916
  197.7 3.9 %copy-start.9 = (f32[1,1,256]{2,1,0:T(1,128)S(1)}, f32[1,1,256]{2,1,0:T(1,128)}, u32[]{:S(2)}) copy-start(f32[1,1,256]{2,1,0:T(1,128)} %get-tuple-element.18) | copy-start | bytes 3076
  197.8 3.9 %copy-start.10 = (f32[1,1,256]{2,1,0:T(1,128)S(1)}, f32[1,1,256]{2,1,0:T(1,128)}, u32[]{:S(2)}) copy-start(f32[1,1,256]{2,1,0:T(1,128)} %get-tuple-element.19) | copy-start | bytes 3076
  197.8 3.9 %copy-start.11 = (f32[1,1,256]{2,1,0:T(1,128)S(1)}, f32[1,1,256]{2,1,0:T(1,128)}, u32[]{:S(2)}) copy-start(f32[1,1,256]{2,1,0:T(1,128)} %get-tuple-element.20) | copy-start | bytes 3076
  197.8 3.9 %copy-start.13 = (f32[256]{0:T(256)S(1)}, f32[256]{0:T(256)}, u32[]{:S(2)}) copy-start(f32[256]{0:T(256)} %param.12) | copy-start | bytes 3076
Sparse Core Ops, SparseCore 0:
  14.5 76.4 all-gather.6
  97.5 97.8 all-gather.8

commit v12 on v11

--- a/solution.py
+++ b/solution.py
@@ -64,13 +64,11 @@
     return lax.all_to_all(copies, CH, 1, 1)
 
 
-def scattered_terms(terms, lanes):
-    rows, total = terms.shape
-    split = terms.reshape(rows, lanes // 2, 2, total // lanes)
-    pairs = lax.all_to_all(split, "core", 2, 2)
-    pairs = jnp.sum(pairs.astype(jnp.float32), axis=2).astype(jnp.bfloat16)
-    parts = lax.all_to_all(pairs, "cx", 1, 1)
-    return jnp.sum(parts.astype(jnp.float32), axis=1).astype(jnp.bfloat16)
+def scattered_terms(terms):
+    pairs = lax.all_to_all(terms, "core", 0, 0)
+    pairs = jnp.sum(pairs.astype(jnp.float32), axis=0).astype(jnp.bfloat16)
+    parts = lax.all_to_all(pairs, "cx", 0, 0)
+    return jnp.sum(parts.astype(jnp.float32), axis=0).astype(jnp.bfloat16)
 
 
 def make_shards(count, lanes):
@@ -113,8 +111,9 @@
         starts = starts + offsets * incoming[None]
         conv = finish(inner, starts, heads, values, skip)
         hidden = (query * conv).astype(jnp.bfloat16)
-        terms = jnp.einsum("tc,ec->te", hidden, packed[:, width:], preferred_element_type=jnp.float32)
-        return scattered_terms(terms.astype(jnp.bfloat16), lanes)
+        out_w = jnp.transpose(packed[:, width:].reshape(lanes // 2, 2, -1, width), (1, 0, 2, 3))
+        terms = jnp.einsum("tc,yxec->yxte", hidden, out_w, preferred_element_type=jnp.float32)
+        return scattered_terms(terms.astype(jnp.bfloat16))
 
     return shards
 

time: 275 us -> 265 us (0.964)
  local copies, waits for them, and re-layouts: 37.4 us -> 29.3 us
    reshape x2 -> x0, local copies, waits for them, and re-layouts: 10.6 us -> none  [scattered_terms(): split = terms.reshape(rows, lanes // 2, 2, total // lanes)]
  transfers between devices with their start and end apart: 5 -> 5, of which waited for: 3 -> 3; matrix products, arithmetic and copies ran while one was open for 21% -> 22% of each run, Pallas kernels for 0% -> 0%
where the time goes in v12:
time: 265 us; the launch traced here: 263 us
  waiting for transfers between devices  93.3 us (35%)
  blocking collectives  57.8 us (22%)
  matrix products  34.6 us (13%)
  local copies, waits for them, and re-layouts  29.3 us (11%)
  starting transfers between devices  23.9 us (9%)
  between operations  13.9 us (5%)
  other arithmetic  10.6 us (4%)
    all_gather x2, waiting for transfers between devices, across_z(): part = lax.all_gather(part, 'z', axis=2)  78.9 us
    all_to_all x1, blocking collectives, scattered_terms(): parts = lax.all_to_all(pairs, 'cx', 0, 0)  29.8 us
    all_to_all x1, blocking collectives, scattered_terms(): pairs = lax.all_to_all(terms, 'core', 0, 0)  14.7 us
    all_to_all x1, waiting for transfers between devices, carried_in(): every = lax.all_to_all(copies, CTX, 0, 0)  14.3 us
    all_gather x2, blocking collectives, across_yh(): return lax.all_gather(part, 'yh', axis=1)  13.3 us
    all_to_all x1, starting transfers between devices, gathered_tokens(): return lax.all_to_all(copies, CH, 1, 1)  11.7 us
    dot_general x2, matrix products, shortened(): jnp.einsum('tkd,jkdc->jtc', whole, weight, preferred_element_type=jnp.flo...  9.98 us
    all_to_all x1, starting transfers between devices, carried_in(): every = lax.all_to_all(copies, CTX, 0, 0)  9.95 us
  transfers between devices with their start and end apart: 5, of which 3 were waited for; matrix products, arithmetic and copies ran while one was open for 22% of the time, Pallas kernels for 0%

profile of v12, /device:TPU:1, one launch (start us, length us, event | category | flops | bytes accessed | tf_op | source)
XLA Modules:
  0.0 263.4 jit_solution(311783215825935850)
XLA Ops:
  6.5 0.9 slice.129
  7.5 6.9 %all-gather = bf16[2,256,256]{2,1,0:T(8,128)(2,1)} all-gather(bf16[2,128,256]{2,1,0:T(8,128)(2,1)S(1)} %slice.129), channel_id=2, replica_groups=mesh['yh'=2,'z'=16,'cx'=8,'core'=2] {'yh'}, dimensions={1}, use_global_device_ids=true | all-gather | bytes 393216 | tf_op jit(solution)/shard_map/all_gather | solution.py:82
  14.3 3.3 %broadcast_in_dim.17 = bf16[512,16,256]{2,0,1:T(8,128)(2,1)} broadcast(bf16[512,256]{1,0:T(8,128)(2,1)} %param.7), dimensions={0,2} | broadcast | bytes 4456448 | tf_op jit(solution)/shard_map/broadcast_in_dim | solution.py:63
  17.7 11.7 %all-to-all-start = ((bf16[512,16,256]{2,0,1:T(8,128)(2,1)}), bf16[512,16,256]{2,0,1:T(8,128)(2,1)}, u32[]{:S(2)}, u32[]{:S(2)}) async-start(bf16[512,16,256]{2,0,1:T(8,128)(2,1)} %broadcast_in_dim.17), calls=%async_computation | async-start | bytes 8388608 | tf_op jit(solution)/shard_map/all_to_all | solution.py:64
  30.4 60.5 %all-gather.7.cloned.1.call-done = bf16[2,2,2048,256]{3,2,1,0:T(8,128)(2,1)} async-done(((bf16[2,2,128,256]{3,2,1,0:T(8,128)(2,1)}), bf16[2,2,2048,256]{3,2,1,0:T(8,128)(2,1)}) %all-gather.7.cloned.1.call-update) | async-done | bytes 4194320 | tf_op jit(solution)/shard_map/all_gather | solution.py:85
  90.9 6.5 %all-gather.2 = bf16[2,128,512]{2,1,0:T(8,128)(2,1)} all-gather(bf16[1,128,512]{2,1,0:T(8,128)(2,1)S(1)} %maximum_bitcast_fusion), channel_id=4, replica_groups=mesh['yh'=2,'z'=16,'cx'=8,'core'=2] {'yh'}, dimensions={0}, use_global_device_ids=true | all-gather | bytes 393216 | tf_op jit(solution)/shard_map/all_gather | solution.py:82
  98.3 2.8 %multiply_reduce_fusion = (f32[64,256]{0,1:T(8,128)S(1)}, f32[64,256,16]{0,2,1:T(8,128)}) fusion(f32[256,16]{1,0:T(8,128)S(1)} %copy.144, f32[64]{0:T(128)S(1)} %iota_negate_fusion, f32[256,16]{1,0:T(8,128)S(1)} %copy.143), kind=kLoop, calls=%fused_computation.11 | loop fusion | flops 770048 | bytes 1147136 | tf_op jit(solution)/shard_map/reduce_sum | solution.py:35
  101.1 0.9 slice.168
  102.0 2.2 collective-permute-start
  104.2 2.7 %rev.3 = f32[64,256,16]{0,2,1:T(8,128)S(1)} reverse(f32[64,256,16]{0,2,1:T(8,128)} %get-tuple-element.12), dimensions={0} | reverse | bytes 2097152 | tf_op jit(solution)/shard_map/rev | solution.py:41
  107.0 2.8 %fusion.21 = bf16[2,2,256]{2,1,0:T(2,128)(2,1)S(1)} fusion(bf16[2,16,256,256]{3,2,1,0:T(8,128)(2,1)} %bitcast.124, bf16[2,16,256]{2,0,1:T(2,128)(2,1)S(1)} %collective-permute-done), kind=kOutput, calls=%fused_computation.22 | convolution fusion | flops 8389632 | bytes 4212736 | tf_op jit(solution)/shard_map/tkd,jkdc->jtc/dot_general | solution.py:91
  110.0 5.9 %fusion.15 = bf16[2,512,256]{1,2,0:T(8,128)(2,1)S(1)} fusion(bf16[2,16,256,256]{3,2,1,0:T(8,128)(2,1)} %bitcast.125, bf16[512,16,256]{2,0,1:T(8,128)(2,1)} %all-to-all-done), kind=kOutput, calls=%fused_computation.16 | convolution fusion | flops 2147745792 | bytes 8912896 | tf_op jit(solution)/shard_map/tkd,jkdc->jtc/dot_general | solution.py:90
  116.2 0.9 fusion.24
  117.6 2.7 %fusion.54 = f32[256,8,16]{2,1,0:T(8,128)} fusion(bf16[8,64,256]{1,0,2:T(8,128)(2,1)S(1)} %copy.146, f32[64,256,16]{0,2,1:T(8,128)S(1)} %rev.3), kind=kOutput, calls=%fused_computation.91 | convolution fusion | flops 25165824 | bytes 1441792 | tf_op jit(solution)/shard_map/jcm,bjc->bcm/dot_general | solution.py:45
  120.4 1.5 copy.149
  122.2 0.9 broadcast_in_dim.21
  123.0 9.9 %all-to-all-start.1 = ((f32[32,256,16]{1,2,0:T(8,128)}), f32[32,256,16]{1,2,0:T(8,128)S(1)}, u32[]{:S(2)}, u32[]{:S(2)}) async-start(f32[32,256,16]{1,2,0:T(8,128)} %broadcast_in_dim.21), calls=%async_computation.1 | async-start | bytes 1048576 | tf_op jit(solution)/shard_map/all_to_all | solution.py:21
  133.8 3.8 %fusion.6 = f32[64,64,256]{2,1,0:T(8,128)} fusion(s32[64,64]{1,0:T(8,128)S(1)} %iota_subtract_fusion, f32[64,256]{0,1:T(8,128)S(1)} %get-tuple-element.11), kind=kOutput, calls=%fused_computation.9 | convolution fusion | flops 805568512 | bytes 4276224 | tf_op jit(solution)/shard_map/dot_general | solution.py:40
  137.5 9.2 %copy.147 = f32[64,64,256]{1,0,2:T(8,128)} copy(f32[64,64,256]{2,1,0:T(8,128)} %fusion.6) | data formatting | bytes 8388608 | tf_op jit(solution)/shard_map/dot_general | solution.py:40
  146.7 1.3 fusion.53
  148.2 14.3 %all-to-all-done.1 = f32[32,256,16]{1,2,0:T(8,128)S(1)} async-done(((f32[32,256,16]{1,2,0:T(8,128)}), f32[32,256,16]{1,2,0:T(8,128)S(1)}, u32[]{:S(2)}, u32[]{:S(2)}) %all-to-all-start.1) | async-done | bytes 524320 | tf_op jit(solution)/shard_map/all_to_all | solution.py:21
  163.2 4.1 %fusion.4 = f32[256,8,64]{2,1,0:T(8,128)S(1)} fusion(f32[8,256,16]{2,0,1:T(8,128)S(1)} %copy.151, f32[256,16]{1,0:T(8,128)} %copy.150, f32[256,16]{1,0:T(8,128)S(1)} %copy.144, f32[64]{0:T(128)} %copy-done.14, f32[256,16]{1,0:T(8,128)S(1)} %copy.143), kind=kOutput, calls=%fused_computation.5 | convolution fusion | flops 25952256 | bytes 704768 | tf_op jit(solution)/shard_map/icm,bcm->bic/dot_general | solution.py:58
  167.3 9.2 %fusion.11 = f32[8,64,256]{1,0,2:T(8,128)S(1)} fusion(f32[256,8,64]{2,1,0:T(8,128)S(1)} %fusion.4, bf16[8,64,256]{1,0,2:T(8,128)(2,1)S(1)} %copy.146, f32[64,64,256]{1,0,2:T(8,128)} %copy.147), kind=kOutput, calls=%fused_computation.14 | convolution fusion | flops 100794368 | bytes 5505024 | tf_op jit(solution)/shard_map/ijc,bjc->bic/dot_general | solution.py:44
  177.0 18.4 %all-gather.9.cloned.1.call-done = bf16[2,2048,512]{2,1,0:T(8,128)(2,1)} async-done(((bf16[2,128,512]{2,1,0:T(8,128)(2,1)}), bf16[2,2048,512]{2,1,0:T(8,128)(2,1)}) %all-gather.9.cloned.1.call-update) | async-done | bytes 4194320 | tf_op jit(solution)/shard_map/all_gather | solution.py:85
  195.4 2.5 fusion.50
  197.9 1.3 copy-done
  199.8 4.1 %fusion.19 = bf16[1,512,256]{1,2,0:T(8,128)(2,1)S(1)} fusion(bf16[16,256,256]{2,1,0:T(8,128)(2,1)} %bitcast.122, bf16[512,16,256]{2,0,1:T(8,128)(2,1)} %all-to-all-done), kind=kOutput, calls=%fused_computation.19 | convolution fusion | flops 1073872896 | bytes 6553600 | tf_op jit(solution)/shard_map/tkd,jkdc->jtc/dot_general | solution.py:90
  204.2 1.7 convert_bitcast_fusion
  205.9 14.7 %all_to_all.20 = bf16[2,8,512,256]{2,3,1,0:T(8,128)(2,1)} all-to-all(bf16[2,8,512,256]{2,3,1,0:T(8,128)(2,1)S(1)} %convert_bitcast_fusion), channel_id=1, replica_groups=mesh['yh'=2,'z'=16,'cx'=8,'core'=2] {'core'}, dimensions={0} | all-to-all | bytes 8388608 | tf_op jit(solution)/shard_map/all_to_all | solution.py:68
  220.6 3.3 %reduce_sum.44 = bf16[8,512,256]{1,2,0:T(8,128)(2,1)S(1)} reduce(bf16[2,8,512,256]{2,3,1,0:T(8,128)(2,1)} %all_to_all.20, bf16[]{:T(256)} %constant.29.clone.1), dimensions={0}, to_apply=%region_2.3 | reduce | flops 1048576 | bytes 6291458 | tf_op jit(solution)/shard_map/reduce_sum | solution.py:69
  223.9 29.8 %all_to_all.21 = bf16[8,512,256]{1,2,0:T(8,128)(2,1)} all-to-all(bf16[8,512,256]{1,2,0:T(8,128)(2,1)S(1)} %reduce_sum.44), channel_id=1, replica_groups=mesh['yh'=2,'z'=16,'cx'=8,'core'=2] {'cx'}, dimensions={0} | all-to-all | bytes 4194304 | tf_op jit(solution)/shard_map/all_to_all | solution.py:70
  253.7 2.0 reduce_sum.45
  (79 shorter events, 6.8 us)
Async XLA Ops:
  6.5 84.4 %all-gather.7.cloned.1.call-start = ((), (), s32[]{:S(2)}) async-start(), calls=%async_computation.4 | async-start | bytes 4456448 | tf_op jit(solution)/shard_map/all_gather | solution.py:85
  17.7 11.7 %copy-start.5 = (bf16[256,128]{1,0:T(8,128)(2,1)S(1)}, bf16[256,128]{1,0:T(8,128)(2,1)}, u32[]{:S(2)}) copy-start(bf16[256,128]{1,0:T(8,128)(2,1)} %param.13) | copy-start | bytes 196612
  17.7 79.7 %copy-start.1 = (f32[256,16]{0,1:T(8,128)S(1)}, f32[256,16]{0,1:T(8,128)}, u32[]{:S(2)}) copy-start(f32[256,16]{0,1:T(8,128)} %param.10) | copy-start | bytes 49156
  17.7 79.8 %copy-start.8 = (f32[256,16]{0,1:T(8,128)S(1)}, f32[256,16]{0,1:T(8,128)}, u32[]{:S(2)}) copy-start(f32[256,16]{0,1:T(8,128)} %param.11) | copy-start | bytes 49156
  17.7 83.4 %all-to-all-start = ((bf16[512,16,256]{2,0,1:T(8,128)(2,1)}), bf16[512,16,256]{2,0,1:T(8,128)(2,1)}, u32[]{:S(2)}, u32[]{:S(2)}) async-start(bf16[512,16,256]{2,0,1:T(8,128)(2,1)} %broadcast_in_dim.17), calls=%async_computation | async-start | bytes 8388608 | tf_op jit(solution)/shard_map/all_to_all | solution.py:64
  29.4 74.8 %copy-start.9 = (f32[3,3,256]{2,1,0:T(4,128)S(1)}, f32[3,3,256]{2,1,0:T(4,128)}, u32[]{:S(2)}) copy-start(f32[3,3,256]{2,1,0:T(4,128)} %param.9) | copy-start | bytes 27652
  29.4 166.0 %all-gather.9.cloned.1.call-start = ((), (), s32[]{:S(2)}) async-start(), calls=%async_computation.5 | async-start | bytes 4456448 | tf_op jit(solution)/shard_map/all_gather | solution.py:85
  97.6 9.3 %copy-start.14 = (f32[64]{0:T(128)}, f32[64]{0:T(128)S(1)}, u32[]{:S(2)}) copy-start(f32[64]{0:T(128)S(1)} %iota_negate_fusion) | copy-start | bytes 772
  102.0 5.0 %collective-permute-start = (bf16[2,16,256]{2,0,1:T(2,128)(2,1)S(1)}, bf16[2,16,256]{2,0,1:T(2,128)(2,1)S(1)}, u32[]{:S(2)}, u32[]{:S(2)}) collective-permute-start(bf16[2,16,256]{2,0,1:T(2,128)(2,1)S(1)} %slice.168), channel_id=1, source_target_pairs={{0,16},{16,32},{32,48},{48,64},{64,80},{80,96},{96,112},{112,128},... | collective-permute-start | bytes 49160 | tf_op jit(solution)/shard_map/ppermute | solution.py:16
  107.0 2.8 %copy-start.3 = (bf16[2,16,256]{2,0,1:T(2,128)(2,1)}, bf16[2,16,256]{2,0,1:T(2,128)(2,1)S(1)}, u32[]{:S(2)}) copy-start(bf16[2,16,256]{2,0,1:T(2,128)(2,1)S(1)} %collective-permute-done) | copy-start | bytes 49156
  117.6 4.3 %copy-start.2 = (f32[256,16]{0,1:T(8,128)S(1)}, f32[256,16]{0,1:T(8,128)}, u32[]{:S(2)}) copy-start(f32[256,16]{0,1:T(8,128)} %get-tuple-element.19) | copy-start | bytes 49156
  117.6 4.3 %copy-start.7 = (f32[256,16]{0,1:T(8,128)S(1)}, f32[256,16]{0,1:T(8,128)}, u32[]{:S(2)}) copy-start(f32[256,16]{0,1:T(8,128)} %get-tuple-element.18) | copy-start | bytes 49156
  120.4 12.6 %copy-start.6 = (f32[256,16]{0,1:T(8,128)S(1)}, f32[256,16]{0,1:T(8,128)}, u32[]{:S(2)}) copy-start(f32[256,16]{0,1:T(8,128)} %get-tuple-element.17) | copy-start | bytes 49156
  123.0 39.5 %all-to-all-start.1 = ((f32[32,256,16]{1,2,0:T(8,128)}), f32[32,256,16]{1,2,0:T(8,128)S(1)}, u32[]{:S(2)}, u32[]{:S(2)}) async-start(f32[32,256,16]{1,2,0:T(8,128)} %broadcast_in_dim.21), calls=%async_computation.1 | async-start | bytes 1048576 | tf_op jit(solution)/shard_map/all_to_all | solution.py:21
  195.4 3.8 %copy-start.4 = (bf16[2,16,256]{2,0,1:T(2,128)(2,1)S(1)}, bf16[2,16,256]{2,0,1:T(2,128)(2,1)}, u32[]{:S(2)}) copy-start(bf16[2,16,256]{2,0,1:T(2,128)(2,1)} %copy-done.3) | copy-start | bytes 49156
  197.9 1.3 copy-start
  199.8 4.3 %copy-start.10 = (f32[1,1,256]{2,1,0:T(1,128)S(1)}, f32[1,1,256]{2,1,0:T(1,128)}, u32[]{:S(2)}) copy-start(f32[1,1,256]{2,1,0:T(1,128)} %get-tuple-element.20) | copy-start | bytes 3076
  199.8 4.3 %copy-start.11 = (f32[1,1,256]{2,1,0:T(1,128)S(1)}, f32[1,1,256]{2,1,0:T(1,128)}, u32[]{:S(2)}) copy-start(f32[1,1,256]{2,1,0:T(1,128)} %get-tuple-element.21) | copy-start | bytes 3076
  199.8 4.3 %copy-start.12 = (f32[1,1,256]{2,1,0:T(1,128)S(1)}, f32[1,1,256]{2,1,0:T(1,128)}, u32[]{:S(2)}) copy-start(f32[1,1,256]{2,1,0:T(1,128)} %get-tuple-element.22) | copy-start | bytes 3076
  199.8 4.3 %copy-start.13 = (f32[256]{0:T(256)S(1)}, f32[256]{0:T(256)}, u32[]{:S(2)}) copy-start(f32[256]{0:T(256)} %param.12) | copy-start | bytes 3076
Sparse Core Ops, SparseCore 0:
  14.5 76.4 all-gather.6
  97.5 97.8 all-gather.8

commit v13 on v12

--- a/solution.py
+++ b/solution.py
@@ -98,12 +98,13 @@
                 feats = feats + taps[i][:, None, :] * widened[:, SHORT - 1 - i : SHORT - 1 - i + rows, :]
             return feats
 
-        pair = across_z(across_yh(in_weight[1:]))
-        packed = jnp.concatenate([in_weight[0], out_weight.T], axis=1)[None]
-        packed, pair = lax.optimization_barrier((packed, pair))
-        feats = filtered(shortened(pair), short_taps[:, 1:])
+        streams = across_z(across_yh(in_weight))
+        packed = out_weight.T[None]
+        packed, streams = lax.optimization_barrier((packed, streams))
+        feats = filtered(shortened(streams), short_taps)
         packed = across_z(across_yh(packed))[0]
-        query = filtered(shortened(packed[None, :, :width]), short_taps[:, :1])[0]
+        query = feats[0]
+        feats = feats[1:]
         gated = (feats[0] * feats[1]).astype(jnp.bfloat16)
         values = gated.astype(jnp.float32)
         inner, starts, final, heads, offsets = block_terms(values, rates, residues)
@@ -111,7 +112,7 @@
         starts = starts + offsets * incoming[None]
         conv = finish(inner, starts, heads, values, skip)
         hidden = (query * conv).astype(jnp.bfloat16)
-        out_w = jnp.transpose(packed[:, width:].reshape(lanes // 2, 2, -1, width), (1, 0, 2, 3))
+        out_w = jnp.transpose(packed.reshape(lanes // 2, 2, -1, width), (1, 0, 2, 3))
         terms = jnp.einsum("tc,yxec->yxte", hidden, out_w, preferred_element_type=jnp.float32)
         return scattered_terms(terms.astype(jnp.bfloat16))
 

time: 265 us -> 271 us (1.023)
  waiting for transfers between devices: 93.3 us -> 104 us
  local copies, waits for them, and re-layouts: 29.3 us -> 24.1 us
    all_to_all x1, waiting for transfers between devices: 0.01 us -> 49 us  [gathered_tokens(): return lax.all_to_all(copies, CH, 1, 1)]
    all_gather x2, waiting for transfers between devices: 78.9 us -> 35.2 us  [across_z(): part = lax.all_gather(part, 'z', axis=2)]
    all_to_all x1, waiting for transfers between devices: 14.3 us -> 19.4 us  [carried_in(): every = lax.all_to_all(copies, CTX, 0, 0)]
    slice x3 -> x0, local copies, waits for them, and re-layouts: 4.72 us -> none  [the longest x1 2.51 us: shards(): query = filtered(shortened(packed[None, :, :width]), short_taps[:, :1])[0]]
    dot_general x2 -> x1, matrix products: 9.98 us -> 7.47 us  [shortened(): jnp.einsum('tkd,jkdc->jtc', whole, weight, preferred_element_type=jnp.flo...]
  transfers between devices with their start and end apart: 5 -> 5, of which waited for: 3 -> 4; matrix products, arithmetic and copies ran while one was open for 22% -> 15% of each run, Pallas kernels for 0% -> 0%
where the time goes in v13:
time: 271 us; the launch traced here: 270 us
  waiting for transfers between devices  104 us (38%)
  blocking collectives  60.3 us (22%)
  matrix products  33.8 us (12%)
  local copies, waits for them, and re-layouts  24.1 us (9%)
  starting transfers between devices  23.8 us (9%)
  between operations  13.8 us (5%)
  other arithmetic  11 us (4%)
    all_to_all x1, waiting for transfers between devices, gathered_tokens(): return lax.all_to_all(copies, CH, 1, 1)  49 us
    all_gather x2, waiting for transfers between devices, across_z(): part = lax.all_gather(part, 'z', axis=2)  35.2 us
    all_to_all x1, blocking collectives, scattered_terms(): parts = lax.all_to_all(pairs, 'cx', 0, 0)  30.3 us
    all_to_all x1, waiting for transfers between devices, carried_in(): every = lax.all_to_all(copies, CTX, 0, 0)  19.4 us
    all_to_all x1, blocking collectives, scattered_terms(): pairs = lax.all_to_all(terms, 'core', 0, 0)  15.2 us
    all_gather x2, blocking collectives, across_yh(): return lax.all_gather(part, 'yh', axis=1)  14.8 us
    all_to_all x1, starting transfers between devices, carried_in(): every = lax.all_to_all(copies, CTX, 0, 0)  12.4 us
    all_to_all x1, starting transfers between devices, gathered_tokens(): return lax.all_to_all(copies, CH, 1, 1)  10.1 us
  transfers between devices with their start and end apart: 5, of which 4 were waited for; matrix products, arithmetic and copies ran while one was open for 15% of the time, Pallas kernels for 0%

profile of v13, /device:TPU:1, one launch (start us, length us, event | category | flops | bytes accessed | tf_op | source)
XLA Modules:
  0.0 270.3 jit_solution(6929077624485846843)
XLA Ops:
  6.5 9.4 %all-gather = bf16[3,256,256]{2,1,0:T(8,128)(2,1)} all-gather(bf16[3,128,256]{2,1,0:T(8,128)(2,1)} %param.8), channel_id=2, replica_groups=mesh['yh'=2,'z'=16,'cx'=8,'core'=2] {'yh'}, dimensions={1}, use_global_device_ids=true | all-gather | bytes 589824 | tf_op jit(solution)/shard_map/all_gather | solution.py:82
  15.9 3.4 %broadcast_in_dim.17 = bf16[512,16,256]{2,0,1:T(8,128)(2,1)} broadcast(bf16[512,256]{1,0:T(8,128)(2,1)} %param.7), dimensions={0,2} | broadcast | bytes 4456448 | tf_op jit(solution)/shard_map/broadcast_in_dim | solution.py:63
  19.3 10.1 %all-to-all-start = ((bf16[512,16,256]{2,0,1:T(8,128)(2,1)}), bf16[512,16,256]{2,0,1:T(8,128)(2,1)}, u32[]{:S(2)}, u32[]{:S(2)}) async-start(bf16[512,16,256]{2,0,1:T(8,128)(2,1)} %broadcast_in_dim.17), calls=%async_computation | async-start | bytes 8388608 | tf_op jit(solution)/shard_map/all_to_all | solution.py:64
  30.3 2.8 %multiply_reduce_fusion = (f32[64,256]{0,1:T(8,128)S(1)}, f32[64,256,16]{0,2,1:T(8,128)}) fusion(f32[256,16]{1,0:T(8,128)S(1)} %copy.131, f32[64]{0:T(128)S(1)} %iota_negate_fusion, f32[256,16]{1,0:T(8,128)S(1)} %copy.130), kind=kLoop, calls=%fused_computation.11 | loop fusion | flops 770048 | bytes 1147136 | tf_op jit(solution)/shard_map/reduce_sum | solution.py:35
  33.1 49.0 %all-to-all-done = bf16[512,16,256]{2,0,1:T(8,128)(2,1)} async-done(((bf16[512,16,256]{2,0,1:T(8,128)(2,1)}), bf16[512,16,256]{2,0,1:T(8,128)(2,1)}, u32[]{:S(2)}, u32[]{:S(2)}) %all-to-all-start) | async-done | bytes 4194336 | tf_op jit(solution)/shard_map/all_to_all | solution.py:64
  82.2 0.9 slice.125
  83.0 1.3 collective-permute-start
  84.4 0.7 copy.125
  85.1 2.7 %rev.3 = f32[64,256,16]{0,2,1:T(8,128)S(1)} reverse(f32[64,256,16]{0,2,1:T(8,128)} %get-tuple-element.10), dimensions={0} | reverse | bytes 2097152 | tf_op jit(solution)/shard_map/rev | solution.py:41
  87.9 17.6 %all-gather.7.cloned.1.call-done = bf16[3,2,2048,256]{3,2,1,0:T(8,128)(2,1)} async-done(((bf16[3,2,128,256]{3,2,1,0:T(8,128)(2,1)}), bf16[3,2,2048,256]{3,2,1,0:T(8,128)(2,1)}) %all-gather.7.cloned.1.call-update) | async-done | bytes 6291472 | tf_op jit(solution)/shard_map/all_gather | solution.py:85
  105.5 3.7 %fusion.17 = bf16[3,2,256]{2,1,0:T(2,128)(2,1)S(1)} fusion(bf16[3,16,256,256]{3,2,1,0:T(8,128)(2,1)} %bitcast.85, bf16[2,16,256]{2,0,1:T(2,128)(2,1)S(1)} %collective-permute-done), kind=kOutput, calls=%fused_computation.23 | convolution fusion | flops 12584448 | bytes 6310912 | tf_op jit(solution)/shard_map/tkd,jkdc->jtc/dot_general | solution.py:91
  109.4 7.5 %fusion.13 = bf16[3,512,256]{1,2,0:T(8,128)(2,1)S(1)} fusion(bf16[3,16,256,256]{3,2,1,0:T(8,128)(2,1)} %bitcast.86, bf16[512,16,256]{2,0,1:T(8,128)(2,1)} %all-to-all-done), kind=kOutput, calls=%fused_computation.20 | convolution fusion | flops 3221618688 | bytes 11272192 | tf_op jit(solution)/shard_map/tkd,jkdc->jtc/dot_general | solution.py:90
  117.3 1.4 fusion.8
  118.6 1.2 copy-done
  120.4 2.7 %fusion.40 = f32[256,8,16]{2,1,0:T(8,128)} fusion(bf16[8,64,256]{1,0,2:T(8,128)(2,1)S(1)} %copy.133, f32[64,256,16]{0,2,1:T(8,128)S(1)} %rev.3), kind=kOutput, calls=%fused_computation.73 | convolution fusion | flops 25165824 | bytes 1441792 | tf_op jit(solution)/shard_map/jcm,bjc->bcm/dot_general | solution.py:45
  123.1 1.5 copy.136
  124.6 5.4 %all-gather.2 = bf16[2,128,256]{2,1,0:T(8,128)(2,1)} all-gather(bf16[1,128,256]{2,1,0:T(8,128)(2,1)S(1)} %bitcast.94), channel_id=4, replica_groups=mesh['yh'=2,'z'=16,'cx'=8,'core'=2] {'yh'}, dimensions={0}, use_global_device_ids=true | all-gather | bytes 196608 | tf_op jit(solution)/shard_map/all_gather | solution.py:82
  130.3 0.9 broadcast_in_dim.21
  131.2 12.4 %all-to-all-start.1 = ((f32[32,256,16]{1,2,0:T(8,128)}), f32[32,256,16]{1,2,0:T(8,128)S(1)}, u32[]{:S(2)}, u32[]{:S(2)}) async-start(f32[32,256,16]{1,2,0:T(8,128)} %broadcast_in_dim.21), calls=%async_computation.1 | async-start | bytes 1048576 | tf_op jit(solution)/shard_map/all_to_all | solution.py:21
  143.6 0.8 copy.137
  144.3 3.8 %fusion.6 = f32[64,64,256]{2,1,0:T(8,128)} fusion(s32[64,64]{1,0:T(8,128)S(1)} %iota_subtract_fusion, f32[64,256]{0,1:T(8,128)S(1)} %get-tuple-element.9), kind=kOutput, calls=%fused_computation.9 | convolution fusion | flops 805568512 | bytes 4276224 | tf_op jit(solution)/shard_map/dot_general | solution.py:40
  148.1 9.2 %copy.134 = f32[64,64,256]{1,0,2:T(8,128)} copy(f32[64,64,256]{2,1,0:T(8,128)} %fusion.6) | data formatting | bytes 8388608 | tf_op jit(solution)/shard_map/dot_general | solution.py:40
  157.5 19.4 %all-to-all-done.1 = f32[32,256,16]{1,2,0:T(8,128)S(1)} async-done(((f32[32,256,16]{1,2,0:T(8,128)}), f32[32,256,16]{1,2,0:T(8,128)S(1)}, u32[]{:S(2)}, u32[]{:S(2)}) %all-to-all-start.1) | async-done | bytes 524320 | tf_op jit(solution)/shard_map/all_to_all | solution.py:21
  177.6 4.1 %fusion.4 = f32[256,8,64]{2,1,0:T(8,128)S(1)} fusion(f32[8,256,16]{2,0,1:T(8,128)S(1)} %copy.138, f32[256,16]{1,0:T(8,128)} %copy.137, f32[256,16]{1,0:T(8,128)S(1)} %copy.131, f32[64]{0:T(128)} %copy-done.10, f32[256,16]{1,0:T(8,128)S(1)} %copy.130), kind=kOutput, calls=%fused_computation.5 | convolution fusion | flops 25952256 | bytes 704768 | tf_op jit(solution)/shard_map/icm,bcm->bic/dot_general | solution.py:58
  181.6 8.9 %fusion.12 = f32[8,64,256]{1,0,2:T(8,128)S(1)} fusion(f32[256,8,64]{2,1,0:T(8,128)S(1)} %fusion.4, bf16[8,64,256]{1,0,2:T(8,128)(2,1)S(1)} %copy.133, f32[64,64,256]{1,0,2:T(8,128)} %copy.134), kind=kOutput, calls=%fused_computation.19 | convolution fusion | flops 100794368 | bytes 5505024 | tf_op jit(solution)/shard_map/ijc,bjc->bic/dot_general | solution.py:44
  191.2 17.6 %all-gather.9.cloned.1.call-done = bf16[2,2048,256]{2,1,0:T(8,128)(2,1)} async-done(((bf16[2,128,256]{2,1,0:T(8,128)(2,1)}), bf16[2,2048,256]{2,1,0:T(8,128)(2,1)}) %all-gather.9.cloned.1.call-update) | async-done | bytes 2097168 | tf_op jit(solution)/shard_map/all_gather | solution.py:85
  208.8 3.0 %convert_bitcast_fusion = bf16[2,8,512,256]{2,3,1,0:T(8,128)(2,1)S(1)} fusion(bf16[8,2,256,256]{3,2,1,0:T(8,128)(2,1)} %bitcast.88, f32[512,256]{0,1:T(8,128)S(1)} %copy.140, f32[3,512,256]{1,2,0:T(8,128)} %copy-done, bf16[1,512,256]{1,2,0:T(8,128)(2,1)S(1)} %fusion.23, f32[256]{0:T(256)S(1)} %copy-done.9), kind=kOutput, calls=%fused_computation.2 | convolution fusion | flops 1076494336 | bytes 7603200 | tf_op jit(solution)/shard_map/tc,yxec->yxte/dot_general | solution.py:116
  211.9 15.2 %all_to_all.20 = bf16[2,8,512,256]{2,3,1,0:T(8,128)(2,1)} all-to-all(bf16[2,8,512,256]{2,3,1,0:T(8,128)(2,1)S(1)} %convert_bitcast_fusion), channel_id=1, replica_groups=mesh['yh'=2,'z'=16,'cx'=8,'core'=2] {'core'}, dimensions={0} | all-to-all | bytes 8388608 | tf_op jit(solution)/shard_map/all_to_all | solution.py:68
  227.1 3.3 %reduce_sum.44 = bf16[8,512,256]{1,2,0:T(8,128)(2,1)S(1)} reduce(bf16[2,8,512,256]{2,3,1,0:T(8,128)(2,1)} %all_to_all.20, bf16[]{:T(256)} %constant.29.clone.1), dimensions={0}, to_apply=%region_2.3 | reduce | flops 1048576 | bytes 6291458 | tf_op jit(solution)/shard_map/reduce_sum | solution.py:69
  230.4 30.3 %all_to_all.21 = bf16[8,512,256]{1,2,0:T(8,128)(2,1)} all-to-all(bf16[8,512,256]{1,2,0:T(8,128)(2,1)S(1)} %reduce_sum.44), channel_id=1, replica_groups=mesh['yh'=2,'z'=16,'cx'=8,'core'=2] {'cx'}, dimensions={0} | all-to-all | bytes 4194304 | tf_op jit(solution)/shard_map/all_to_all | solution.py:70
  260.7 2.0 reduce_sum.45
  262.7 0.8 copy.142
  (62 shorter events, 3.6 us)
Async XLA Ops:
  6.5 98.9 %all-gather.7.cloned.1.call-start = ((), (), s32[]{:S(2)}) async-start(), calls=%async_computation.4 | async-start | bytes 6684672 | tf_op jit(solution)/shard_map/all_gather | solution.py:85
  19.3 10.2 %copy-start.7 = (f32[256,16]{0,1:T(8,128)S(1)}, f32[256,16]{0,1:T(8,128)}, u32[]{:S(2)}) copy-start(f32[256,16]{0,1:T(8,128)} %param.11) | copy-start | bytes 49156
  19.3 10.3 %copy-start.1 = (f32[256,16]{0,1:T(8,128)S(1)}, f32[256,16]{0,1:T(8,128)}, u32[]{:S(2)}) copy-start(f32[256,16]{0,1:T(8,128)} %param.10) | copy-start | bytes 49156
  19.3 62.8 %all-to-all-start = ((bf16[512,16,256]{2,0,1:T(8,128)(2,1)}), bf16[512,16,256]{2,0,1:T(8,128)(2,1)}, u32[]{:S(2)}, u32[]{:S(2)}) async-start(bf16[512,16,256]{2,0,1:T(8,128)(2,1)} %broadcast_in_dim.17), calls=%async_computation | async-start | bytes 8388608 | tf_op jit(solution)/shard_map/all_to_all | solution.py:64
  29.4 54.9 %copy-start.8 = (f32[3,3,256]{2,1,0:T(4,128)S(1)}, f32[3,3,256]{2,1,0:T(4,128)}, u32[]{:S(2)}) copy-start(f32[3,3,256]{2,1,0:T(4,128)} %param.9) | copy-start | bytes 27652
  29.4 54.9 %copy-start.4 = (bf16[256,128]{1,0:T(8,128)(2,1)S(1)}, bf16[256,128]{1,0:T(8,128)(2,1)}, u32[]{:S(2)}) copy-start(bf16[256,128]{1,0:T(8,128)(2,1)} %param.13) | copy-start | bytes 196612
  29.4 179.4 %all-gather.9.cloned.1.call-start = ((), (), s32[]{:S(2)}) async-start(), calls=%async_computation.5 | async-start | bytes 2228224 | tf_op jit(solution)/shard_map/all_gather | solution.py:85
  29.7 58.1 %copy-start.10 = (f32[64]{0:T(128)}, f32[64]{0:T(128)S(1)}, u32[]{:S(2)}) copy-start(f32[64]{0:T(128)S(1)} %iota_negate_fusion) | copy-start | bytes 772
  83.0 22.4 %collective-permute-start = (bf16[2,16,256]{2,0,1:T(2,128)(2,1)S(1)}, bf16[2,16,256]{2,0,1:T(2,128)(2,1)S(1)}, u32[]{:S(2)}, u32[]{:S(2)}) collective-permute-start(bf16[2,16,256]{2,0,1:T(2,128)(2,1)S(1)} %slice.125), channel_id=1, source_target_pairs={{0,16},{16,32},{32,48},{48,64},{64,80},{80,96},{96,112},{112,128},... | collective-permute-start | bytes 49160 | tf_op jit(solution)/shard_map/ppermute | solution.py:16
  118.6 1.2 copy-start
  120.3 4.3 %copy-start.2 = (bf16[256,128]{0,1:T(8,128)(2,1)S(1)}, bf16[256,128]{0,1:T(8,128)(2,1)}, u32[]{:S(2)}) copy-start(bf16[256,128]{0,1:T(8,128)(2,1)} %copy.125) | copy-start | bytes 196612
  120.3 9.7 %copy-start.3 = (f32[256,16]{0,1:T(8,128)S(1)}, f32[256,16]{0,1:T(8,128)}, u32[]{:S(2)}) copy-start(f32[256,16]{0,1:T(8,128)} %get-tuple-element.17) | copy-start | bytes 49156
  120.3 9.7 %copy-start.6 = (f32[256,16]{0,1:T(8,128)S(1)}, f32[256,16]{0,1:T(8,128)}, u32[]{:S(2)}) copy-start(f32[256,16]{0,1:T(8,128)} %get-tuple-element.16) | copy-start | bytes 49156
  123.1 20.5 %copy-start.5 = (f32[256,16]{0,1:T(8,128)S(1)}, f32[256,16]{0,1:T(8,128)}, u32[]{:S(2)}) copy-start(f32[256,16]{0,1:T(8,128)} %get-tuple-element.15) | copy-start | bytes 49156
  131.2 45.7 %all-to-all-start.1 = ((f32[32,256,16]{1,2,0:T(8,128)}), f32[32,256,16]{1,2,0:T(8,128)S(1)}, u32[]{:S(2)}, u32[]{:S(2)}) async-start(f32[32,256,16]{1,2,0:T(8,128)} %broadcast_in_dim.21), calls=%async_computation.1 | async-start | bytes 1048576 | tf_op jit(solution)/shard_map/all_to_all | solution.py:21
  190.6 18.2 %copy-start.9 = (f32[256]{0:T(256)S(1)}, f32[256]{0:T(256)}, u32[]{:S(2)}) copy-start(f32[256]{0:T(256)} %param.12) | copy-start | bytes 3076
Sparse Core Ops, SparseCore 0:
  16.0 89.3 all-gather.6
  130.2 78.5 all-gather.8

commit v14 on v13

--- a/solution.py
+++ b/solution.py
@@ -98,11 +98,13 @@
                 feats = feats + taps[i][:, None, :] * widened[:, SHORT - 1 - i : SHORT - 1 - i + rows, :]
             return feats
 
-        streams = across_z(across_yh(in_weight))
-        packed = out_weight.T[None]
+        streams = across_yh(in_weight)
+        packed = lax.all_gather(out_weight, "yh", axis=1)
+        packed, streams = lax.optimization_barrier((packed, streams))
+        streams = across_z(streams)
         packed, streams = lax.optimization_barrier((packed, streams))
         feats = filtered(shortened(streams), short_taps)
-        packed = across_z(across_yh(packed))[0]
+        packed = lax.all_gather(packed, "z", axis=2).reshape(width, -1)
         query = feats[0]
         feats = feats[1:]
         gated = (feats[0] * feats[1]).astype(jnp.bfloat16)
@@ -112,8 +114,8 @@
         starts = starts + offsets * incoming[None]
         conv = finish(inner, starts, heads, values, skip)
         hidden = (query * conv).astype(jnp.bfloat16)
-        out_w = jnp.transpose(packed.reshape(lanes // 2, 2, -1, width), (1, 0, 2, 3))
-        terms = jnp.einsum("tc,yxec->yxte", hidden, out_w, preferred_element_type=jnp.float32)
+        out_w = jnp.transpose(packed.reshape(width, lanes // 2, 2, -1), (0, 2, 1, 3))
+        terms = jnp.einsum("tc,cyxe->yxte", hidden, out_w, preferred_element_type=jnp.float32)
         return scattered_terms(terms.astype(jnp.bfloat16))
 
     return shards

time: 271 us -> 273 us (level)
    all_gather x2 -> x1, waiting for transfers between devices: 35.2 us -> 18.4 us  [across_z(): part = lax.all_gather(part, 'z', axis=2)]
    all_gather x0 -> x1, waiting for transfers between devices: none -> 14.3 us  [shards(): packed = lax.all_gather(packed, 'z', axis=2).reshape(width, -1)]
    all_gather x0 -> x1, blocking collectives: none -> 5.59 us  [shards(): packed = lax.all_gather(out_weight, 'yh', axis=1)]
    all_gather x2 -> x1, blocking collectives: 14.8 us -> 9.37 us  [across_yh(): return lax.all_gather(part, 'yh', axis=1)]
    all_to_all x1, waiting for transfers between devices: 19.4 us -> 23.7 us  [carried_in(): every = lax.all_to_all(copies, CTX, 0, 0)]
where the time goes in v14:
time: 273 us; the launch traced here: 272 us
  waiting for transfers between devices  105 us (38%)
  blocking collectives  59.3 us (22%)
  matrix products  33.8 us (12%)
  starting transfers between devices  24.8 us (9%)
  local copies, waits for them, and re-layouts  24.1 us (9%)
  between operations  13.8 us (5%)
  other arithmetic  11 us (4%)
    all_to_all x1, waiting for transfers between devices, gathered_tokens(): return lax.all_to_all(copies, CH, 1, 1)  49 us
    all_to_all x1, blocking collectives, scattered_terms(): parts = lax.all_to_all(pairs, 'cx', 0, 0)  30 us
    all_to_all x1, waiting for transfers between devices, carried_in(): every = lax.all_to_all(copies, CTX, 0, 0)  23.7 us
    all_gather x1, waiting for transfers between devices, across_z(): part = lax.all_gather(part, 'z', axis=2)  18.4 us
    all_to_all x1, blocking collectives, scattered_terms(): pairs = lax.all_to_all(terms, 'core', 0, 0)  14.3 us
    all_gather x1, waiting for transfers between devices, shards(): packed = lax.all_gather(packed, 'z', axis=2).reshape(width, -1)  14.3 us
    all_to_all x1, starting transfers between devices, carried_in(): every = lax.all_to_all(copies, CTX, 0, 0)  12.4 us
    all_to_all x1, starting transfers between devices, gathered_tokens(): return lax.all_to_all(copies, CH, 1, 1)  11.1 us
  transfers between devices with their start and end apart: 5, of which 4 were waited for; matrix products, arithmetic and copies ran while one was open for 15% of the time, Pallas kernels for 0%

profile of v14, /device:TPU:1, one launch (start us, length us, event | category | flops | bytes accessed | tf_op | source)
XLA Modules:
  0.0 272.2 jit_solution(17315133942298958353)
XLA Ops:
  6.5 9.4 %all-gather.1 = bf16[3,256,256]{2,1,0:T(8,128)(2,1)} all-gather(bf16[3,128,256]{2,1,0:T(8,128)(2,1)} %param.8), channel_id=3, replica_groups=mesh['yh'=2,'z'=16,'cx'=8,'core'=2] {'yh'}, dimensions={1}, use_global_device_ids=true | all-gather | bytes 589824 | tf_op jit(solution)/shard_map/all_gather | solution.py:82
  15.9 5.6 %all-gather = bf16[256,256]{1,0:T(8,128)(2,1)S(1)} all-gather(bf16[256,128]{1,0:T(8,128)(2,1)} %param.13), channel_id=2, replica_groups=mesh['yh'=2,'z'=16,'cx'=8,'core'=2] {'yh'}, dimensions={1}, use_global_device_ids=true | all-gather | bytes 196608 | tf_op jit(solution)/shard_map/all_gather | solution.py:102
  21.5 0.8 copy.125
  22.3 3.4 %broadcast_in_dim.14 = bf16[512,16,256]{2,0,1:T(8,128)(2,1)} broadcast(bf16[512,256]{1,0:T(8,128)(2,1)} %param.7), dimensions={0,2} | broadcast | bytes 4456448 | tf_op jit(solution)/shard_map/broadcast_in_dim | solution.py:63
  25.7 11.1 %all-to-all-start = ((bf16[512,16,256]{2,0,1:T(8,128)(2,1)}), bf16[512,16,256]{2,0,1:T(8,128)(2,1)}, u32[]{:S(2)}, u32[]{:S(2)}) async-start(bf16[512,16,256]{2,0,1:T(8,128)(2,1)} %broadcast_in_dim.14), calls=%async_computation | async-start | bytes 8388608 | tf_op jit(solution)/shard_map/all_to_all | solution.py:64
  37.7 2.8 %multiply_reduce_fusion = (f32[64,256]{0,1:T(8,128)S(1)}, f32[64,256,16]{0,2,1:T(8,128)}) fusion(f32[256,16]{1,0:T(8,128)S(1)} %copy.131, f32[64]{0:T(128)S(1)} %iota_negate_fusion, f32[256,16]{1,0:T(8,128)S(1)} %copy.130), kind=kLoop, calls=%fused_computation.11 | loop fusion | flops 770048 | bytes 1147136 | tf_op jit(solution)/shard_map/reduce_sum | solution.py:35
  40.5 49.0 %all-to-all-done = bf16[512,16,256]{2,0,1:T(8,128)(2,1)} async-done(((bf16[512,16,256]{2,0,1:T(8,128)(2,1)}), bf16[512,16,256]{2,0,1:T(8,128)(2,1)}, u32[]{:S(2)}, u32[]{:S(2)}) %all-to-all-start) | async-done | bytes 4194336 | tf_op jit(solution)/shard_map/all_to_all | solution.py:64
  89.6 0.9 slice.125
  90.4 1.3 collective-permute-start
  91.8 2.8 %rev.3 = f32[64,256,16]{0,2,1:T(8,128)S(1)} reverse(f32[64,256,16]{0,2,1:T(8,128)} %get-tuple-element.14), dimensions={0} | reverse | bytes 2097152 | tf_op jit(solution)/shard_map/rev | solution.py:41
  94.5 18.4 %all-gather.7.cloned.1.call-done = bf16[3,2,2048,256]{3,2,1,0:T(8,128)(2,1)} async-done(((bf16[3,2,128,256]{3,2,1,0:T(8,128)(2,1)}), bf16[3,2,2048,256]{3,2,1,0:T(8,128)(2,1)}) %all-gather.7.cloned.1.call-update) | async-done | bytes 6291472 | tf_op jit(solution)/shard_map/all_gather | solution.py:85
  112.9 3.7 %fusion.17 = bf16[3,2,256]{2,1,0:T(2,128)(2,1)S(1)} fusion(bf16[3,16,256,256]{3,2,1,0:T(8,128)(2,1)} %bitcast.83, bf16[2,16,256]{2,0,1:T(2,128)(2,1)S(1)} %collective-permute-done), kind=kOutput, calls=%fused_computation.23 | convolution fusion | flops 12584448 | bytes 6310912 | tf_op jit(solution)/shard_map/tkd,jkdc->jtc/dot_general | solution.py:91
  116.8 7.5 %fusion.13 = bf16[3,512,256]{1,2,0:T(8,128)(2,1)S(1)} fusion(bf16[3,16,256,256]{3,2,1,0:T(8,128)(2,1)} %bitcast.84, bf16[512,16,256]{2,0,1:T(8,128)(2,1)} %all-to-all-done), kind=kOutput, calls=%fused_computation.20 | convolution fusion | flops 3221618688 | bytes 11272192 | tf_op jit(solution)/shard_map/tkd,jkdc->jtc/dot_general | solution.py:90
  124.7 1.4 fusion.8
  126.1 1.2 copy-done
  127.8 2.7 fusion.40
  130.5 1.5 copy.136
  132.3 0.9 broadcast_in_dim.18
  133.2 12.4 %all-to-all-start.1 = ((f32[32,256,16]{1,2,0:T(8,128)}), f32[32,256,16]{1,2,0:T(8,128)S(1)}, u32[]{:S(2)}, u32[]{:S(2)}) async-start(f32[32,256,16]{1,2,0:T(8,128)} %broadcast_in_dim.18), calls=%async_computation.1 | async-start | bytes 1048576 | tf_op jit(solution)/shard_map/all_to_all | solution.py:21
  145.6 0.8 copy.137
  146.3 3.8 %fusion.6 = f32[64,64,256]{2,1,0:T(8,128)} fusion(s32[64,64]{1,0:T(8,128)S(1)} %iota_subtract_fusion, f32[64,256]{0,1:T(8,128)S(1)} %get-tuple-element.13), kind=kOutput, calls=%fused_computation.9 | convolution fusion | flops 805568512 | bytes 4276224 | tf_op jit(solution)/shard_map/dot_general | solution.py:40
  150.2 9.2 %copy.134 = f32[64,64,256]{1,0,2:T(8,128)} copy(f32[64,64,256]{2,1,0:T(8,128)} %fusion.6) | data formatting | bytes 8388608 | tf_op jit(solution)/shard_map/dot_general | solution.py:40
  159.5 23.7 %all-to-all-done.1 = f32[32,256,16]{1,2,0:T(8,128)S(1)} async-done(((f32[32,256,16]{1,2,0:T(8,128)}), f32[32,256,16]{1,2,0:T(8,128)S(1)}, u32[]{:S(2)}, u32[]{:S(2)}) %all-to-all-start.1) | async-done | bytes 524320 | tf_op jit(solution)/shard_map/all_to_all | solution.py:21
  184.0 4.1 %fusion.4 = f32[256,8,64]{2,1,0:T(8,128)S(1)} fusion(f32[8,256,16]{2,0,1:T(8,128)S(1)} %copy.138, f32[256,16]{1,0:T(8,128)} %copy.137, f32[256,16]{1,0:T(8,128)S(1)} %copy.131, f32[64]{0:T(128)} %copy-done.8, f32[256,16]{1,0:T(8,128)S(1)} %copy.130), kind=kOutput, calls=%fused_computation.5 | convolution fusion | flops 25952256 | bytes 704768 | tf_op jit(solution)/shard_map/icm,bcm->bic/dot_general | solution.py:58
  188.0 8.9 %fusion.12 = f32[8,64,256]{1,0,2:T(8,128)S(1)} fusion(f32[256,8,64]{2,1,0:T(8,128)S(1)} %fusion.4, bf16[8,64,256]{1,0,2:T(8,128)(2,1)S(1)} %copy.133, f32[64,64,256]{1,0,2:T(8,128)} %copy.134), kind=kOutput, calls=%fused_computation.19 | convolution fusion | flops 100794368 | bytes 5505024 | tf_op jit(solution)/shard_map/ijc,bjc->bic/dot_general | solution.py:44
  197.6 14.3 %all-gather.9.cloned.1.call-done = bf16[256,2,2048]{0,2,1:T(8,128)(2,1)} async-done(((bf16[256,2,128]{0,2,1:T(8,128)(2,1)}), bf16[256,2,2048]{0,2,1:T(8,128)(2,1)}) %all-gather.9.cloned.1.call-update) | async-done | bytes 2097168 | tf_op jit(solution)/shard_map/all_gather | solution.py:107
  211.8 3.0 %convert_bitcast_fusion = bf16[2,8,512,256]{2,3,1,0:T(8,128)(2,1)S(1)} fusion(bf16[256,8,2,256]{0,3,2,1:T(8,128)(2,1)} %bitcast.86, f32[512,256]{0,1:T(8,128)S(1)} %copy.140, f32[3,512,256]{1,2,0:T(8,128)} %copy-done, bf16[1,512,256]{1,2,0:T(8,128)(2,1)S(1)} %fusion.23, f32[256]{0:T(256)S(1)} %copy-done.7), kind=kOutput, calls=%fused_computation.2 | convolution fusion | flops 1076494336 | bytes 7603200 | tf_op jit(solution)/shard_map/tc,cyxe->yxte/dot_general | solution.py:118
  214.9 14.3 %all_to_all.20 = bf16[2,8,512,256]{2,3,1,0:T(8,128)(2,1)} all-to-all(bf16[2,8,512,256]{2,3,1,0:T(8,128)(2,1)S(1)} %convert_bitcast_fusion), channel_id=1, replica_groups=mesh['yh'=2,'z'=16,'cx'=8,'core'=2] {'core'}, dimensions={0} | all-to-all | bytes 8388608 | tf_op jit(solution)/shard_map/all_to_all | solution.py:68
  229.2 3.3 %reduce_sum.44 = bf16[8,512,256]{1,2,0:T(8,128)(2,1)S(1)} reduce(bf16[2,8,512,256]{2,3,1,0:T(8,128)(2,1)} %all_to_all.20, bf16[]{:T(256)} %constant.29.clone.1), dimensions={0}, to_apply=%region_2.3 | reduce | flops 1048576 | bytes 6291458 | tf_op jit(solution)/shard_map/reduce_sum | solution.py:69
  232.6 30.0 %all_to_all.21 = bf16[8,512,256]{1,2,0:T(8,128)(2,1)} all-to-all(bf16[8,512,256]{1,2,0:T(8,128)(2,1)S(1)} %reduce_sum.44), channel_id=1, replica_groups=mesh['yh'=2,'z'=16,'cx'=8,'core'=2] {'cx'}, dimensions={0} | all-to-all | bytes 4194304 | tf_op jit(solution)/shard_map/all_to_all | solution.py:70
  262.6 2.0 reduce_sum.45
  264.5 0.8 copy.142
  (58 shorter events, 3.6 us)
Async XLA Ops:
  6.5 106.4 %all-gather.7.cloned.1.call-start = ((), (), s32[]{:S(2)}) async-start(), calls=%async_computation.4 | async-start | bytes 6684672 | tf_op jit(solution)/shard_map/all_gather | solution.py:85
  25.7 11.2 %copy-start.5 = (f32[256,16]{0,1:T(8,128)S(1)}, f32[256,16]{0,1:T(8,128)}, u32[]{:S(2)}) copy-start(f32[256,16]{0,1:T(8,128)} %param.11) | copy-start | bytes 49156
  25.7 11.3 %copy-start.1 = (f32[256,16]{0,1:T(8,128)S(1)}, f32[256,16]{0,1:T(8,128)}, u32[]{:S(2)}) copy-start(f32[256,16]{0,1:T(8,128)} %param.10) | copy-start | bytes 49156
  25.7 63.9 %all-to-all-start = ((bf16[512,16,256]{2,0,1:T(8,128)(2,1)}), bf16[512,16,256]{2,0,1:T(8,128)(2,1)}, u32[]{:S(2)}, u32[]{:S(2)}) async-start(bf16[512,16,256]{2,0,1:T(8,128)(2,1)} %broadcast_in_dim.14), calls=%async_computation | async-start | bytes 8388608 | tf_op jit(solution)/shard_map/all_to_all | solution.py:64
  36.8 54.9 %copy-start.6 = (f32[3,3,256]{2,1,0:T(4,128)S(1)}, f32[3,3,256]{2,1,0:T(4,128)}, u32[]{:S(2)}) copy-start(f32[3,3,256]{2,1,0:T(4,128)} %param.9) | copy-start | bytes 27652
  36.8 175.0 %all-gather.9.cloned.1.call-start = ((), (), s32[]{:S(2)}) async-start(), calls=%async_computation.5 | async-start | bytes 2228224 | tf_op jit(solution)/shard_map/all_gather | solution.py:107
  37.1 57.4 %copy-start.8 = (f32[64]{0:T(128)}, f32[64]{0:T(128)S(1)}, u32[]{:S(2)}) copy-start(f32[64]{0:T(128)S(1)} %iota_negate_fusion) | copy-start | bytes 772
  90.4 22.4 %collective-permute-start = (bf16[2,16,256]{2,0,1:T(2,128)(2,1)S(1)}, bf16[2,16,256]{2,0,1:T(2,128)(2,1)S(1)}, u32[]{:S(2)}, u32[]{:S(2)}) collective-permute-start(bf16[2,16,256]{2,0,1:T(2,128)(2,1)S(1)} %slice.125), channel_id=1, source_target_pairs={{0,16},{16,32},{32,48},{48,64},{64,80},{80,96},{96,112},{112,128},... | collective-permute-start | bytes 49160 | tf_op jit(solution)/shard_map/ppermute | solution.py:16
  126.1 1.2 copy-start
  127.8 4.3 %copy-start.2 = (f32[256,16]{0,1:T(8,128)S(1)}, f32[256,16]{0,1:T(8,128)}, u32[]{:S(2)}) copy-start(f32[256,16]{0,1:T(8,128)} %get-tuple-element.21) | copy-start | bytes 49156
  127.8 4.3 %copy-start.4 = (f32[256,16]{0,1:T(8,128)S(1)}, f32[256,16]{0,1:T(8,128)}, u32[]{:S(2)}) copy-start(f32[256,16]{0,1:T(8,128)} %get-tuple-element.20) | copy-start | bytes 49156
  130.5 15.1 %copy-start.3 = (f32[256,16]{0,1:T(8,128)S(1)}, f32[256,16]{0,1:T(8,128)}, u32[]{:S(2)}) copy-start(f32[256,16]{0,1:T(8,128)} %get-tuple-element.19) | copy-start | bytes 49156
  133.2 50.1 %all-to-all-start.1 = ((f32[32,256,16]{1,2,0:T(8,128)}), f32[32,256,16]{1,2,0:T(8,128)S(1)}, u32[]{:S(2)}, u32[]{:S(2)}) async-start(f32[32,256,16]{1,2,0:T(8,128)} %broadcast_in_dim.18), calls=%async_computation.1 | async-start | bytes 1048576 | tf_op jit(solution)/shard_map/all_to_all | solution.py:21
  197.0 14.9 %copy-start.7 = (f32[256]{0:T(256)S(1)}, f32[256]{0:T(256)}, u32[]{:S(2)}) copy-start(f32[256]{0:T(256)} %param.12) | copy-start | bytes 3076
Sparse Core Ops, SparseCore 0:
  22.4 90.4 all-gather.6
  132.2 79.5 all-gather.8

commit v15 on v14

--- a/solution.py
+++ b/solution.py
@@ -102,7 +102,6 @@
         packed = lax.all_gather(out_weight, "yh", axis=1)
         packed, streams = lax.optimization_barrier((packed, streams))
         streams = across_z(streams)
-        packed, streams = lax.optimization_barrier((packed, streams))
         feats = filtered(shortened(streams), short_taps)
         packed = lax.all_gather(packed, "z", axis=2).reshape(width, -1)
         query = feats[0]

time: 273 us -> 257 us (0.941)
  waiting for transfers between devices: 105 us -> 91.8 us
    all_gather x1, waiting for transfers between devices: 14.3 us -> 0.02 us  [shards(): packed = lax.all_gather(packed, 'z', axis=2).reshape(width, -1)]
  transfers between devices with their start and end apart: 5 -> 5, of which waited for: 4 -> 3; matrix products, arithmetic and copies ran while one was open for 15% -> 23% of each run, Pallas kernels for 0% -> 0%
where the time goes in v15:
time: 257 us; the launch traced here: 256 us
  waiting for transfers between devices  91.8 us (36%)
  blocking collectives  57.1 us (22%)
  matrix products  33.8 us (13%)
  starting transfers between devices  24.7 us (10%)
  local copies, waits for them, and re-layouts  24.1 us (9%)
  between operations  13.8 us (5%)
  other arithmetic  11 us (4%)
    all_to_all x1, waiting for transfers between devices, gathered_tokens(): return lax.all_to_all(copies, CH, 1, 1)  48.3 us
    all_to_all x1, blocking collectives, scattered_terms(): parts = lax.all_to_all(pairs, 'cx', 0, 0)  30.1 us
    all_to_all x1, waiting for transfers between devices, carried_in(): every = lax.all_to_all(copies, CTX, 0, 0)  24.2 us
    all_gather x1, waiting for transfers between devices, across_z(): part = lax.all_gather(part, 'z', axis=2)  18.4 us
    all_to_all x1, starting transfers between devices, carried_in(): every = lax.all_to_all(copies, CTX, 0, 0)  12.2 us
    all_to_all x1, blocking collectives, scattered_terms(): pairs = lax.all_to_all(terms, 'core', 0, 0)  12.1 us
    all_to_all x1, starting transfers between devices, gathered_tokens(): return lax.all_to_all(copies, CH, 1, 1)  11.2 us
    all_gather x1, blocking collectives, across_yh(): return lax.all_gather(part, 'yh', axis=1)  9.35 us
  transfers between devices with their start and end apart: 5, of which 3 were waited for; matrix products, arithmetic and copies ran while one was open for 23% of the time, Pallas kernels for 0%

profile of v15, /device:TPU:1, one launch (start us, length us, event | category | flops | bytes accessed | tf_op | source)
XLA Modules:
  0.0 256.3 jit_solution(15710196350259295035)
XLA Ops:
  6.5 9.3 %all-gather.1 = bf16[3,256,256]{2,1,0:T(8,128)(2,1)} all-gather(bf16[3,128,256]{2,1,0:T(8,128)(2,1)} %param.8), channel_id=3, replica_groups=mesh['yh'=2,'z'=16,'cx'=8,'core'=2] {'yh'}, dimensions={1}, use_global_device_ids=true | all-gather | bytes 589824 | tf_op jit(solution)/shard_map/all_gather | solution.py:82
  15.9 5.6 %all-gather = bf16[256,256]{1,0:T(8,128)(2,1)S(1)} all-gather(bf16[256,128]{1,0:T(8,128)(2,1)} %param.13), channel_id=2, replica_groups=mesh['yh'=2,'z'=16,'cx'=8,'core'=2] {'yh'}, dimensions={1}, use_global_device_ids=true | all-gather | bytes 196608 | tf_op jit(solution)/shard_map/all_gather | solution.py:102
  21.5 0.8 copy.125
  22.3 3.4 %broadcast_in_dim.14 = bf16[512,16,256]{2,0,1:T(8,128)(2,1)} broadcast(bf16[512,256]{1,0:T(8,128)(2,1)} %param.7), dimensions={0,2} | broadcast | bytes 4456448 | tf_op jit(solution)/shard_map/broadcast_in_dim | solution.py:63
  25.7 11.2 %all-to-all-start = ((bf16[512,16,256]{2,0,1:T(8,128)(2,1)}), bf16[512,16,256]{2,0,1:T(8,128)(2,1)}, u32[]{:S(2)}, u32[]{:S(2)}) async-start(bf16[512,16,256]{2,0,1:T(8,128)(2,1)} %broadcast_in_dim.14), calls=%async_computation | async-start | bytes 8388608 | tf_op jit(solution)/shard_map/all_to_all | solution.py:64
  36.9 0.7 all-gather.7.cloned.1.call-update
  38.5 2.8 %multiply_reduce_fusion = (f32[64,256]{0,1:T(8,128)S(1)}, f32[64,256,16]{0,2,1:T(8,128)}) fusion(f32[256,16]{1,0:T(8,128)S(1)} %copy.131, f32[64]{0:T(128)S(1)} %iota_negate_fusion, f32[256,16]{1,0:T(8,128)S(1)} %copy.130), kind=kLoop, calls=%fused_computation.11 | loop fusion | flops 770048 | bytes 1147136 | tf_op jit(solution)/shard_map/reduce_sum | solution.py:35
  41.3 48.3 %all-to-all-done = bf16[512,16,256]{2,0,1:T(8,128)(2,1)} async-done(((bf16[512,16,256]{2,0,1:T(8,128)(2,1)}), bf16[512,16,256]{2,0,1:T(8,128)(2,1)}, u32[]{:S(2)}, u32[]{:S(2)}) %all-to-all-start) | async-done | bytes 4194336 | tf_op jit(solution)/shard_map/all_to_all | solution.py:64
  89.6 0.9 slice.125
  90.5 1.3 collective-permute-start
  91.8 2.8 %rev.3 = f32[64,256,16]{0,2,1:T(8,128)S(1)} reverse(f32[64,256,16]{0,2,1:T(8,128)} %get-tuple-element.10), dimensions={0} | reverse | bytes 2097152 | tf_op jit(solution)/shard_map/rev | solution.py:41
  94.6 18.4 %all-gather.9.cloned.1.call-done = bf16[3,2,2048,256]{3,2,1,0:T(8,128)(2,1)} async-done(((bf16[3,2,128,256]{3,2,1,0:T(8,128)(2,1)}), bf16[3,2,2048,256]{3,2,1,0:T(8,128)(2,1)}) %all-gather.9.cloned.1.call-update) | async-done | bytes 6291472 | tf_op jit(solution)/shard_map/all_gather | solution.py:85
  113.0 3.7 %fusion.17 = bf16[3,2,256]{2,1,0:T(2,128)(2,1)S(1)} fusion(bf16[3,16,256,256]{3,2,1,0:T(8,128)(2,1)} %bitcast.82, bf16[2,16,256]{2,0,1:T(2,128)(2,1)S(1)} %collective-permute-done), kind=kOutput, calls=%fused_computation.23 | convolution fusion | flops 12584448 | bytes 6310912 | tf_op jit(solution)/shard_map/tkd,jkdc->jtc/dot_general | solution.py:91
  116.9 7.5 %fusion.13 = bf16[3,512,256]{1,2,0:T(8,128)(2,1)S(1)} fusion(bf16[3,16,256,256]{3,2,1,0:T(8,128)(2,1)} %bitcast.83, bf16[512,16,256]{2,0,1:T(8,128)(2,1)} %all-to-all-done), kind=kOutput, calls=%fused_computation.20 | convolution fusion | flops 3221618688 | bytes 11272192 | tf_op jit(solution)/shard_map/tkd,jkdc->jtc/dot_general | solution.py:90
  124.8 1.4 fusion.8
  126.2 1.2 copy-done
  127.9 2.7 %fusion.40 = f32[256,8,16]{2,1,0:T(8,128)} fusion(bf16[8,64,256]{1,0,2:T(8,128)(2,1)S(1)} %copy.133, f32[64,256,16]{0,2,1:T(8,128)S(1)} %rev.3), kind=kOutput, calls=%fused_computation.73 | convolution fusion | flops 25165824 | bytes 1441792 | tf_op jit(solution)/shard_map/jcm,bjc->bcm/dot_general | solution.py:45
  130.6 1.5 copy.136
  132.4 0.8 broadcast_in_dim.18
  133.2 12.2 %all-to-all-start.1 = ((f32[32,256,16]{1,2,0:T(8,128)}), f32[32,256,16]{1,2,0:T(8,128)S(1)}, u32[]{:S(2)}, u32[]{:S(2)}) async-start(f32[32,256,16]{1,2,0:T(8,128)} %broadcast_in_dim.18), calls=%async_computation.1 | async-start | bytes 1048576 | tf_op jit(solution)/shard_map/all_to_all | solution.py:21
  145.5 0.8 copy.137
  146.3 3.8 %fusion.6 = f32[64,64,256]{2,1,0:T(8,128)} fusion(s32[64,64]{1,0:T(8,128)S(1)} %iota_subtract_fusion, f32[64,256]{0,1:T(8,128)S(1)} %get-tuple-element.9), kind=kOutput, calls=%fused_computation.9 | convolution fusion | flops 805568512 | bytes 4276224 | tf_op jit(solution)/shard_map/dot_general | solution.py:40
  150.1 9.2 %copy.134 = f32[64,64,256]{1,0,2:T(8,128)} copy(f32[64,64,256]{2,1,0:T(8,128)} %fusion.6) | data formatting | bytes 8388608 | tf_op jit(solution)/shard_map/dot_general | solution.py:40
  159.4 24.2 %all-to-all-done.1 = f32[32,256,16]{1,2,0:T(8,128)S(1)} async-done(((f32[32,256,16]{1,2,0:T(8,128)}), f32[32,256,16]{1,2,0:T(8,128)S(1)}, u32[]{:S(2)}, u32[]{:S(2)}) %all-to-all-start.1) | async-done | bytes 524320 | tf_op jit(solution)/shard_map/all_to_all | solution.py:21
  184.4 4.1 %fusion.4 = f32[256,8,64]{2,1,0:T(8,128)S(1)} fusion(f32[8,256,16]{2,0,1:T(8,128)S(1)} %copy.138, f32[256,16]{1,0:T(8,128)} %copy.137, f32[256,16]{1,0:T(8,128)S(1)} %copy.131, f32[64]{0:T(128)} %copy-done.8, f32[256,16]{1,0:T(8,128)S(1)} %copy.130), kind=kOutput, calls=%fused_computation.5 | convolution fusion | flops 25952256 | bytes 704768 | tf_op jit(solution)/shard_map/icm,bcm->bic/dot_general | solution.py:58
  188.5 8.9 %fusion.12 = f32[8,64,256]{1,0,2:T(8,128)S(1)} fusion(f32[256,8,64]{2,1,0:T(8,128)S(1)} %fusion.4, bf16[8,64,256]{1,0,2:T(8,128)(2,1)S(1)} %copy.133, f32[64,64,256]{1,0,2:T(8,128)} %copy.134), kind=kOutput, calls=%fused_computation.19 | convolution fusion | flops 100794368 | bytes 5505024 | tf_op jit(solution)/shard_map/ijc,bjc->bic/dot_general | solution.py:44
  198.1 3.0 %convert_bitcast_fusion = bf16[2,8,512,256]{2,3,1,0:T(8,128)(2,1)S(1)} fusion(bf16[256,8,2,256]{0,3,2,1:T(8,128)(2,1)} %bitcast.85, f32[512,256]{0,1:T(8,128)S(1)} %copy.140, f32[3,512,256]{1,2,0:T(8,128)} %copy-done, bf16[1,512,256]{1,2,0:T(8,128)(2,1)S(1)} %fusion.23, f32[256]{0:T(256)S(1)} %copy-done.7), kind=kOutput, calls=%fused_computation.2 | convolution fusion | flops 1076494336 | bytes 7603200 | tf_op jit(solution)/shard_map/tc,cyxe->yxte/dot_general | solution.py:117
  201.1 12.1 %all_to_all.20 = bf16[2,8,512,256]{2,3,1,0:T(8,128)(2,1)} all-to-all(bf16[2,8,512,256]{2,3,1,0:T(8,128)(2,1)S(1)} %convert_bitcast_fusion), channel_id=1, replica_groups=mesh['yh'=2,'z'=16,'cx'=8,'core'=2] {'core'}, dimensions={0} | all-to-all | bytes 8388608 | tf_op jit(solution)/shard_map/all_to_all | solution.py:68
  213.2 3.3 %reduce_sum.44 = bf16[8,512,256]{1,2,0:T(8,128)(2,1)S(1)} reduce(bf16[2,8,512,256]{2,3,1,0:T(8,128)(2,1)} %all_to_all.20, bf16[]{:T(256)} %constant.29.clone.1), dimensions={0}, to_apply=%region_2.3 | reduce | flops 1048576 | bytes 6291458 | tf_op jit(solution)/shard_map/reduce_sum | solution.py:69
  216.5 30.1 %all_to_all.21 = bf16[8,512,256]{1,2,0:T(8,128)(2,1)} all-to-all(bf16[8,512,256]{1,2,0:T(8,128)(2,1)S(1)} %reduce_sum.44), channel_id=1, replica_groups=mesh['yh'=2,'z'=16,'cx'=8,'core'=2] {'cx'}, dimensions={0} | all-to-all | bytes 4194304 | tf_op jit(solution)/shard_map/all_to_all | solution.py:70
  246.6 2.0 reduce_sum.45
  248.6 0.8 copy.142
  (58 shorter events, 3.7 us)
Async XLA Ops:
  6.5 106.5 %all-gather.9.cloned.1.call-start = ((), (), s32[]{:S(2)}) async-start(), calls=%async_computation.5 | async-start | bytes 6684672 | tf_op jit(solution)/shard_map/all_gather | solution.py:85
  25.7 11.9 %copy-start.5 = (f32[256,16]{0,1:T(8,128)S(1)}, f32[256,16]{0,1:T(8,128)}, u32[]{:S(2)}) copy-start(f32[256,16]{0,1:T(8,128)} %param.11) | copy-start | bytes 49156
  25.7 12.0 %copy-start.1 = (f32[256,16]{0,1:T(8,128)S(1)}, f32[256,16]{0,1:T(8,128)}, u32[]{:S(2)}) copy-start(f32[256,16]{0,1:T(8,128)} %param.10) | copy-start | bytes 49156
  25.7 63.9 %all-to-all-start = ((bf16[512,16,256]{2,0,1:T(8,128)(2,1)}), bf16[512,16,256]{2,0,1:T(8,128)(2,1)}, u32[]{:S(2)}, u32[]{:S(2)}) async-start(bf16[512,16,256]{2,0,1:T(8,128)(2,1)} %broadcast_in_dim.14), calls=%async_computation | async-start | bytes 8388608 | tf_op jit(solution)/shard_map/all_to_all | solution.py:64
  36.9 54.9 %copy-start.6 = (f32[3,3,256]{2,1,0:T(4,128)S(1)}, f32[3,3,256]{2,1,0:T(4,128)}, u32[]{:S(2)}) copy-start(f32[3,3,256]{2,1,0:T(4,128)} %param.9) | copy-start | bytes 27652
  36.9 161.2 %all-gather.7.cloned.1.call-start = ((), (), s32[]{:S(2)}) async-start(), calls=%async_computation.4 | async-start | bytes 2228224 | tf_op jit(solution)/shard_map/all_gather | solution.py:106
  37.8 56.7 %copy-start.8 = (f32[64]{0:T(128)}, f32[64]{0:T(128)S(1)}, u32[]{:S(2)}) copy-start(f32[64]{0:T(128)S(1)} %iota_negate_fusion) | copy-start | bytes 772
  90.5 4.1 %collective-permute-start = (bf16[2,16,256]{2,0,1:T(2,128)(2,1)S(1)}, bf16[2,16,256]{2,0,1:T(2,128)(2,1)S(1)}, u32[]{:S(2)}, u32[]{:S(2)}) collective-permute-start(bf16[2,16,256]{2,0,1:T(2,128)(2,1)S(1)} %slice.125), channel_id=1, source_target_pairs={{0,16},{16,32},{32,48},{48,64},{64,80},{80,96},{96,112},{112,128},... | collective-permute-start | bytes 49160 | tf_op jit(solution)/shard_map/ppermute | solution.py:16
  126.2 1.2 copy-start
  127.9 4.3 %copy-start.2 = (f32[256,16]{0,1:T(8,128)S(1)}, f32[256,16]{0,1:T(8,128)}, u32[]{:S(2)}) copy-start(f32[256,16]{0,1:T(8,128)} %get-tuple-element.17) | copy-start | bytes 49156
  127.9 4.3 %copy-start.4 = (f32[256,16]{0,1:T(8,128)S(1)}, f32[256,16]{0,1:T(8,128)}, u32[]{:S(2)}) copy-start(f32[256,16]{0,1:T(8,128)} %get-tuple-element.16) | copy-start | bytes 49156
  130.6 14.9 %copy-start.3 = (f32[256,16]{0,1:T(8,128)S(1)}, f32[256,16]{0,1:T(8,128)}, u32[]{:S(2)}) copy-start(f32[256,16]{0,1:T(8,128)} %get-tuple-element.15) | copy-start | bytes 49156
  133.2 50.4 %all-to-all-start.1 = ((f32[32,256,16]{1,2,0:T(8,128)}), f32[32,256,16]{1,2,0:T(8,128)S(1)}, u32[]{:S(2)}, u32[]{:S(2)}) async-start(f32[32,256,16]{1,2,0:T(8,128)} %broadcast_in_dim.18), calls=%async_computation.1 | async-start | bytes 1048576 | tf_op jit(solution)/shard_map/all_to_all | solution.py:21
  197.4 0.7 copy-start.7
Sparse Core Ops, SparseCore 0:
  22.4 90.5 all-gather.8
  115.1 79.4 all-gather.6

commit v16 on v15

--- a/solution.py
+++ b/solution.py
@@ -99,9 +99,9 @@
             return feats
 
         streams = across_yh(in_weight)
-        packed = lax.all_gather(out_weight, "yh", axis=1)
-        packed, streams = lax.optimization_barrier((packed, streams))
+        packed, streams = lax.optimization_barrier((out_weight, streams))
         streams = across_z(streams)
+        packed = lax.all_gather(packed, "yh", axis=1)
         feats = filtered(shortened(streams), short_taps)
         packed = lax.all_gather(packed, "z", axis=2).reshape(width, -1)
         query = feats[0]

time: 257 us -> 250 us (0.973)
  waiting for transfers between devices: 91.8 us -> 69.7 us
  blocking collectives: 57.1 us -> 72.5 us
    all_to_all x1, waiting for transfers between devices: 48.3 us -> 27.4 us  [gathered_tokens(): return lax.all_to_all(copies, CH, 1, 1)]
    all_gather x1, blocking collectives: 5.61 us -> 20.9 us  [shards(): packed = lax.all_gather(packed, 'yh', axis=1)]
  transfers between devices with their start and end apart: 5 -> 5, of which waited for: 3 -> 3; matrix products, arithmetic and copies ran while one was open for 23% -> 24% of each run, Pallas kernels for 0% -> 0%
where the time goes in v16:
time: 250 us; the launch traced here: 249 us
  blocking collectives  72.5 us (29%)
  waiting for transfers between devices  69.7 us (28%)
  matrix products  33.8 us (14%)
  local copies, waits for them, and re-layouts  24.2 us (10%)
  starting transfers between devices  23.9 us (10%)
  between operations  13.8 us (6%)
  other arithmetic  11 us (4%)
    all_to_all x1, blocking collectives, scattered_terms(): parts = lax.all_to_all(pairs, 'cx', 0, 0)  29.9 us
    all_to_all x1, waiting for transfers between devices, gathered_tokens(): return lax.all_to_all(copies, CH, 1, 1)  27.4 us
    all_to_all x1, waiting for transfers between devices, carried_in(): every = lax.all_to_all(copies, CTX, 0, 0)  24.1 us
    all_gather x1, blocking collectives, shards(): packed = lax.all_gather(packed, 'yh', axis=1)  20.9 us
    all_gather x1, waiting for transfers between devices, across_z(): part = lax.all_gather(part, 'z', axis=2)  18.2 us
    all_to_all x1, starting transfers between devices, carried_in(): every = lax.all_to_all(copies, CTX, 0, 0)  12.5 us
    all_to_all x1, blocking collectives, scattered_terms(): pairs = lax.all_to_all(terms, 'core', 0, 0)  12.4 us
    all_to_all x1, starting transfers between devices, gathered_tokens(): return lax.all_to_all(copies, CH, 1, 1)  10 us
  transfers between devices with their start and end apart: 5, of which 3 were waited for; matrix products, arithmetic and copies ran while one was open for 24% of the time, Pallas kernels for 0%

profile of v16, /device:TPU:1, one launch (start us, length us, event | category | flops | bytes accessed | tf_op | source)
XLA Modules:
  0.0 248.8 jit_solution(4996050319622644335)
XLA Ops:
  6.5 9.4 %all-gather = bf16[3,256,256]{2,1,0:T(8,128)(2,1)} all-gather(bf16[3,128,256]{2,1,0:T(8,128)(2,1)} %param.8), channel_id=2, replica_groups=mesh['yh'=2,'z'=16,'cx'=8,'core'=2] {'yh'}, dimensions={1}, use_global_device_ids=true | all-gather | bytes 589824 | tf_op jit(solution)/shard_map/all_gather | solution.py:82
  15.9 3.4 %broadcast_in_dim.14 = bf16[512,16,256]{2,0,1:T(8,128)(2,1)} broadcast(bf16[512,256]{1,0:T(8,128)(2,1)} %param.7), dimensions={0,2} | broadcast | bytes 4456448 | tf_op jit(solution)/shard_map/broadcast_in_dim | solution.py:63
  19.4 10.0 %all-to-all-start = ((bf16[512,16,256]{2,0,1:T(8,128)(2,1)}), bf16[512,16,256]{2,0,1:T(8,128)(2,1)}, u32[]{:S(2)}, u32[]{:S(2)}) async-start(bf16[512,16,256]{2,0,1:T(8,128)(2,1)} %broadcast_in_dim.14), calls=%async_computation | async-start | bytes 8388608 | tf_op jit(solution)/shard_map/all_to_all | solution.py:64
  29.5 20.9 %all-gather.1 = bf16[256,256]{1,0:T(8,128)(2,1)S(1)} all-gather(bf16[256,128]{1,0:T(8,128)(2,1)S(1)} %copy-done.3), channel_id=3, replica_groups=mesh['yh'=2,'z'=16,'cx'=8,'core'=2] {'yh'}, dimensions={1}, use_global_device_ids=true | all-gather | bytes 196608 | tf_op jit(solution)/shard_map/all_gather | solution.py:104
  50.4 0.8 copy.125
  51.4 0.6 negate_exponential_fusion
  52.0 2.8 %multiply_reduce_fusion = (f32[64,256]{0,1:T(8,128)S(1)}, f32[64,256,16]{0,2,1:T(8,128)}) fusion(f32[256,16]{1,0:T(8,128)S(1)} %copy.131, f32[64]{0:T(128)S(1)} %iota_negate_fusion, f32[256,16]{1,0:T(8,128)S(1)} %copy.130), kind=kLoop, calls=%fused_computation.11 | loop fusion | flops 770048 | bytes 1147136 | tf_op jit(solution)/shard_map/reduce_sum | solution.py:35
  54.8 27.4 %all-to-all-done = bf16[512,16,256]{2,0,1:T(8,128)(2,1)} async-done(((bf16[512,16,256]{2,0,1:T(8,128)(2,1)}), bf16[512,16,256]{2,0,1:T(8,128)(2,1)}, u32[]{:S(2)}, u32[]{:S(2)}) %all-to-all-start) | async-done | bytes 4194336 | tf_op jit(solution)/shard_map/all_to_all | solution.py:64
  82.2 0.9 slice.125
  83.0 1.3 collective-permute-start
  84.3 2.7 %rev.3 = f32[64,256,16]{0,2,1:T(8,128)S(1)} reverse(f32[64,256,16]{0,2,1:T(8,128)} %get-tuple-element.10), dimensions={0} | reverse | bytes 2097152 | tf_op jit(solution)/shard_map/rev | solution.py:41
  87.1 18.2 %all-gather.9.cloned.1.call-done = bf16[3,2,2048,256]{3,2,1,0:T(8,128)(2,1)} async-done(((bf16[3,2,128,256]{3,2,1,0:T(8,128)(2,1)}), bf16[3,2,2048,256]{3,2,1,0:T(8,128)(2,1)}) %all-gather.9.cloned.1.call-update) | async-done | bytes 6291472 | tf_op jit(solution)/shard_map/all_gather | solution.py:85
  105.3 3.7 %fusion.17 = bf16[3,2,256]{2,1,0:T(2,128)(2,1)S(1)} fusion(bf16[3,16,256,256]{3,2,1,0:T(8,128)(2,1)} %bitcast.82, bf16[2,16,256]{2,0,1:T(2,128)(2,1)S(1)} %collective-permute-done), kind=kOutput, calls=%fused_computation.23 | convolution fusion | flops 12584448 | bytes 6310912 | tf_op jit(solution)/shard_map/tkd,jkdc->jtc/dot_general | solution.py:91
  109.2 7.5 %fusion.13 = bf16[3,512,256]{1,2,0:T(8,128)(2,1)S(1)} fusion(bf16[3,16,256,256]{3,2,1,0:T(8,128)(2,1)} %bitcast.83, bf16[512,16,256]{2,0,1:T(8,128)(2,1)} %all-to-all-done), kind=kOutput, calls=%fused_computation.20 | convolution fusion | flops 3221618688 | bytes 11272192 | tf_op jit(solution)/shard_map/tkd,jkdc->jtc/dot_general | solution.py:90
  117.1 1.4 fusion.8
  118.4 1.2 copy-done
  120.2 2.7 %fusion.40 = f32[256,8,16]{2,1,0:T(8,128)} fusion(bf16[8,64,256]{1,0,2:T(8,128)(2,1)S(1)} %copy.133, f32[64,256,16]{0,2,1:T(8,128)S(1)} %rev.3), kind=kOutput, calls=%fused_computation.73 | convolution fusion | flops 25165824 | bytes 1441792 | tf_op jit(solution)/shard_map/jcm,bjc->bcm/dot_general | solution.py:45
  122.9 1.5 copy.136
  124.7 0.9 broadcast_in_dim.18
  125.6 12.5 %all-to-all-start.1 = ((f32[32,256,16]{1,2,0:T(8,128)}), f32[32,256,16]{1,2,0:T(8,128)S(1)}, u32[]{:S(2)}, u32[]{:S(2)}) async-start(f32[32,256,16]{1,2,0:T(8,128)} %broadcast_in_dim.18), calls=%async_computation.1 | async-start | bytes 1048576 | tf_op jit(solution)/shard_map/all_to_all | solution.py:21
  138.1 0.8 copy.137
  138.9 3.8 %fusion.6 = f32[64,64,256]{2,1,0:T(8,128)} fusion(s32[64,64]{1,0:T(8,128)S(1)} %iota_subtract_fusion, f32[64,256]{0,1:T(8,128)S(1)} %get-tuple-element.9), kind=kOutput, calls=%fused_computation.9 | convolution fusion | flops 805568512 | bytes 4276224 | tf_op jit(solution)/shard_map/dot_general | solution.py:40
  142.7 9.2 %copy.134 = f32[64,64,256]{1,0,2:T(8,128)} copy(f32[64,64,256]{2,1,0:T(8,128)} %fusion.6) | data formatting | bytes 8388608 | tf_op jit(solution)/shard_map/dot_general | solution.py:40
  152.1 24.1 %all-to-all-done.1 = f32[32,256,16]{1,2,0:T(8,128)S(1)} async-done(((f32[32,256,16]{1,2,0:T(8,128)}), f32[32,256,16]{1,2,0:T(8,128)S(1)}, u32[]{:S(2)}, u32[]{:S(2)}) %all-to-all-start.1) | async-done | bytes 524320 | tf_op jit(solution)/shard_map/all_to_all | solution.py:21
  176.9 4.1 %fusion.4 = f32[256,8,64]{2,1,0:T(8,128)S(1)} fusion(f32[8,256,16]{2,0,1:T(8,128)S(1)} %copy.138, f32[256,16]{1,0:T(8,128)} %copy.137, f32[256,16]{1,0:T(8,128)S(1)} %copy.131, f32[64]{0:T(128)} %copy-done.9, f32[256,16]{1,0:T(8,128)S(1)} %copy.130), kind=kOutput, calls=%fused_computation.5 | convolution fusion | flops 25952256 | bytes 704768 | tf_op jit(solution)/shard_map/icm,bcm->bic/dot_general | solution.py:58
  181.0 8.9 %fusion.12 = f32[8,64,256]{1,0,2:T(8,128)S(1)} fusion(f32[256,8,64]{2,1,0:T(8,128)S(1)} %fusion.4, bf16[8,64,256]{1,0,2:T(8,128)(2,1)S(1)} %copy.133, f32[64,64,256]{1,0,2:T(8,128)} %copy.134), kind=kOutput, calls=%fused_computation.19 | convolution fusion | flops 100794368 | bytes 5505024 | tf_op jit(solution)/shard_map/ijc,bjc->bic/dot_general | solution.py:44
  190.6 3.0 %convert_bitcast_fusion = bf16[2,8,512,256]{2,3,1,0:T(8,128)(2,1)S(1)} fusion(bf16[256,8,2,256]{0,3,2,1:T(8,128)(2,1)} %bitcast.85, f32[512,256]{0,1:T(8,128)S(1)} %copy.140, f32[3,512,256]{1,2,0:T(8,128)} %copy-done, bf16[1,512,256]{1,2,0:T(8,128)(2,1)S(1)} %fusion.23, f32[256]{0:T(256)S(1)} %copy-done.8), kind=kOutput, calls=%fused_computation.2 | convolution fusion | flops 1076494336 | bytes 7603200 | tf_op jit(solution)/shard_map/tc,cyxe->yxte/dot_general | solution.py:117
  193.6 12.4 %all_to_all.20 = bf16[2,8,512,256]{2,3,1,0:T(8,128)(2,1)} all-to-all(bf16[2,8,512,256]{2,3,1,0:T(8,128)(2,1)S(1)} %convert_bitcast_fusion), channel_id=1, replica_groups=mesh['yh'=2,'z'=16,'cx'=8,'core'=2] {'core'}, dimensions={0} | all-to-all | bytes 8388608 | tf_op jit(solution)/shard_map/all_to_all | solution.py:68
  206.0 3.3 %reduce_sum.44 = bf16[8,512,256]{1,2,0:T(8,128)(2,1)S(1)} reduce(bf16[2,8,512,256]{2,3,1,0:T(8,128)(2,1)} %all_to_all.20, bf16[]{:T(256)} %constant.29.clone.1), dimensions={0}, to_apply=%region_2.3 | reduce | flops 1048576 | bytes 6291458 | tf_op jit(solution)/shard_map/reduce_sum | solution.py:69
  209.3 29.9 %all_to_all.21 = bf16[8,512,256]{1,2,0:T(8,128)(2,1)} all-to-all(bf16[8,512,256]{1,2,0:T(8,128)(2,1)S(1)} %reduce_sum.44), channel_id=1, replica_groups=mesh['yh'=2,'z'=16,'cx'=8,'core'=2] {'cx'}, dimensions={0} | all-to-all | bytes 4194304 | tf_op jit(solution)/shard_map/all_to_all | solution.py:70
  239.2 2.0 reduce_sum.45
  241.1 0.8 copy.142
  (60 shorter events, 3.1 us)
Async XLA Ops:
  6.5 98.7 %all-gather.9.cloned.1.call-start = ((), (), s32[]{:S(2)}) async-start(), calls=%async_computation.5 | async-start | bytes 6684672 | tf_op jit(solution)/shard_map/all_gather | solution.py:85
  19.4 10.1 %copy-start.3 = (bf16[256,128]{1,0:T(8,128)(2,1)S(1)}, bf16[256,128]{1,0:T(8,128)(2,1)}, u32[]{:S(2)}) copy-start(bf16[256,128]{1,0:T(8,128)(2,1)} %param.13) | copy-start | bytes 196612
  19.4 31.8 %copy-start.6 = (f32[256,16]{0,1:T(8,128)S(1)}, f32[256,16]{0,1:T(8,128)}, u32[]{:S(2)}) copy-start(f32[256,16]{0,1:T(8,128)} %param.11) | copy-start | bytes 49156
  19.4 31.9 %copy-start.1 = (f32[256,16]{0,1:T(8,128)S(1)}, f32[256,16]{0,1:T(8,128)}, u32[]{:S(2)}) copy-start(f32[256,16]{0,1:T(8,128)} %param.10) | copy-start | bytes 49156
  19.4 62.8 %all-to-all-start = ((bf16[512,16,256]{2,0,1:T(8,128)(2,1)}), bf16[512,16,256]{2,0,1:T(8,128)(2,1)}, u32[]{:S(2)}, u32[]{:S(2)}) async-start(bf16[512,16,256]{2,0,1:T(8,128)(2,1)} %broadcast_in_dim.14), calls=%async_computation | async-start | bytes 8388608 | tf_op jit(solution)/shard_map/all_to_all | solution.py:64
  29.4 54.9 %copy-start.7 = (f32[3,3,256]{2,1,0:T(4,128)S(1)}, f32[3,3,256]{2,1,0:T(4,128)}, u32[]{:S(2)}) copy-start(f32[3,3,256]{2,1,0:T(4,128)} %param.9) | copy-start | bytes 27652
  29.4 161.1 %all-gather.7.cloned.1.call-start = ((), (), s32[]{:S(2)}) async-start(), calls=%async_computation.4 | async-start | bytes 2228224 | tf_op jit(solution)/shard_map/all_gather | solution.py:106
  51.4 35.7 %copy-start.9 = (f32[64]{0:T(128)}, f32[64]{0:T(128)S(1)}, u32[]{:S(2)}) copy-start(f32[64]{0:T(128)S(1)} %iota_negate_fusion) | copy-start | bytes 772
  83.0 4.1 %collective-permute-start = (bf16[2,16,256]{2,0,1:T(2,128)(2,1)S(1)}, bf16[2,16,256]{2,0,1:T(2,128)(2,1)S(1)}, u32[]{:S(2)}, u32[]{:S(2)}) collective-permute-start(bf16[2,16,256]{2,0,1:T(2,128)(2,1)S(1)} %slice.125), channel_id=1, source_target_pairs={{0,16},{16,32},{32,48},{48,64},{64,80},{80,96},{96,112},{112,128},... | collective-permute-start | bytes 49160 | tf_op jit(solution)/shard_map/ppermute | solution.py:16
  118.4 1.2 copy-start
  120.1 4.3 %copy-start.2 = (f32[256,16]{0,1:T(8,128)S(1)}, f32[256,16]{0,1:T(8,128)}, u32[]{:S(2)}) copy-start(f32[256,16]{0,1:T(8,128)} %get-tuple-element.17) | copy-start | bytes 49156
  120.2 4.3 %copy-start.5 = (f32[256,16]{0,1:T(8,128)S(1)}, f32[256,16]{0,1:T(8,128)}, u32[]{:S(2)}) copy-start(f32[256,16]{0,1:T(8,128)} %get-tuple-element.16) | copy-start | bytes 49156
  122.9 15.2 %copy-start.4 = (f32[256,16]{0,1:T(8,128)S(1)}, f32[256,16]{0,1:T(8,128)}, u32[]{:S(2)}) copy-start(f32[256,16]{0,1:T(8,128)} %get-tuple-element.15) | copy-start | bytes 49156
  125.6 50.6 %all-to-all-start.1 = ((f32[32,256,16]{1,2,0:T(8,128)}), f32[32,256,16]{1,2,0:T(8,128)S(1)}, u32[]{:S(2)}, u32[]{:S(2)}) async-start(f32[32,256,16]{1,2,0:T(8,128)} %broadcast_in_dim.18), calls=%async_computation.1 | async-start | bytes 1048576 | tf_op jit(solution)/shard_map/all_to_all | solution.py:21
  189.9 0.7 copy-start.8
Sparse Core Ops, SparseCore 0:
  16.1 89.1 all-gather.8
  107.4 79.9 all-gather.6

commit v17 on v16

--- a/solution.py
+++ b/solution.py
@@ -60,8 +60,11 @@
 
 
 def gathered_tokens(tokens, lanes):
-    copies = jnp.broadcast_to(tokens[:, None], (tokens.shape[0], lanes, tokens.shape[1]))
-    return lax.all_to_all(copies, CH, 1, 1)
+    rows, width = tokens.shape
+    copies = jnp.broadcast_to(tokens[:, None], (rows, lanes // 2, width))
+    chips = lax.all_to_all(copies, "cx", 1, 1)
+    copies = jnp.broadcast_to(chips[:, None], (rows, 2, lanes // 2, width))
+    return lax.all_to_all(copies, "core", 1, 1)
 
 
 def scattered_terms(terms):
@@ -86,9 +89,9 @@
             return part.reshape(part.shape[0], -1, part.shape[-1])
 
         def shortened(weight):
-            weight = weight.reshape(weight.shape[0], lanes, -1, weight.shape[-1])
-            proj = jnp.einsum("tkd,jkdc->jtc", whole, weight, preferred_element_type=jnp.float32)
-            earlier = jnp.einsum("tkd,jkdc->jtc", halo, weight, preferred_element_type=jnp.float32)
+            weight = weight.reshape(weight.shape[0], lanes // 2, 2, -1, weight.shape[-1])
+            proj = jnp.einsum("toxd,jxodc->jtc", whole, weight, preferred_element_type=jnp.float32)
+            earlier = jnp.einsum("toxd,jxodc->jtc", halo, weight, preferred_element_type=jnp.float32)
             proj = jnp.concatenate([earlier, proj], axis=1).astype(jnp.bfloat16)
             return proj.astype(jnp.float32)
 

time: 250 us -> 250 us (level)
  blocking collectives: 72.5 us -> 83.2 us
  waiting for transfers between devices: 69.7 us -> 61.4 us
    all_to_all x1, waiting for transfers between devices: 27.4 us -> 1.22 us  [gathered_tokens(): chips = lax.all_to_all(copies, 'cx', 1, 1)]
    all_gather x1, waiting for transfers between devices: 18.2 us -> 36.1 us  [across_z(): part = lax.all_gather(part, 'z', axis=2)]
    all_to_all x0 -> x1, blocking collectives: none -> 9.44 us  [gathered_tokens(): return lax.all_to_all(copies, 'core', 1, 1)]
    all_to_all x1, starting transfers between devices: 10 us -> 5.83 us  [gathered_tokens(): chips = lax.all_to_all(copies, 'cx', 1, 1)]
    ppermute x1, starting transfers between devices: 1.29 us -> 4.6 us  [passed_along(): return lax.ppermute(block, axis, route)]
  transfers between devices with their start and end apart: 5 -> 5, of which waited for: 3 -> 3; matrix products, arithmetic and copies ran while one was open for 24% -> 23% of each run, Pallas kernels for 0% -> 0%
where the time goes in v17:
time: 250 us; the launch traced here: 249 us
  blocking collectives  83.2 us (33%)
  waiting for transfers between devices  61.4 us (25%)
  matrix products  33.8 us (14%)
  starting transfers between devices  22.8 us (9%)
  local copies, waits for them, and re-layouts  22.8 us (9%)
  between operations  13.8 us (6%)
  other arithmetic  11 us (4%)
    all_gather x1, waiting for transfers between devices, across_z(): part = lax.all_gather(part, 'z', axis=2)  36.1 us
    all_to_all x1, blocking collectives, scattered_terms(): parts = lax.all_to_all(pairs, 'cx', 0, 0)  30 us
    all_to_all x1, waiting for transfers between devices, carried_in(): every = lax.all_to_all(copies, CTX, 0, 0)  24.1 us
    all_gather x1, blocking collectives, shards(): packed = lax.all_gather(packed, 'yh', axis=1)  22.1 us
    all_to_all x1, starting transfers between devices, carried_in(): every = lax.all_to_all(copies, CTX, 0, 0)  12.4 us
    all_to_all x1, blocking collectives, scattered_terms(): pairs = lax.all_to_all(terms, 'core', 0, 0)  12.3 us
    all_to_all x1, blocking collectives, gathered_tokens(): return lax.all_to_all(copies, 'core', 1, 1)  9.44 us
    all_gather x1, blocking collectives, across_yh(): return lax.all_gather(part, 'yh', axis=1)  9.36 us
  transfers between devices with their start and end apart: 5, of which 3 were waited for; matrix products, arithmetic and copies ran while one was open for 23% of the time, Pallas kernels for 0%

profile of v17, /device:TPU:1, one launch (start us, length us, event | category | flops | bytes accessed | tf_op | source)
XLA Modules:
  0.0 248.8 jit_solution(4527305992885962777)
XLA Ops:
  6.5 9.4 %all-gather = bf16[3,256,256]{2,1,0:T(8,128)(2,1)} all-gather(bf16[3,128,256]{2,1,0:T(8,128)(2,1)} %param.8), channel_id=2, replica_groups=mesh['yh'=2,'z'=16,'cx'=8,'core'=2] {'yh'}, dimensions={1}, use_global_device_ids=true | all-gather | bytes 589824 | tf_op jit(solution)/shard_map/all_gather | solution.py:85
  15.9 2.4 broadcast_in_dim.16
  18.4 5.8 %all-to-all-start = ((bf16[512,8,256]{2,0,1:T(8,128)(2,1)}), bf16[512,8,256]{2,0,1:T(8,128)(2,1)S(1)}, u32[]{:S(2)}, u32[]{:S(2)}) async-start(bf16[512,8,256]{2,0,1:T(8,128)(2,1)} %broadcast_in_dim.16), calls=%async_computation | async-start | bytes 4194304 | tf_op jit(solution)/shard_map/all_to_all | solution.py:65
  24.2 22.1 %all-gather.1 = bf16[256,256]{1,0:T(8,128)(2,1)S(1)} all-gather(bf16[256,128]{1,0:T(8,128)(2,1)S(1)} %copy-done.4), channel_id=3, replica_groups=mesh['yh'=2,'z'=16,'cx'=8,'core'=2] {'yh'}, dimensions={1}, use_global_device_ids=true | all-gather | bytes 196608 | tf_op jit(solution)/shard_map/all_gather | solution.py:107
  46.4 0.8 copy.133
  47.4 0.6 negate_exponential_fusion
  48.0 2.8 %multiply_reduce_fusion = (f32[64,256]{0,1:T(8,128)S(1)}, f32[64,256,16]{0,2,1:T(8,128)}) fusion(f32[256,16]{1,0:T(8,128)S(1)} %copy.142, f32[64]{0:T(128)S(1)} %iota_negate_fusion, f32[256,16]{1,0:T(8,128)S(1)} %copy.141), kind=kLoop, calls=%fused_computation.12 | loop fusion | flops 770048 | bytes 1147136 | tf_op jit(solution)/shard_map/reduce_sum | solution.py:35
  50.8 1.2 all-to-all-done
  52.5 9.4 %all_to_all.25 = bf16[512,2,8,256]{3,0,2,1:T(8,128)(2,1)S(1)} all-to-all(bf16[512,2,8,256]{3,0,2,1:T(8,128)(2,1)S(1)} %broadcast_in_dim.17), channel_id=1, replica_groups=mesh['yh'=2,'z'=16,'cx'=8,'core'=2] {'core'}, dimensions={1} | all-to-all | bytes 8388608 | tf_op jit(solution)/shard_map/all_to_all | solution.py:67
  62.0 4.6 %collective-permute-start = (bf16[2,2,8,256]{3,0,1,2:T(2,128)(2,1)S(1)}, bf16[2,2,8,256]{3,0,1,2:T(2,128)(2,1)S(1)}, u32[]{:S(2)}, u32[]{:S(2)}) collective-permute-start(bf16[2,2,8,256]{3,0,1,2:T(2,128)(2,1)S(1)} %copy.166), channel_id=1, source_target_pairs={{0,16},{16,32},{32,48},{48,64},{64,80},{80,96},{96,112},{112,128},... | collective-permute-start | bytes 49160 | tf_op jit(solution)/shard_map/ppermute | solution.py:16
  66.6 2.8 %rev.3 = f32[64,256,16]{0,2,1:T(8,128)S(1)} reverse(f32[64,256,16]{0,2,1:T(8,128)} %get-tuple-element.10), dimensions={0} | reverse | bytes 2097152 | tf_op jit(solution)/shard_map/rev | solution.py:41
  69.4 36.1 %all-gather.9.cloned.1.call-done = bf16[3,2,2048,256]{3,2,1,0:T(8,128)(2,1)} async-done(((bf16[3,2,128,256]{3,2,1,0:T(8,128)(2,1)}), bf16[3,2,2048,256]{3,2,1,0:T(8,128)(2,1)}) %all-gather.9.cloned.1.call-update) | async-done | bytes 6291472 | tf_op jit(solution)/shard_map/all_gather | solution.py:88
  105.5 3.7 %fusion.18 = bf16[3,2,256]{2,1,0:T(2,128)(2,1)S(1)} fusion(bf16[3,8,2,256,256]{4,3,2,1,0:T(8,128)(2,1)} %bitcast.96, bf16[2,2,8,256]{3,0,1,2:T(2,128)(2,1)S(1)} %collective-permute-done), kind=kOutput, calls=%fused_computation.24 | convolution fusion | flops 12584448 | bytes 6310912 | tf_op jit(solution)/shard_map/toxd,jxodc->jtc/dot_general | solution.py:94
  109.4 7.5 %fusion.14 = bf16[3,512,256]{1,2,0:T(8,128)(2,1)S(1)} fusion(bf16[3,8,2,256,256]{4,3,2,1,0:T(8,128)(2,1)} %bitcast.97, bf16[512,2,8,256]{3,0,2,1:T(8,128)(2,1)} %copy-done.1), kind=kOutput, calls=%fused_computation.21 | convolution fusion | flops 3221618688 | bytes 11272192 | tf_op jit(solution)/shard_map/toxd,jxodc->jtc/dot_general | solution.py:93
  117.2 1.4 fusion.9
  118.6 1.2 copy-done
  120.3 2.7 %fusion.41 = f32[256,8,16]{2,1,0:T(8,128)} fusion(bf16[8,64,256]{1,0,2:T(8,128)(2,1)S(1)} %copy.144, f32[64,256,16]{0,2,1:T(8,128)S(1)} %rev.3), kind=kOutput, calls=%fused_computation.74 | convolution fusion | flops 25165824 | bytes 1441792 | tf_op jit(solution)/shard_map/jcm,bjc->bcm/dot_general | solution.py:45
  123.1 1.5 copy.147
  124.9 0.9 broadcast_in_dim.21
  125.7 12.4 %all-to-all-start.2 = ((f32[32,256,16]{1,2,0:T(8,128)}), f32[32,256,16]{1,2,0:T(8,128)S(1)}, u32[]{:S(2)}, u32[]{:S(2)}) async-start(f32[32,256,16]{1,2,0:T(8,128)} %broadcast_in_dim.21), calls=%async_computation.2 | async-start | bytes 1048576 | tf_op jit(solution)/shard_map/all_to_all | solution.py:21
  138.1 0.8 copy.148
  138.9 3.8 %fusion.7 = f32[64,64,256]{2,1,0:T(8,128)} fusion(s32[64,64]{1,0:T(8,128)S(1)} %iota_subtract_fusion, f32[64,256]{0,1:T(8,128)S(1)} %get-tuple-element.9), kind=kOutput, calls=%fused_computation.10 | convolution fusion | flops 805568512 | bytes 4276224 | tf_op jit(solution)/shard_map/dot_general | solution.py:40
  142.7 9.2 %copy.145 = f32[64,64,256]{1,0,2:T(8,128)} copy(f32[64,64,256]{2,1,0:T(8,128)} %fusion.7) | data formatting | bytes 8388608 | tf_op jit(solution)/shard_map/dot_general | solution.py:40
  152.1 24.1 %all-to-all-done.2 = f32[32,256,16]{1,2,0:T(8,128)S(1)} async-done(((f32[32,256,16]{1,2,0:T(8,128)}), f32[32,256,16]{1,2,0:T(8,128)S(1)}, u32[]{:S(2)}, u32[]{:S(2)}) %all-to-all-start.2) | async-done | bytes 524320 | tf_op jit(solution)/shard_map/all_to_all | solution.py:21
  176.8 4.1 %fusion.5 = f32[256,8,64]{2,1,0:T(8,128)S(1)} fusion(f32[8,256,16]{2,0,1:T(8,128)S(1)} %copy.149, f32[256,16]{1,0:T(8,128)} %copy.148, f32[256,16]{1,0:T(8,128)S(1)} %copy.142, f32[64]{0:T(128)} %copy-done.10, f32[256,16]{1,0:T(8,128)S(1)} %copy.141), kind=kOutput, calls=%fused_computation.6 | convolution fusion | flops 25952256 | bytes 704768 | tf_op jit(solution)/shard_map/icm,bcm->bic/dot_general | solution.py:58
  180.9 8.9 %fusion.13 = f32[8,64,256]{1,0,2:T(8,128)S(1)} fusion(f32[256,8,64]{2,1,0:T(8,128)S(1)} %fusion.5, bf16[8,64,256]{1,0,2:T(8,128)(2,1)S(1)} %copy.144, f32[64,64,256]{1,0,2:T(8,128)} %copy.145), kind=kOutput, calls=%fused_computation.20 | convolution fusion | flops 100794368 | bytes 5505024 | tf_op jit(solution)/shard_map/ijc,bjc->bic/dot_general | solution.py:44
  190.5 3.0 %convert_bitcast_fusion = bf16[2,8,512,256]{2,3,1,0:T(8,128)(2,1)S(1)} fusion(bf16[256,8,2,256]{0,3,2,1:T(8,128)(2,1)} %bitcast.99, f32[512,256]{0,1:T(8,128)S(1)} %copy.151, f32[3,512,256]{1,2,0:T(8,128)} %copy-done, bf16[1,512,256]{1,2,0:T(8,128)(2,1)S(1)} %fusion.24, f32[256]{0:T(256)S(1)} %copy-done.9), kind=kOutput, calls=%fused_computation.3 | convolution fusion | flops 1076494336 | bytes 7603200 | tf_op jit(solution)/shard_map/tc,cyxe->yxte/dot_general | solution.py:120
  193.6 12.3 %all_to_all.26 = bf16[2,8,512,256]{2,3,1,0:T(8,128)(2,1)} all-to-all(bf16[2,8,512,256]{2,3,1,0:T(8,128)(2,1)S(1)} %convert_bitcast_fusion), channel_id=1, replica_groups=mesh['yh'=2,'z'=16,'cx'=8,'core'=2] {'core'}, dimensions={0} | all-to-all | bytes 8388608 | tf_op jit(solution)/shard_map/all_to_all | solution.py:71
  205.8 3.3 %reduce_sum.44 = bf16[8,512,256]{1,2,0:T(8,128)(2,1)S(1)} reduce(bf16[2,8,512,256]{2,3,1,0:T(8,128)(2,1)} %all_to_all.26, bf16[]{:T(256)} %constant.29.clone.1), dimensions={0}, to_apply=%region_2.3 | reduce | flops 1048576 | bytes 6291458 | tf_op jit(solution)/shard_map/reduce_sum | solution.py:72
  209.2 30.0 %all_to_all.27 = bf16[8,512,256]{1,2,0:T(8,128)(2,1)} all-to-all(bf16[8,512,256]{1,2,0:T(8,128)(2,1)S(1)} %reduce_sum.44), channel_id=1, replica_groups=mesh['yh'=2,'z'=16,'cx'=8,'core'=2] {'cx'}, dimensions={0} | all-to-all | bytes 4194304 | tf_op jit(solution)/shard_map/all_to_all | solution.py:73
  239.2 2.0 reduce_sum.45
  241.1 0.8 copy.153
  (65 shorter events, 3.5 us)
Async XLA Ops:
  6.5 98.9 %all-gather.9.cloned.1.call-start = ((), (), s32[]{:S(2)}) async-start(), calls=%async_computation.6 | async-start | bytes 6684672 | tf_op jit(solution)/shard_map/all_gather | solution.py:88
  18.3 5.9 %copy-start.4 = (bf16[256,128]{1,0:T(8,128)(2,1)S(1)}, bf16[256,128]{1,0:T(8,128)(2,1)}, u32[]{:S(2)}) copy-start(bf16[256,128]{1,0:T(8,128)(2,1)} %param.13) | copy-start | bytes 196612
  18.3 28.8 %copy-start.7 = (f32[256,16]{0,1:T(8,128)S(1)}, f32[256,16]{0,1:T(8,128)}, u32[]{:S(2)}) copy-start(f32[256,16]{0,1:T(8,128)} %param.11) | copy-start | bytes 49156
  18.3 28.9 %copy-start.2 = (f32[256,16]{0,1:T(8,128)S(1)}, f32[256,16]{0,1:T(8,128)}, u32[]{:S(2)}) copy-start(f32[256,16]{0,1:T(8,128)} %param.10) | copy-start | bytes 49156
  18.4 33.7 %all-to-all-start = ((bf16[512,8,256]{2,0,1:T(8,128)(2,1)}), bf16[512,8,256]{2,0,1:T(8,128)(2,1)S(1)}, u32[]{:S(2)}, u32[]{:S(2)}) async-start(bf16[512,8,256]{2,0,1:T(8,128)(2,1)} %broadcast_in_dim.16), calls=%async_computation | async-start | bytes 4194304 | tf_op jit(solution)/shard_map/all_to_all | solution.py:65
  24.2 166.3 %all-gather.7.cloned.1.call-start = ((), (), s32[]{:S(2)}) async-start(), calls=%async_computation.5 | async-start | bytes 2228224 | tf_op jit(solution)/shard_map/all_gather | solution.py:109
  47.4 5.1 %copy-start.10 = (f32[64]{0:T(128)}, f32[64]{0:T(128)S(1)}, u32[]{:S(2)}) copy-start(f32[64]{0:T(128)S(1)} %iota_negate_fusion) | copy-start | bytes 772
  52.5 14.1 %copy-start.8 = (f32[3,3,256]{2,1,0:T(4,128)S(1)}, f32[3,3,256]{2,1,0:T(4,128)}, u32[]{:S(2)}) copy-start(f32[3,3,256]{2,1,0:T(4,128)} %param.9) | copy-start | bytes 27652
  61.9 4.7 %copy-start.1 = (bf16[512,2,8,256]{3,0,2,1:T(8,128)(2,1)}, bf16[512,2,8,256]{3,0,2,1:T(8,128)(2,1)S(1)}, u32[]{:S(2)}) copy-start(bf16[512,2,8,256]{3,0,2,1:T(8,128)(2,1)S(1)} %all_to_all.25) | copy-start | bytes 12582916
  62.0 7.4 %collective-permute-start = (bf16[2,2,8,256]{3,0,1,2:T(2,128)(2,1)S(1)}, bf16[2,2,8,256]{3,0,1,2:T(2,128)(2,1)S(1)}, u32[]{:S(2)}, u32[]{:S(2)}) collective-permute-start(bf16[2,2,8,256]{3,0,1,2:T(2,128)(2,1)S(1)} %copy.166), channel_id=1, source_target_pairs={{0,16},{16,32},{32,48},{48,64},{64,80},{80,96},{96,112},{112,128},... | collective-permute-start | bytes 49160 | tf_op jit(solution)/shard_map/ppermute | solution.py:16
  118.6 1.2 copy-start
  120.3 4.3 %copy-start.3 = (f32[256,16]{0,1:T(8,128)S(1)}, f32[256,16]{0,1:T(8,128)}, u32[]{:S(2)}) copy-start(f32[256,16]{0,1:T(8,128)} %get-tuple-element.17) | copy-start | bytes 49156
  120.3 4.3 %copy-start.6 = (f32[256,16]{0,1:T(8,128)S(1)}, f32[256,16]{0,1:T(8,128)}, u32[]{:S(2)}) copy-start(f32[256,16]{0,1:T(8,128)} %get-tuple-element.16) | copy-start | bytes 49156
  123.1 15.1 %copy-start.5 = (f32[256,16]{0,1:T(8,128)S(1)}, f32[256,16]{0,1:T(8,128)}, u32[]{:S(2)}) copy-start(f32[256,16]{0,1:T(8,128)} %get-tuple-element.15) | copy-start | bytes 49156
  125.7 50.4 %all-to-all-start.2 = ((f32[32,256,16]{1,2,0:T(8,128)}), f32[32,256,16]{1,2,0:T(8,128)S(1)}, u32[]{:S(2)}, u32[]{:S(2)}) async-start(f32[32,256,16]{1,2,0:T(8,128)} %broadcast_in_dim.21), calls=%async_computation.2 | async-start | bytes 1048576 | tf_op jit(solution)/shard_map/all_to_all | solution.py:21
  189.8 0.7 copy-start.9
Sparse Core Ops, SparseCore 0:
  16.0 89.3 all-gather.8
  107.5 79.6 all-gather.6

commit v18 on v16

--- a/solution.py
+++ b/solution.py
@@ -113,8 +113,10 @@
         starts = starts + offsets * incoming[None]
         conv = finish(inner, starts, heads, values, skip)
         hidden = (query * conv).astype(jnp.bfloat16)
-        out_w = jnp.transpose(packed.reshape(width, lanes // 2, 2, -1), (0, 2, 1, 3))
-        terms = jnp.einsum("tc,cyxe->yxte", hidden, out_w, preferred_element_type=jnp.float32)
+        out_w = packed.reshape(width, lanes // 2, 2, -1)
+        terms = jnp.stack(
+            [jnp.einsum("tc,cxe->xte", hidden, out_w[:, :, y], preferred_element_type=jnp.float32) for y in range(2)]
+        )
         return scattered_terms(terms.astype(jnp.bfloat16))
 
     return shards

time: 250 us -> 250 us (level)
  local copies, waits for them, and re-layouts: 24.2 us -> 21.5 us
  transfers between devices with their start and end apart: 5 -> 5, of which waited for: 3 -> 3; matrix products, arithmetic and copies ran while one was open for 24% -> 23% of each run, Pallas kernels for 0% -> 0%
where the time goes in v18:
time: 250 us; the launch traced here: 249 us
  blocking collectives  72.6 us (29%)
  waiting for transfers between devices  71.9 us (29%)
  matrix products  34.1 us (14%)
  starting transfers between devices  23.8 us (10%)
  local copies, waits for them, and re-layouts  21.5 us (9%)
  between operations  13.8 us (6%)
  other arithmetic  11.3 us (5%)
    all_to_all x1, blocking collectives, scattered_terms(): parts = lax.all_to_all(pairs, 'cx', 0, 0)  30.2 us
    all_to_all x1, waiting for transfers between devices, gathered_tokens(): return lax.all_to_all(copies, CH, 1, 1)  29 us
    all_to_all x1, waiting for transfers between devices, carried_in(): every = lax.all_to_all(copies, CTX, 0, 0)  24.2 us
    all_gather x1, blocking collectives, shards(): packed = lax.all_gather(packed, 'yh', axis=1)  20.9 us
    all_gather x1, waiting for transfers between devices, across_z(): part = lax.all_gather(part, 'z', axis=2)  18.7 us
    all_to_all x1, starting transfers between devices, carried_in(): every = lax.all_to_all(copies, CTX, 0, 0)  12.4 us
    all_to_all x1, blocking collectives, scattered_terms(): pairs = lax.all_to_all(terms, 'core', 0, 0)  12.1 us
    all_to_all x1, starting transfers between devices, gathered_tokens(): return lax.all_to_all(copies, CH, 1, 1)  10.1 us
  transfers between devices with their start and end apart: 5, of which 3 were waited for; matrix products, arithmetic and copies ran while one was open for 23% of the time, Pallas kernels for 0%

profile of v18, /device:TPU:1, one launch (start us, length us, event | category | flops | bytes accessed | tf_op | source)
XLA Modules:
  0.0 249.1 jit_solution(10740553233613562247)
XLA Ops:
  6.5 9.4 %all-gather = bf16[3,256,256]{2,1,0:T(8,128)(2,1)} all-gather(bf16[3,128,256]{2,1,0:T(8,128)(2,1)} %param.8), channel_id=2, replica_groups=mesh['yh'=2,'z'=16,'cx'=8,'core'=2] {'yh'}, dimensions={1}, use_global_device_ids=true | all-gather | bytes 589824 | tf_op jit(solution)/shard_map/all_gather | solution.py:82
  15.9 3.4 %broadcast_in_dim.14 = bf16[512,16,256]{2,0,1:T(8,128)(2,1)} broadcast(bf16[512,256]{1,0:T(8,128)(2,1)} %param.7), dimensions={0,2} | broadcast | bytes 4456448 | tf_op jit(solution)/shard_map/broadcast_in_dim | solution.py:63
  19.3 10.1 %all-to-all-start = ((bf16[512,16,256]{2,0,1:T(8,128)(2,1)}), bf16[512,16,256]{2,0,1:T(8,128)(2,1)}, u32[]{:S(2)}, u32[]{:S(2)}) async-start(bf16[512,16,256]{2,0,1:T(8,128)(2,1)} %broadcast_in_dim.14), calls=%async_computation | async-start | bytes 8388608 | tf_op jit(solution)/shard_map/all_to_all | solution.py:64
  29.5 20.9 %all-gather.1 = bf16[256,256]{1,0:T(8,128)(2,1)S(1)} all-gather(bf16[256,128]{1,0:T(8,128)(2,1)S(1)} %copy-done.5), channel_id=3, replica_groups=mesh['yh'=2,'z'=16,'cx'=8,'core'=2] {'yh'}, dimensions={1}, use_global_device_ids=true | all-gather | bytes 196608 | tf_op jit(solution)/shard_map/all_gather | solution.py:104
  50.3 0.7 copy.134
  52.0 1.2 multiply_reduce_fusion
  53.2 29.0 %all-to-all-done = bf16[512,16,256]{2,0,1:T(8,128)(2,1)} async-done(((bf16[512,16,256]{2,0,1:T(8,128)(2,1)}), bf16[512,16,256]{2,0,1:T(8,128)(2,1)}, u32[]{:S(2)}, u32[]{:S(2)}) %all-to-all-start) | async-done | bytes 4194336 | tf_op jit(solution)/shard_map/all_to_all | solution.py:64
  82.2 0.9 slice.134
  83.0 1.3 collective-permute-start
  84.3 2.3 rev.3
  86.7 18.7 %all-gather.9.cloned.1.call-done = bf16[3,2,2048,256]{3,2,1,0:T(8,128)(2,1)} async-done(((bf16[3,2,128,256]{3,2,1,0:T(8,128)(2,1)}), bf16[3,2,2048,256]{3,2,1,0:T(8,128)(2,1)}) %all-gather.9.cloned.1.call-update) | async-done | bytes 6291472 | tf_op jit(solution)/shard_map/all_gather | solution.py:85
  105.4 3.7 %fusion.15 = bf16[3,2,256]{2,1,0:T(2,128)(2,1)S(1)} fusion(bf16[3,16,256,256]{3,2,1,0:T(8,128)(2,1)} %bitcast.84, bf16[2,16,256]{2,0,1:T(2,128)(2,1)S(1)} %collective-permute-done), kind=kOutput, calls=%fused_computation.23 | convolution fusion | flops 12584448 | bytes 6310912 | tf_op jit(solution)/shard_map/tkd,jkdc->jtc/dot_general | solution.py:91
  109.3 7.5 %fusion.11 = bf16[3,512,256]{1,2,0:T(8,128)(2,1)S(1)} fusion(bf16[3,16,256,256]{3,2,1,0:T(8,128)(2,1)} %bitcast.85, bf16[512,16,256]{2,0,1:T(8,128)(2,1)} %all-to-all-done), kind=kOutput, calls=%fused_computation.20 | convolution fusion | flops 3221618688 | bytes 11272192 | tf_op jit(solution)/shard_map/tkd,jkdc->jtc/dot_general | solution.py:90
  117.2 1.4 fusion.6
  119.1 3.3 %fusion.33 = f32[256,8,16]{2,1,0:T(8,128)S(1)} fusion(bf16[8,64,256]{1,0,2:T(8,128)(2,1)S(1)} %copy.142, f32[64,256,16]{0,2,1:T(8,128)} %rev.3), kind=kOutput, calls=%fused_computation.70 | convolution fusion | flops 25165824 | bytes 1441792 | tf_op jit(solution)/shard_map/jcm,bjc->bcm/dot_general | solution.py:45
  122.8 0.8 multiply_add_fusion.1
  123.5 0.7 multiply_add_fusion.2
  124.5 0.9 broadcast_in_dim.18
  125.4 12.4 %all-to-all-start.1 = ((f32[32,256,16]{1,2,0:T(8,128)}), f32[32,256,16]{1,2,0:T(8,128)S(1)}, u32[]{:S(2)}, u32[]{:S(2)}) async-start(f32[32,256,16]{1,2,0:T(8,128)} %broadcast_in_dim.18), calls=%async_computation.1 | async-start | bytes 1048576 | tf_op jit(solution)/shard_map/all_to_all | solution.py:21
  137.8 0.8 copy.146
  138.6 3.8 %fusion.4 = f32[64,64,256]{2,1,0:T(8,128)} fusion(s32[64,64]{1,0:T(8,128)S(1)} %iota_subtract_fusion, f32[64,256]{0,1:T(8,128)S(1)} %get-tuple-element.9), kind=kOutput, calls=%fused_computation.9 | convolution fusion | flops 805568512 | bytes 4276224 | tf_op jit(solution)/shard_map/dot_general | solution.py:40
  142.4 9.2 %copy.143 = f32[64,64,256]{1,0,2:T(8,128)} copy(f32[64,64,256]{2,1,0:T(8,128)} %fusion.4) | data formatting | bytes 8388608 | tf_op jit(solution)/shard_map/dot_general | solution.py:40
  151.8 24.2 %all-to-all-done.1 = f32[32,256,16]{1,2,0:T(8,128)S(1)} async-done(((f32[32,256,16]{1,2,0:T(8,128)}), f32[32,256,16]{1,2,0:T(8,128)S(1)}, u32[]{:S(2)}, u32[]{:S(2)}) %all-to-all-start.1) | async-done | bytes 524320 | tf_op jit(solution)/shard_map/all_to_all | solution.py:21
  176.7 4.1 %fusion.2 = f32[256,8,64]{2,1,0:T(8,128)S(1)} fusion(f32[8,256,16]{2,0,1:T(8,128)S(1)} %copy.147, f32[256,16]{1,0:T(8,128)} %copy.146, f32[256,16]{1,0:T(8,128)S(1)} %copy-done.3, f32[64]{0:T(128)} %copy-done.10, f32[256,16]{1,0:T(8,128)S(1)} %copy.139), kind=kOutput, calls=%fused_computation.5 | convolution fusion | flops 25952256 | bytes 704768 | tf_op jit(solution)/shard_map/icm,bcm->bic/dot_general | solution.py:58
  180.7 8.9 %fusion.10 = f32[8,64,256]{1,0,2:T(8,128)S(1)} fusion(f32[256,8,64]{2,1,0:T(8,128)S(1)} %fusion.2, bf16[8,64,256]{1,0,2:T(8,128)(2,1)S(1)} %copy.142, f32[64,64,256]{1,0,2:T(8,128)} %copy.143), kind=kOutput, calls=%fused_computation.19 | convolution fusion | flops 100794368 | bytes 5505024 | tf_op jit(solution)/shard_map/ijc,bjc->bic/dot_general | solution.py:44
  190.6 2.1 convert_bitcast_fusion.1
  192.7 0.7 convert_bitcast_fusion
  193.8 12.1 %all_to_all.20 = bf16[2,8,512,256]{2,3,1,0:T(8,128)(2,1)} all-to-all(bf16[2,8,512,256]{2,3,1,0:T(8,128)(2,1)S(1)} %pad_maximum_fusion), channel_id=1, replica_groups=mesh['yh'=2,'z'=16,'cx'=8,'core'=2] {'core'}, dimensions={0} | all-to-all | bytes 8388608 | tf_op jit(solution)/shard_map/all_to_all | solution.py:68
  205.9 3.3 %reduce_sum.44 = bf16[8,512,256]{1,2,0:T(8,128)(2,1)S(1)} reduce(bf16[2,8,512,256]{2,3,1,0:T(8,128)(2,1)} %all_to_all.20, bf16[]{:T(256)} %constant.29.clone.1), dimensions={0}, to_apply=%region_2.3 | reduce | flops 1048576 | bytes 6291458 | tf_op jit(solution)/shard_map/reduce_sum | solution.py:69
  209.2 30.2 %all_to_all.21 = bf16[8,512,256]{1,2,0:T(8,128)(2,1)} all-to-all(bf16[8,512,256]{1,2,0:T(8,128)(2,1)S(1)} %reduce_sum.44), channel_id=1, replica_groups=mesh['yh'=2,'z'=16,'cx'=8,'core'=2] {'cx'}, dimensions={0} | all-to-all | bytes 4194304 | tf_op jit(solution)/shard_map/all_to_all | solution.py:70
  239.4 2.0 reduce_sum.45
  241.4 0.8 copy.153
  (65 shorter events, 4.6 us)
Async XLA Ops:
  6.5 98.9 %all-gather.9.cloned.1.call-start = ((), (), s32[]{:S(2)}) async-start(), calls=%async_computation.5 | async-start | bytes 6684672 | tf_op jit(solution)/shard_map/all_gather | solution.py:85
  19.3 10.1 %copy-start.5 = (bf16[256,128]{1,0:T(8,128)(2,1)S(1)}, bf16[256,128]{1,0:T(8,128)(2,1)}, u32[]{:S(2)}) copy-start(bf16[256,128]{1,0:T(8,128)(2,1)} %param.13) | copy-start | bytes 196612
  19.3 31.8 %copy-start.7 = (f32[256,16]{0,1:T(8,128)S(1)}, f32[256,16]{0,1:T(8,128)}, u32[]{:S(2)}) copy-start(f32[256,16]{0,1:T(8,128)} %param.11) | copy-start | bytes 49156
  19.3 31.9 %copy-start.1 = (f32[256,16]{0,1:T(8,128)S(1)}, f32[256,16]{0,1:T(8,128)}, u32[]{:S(2)}) copy-start(f32[256,16]{0,1:T(8,128)} %param.10) | copy-start | bytes 49156
  19.3 62.8 %all-to-all-start = ((bf16[512,16,256]{2,0,1:T(8,128)(2,1)}), bf16[512,16,256]{2,0,1:T(8,128)(2,1)}, u32[]{:S(2)}, u32[]{:S(2)}) async-start(bf16[512,16,256]{2,0,1:T(8,128)(2,1)} %broadcast_in_dim.14), calls=%async_computation | async-start | bytes 8388608 | tf_op jit(solution)/shard_map/all_to_all | solution.py:64
  29.4 54.9 %copy-start.8 = (f32[3,3,256]{2,1,0:T(4,128)S(1)}, f32[3,3,256]{2,1,0:T(4,128)}, u32[]{:S(2)}) copy-start(f32[3,3,256]{2,1,0:T(4,128)} %param.9) | copy-start | bytes 27652
  29.4 161.1 %all-gather.7.cloned.1.call-start = ((), (), s32[]{:S(2)}) async-start(), calls=%async_computation.4 | async-start | bytes 2228224 | tf_op jit(solution)/shard_map/all_gather | solution.py:106
  51.3 35.3 %copy-start.2 = (f32[256,16]{1,0:T(8,128)}, f32[256,16]{1,0:T(8,128)S(1)}, u32[]{:S(2)}) copy-start(f32[256,16]{1,0:T(8,128)S(1)} %copy.140) | copy-start | bytes 49156
  51.4 30.8 %copy-start.10 = (f32[64]{0:T(128)}, f32[64]{0:T(128)S(1)}, u32[]{:S(2)}) copy-start(f32[64]{0:T(128)S(1)} %iota_negate_fusion) | copy-start | bytes 772
  83.0 3.7 %collective-permute-start = (bf16[2,16,256]{2,0,1:T(2,128)(2,1)S(1)}, bf16[2,16,256]{2,0,1:T(2,128)(2,1)S(1)}, u32[]{:S(2)}, u32[]{:S(2)}) collective-permute-start(bf16[2,16,256]{2,0,1:T(2,128)(2,1)S(1)} %slice.134), channel_id=1, source_target_pairs={{0,16},{16,32},{32,48},{48,64},{64,80},{80,96},{96,112},{112,128},... | collective-permute-start | bytes 49160 | tf_op jit(solution)/shard_map/ppermute | solution.py:16
  122.8 15.0 %copy-start.6 = (f32[256,16]{0,1:T(8,128)S(1)}, f32[256,16]{0,1:T(8,128)}, u32[]{:S(2)}) copy-start(f32[256,16]{0,1:T(8,128)} %get-tuple-element.15) | copy-start | bytes 49156
  125.4 50.6 %all-to-all-start.1 = ((f32[32,256,16]{1,2,0:T(8,128)}), f32[32,256,16]{1,2,0:T(8,128)S(1)}, u32[]{:S(2)}, u32[]{:S(2)}) async-start(f32[32,256,16]{1,2,0:T(8,128)} %broadcast_in_dim.18), calls=%async_computation.1 | async-start | bytes 1048576 | tf_op jit(solution)/shard_map/all_to_all | solution.py:21
  142.4 9.3 %copy-start.4 = (f32[256,16]{0,1:T(8,128)S(1)}, f32[256,16]{0,1:T(8,128)}, u32[]{:S(2)}) copy-start(f32[256,16]{0,1:T(8,128)} %get-tuple-element.17) | copy-start | bytes 49156
  151.6 25.1 %copy-start.3 = (f32[256,16]{1,0:T(8,128)S(1)}, f32[256,16]{1,0:T(8,128)}, u32[]{:S(2)}) copy-start(f32[256,16]{1,0:T(8,128)} %copy-done.2) | copy-start | bytes 49156
  189.7 0.7 copy-start.9
  190.6 2.1 copy-start
Sparse Core Ops, SparseCore 0:
  16.0 89.3 all-gather.8
  107.5 79.5 all-gather.6
